TPU v7x, 32 devices: a whole 2x2x4 slice. The times are simulated.
32 devices in a mesh: shot: 4 (over y, core), mesh: 8 (over z, x).
Axes of the slice: x: 2, y: 2, z: 4, core: 2. Of those that a mesh axis runs over, the one named last changes fastest.
Arguments:
- adjoint_state: float32 [4, 13, 35, 1024], P('shot', None, None, 'mesh'), may hold values from -6 to 6
- forward_states: float32 [4, 2, 13, 35, 1024], P('shot', None, None, None, 'mesh'), may hold values from -6 to 6
- material: float32 [6, 35, 1024], P(None, None, 'mesh'), may hold values from 0.5 to 2
- coupling: float32 [3, 6, 13, 13], replicated, may hold values from -0.375 to 0.375
- metric: float32 [3, 3, 1024], P(None, None, 'mesh'), may hold values from -4 to 4
- face_normals: float32 [3, 4, 1024], P(None, None, 'mesh'), may hold values from -4 to 4
- face_scale: float32 [4, 1024], P(None, 'mesh'), may hold values from 1 to 3
- face_neighbours: int32 [4, 1024], P(None, 'mesh'), may hold values from 0 to 639, as said below
- face_orientation: int32 [4, 1024], P(None, 'mesh'), may hold values from 0 to 5
- send_faces: int32 [1024], P('mesh'), may hold values from 0 to 511, as said below
- history_steps: float32 [5, 6, 35, 1024], P(None, None, None, 'mesh')
- history_changes: float32 [5, 6, 35, 1024], P(None, None, None, 'mesh'), as said below
Outputs:
- adjoint_final: float32 [4, 13, 35, 1024], P('shot', None, None, 'mesh')
- direction: float32 [6, 35, 1024], P(None, None, ('mesh', 'shot'))
Inputs may be any that keep to these rules, and one draw needn't show every extreme that they name: `face_neighbours`: local faces of a partition are numbered x * 128 + e. Each face either forms a pair with another local face (each names the other) or reads exactly one of the 128 ghost slots, and every ghost slot is read by exactly one face; on every partition the face that reads slot 512 + j is send_faces[j] and the face that reads slot 576 + j is send_faces[64 + j]. `send_faces`: the 128 entries of one partition are distinct local face numbers. `history_changes`: for every stored pair, s_i . y_i is positive.
All inputs are finite; a program needn't handle non-finite values.
Results may differ from a plain program's by a relative error of at most 0.0003.
Values sent between devices are 32-bit elements; how exact they have to be, the bound alone decides.
No kernel may reach another device: no remote copies, remote signals or barrier semaphores. Data moves between devices by JAX's collectives and lax.ppermute only.
A program may use at most 64 MiB of HBM per device.

v0:
```python
import math

import jax
import jax.numpy as jnp
import numpy as np
from jax import lax
from jax.sharding import PartitionSpec as P

HIGH = lax.Precision.HIGHEST
STEP_SIZE = 0.02


def padded(x, sides, width):
    for axis, dim in sides:
        devices, length = (lax.axis_size(axis), x.shape[dim])
        up = [(i, (i + 1) % devices) for i in range(devices - 1)]
        down = [(j, i) for i, j in up]
        last = lax.slice_in_dim(x, length - width, length, axis=dim)
        first = lax.slice_in_dim(x, 0, width, axis=dim)
        before = lax.ppermute(last, axis, up)
        after = lax.ppermute(first, axis, down)
        x = jnp.concatenate([before, x, after], axis=dim)
    return x


def invert_matrix(matrix):
    order_count = matrix.shape[0]
    working = np.concatenate([matrix * 1.0, np.eye(order_count)], axis=1)
    for column in range(order_count):
        pivot_row = column + int(np.argmax(np.abs(working[column:, column])))
        working[[column, pivot_row]] = working[[pivot_row, column]]
        working[column] = working[column] / working[column, column]
        for target in range(order_count):
            if target != column:
                working[target] = working[target] - working[target, column] * working[column]
    return working[:, order_count:]


def basis_tables():
    points = [
        (across, along, upward)
        for upward in range(5)
        for along in range(5 - upward)
        for across in range(5 - upward - along)
    ]
    exponents = np.array(points) * 1.0
    coords = exponents / 4.0
    vander = np.prod(coords[:, None, :] ** exponents[None, :, :], axis=2)
    inverse = invert_matrix(vander)
    derivs = []
    for direction_axis in range(3):
        lowered = np.maximum(exponents - np.eye(3)[direction_axis], 0.0)
        slopes = exponents[None, :, direction_axis] * np.prod(
            coords[:, None, :] ** lowered[None, :, :], axis=2
        )
        derivs.append(slopes @ inverse)
    moments = np.array(
        [
            [
                math.factorial(first[0] + second[0])
                * math.factorial(first[1] + second[1])
                * math.factorial(first[2] + second[2])
                / math.factorial(sum(first) + sum(second) + 3)
                for second in points
            ]
            for first in points
        ]
    )
    mass_matrix = inverse.T @ moments @ inverse
    lattice = [(across, along) for along in range(5) for across in range(5 - along)]
    lattice_powers = np.array(lattice) * 1.0
    face_vander = np.prod((lattice_powers / 4.0)[:, None, :] ** lattice_powers[None, :, :], axis=2)
    face_inverse = invert_matrix(face_vander)
    face_moments = np.array(
        [
            [
                math.factorial(first[0] + second[0])
                * math.factorial(first[1] + second[1])
                / math.factorial(sum(first) + sum(second) + 2)
                for second in lattice
            ]
            for first in lattice
        ]
    )
    face_mass = face_inverse.T @ face_moments @ face_inverse
    numbers = {point: number for number, point in enumerate(points)}
    face_points = [
        [(across, along, 0) for across, along in lattice],
        [(across, 0, along) for across, along in lattice],
        [(0, across, along) for across, along in lattice],
        [(across, along, 4 - across - along) for across, along in lattice],
    ]
    face_nodes = np.array(
        [[numbers[point] for point in listing] for listing in face_points], np.int32
    )
    mass_inverse = invert_matrix(mass_matrix)
    lift_tables = []
    for face_number in range(4):
        selector = np.eye(35)[face_nodes[face_number]]
        lift_tables.append(mass_inverse @ selector.T @ face_mass)
    orderings = [(0, 1, 2), (1, 2, 0), (2, 0, 1), (1, 0, 2), (0, 2, 1), (2, 1, 0)]
    lattice_numbers = {point: number for number, point in enumerate(lattice)}
    triples = [(across, along, 4 - across - along) for across, along in lattice]
    turn_nodes = np.array(
        [
            [lattice_numbers[triple[ordering[0]], triple[ordering[1]]] for triple in triples]
            for ordering in orderings
        ],
        np.int32,
    )
    return (
        jnp.asarray(np.stack(derivs), jnp.float32),
        jnp.asarray(np.stack(lift_tables), jnp.float32),
        face_nodes,
        turn_nodes,
    )


def spatial_of(field, metric, derivs):
    reference_grads = jnp.einsum("rab,fbe->rfae", derivs, field, precision=HIGH)
    rows = []
    for direction_axis in range(3):
        total = metric[0, direction_axis] * reference_grads[0]
        total = total + metric[1, direction_axis] * reference_grads[1]
        total = total + metric[2, direction_axis] * reference_grads[2]
        rows.append(total)
    return jnp.stack(rows)


def volume_term(adjoint, material, coupling, metric, derivs):
    spatial = spatial_of(adjoint, metric, derivs)
    mixing = jnp.einsum("dpfg,dfae->pgae", coupling, spatial, precision=HIGH)
    return jnp.sum(material[:, None] * mixing, axis=0)


def kernel_term(adjoint, forward, coupling, metric, derivs):
    spatial = spatial_of(forward, metric, derivs)
    mixing = jnp.einsum("dpfg,dgae->pfae", coupling, spatial, precision=HIGH)
    return jnp.sum(mixing * adjoint[None], axis=1)


def surface_term(jump_trace, face_material, face_normals, face_scale, coupling, lift_tables):
    weighted = face_normals[:, None, None] * jump_trace[None]
    mixing = jnp.einsum("dpfg,dfnxe->pgnxe", coupling, weighted, precision=HIGH)
    face_flux = 0.5 * jnp.sum(face_material[:, None] * mixing, axis=0) + 0.5 * jump_trace
    return jnp.einsum(
        "xan,fnxe->fae", lift_tables, face_flux * face_scale[None, None], precision=HIGH
    )


def search_direction(total_grad, step_rows, change_rows, combine_sums):
    pairs = step_rows.shape[0]
    summed = combine_sums(
        jnp.concatenate(
            [
                jnp.sum(step_rows * change_rows, axis=(1, 2, 3)),
                jnp.sum(change_rows[pairs - 1] * change_rows[pairs - 1])[None],
            ]
        )
    )
    curvature = summed[:pairs]
    alphas = [None] * pairs
    work = total_grad
    for slot in reversed(range(pairs)):
        alphas[slot] = combine_sums(jnp.sum(step_rows[slot] * work)) / curvature[slot]
        work = work - alphas[slot] * change_rows[slot]
    work = curvature[pairs - 1] / summed[pairs] * work
    for slot in range(pairs):
        beta_now = combine_sums(jnp.sum(change_rows[slot] * work)) / curvature[slot]
        work = work + (alphas[slot] - beta_now) * step_rows[slot]
    return -work


def shards(
    adjoint_state,
    forward_states,
    material,
    coupling,
    metric,
    face_normals,
    face_scale,
    face_neighbours,
    face_orientation,
    send_faces,
    history_steps,
    history_changes,
):
    derivs, lift_tables, face_nodes, turn_nodes = basis_tables()
    fields = adjoint_state.shape[1]
    elements = adjoint_state.shape[3]
    node_count = material.shape[1]
    params = material.shape[0]
    face_width = face_nodes.shape[1]
    border = send_faces.shape[0] // 2
    slot_count = 4 * elements + 2 * border
    adjoint = adjoint_state[0]
    face_material = material[:, face_nodes.T, :]
    neighbours = face_neighbours.reshape(-1)
    orient = face_orientation.reshape(-1)
    node_pick = jnp.zeros((face_width, 4 * elements), jnp.int32)
    for option in range(turn_nodes.shape[0]):
        node_pick = (
            node_pick
            + (orient == option).astype(jnp.int32)[None, :]
            * jnp.asarray(turn_nodes[option], jnp.int32)[:, None]
        )
    flat_index = (node_pick * slot_count + neighbours[None, :]).reshape(-1)
    gradient = jnp.zeros((params, node_count, elements), jnp.float32)
    for step_index in range(forward_states.shape[1]):
        inner_trace = adjoint[:, face_nodes.T, :]
        flat_trace = inner_trace.reshape(fields, face_width, 4 * elements)
        sent_traces = flat_trace[:, :, send_faces]
        extended = padded(sent_traces, (("mesh", 2),), border)
        ghosts = jnp.concatenate(
            [flat_trace, extended[:, :, :border], extended[:, :, 3 * border :]], axis=2
        )
        turned = ghosts.reshape(fields, face_width * slot_count)[:, flat_index]
        jump_trace = turned.reshape(fields, face_width, 4, elements) - inner_trace
        change = volume_term(adjoint, material, coupling, metric, derivs) + surface_term(
            jump_trace, face_material, face_normals, face_scale, coupling, lift_tables
        )
        adjoint = adjoint + STEP_SIZE * change
        gradient = gradient + STEP_SIZE * kernel_term(
            adjoint, forward_states[0, step_index], coupling, metric, derivs
        )
    total_grad = lax.psum(gradient, "shot")

    def combine_sums(values):
        return lax.psum(values, "mesh")

    result = search_direction(total_grad, history_steps, history_changes, combine_sums)
    share_width = elements // lax.axis_size("shot")
    result = lax.dynamic_slice_in_dim(result, lax.axis_index("shot") * share_width, share_width, 2)
    return (adjoint[None], result)


def solution(mesh):
    placed = (
        P("shot", None, None, "mesh"),
        P("shot", None, None, None, "mesh"),
        P(None, None, "mesh"),
        P(),
        P(None, None, "mesh"),
        P(None, None, "mesh"),
        P(None, "mesh"),
        P(None, "mesh"),
        P(None, "mesh"),
        P("mesh"),
        P(None, None, None, "mesh"),
        P(None, None, None, "mesh"),
    )
    return jax.shard_map(
        shards,
        mesh=mesh,
        in_specs=placed,
        out_specs=(P("shot", None, None, "mesh"), P(None, None, ("mesh", "shot"))),
        check_vma=False,
    )
```

profile of v0, /device:TPU:0, one launch (start us, length us, event | category | flops | bytes accessed | tf_op | source)
XLA Modules:
  0.0 404.9 jit_solution(5212843150309654842)
XLA Ops:
  7.9 1.0 copy.410
  9.8 3.6 copy.157
  13.5 3.8 gather_fusion.2
  17.4 2.4 fusion.84
  19.8 1.4 collective-permute-start.1
  21.2 6.3 %collective-permute-start = (f32[13,15,64]{1,0,2:T(8,128)}, f32[13,15,64]{1,0,2:T(8,128)}, u32[]{:S(2)}, u32[]{:S(2)}) collective-permute-start(f32[13,15,64]{1,0,2:T(8,128)} %get-tuple-element.22), channel_id=1, source_target_pairs={{0,1},{1,2},{2,3},{3,4},{4,5},{5,6},{6,7},{8,9},{9,10},{10,11},{11... | collective-permute-start | bytes 149768 | tf_op jit(solution)/shard_map/ppermute | solution.py:20
  27.5 0.8 fusion.85
  28.4 0.7 multiply_reduce_fusion
  29.4 0.8 convolution_bitcast_fusion.3
  30.7 0.8 convolution_bitcast_fusion.1
  31.8 0.8 convolution_bitcast_fusion
  33.5 2.3 fusion.5
  35.8 1.0 maximum_bitcast_fusion.2
  36.8 1.1 maximum_bitcast_fusion.3
  37.9 0.8 gather_fusion
  38.7 0.8 copy.222
  39.6 1.3 copy.159
  40.8 7.6 %collective-permute-done = f32[13,15,64]{1,0,2:T(8,128)} collective-permute-done((f32[13,15,64]{1,0,2:T(8,128)}, f32[13,15,64]{1,0,2:T(8,128)}, u32[]{:S(2)}, u32[]{:S(2)}) %collective-permute-start) | collective-permute-done | bytes 49952 | tf_op jit(solution)/shard_map/ppermute | solution.py:20
  48.4 1.3 copy.158
  49.8 3.2 copy.160
  53.0 17.3 %gather_fusion.3 = f32[7680,13]{1,0:T(8,128)} fusion(f32[13,9600]{0,1:T(8,128)} %bitcast.349, s32[8192]{0:T(1024)S(1)} %pad_clamp_fusion), kind=kCustom, calls=%fused_computation.3 | custom fusion | bytes 829440 | tf_op jit(solution)/shard_map/gather | solution.py:217
  70.3 2.7 copy.161
  73.1 3.6 fusion.1
  76.9 0.7 fusion.12
  77.7 0.8 convolution_bitcast_fusion.2
  79.1 0.9 copy.169
  80.0 1.2 reshape.275
  81.2 3.6 copy.170
  84.8 3.9 gather_fusion.5
  88.7 2.2 fusion.83
  90.9 1.3 collective-permute-start.3
  92.2 5.8 %collective-permute-start.2 = (f32[13,15,64]{1,0,2:T(8,128)}, f32[13,15,64]{1,0,2:T(8,128)}, u32[]{:S(2)}, u32[]{:S(2)}) collective-permute-start(f32[13,15,64]{1,0,2:T(8,128)} %get-tuple-element.20), channel_id=1, source_target_pairs={{0,1},{1,2},{2,3},{3,4},{4,5},{5,6},{6,7},{8,9},{9,10},{10,11},{11... | collective-permute-start | bytes 149768 | tf_op jit(solution)/shard_map/ppermute | solution.py:20
  98.2 2.4 fusion.3
  100.7 2.3 fusion.4
  103.0 4.5 %collective-permute-done.3 = f32[13,15,64]{1,0,2:T(8,128)} collective-permute-done((f32[13,15,64]{1,0,2:T(8,128)S(1)}, f32[13,15,64]{1,0,2:T(8,128)}, u32[]{:S(2)}, u32[]{:S(2)}) %collective-permute-start.3) | collective-permute-done | bytes 49952 | tf_op jit(solution)/shard_map/ppermute | solution.py:21
  107.5 1.3 copy.172
  108.7 10.1 %collective-permute-done.2 = f32[13,15,64]{1,0,2:T(8,128)} collective-permute-done((f32[13,15,64]{1,0,2:T(8,128)}, f32[13,15,64]{1,0,2:T(8,128)}, u32[]{:S(2)}, u32[]{:S(2)}) %collective-permute-start.2) | collective-permute-done | bytes 49952 | tf_op jit(solution)/shard_map/ppermute | solution.py:20
  118.9 1.3 copy.171
  120.2 3.2 copy.173
  123.5 17.3 %gather_fusion.6 = f32[7680,13]{1,0:T(8,128)} fusion(f32[13,9600]{0,1:T(8,128)} %bitcast.348, s32[8192]{0:T(1024)S(1)} %pad_clamp_fusion), kind=kCustom, calls=%fused_computation.6 | custom fusion | bytes 829440 | tf_op jit(solution)/shard_map/gather | solution.py:217
  140.8 2.8 copy.174
  143.7 2.7 fusion
  146.6 0.7 fusion.15
  147.4 1.8 fusion.2
  149.2 0.7 add_multiply_fusion.2
  150.6 31.2 %all-reduce.3.cloned.1.call-done = f32[6,35,128]{2,0,1:T(8,128)} async-done(((f32[6,35,128]{2,0,1:T(8,128)}), f32[6,35,128]{2,0,1:T(8,128)}) %all-reduce.3.cloned.1.call-update) | async-done | bytes 107536 | tf_op jit(solution)/shard_map/psum | solution.py:226
  181.7 1.6 multiply_reduce_fusion.1
  183.3 22.0 %all-reduce = (f32[]{:T(128)}, f32[6]{0:T(128)S(1)}) all-reduce(f32[]{:T(128)} %multiply_reduce_fusion.1, f32[6]{0:T(128)S(1)} %pad_maximum_fusion.2), channel_id=1, replica_groups=mesh['shot'=4,'mesh'=8] {'mesh'}, use_global_device_ids=true, to_apply=%region_11.0 | all-reduce | flops 7 | bytes 56 | tf_op jit(solution)/shard_map/psum | solution.py:229
  207.2 1.6 fusion.63
  208.8 17.8 %psum.87 = f32[]{:T(128)} all-reduce(f32[]{:T(128)} %fusion.63), channel_id=1, replica_groups=mesh['shot'=4,'mesh'=8] {'mesh'}, use_global_device_ids=true, to_apply=%region_13.0 | all-reduce | flops 1 | bytes 8 | tf_op jit(solution)/shard_map/psum | solution.py:229
  227.9 1.6 fusion.55
  229.5 19.7 %psum.88 = f32[]{:T(128)} all-reduce(f32[]{:T(128)} %get-tuple-element.18), channel_id=1, replica_groups=mesh['shot'=4,'mesh'=8] {'mesh'}, use_global_device_ids=true, to_apply=%region_15.0 | all-reduce | flops 1 | bytes 8 | tf_op jit(solution)/shard_map/psum | solution.py:229
  251.2 17.8 %psum.89 = f32[]{:T(128)} all-reduce(f32[]{:T(128)} %fusion.47), channel_id=1, replica_groups=mesh['shot'=4,'mesh'=8] {'mesh'}, use_global_device_ids=true, to_apply=%region_17.0 | all-reduce | flops 1 | bytes 8 | tf_op jit(solution)/shard_map/psum | solution.py:229
  270.3 0.7 fusion.39
  271.0 19.7 %psum.90 = f32[]{:T(128)} all-reduce(f32[]{:T(128)} %get-tuple-element.16), channel_id=1, replica_groups=mesh['shot'=4,'mesh'=8] {'mesh'}, use_global_device_ids=true, to_apply=%region_19.0 | all-reduce | flops 1 | bytes 8 | tf_op jit(solution)/shard_map/psum | solution.py:229
  294.1 17.8 %psum.91 = f32[]{:T(128)} all-reduce(f32[]{:T(128)} %fusion.36), channel_id=1, replica_groups=mesh['shot'=4,'mesh'=8] {'mesh'}, use_global_device_ids=true, to_apply=%region_21.0 | all-reduce | flops 1 | bytes 8 | tf_op jit(solution)/shard_map/psum | solution.py:229
  313.9 19.8 %psum.92 = f32[]{:T(128)} all-reduce(f32[]{:T(128)} %fusion.44), channel_id=1, replica_groups=mesh['shot'=4,'mesh'=8] {'mesh'}, use_global_device_ids=true, to_apply=%region_23.0 | all-reduce | flops 1 | bytes 8 | tf_op jit(solution)/shard_map/psum | solution.py:229
  335.0 0.7 fusion.52
  335.7 17.7 %psum.93 = f32[]{:T(128)} all-reduce(f32[]{:T(128)} %get-tuple-element.14), channel_id=1, replica_groups=mesh['shot'=4,'mesh'=8] {'mesh'}, use_global_device_ids=true, to_apply=%region_25.0 | all-reduce | flops 1 | bytes 8 | tf_op jit(solution)/shard_map/psum | solution.py:229
  355.4 0.9 copy.196
  356.3 19.7 %psum.94 = f32[]{:T(128)} all-reduce(f32[]{:T(128)} %fusion.60), channel_id=1, replica_groups=mesh['shot'=4,'mesh'=8] {'mesh'}, use_global_device_ids=true, to_apply=%region_27.0 | all-reduce | flops 1 | bytes 8 | tf_op jit(solution)/shard_map/psum | solution.py:229
  377.4 0.7 fusion.70
  378.1 17.7 %psum.95 = f32[]{:T(128)} all-reduce(f32[]{:T(128)} %get-tuple-element.12), channel_id=1, replica_groups=mesh['shot'=4,'mesh'=8] {'mesh'}, use_global_device_ids=true, to_apply=%region_29.0 | all-reduce | flops 1 | bytes 8 | tf_op jit(solution)/shard_map/psum | solution.py:229
  397.3 0.8 copy.197
  (115 shorter events, 9.1 us)
Async XLA Ops:
  7.2 174.6 %all-reduce.3.cloned.1.call-start = ((), (), s32[]{:S(2)}) async-start(), calls=%async_computation | async-start | bytes 286720 | tf_op jit(solution)/shard_map/psum | solution.py:226
  9.5 4.0 copy-start.35
  9.8 17.7 %copy-start.2 = (f32[5,6,35,128]{3,2,1,0:T(8,128)S(1)}, f32[5,6,35,128]{3,2,1,0:T(8,128)}, u32[]{:S(2)}) copy-start(f32[5,6,35,128]{3,2,1,0:T(8,128)} %param.37) | copy-start | bytes 1612804
  9.8 17.7 %copy-start.3 = (f32[5,6,35,128]{3,2,1,0:T(8,128)S(1)}, f32[5,6,35,128]{3,2,1,0:T(8,128)}, u32[]{:S(2)}) copy-start(f32[5,6,35,128]{3,2,1,0:T(8,128)} %param.36) | copy-start | bytes 1612804
  13.5 3.9 copy-start.23
  13.5 15.6 %copy-start.26 = (s32[4,128]{1,0:T(4,128)S(1)}, s32[4,128]{1,0:T(4,128)}, u32[]{:S(2)}) copy-start(s32[4,128]{1,0:T(4,128)} %param.34) | copy-start | bytes 6148
  17.3 11.8 %copy-start.27 = (s32[4,128]{1,0:T(4,128)S(1)}, s32[4,128]{1,0:T(4,128)}, u32[]{:S(2)}) copy-start(s32[4,128]{1,0:T(4,128)} %param.33) | copy-start | bytes 6148
  17.3 11.8 %copy-start.30 = (s32[15]{0:T(128)S(1)}, s32[15]{0:T(128)}, u32[]{:S(2)}) copy-start(s32[15]{0:T(128)} %constant.67.clone) | copy-start | bytes 184
  17.3 11.8 %copy-start.31 = (s32[15]{0:T(128)S(1)}, s32[15]{0:T(128)}, u32[]{:S(2)}) copy-start(s32[15]{0:T(128)} %constant.66.clone) | copy-start | bytes 184
  17.3 11.8 %copy-start.32 = (s32[15]{0:T(128)S(1)}, s32[15]{0:T(128)}, u32[]{:S(2)}) copy-start(s32[15]{0:T(128)} %constant.65.clone) | copy-start | bytes 184
  17.3 11.8 %copy-start.33 = (s32[15]{0:T(128)S(1)}, s32[15]{0:T(128)}, u32[]{:S(2)}) copy-start(s32[15]{0:T(128)} %constant.64.clone) | copy-start | bytes 184
  17.3 11.8 %copy-start.34 = (s32[15]{0:T(128)S(1)}, s32[15]{0:T(128)}, u32[]{:S(2)}) copy-start(s32[15]{0:T(128)} %constant.63.clone) | copy-start | bytes 184
  17.4 12.0 %copy-start.28 = (f32[4,128]{1,0:T(4,128)S(1)}, f32[4,128]{1,0:T(4,128)}, u32[]{:S(2)}) copy-start(f32[4,128]{1,0:T(4,128)} %param.32) | copy-start | bytes 6148
  17.4 12.0 %copy-start.1 = (f32[1,13,35,128]{3,0,2,1:T(1,128)S(1)}, f32[1,13,35,128]{3,0,2,1:T(1,128)}, u32[]{:S(2)}) copy-start(f32[1,13,35,128]{3,0,2,1:T(1,128)} %param.26) | copy-start | bytes 698884
  17.4 12.0 %copy-start.10 = (f32[3,35,35,1]{2,1,3,0:T(8,128)S(1)}, f32[3,35,35,1]{2,1,3,0:T(8,128)}, u32[]{:S(2)}) copy-start(f32[3,35,35,1]{2,1,3,0:T(8,128)} %constant.74) | copy-start | bytes 44104
  19.8 10.5 %copy-start.25 = (f32[3,3,128]{2,1,0:T(4,128)S(1)}, f32[3,3,128]{2,1,0:T(4,128)}, u32[]{:S(2)}) copy-start(f32[3,3,128]{2,1,0:T(4,128)} %param.30) | copy-start | bytes 13828
  19.8 10.5 %copy-start = (f32[6,35,128]{2,1,0:T(8,128)S(1)}, f32[6,35,128]{2,1,0:T(8,128)}, u32[]{:S(2)}) copy-start(f32[6,35,128]{2,1,0:T(8,128)} %param.28) | copy-start | bytes 322564
  19.8 10.5 %copy-start.16 = (f32[1,2,13,35,128]{4,1,3,2,0:T(2,128)S(1)}, f32[1,2,13,35,128]{4,1,3,2,0:T(2,128)}, u32[]{:S(2)}) copy-start(f32[1,2,13,35,128]{4,1,3,2,0:T(2,128)} %param.27) | copy-start | bytes 1397764
  19.8 19.8 %collective-permute-start.1 = (f32[13,15,64]{1,0,2:T(8,128)}, f32[13,15,64]{1,0,2:T(8,128)}, u32[]{:S(2)}, u32[]{:S(2)}) collective-permute-start(f32[13,15,64]{1,0,2:T(8,128)} %get-tuple-element.23), channel_id=1, source_target_pairs={{1,0},{2,1},{3,2},{4,3},{5,4},{6,5},{7,6},{9,8},{10,9},{11,10},{12... | collective-permute-start | bytes 149768 | tf_op jit(solution)/shard_map/ppermute | solution.py:21
  21.2 27.2 %collective-permute-start = (f32[13,15,64]{1,0,2:T(8,128)}, f32[13,15,64]{1,0,2:T(8,128)}, u32[]{:S(2)}, u32[]{:S(2)}) collective-permute-start(f32[13,15,64]{1,0,2:T(8,128)} %get-tuple-element.22), channel_id=1, source_target_pairs={{0,1},{1,2},{2,3},{3,4},{4,5},{5,6},{6,7},{8,9},{9,10},{10,11},{11... | collective-permute-start | bytes 149768 | tf_op jit(solution)/shard_map/ppermute | solution.py:20
  31.7 1.8 copy-start.13
  35.8 3.7 copy-start.24
  39.6 33.6 %copy-start.21 = (f32[3,4,128]{2,0,1:T(4,128)}, f32[3,4,128]{2,0,1:T(4,128)S(1)}, u32[]{:S(2)}) copy-start(f32[3,4,128]{2,0,1:T(4,128)S(1)} %copy.154) | copy-start | bytes 18436
  73.0 3.8 copy-start.8
  73.0 3.8 copy-start.19
  88.7 9.4 %copy-start.12 = (f32[3,13,35,128,1]{3,2,1,0,4:T(8,128)S(1)}, f32[3,13,35,128,1]{3,2,1,0,4:T(8,128)}, u32[]{:S(2)}) copy-start(f32[3,13,35,128,1]{3,2,1,0,4:T(8,128)} %maximum_bitcast_fusion.2) | copy-start | bytes 2096644
  88.7 9.4 %copy-start.14 = (f32[3,6,13,13]{3,2,1,0:T(8,128)S(1)}, f32[3,6,13,13]{3,2,1,0:T(8,128)}, u32[]{:S(2)}) copy-start(f32[3,6,13,13]{3,2,1,0:T(8,128)} %param.29) | copy-start | bytes 36508
  90.9 16.6 %collective-permute-start.3 = (f32[13,15,64]{1,0,2:T(8,128)S(1)}, f32[13,15,64]{1,0,2:T(8,128)}, u32[]{:S(2)}, u32[]{:S(2)}) collective-permute-start(f32[13,15,64]{1,0,2:T(8,128)S(1)} %get-tuple-element.21), channel_id=1, source_target_pairs={{1,0},{2,1},{3,2},{4,3},{5,4},{6,5},{7,6},{9,8},{10,9},{11,10},{12... | collective-permute-start | bytes 149768 | tf_op jit(solution)/shard_map/ppermute | solution.py:21
  92.2 26.7 %collective-permute-start.2 = (f32[13,15,64]{1,0,2:T(8,128)}, f32[13,15,64]{1,0,2:T(8,128)}, u32[]{:S(2)}, u32[]{:S(2)}) collective-permute-start(f32[13,15,64]{1,0,2:T(8,128)} %get-tuple-element.20), channel_id=1, source_target_pairs={{0,1},{1,2},{2,3},{3,4},{4,5},{5,6},{6,7},{8,9},{9,10},{10,11},{11... | collective-permute-start | bytes 149768 | tf_op jit(solution)/shard_map/ppermute | solution.py:20
  140.8 2.9 copy-start.15
  140.8 2.9 copy-start.17
  140.8 2.9 copy-start.22
  143.6 2.9 copy-start.9
  143.6 2.9 copy-start.20
  143.7 3.7 copy-start.11
  146.4 2.8 copy-start.18
  146.4 3.5 copy-start.29
  146.4 4.1 %copy-start.6 = (f32[1,6,35,128]{3,2,1,0:T(8,128)S(1)}, f32[1,6,35,128]{3,2,1,0:T(8,128)}, u32[]{:S(2)}) copy-start(f32[1,6,35,128]{3,2,1,0:T(8,128)} %get-tuple-element.69) | copy-start | bytes 322564
  146.5 81.4 %copy-start.4 = (f32[1,6,35,128]{3,2,1,0:T(8,128)S(1)}, f32[1,6,35,128]{3,2,1,0:T(8,128)}, u32[]{:S(2)}) copy-start(f32[1,6,35,128]{3,2,1,0:T(8,128)} %get-tuple-element.39) | copy-start | bytes 322564
  146.6 104.0 %copy-start.5 = (f32[1,6,35,128]{3,2,1,0:T(8,128)S(1)}, f32[1,6,35,128]{3,2,1,0:T(8,128)}, u32[]{:S(2)}) copy-start(f32[1,6,35,128]{3,2,1,0:T(8,128)} %get-tuple-element.72) | copy-start | bytes 322564
  146.6 123.8 %copy-start.7 = (f32[1,6,35,128]{3,2,1,0:T(8,128)S(1)}, f32[1,6,35,128]{3,2,1,0:T(8,128)}, u32[]{:S(2)}) copy-start(f32[1,6,35,128]{3,2,1,0:T(8,128)} %get-tuple-element.37) | copy-start | bytes 322564
Sparse Core Ops, SparseCore 0:
  150.0 31.6 all-reduce.2
where the time goes:
time: 406 us; the launch traced here: 405 us
  blocking collectives  190 us (47%)
  local copies, waits for them, and re-layouts  81.3 us (20%)
  waiting for transfers between devices  53.4 us (13%)
  between operations  29.4 us (7%)
  matrix products  19.8 us (5%)
  other arithmetic  16.3 us (4%)
  starting transfers between devices  14.9 us (4%)
    psum x10, blocking collectives, combine_sums(): return lax.psum(values, 'mesh')  190 us
    gather x2, local copies, waits for them, and re-layouts, shards(): turned = ghosts.reshape(fields, face_width * slot_count)[:, flat_index]  34.6 us
    psum x1, waiting for transfers between devices, shards(): total_grad = lax.psum(gradient, 'shot')  31.2 us
    ppermute x2, waiting for transfers between devices, padded(): before = lax.ppermute(last, axis, up)  17.7 us
    ppermute x2, starting transfers between devices, padded(): before = lax.ppermute(last, axis, up)  12.1 us
    reshape x4, local copies, waits for them, and re-layouts, shards(): flat_trace = inner_trace.reshape(fields, face_width, 4 * elements)  8.56 us
  transfers between devices with their start and end apart: 5, of which 4 were waited for; matrix products, arithmetic and copies ran while one was open for 5% of the time, Pallas kernels for 0%

commit v1 on v0

--- a/solution.py
+++ b/solution.py
@@ -148,26 +148,46 @@
     )
 
 
-def search_direction(total_grad, step_rows, change_rows, combine_sums):
+def search_direction(grad_share, local_grad, step_rows, change_rows, own_share, combine_sums):
     pairs = step_rows.shape[0]
+    step_share = own_share(step_rows)
+    change_share = own_share(change_rows)
+    step_grad = jnp.sum(step_rows * local_grad[None], axis=(1, 2, 3))
+    change_grad = jnp.sum(change_rows * local_grad[None], axis=(1, 2, 3))
+    step_change = jnp.sum(step_share[:, None] * change_share[None, :], axis=(2, 3, 4))
+    change_change = jnp.sum(change_share[:, None] * change_share[None, :], axis=(2, 3, 4))
     summed = combine_sums(
         jnp.concatenate(
-            [
-                jnp.sum(step_rows * change_rows, axis=(1, 2, 3)),
-                jnp.sum(change_rows[pairs - 1] * change_rows[pairs - 1])[None],
-            ]
-        )
-    )
-    curvature = summed[:pairs]
+            [step_grad, change_grad, step_change.reshape(-1), change_change.reshape(-1)]
+        )
+    )
+    step_grad = summed[:pairs]
+    change_grad = summed[pairs : 2 * pairs]
+    step_change = summed[2 * pairs : 2 * pairs + pairs * pairs].reshape(pairs, pairs)
+    change_change = summed[2 * pairs + pairs * pairs :].reshape(pairs, pairs)
+    curvature = [step_change[slot, slot] for slot in range(pairs)]
     alphas = [None] * pairs
-    work = total_grad
     for slot in reversed(range(pairs)):
-        alphas[slot] = combine_sums(jnp.sum(step_rows[slot] * work)) / curvature[slot]
-        work = work - alphas[slot] * change_rows[slot]
-    work = curvature[pairs - 1] / summed[pairs] * work
+        projected = step_grad[slot]
+        for later in range(slot + 1, pairs):
+            projected = projected - alphas[later] * step_change[slot, later]
+        alphas[slot] = projected / curvature[slot]
+    scaling = curvature[pairs - 1] / change_change[pairs - 1, pairs - 1]
+    weights = [None] * pairs
     for slot in range(pairs):
-        beta_now = combine_sums(jnp.sum(change_rows[slot] * work)) / curvature[slot]
-        work = work + (alphas[slot] - beta_now) * step_rows[slot]
+        along = change_grad[slot]
+        for other in range(pairs):
+            along = along - alphas[other] * change_change[slot, other]
+        along = scaling * along
+        for earlier in range(slot):
+            along = along + weights[earlier] * step_change[earlier, slot]
+        beta_now = along / curvature[slot]
+        weights[slot] = alphas[slot] - beta_now
+    work = scaling * grad_share
+    for slot in range(pairs):
+        work = work - (scaling * alphas[slot]) * change_share[slot]
+    for slot in range(pairs):
+        work = work + weights[slot] * step_share[slot]
     return -work
 
 
@@ -223,14 +243,20 @@
         gradient = gradient + STEP_SIZE * kernel_term(
             adjoint, forward_states[0, step_index], coupling, metric, derivs
         )
-    total_grad = lax.psum(gradient, "shot")
+    shot_count = lax.axis_size("shot")
+    share_width = elements // shot_count
+    share_start = lax.axis_index("shot") * share_width
+
+    def own_share(rows):
+        return lax.dynamic_slice_in_dim(rows, share_start, share_width, rows.ndim - 1)
 
     def combine_sums(values):
-        return lax.psum(values, "mesh")
-
-    result = search_direction(total_grad, history_steps, history_changes, combine_sums)
-    share_width = elements // lax.axis_size("shot")
-    result = lax.dynamic_slice_in_dim(result, lax.axis_index("shot") * share_width, share_width, 2)
+        return lax.psum(values, ("shot", "mesh"))
+
+    grad_share = lax.psum_scatter(gradient, "shot", scatter_dimension=2, tiled=True)
+    result = search_direction(
+        grad_share, gradient, history_steps, history_changes, own_share, combine_sums
+    )
     return (adjoint[None], result)
 
 

time: 406 us -> 259 us (0.64)
  blocking collectives: 190 us -> 41.4 us
  waiting for transfers between devices: 53.4 us -> 13.8 us
  between operations: 29.4 us -> 57.5 us
  local copies, waits for them, and re-layouts: 81.3 us -> 100 us
  other arithmetic: 16.3 us -> 11 us
    psum x10 -> x1, blocking collectives: 190 us -> 41.4 us  [combine_sums(): return lax.psum(values, ('shot', 'mesh'))]
    psum x1 -> x0, waiting for transfers between devices: 31.2 us -> none  [shards(): total_grad = lax.psum(gradient, 'shot')]
    unnamed x79 -> x134, local copies, waits for them, and re-layouts: 2.93 us -> 14.9 us
    reduce_sum x12 -> x2, other arithmetic: 10.8 us -> 0.85 us  [the longest x1 0.63 us: search_direction(): jnp.sum(step_share[:, None] * change_share[None, :], axis=(2, 3, 4))]
    ppermute x2, waiting for transfers between devices: 17.7 us -> 10.1 us  [padded(): before = lax.ppermute(last, axis, up)]
    dynamic_slice x0 -> x3, local copies, waits for them, and re-layouts: none -> 4.12 us  [own_share(): lax.dynamic_slice_in_dim(rows, share_start, share_width, rows.ndim - 1)]
  transfers between devices with their start and end apart: 5 -> 5, of which waited for: 4 -> 2; matrix products, arithmetic and copies ran while one was open for 5% -> 17% of each run, Pallas kernels for 0% -> 0%
where the time goes in v1:
time: 259 us; the launch traced here: 258 us
  local copies, waits for them, and re-layouts  100 us (39%)
  between operations  57.5 us (22%)
  blocking collectives  41.4 us (16%)
  matrix products  19.2 us (7%)
  starting transfers between devices  14.5 us (6%)
  waiting for transfers between devices  13.8 us (5%)
  other arithmetic  11 us (4%)
    psum x1, blocking collectives, combine_sums(): return lax.psum(values, ('shot', 'mesh'))  41.4 us
    gather x2, local copies, waits for them, and re-layouts, shards(): turned = ghosts.reshape(fields, face_width * slot_count)[:, flat_index]  34.6 us
    unnamed x134, local copies, waits for them, and re-layouts  14.9 us
    ppermute x2, starting transfers between devices, padded(): before = lax.ppermute(last, axis, up)  11.9 us
    ppermute x2, waiting for transfers between devices, padded(): before = lax.ppermute(last, axis, up)  10.1 us
    reshape x4, local copies, waits for them, and re-layouts, shards(): flat_trace = inner_trace.reshape(fields, face_width, 4 * elements)  8.64 us
    gather x2, local copies, waits for them, and re-layouts, shards(): sent_traces = flat_trace[:, :, send_faces]  6.84 us
    concatenate x2, local copies, waits for them, and re-layouts, shards(): jnp.concatenate([flat_trace, extended[:, :, :border], extended[:, :, 3 *...  6.56 us
  transfers between devices with their start and end apart: 5, of which 2 were waited for; matrix products, arithmetic and copies ran while one was open for 17% of the time, Pallas kernels for 0%

profile of v1, /device:TPU:0, one launch (start us, length us, event | category | flops | bytes accessed | tf_op | source)
XLA Modules:
  0.0 257.8 jit_solution(17985935043041204330)
XLA Ops:
  7.9 1.0 copy.371
  9.9 3.7 %copy.235 = f32[13,15,512]{1,0,2:T(8,128)} copy(f32[13,15,512]{2,1,0:T(8,128)S(1)} %reshape.330) | data formatting | bytes 798720 | tf_op jit(solution)/shard_map/reshape | solution.py:231
  13.7 2.9 %gather_fusion.2 = f32[128,13,15]{2,1,0:T(8,128)S(1)} fusion(f32[13,15,512]{1,0,2:T(8,128)} %copy.235, s32[1024]{0:T(1024)S(1)} %pad_clamp_fusion.1), kind=kCustom, calls=%fused_computation.2 | custom fusion | bytes 200192 | tf_op jit(solution)/shard_map/gather | solution.py:232
  16.6 1.0 fusion.42
  17.6 1.3 collective-permute-start.1
  18.9 6.3 %collective-permute-start = (f32[13,15,64]{1,0,2:T(8,128)}, f32[13,15,64]{1,0,2:T(8,128)}, u32[]{:S(2)}, u32[]{:S(2)}) collective-permute-start(f32[13,15,64]{1,0,2:T(8,128)} %get-tuple-element.20), channel_id=1, source_target_pairs={{0,1},{1,2},{2,3},{3,4},{4,5},{5,6},{6,7},{8,9},{9,10},{10,11},{11... | collective-permute-start | bytes 149768 | tf_op jit(solution)/shard_map/ppermute | solution.py:20
  26.1 0.8 convolution_bitcast_fusion.3
  28.1 0.8 convolution_bitcast_fusion
  28.9 0.9 multiply_add_fusion.11
  29.9 0.9 multiply_add_fusion.2
  30.8 0.8 convolution_bitcast_fusion.1
  31.7 1.0 multiply_add_fusion.5
  32.6 1.4 constant_dynamic-slice_fusion.9
  34.1 1.3 copy.269
  35.4 1.3 copy.267
  37.5 1.2 maximum_bitcast_fusion
  38.7 2.3 fusion.5
  41.1 1.0 maximum_bitcast_fusion.3
  42.1 1.0 maximum_bitcast_fusion.2
  43.1 1.1 constant_dynamic-slice_fusion.3
  44.2 0.8 gather_fusion
  45.1 0.8 copy.298
  45.9 1.7 copy.329
  47.5 1.7 copy.328
  49.2 1.7 copy.327
  50.9 1.7 copy.326
  52.5 0.8 copy.325
  53.3 0.8 copy.324
  54.1 0.8 copy.323
  54.9 0.8 copy.322
  55.7 0.8 copy.321
  56.4 0.8 copy.320
  58.5 1.3 copy.237
  59.8 1.3 copy.236
  61.2 3.3 %copy.238 = f32[13,15,640]{0,2,1:T(8,128)} copy(f32[13,15,640]{2,1,0:T(8,128)S(1)} %pad_maximum_fusion) | data formatting | bytes 998400 | tf_op jit(solution)/shard_map/concatenate | solution.py:234
  64.4 17.3 %gather_fusion.3 = f32[7680,13]{1,0:T(8,128)} fusion(f32[13,9600]{0,1:T(8,128)} %bitcast.298, s32[8192]{0:T(1024)S(1)} %pad_clamp_fusion), kind=kCustom, calls=%fused_computation.3 | custom fusion | bytes 829440 | tf_op jit(solution)/shard_map/gather | solution.py:237
  81.7 2.8 %copy.239 = f32[13,15,4,128]{3,0,2,1:T(8,128)S(1)} copy(f32[13,15,4,128]{0,3,2,1:T(8,128)} %bitcast.300) | data formatting | bytes 798720 | tf_op jit(solution)/shard_map/reshape | solution.py:238
  84.6 3.7 %fusion.1 = f32[13,15,4,128]{3,0,2,1:T(8,128)S(1)} fusion(f32[6,15,4,128]{3,0,2,1:T(8,128)} %bitcast.309, f32[13,15,4,128]{3,0,2,1:T(8,128)S(1)} %sub.149, f32[3,4,128]{2,0,1:T(4,128)S(1)} %copy.232, f32[3,6,13,13]{3,2,1,0:T(8,128)S(1)} %copy-done.18), kind=kOutput, calls=%fused_computation.10 | convolution fusion | flops 281748480 | bytes 1001352 | tf_op jit(solution)/shard_map/dpfg,dfnxe->pgnxe/dot_general | solution.py:144
  89.2 0.8 convolution_bitcast_fusion.2
  90.7 0.9 copy.247
  91.6 1.2 reshape.333
  92.8 3.7 %copy.248 = f32[13,15,512]{1,0,2:T(8,128)} copy(f32[13,15,512]{2,1,0:T(8,128)S(1)} %reshape.333) | data formatting | bytes 798720 | tf_op jit(solution)/shard_map/reshape | solution.py:231
  96.4 3.9 %gather_fusion.5 = f32[128,13,15]{2,1,0:T(8,128)} fusion(f32[13,15,512]{1,0,2:T(8,128)} %copy.248, s32[1024]{0:T(1024)} %copy-done.45), kind=kCustom, calls=%fused_computation.5 | custom fusion | bytes 200192 | tf_op jit(solution)/shard_map/gather | solution.py:232
  100.4 2.1 fusion.41
  102.5 1.3 collective-permute-start.3
  103.8 5.6 %collective-permute-start.2 = (f32[13,15,64]{1,0,2:T(8,128)}, f32[13,15,64]{1,0,2:T(8,128)}, u32[]{:S(2)}, u32[]{:S(2)}) collective-permute-start(f32[13,15,64]{1,0,2:T(8,128)} %get-tuple-element.18), channel_id=1, source_target_pairs={{0,1},{1,2},{2,3},{3,4},{4,5},{5,6},{6,7},{8,9},{9,10},{10,11},{11... | collective-permute-start | bytes 149768 | tf_op jit(solution)/shard_map/ppermute | solution.py:20
  109.5 0.8 multiply_add_fusion.8
  110.3 2.4 fusion.3
  112.8 1.6 fusion.4
  114.4 3.7 %collective-permute-done.3 = f32[13,15,64]{1,0,2:T(8,128)} collective-permute-done((f32[13,15,64]{1,0,2:T(8,128)S(1)}, f32[13,15,64]{1,0,2:T(8,128)}, u32[]{:S(2)}, u32[]{:S(2)}) %collective-permute-start.3) | collective-permute-done | bytes 49952 | tf_op jit(solution)/shard_map/ppermute | solution.py:21
  118.1 1.3 copy.250
  119.3 10.1 %collective-permute-done.2 = f32[13,15,64]{1,0,2:T(8,128)} collective-permute-done((f32[13,15,64]{1,0,2:T(8,128)}, f32[13,15,64]{1,0,2:T(8,128)}, u32[]{:S(2)}, u32[]{:S(2)}) %collective-permute-start.2) | collective-permute-done | bytes 49952 | tf_op jit(solution)/shard_map/ppermute | solution.py:20
  129.4 1.3 copy.249
  130.8 3.3 %copy.251 = f32[13,15,640]{0,2,1:T(8,128)} copy(f32[13,15,640]{2,1,0:T(8,128)S(1)} %pad_maximum_fusion.1) | data formatting | bytes 998400 | tf_op jit(solution)/shard_map/concatenate | solution.py:234
  134.1 17.3 %gather_fusion.6 = f32[7680,13]{1,0:T(8,128)} fusion(f32[13,9600]{0,1:T(8,128)} %bitcast.297, s32[8192]{0:T(1024)S(1)} %pad_clamp_fusion), kind=kCustom, calls=%fused_computation.6 | custom fusion | bytes 829440 | tf_op jit(solution)/shard_map/gather | solution.py:237
  151.4 2.8 %copy.252 = f32[13,15,4,128]{3,0,2,1:T(8,128)S(1)} copy(f32[13,15,4,128]{0,3,2,1:T(8,128)} %bitcast.299) | data formatting | bytes 798720 | tf_op jit(solution)/shard_map/reshape | solution.py:238
  154.4 2.7 %fusion = f32[13,15,4,128]{3,0,2,1:T(8,128)S(1)} fusion(f32[6,15,4,128]{3,0,2,1:T(8,128)S(1)} %bitcast.310, f32[13,15,4,128]{3,0,2,1:T(8,128)S(1)} %sub.150, f32[3,4,128]{2,0,1:T(4,128)S(1)} %copy-done.44, f32[3,6,13,13]{3,2,1,0:T(8,128)S(1)} %copy-done.20), kind=kOutput, calls=%fused_computation.8 | convolution fusion | flops 281748480 | bytes 1001352 | tf_op jit(solution)/shard_map/dpfg,dfnxe->pgnxe/dot_general | solution.py:144
  157.2 0.7 fusion.15
  158.1 1.8 fusion.2
  159.9 1.0 copy.271
  161.3 41.4 %psum.7 = f32[60]{0:T(128)S(1)} all-reduce(f32[60]{0:T(128)S(1)} %pad_maximum_fusion.2), channel_id=1, replica_groups=mesh['shot'=4,'mesh'=8] {'shot','mesh'}, use_global_device_ids=true, to_apply=%region_10.0 | all-reduce | flops 60 | bytes 480 | tf_op jit(solution)/shard_map/psum | solution.py:254
  226.0 0.7 fusion.44
  239.3 0.9 copy.272
  249.2 1.0 fusion.35
  (163 shorter events, 11.2 us)
Async XLA Ops:
  7.2 242.0 %reduce-scatter.2.cloned.1.call-start = ((), (), s32[]{:S(2)}) async-start(), calls=%async_computation.1 | async-start | bytes 655360 | tf_op jit(solution)/shard_map/reduce_scatter | solution.py:256
  9.8 3.8 %copy-start.58 = (s32[128]{0:T(128)S(1)}, s32[128]{0:T(128)}, u32[]{:S(2)}) copy-start(s32[128]{0:T(128)} %param.35) | copy-start | bytes 1540
  9.8 15.4 %copy-start.48 = (s32[4,128]{1,0:T(4,128)S(1)}, s32[4,128]{1,0:T(4,128)}, u32[]{:S(2)}) copy-start(s32[4,128]{1,0:T(4,128)} %param.34) | copy-start | bytes 6148
  9.8 15.4 %copy-start.49 = (s32[4,128]{1,0:T(4,128)S(1)}, s32[4,128]{1,0:T(4,128)}, u32[]{:S(2)}) copy-start(s32[4,128]{1,0:T(4,128)} %param.33) | copy-start | bytes 6148
  9.8 15.4 %copy-start.53 = (s32[15]{0:T(128)S(1)}, s32[15]{0:T(128)}, u32[]{:S(2)}) copy-start(s32[15]{0:T(128)} %constant.67.clone) | copy-start | bytes 184
  9.9 15.4 %copy-start.54 = (s32[15]{0:T(128)S(1)}, s32[15]{0:T(128)}, u32[]{:S(2)}) copy-start(s32[15]{0:T(128)} %constant.66.clone) | copy-start | bytes 184
  9.9 15.4 %copy-start.55 = (s32[15]{0:T(128)S(1)}, s32[15]{0:T(128)}, u32[]{:S(2)}) copy-start(s32[15]{0:T(128)} %constant.65.clone) | copy-start | bytes 184
  9.9 15.4 %copy-start.56 = (s32[15]{0:T(128)S(1)}, s32[15]{0:T(128)}, u32[]{:S(2)}) copy-start(s32[15]{0:T(128)} %constant.64.clone) | copy-start | bytes 184
  9.9 15.4 %copy-start.57 = (s32[15]{0:T(128)S(1)}, s32[15]{0:T(128)}, u32[]{:S(2)}) copy-start(s32[15]{0:T(128)} %constant.63.clone) | copy-start | bytes 184
  9.9 16.2 %copy-start.52 = (f32[4,128]{1,0:T(4,128)S(1)}, f32[4,128]{1,0:T(4,128)}, u32[]{:S(2)}) copy-start(f32[4,128]{1,0:T(4,128)} %param.32) | copy-start | bytes 6148
  9.9 16.2 %copy-start.3 = (f32[1,13,35,128]{3,0,2,1:T(1,128)S(1)}, f32[1,13,35,128]{3,0,2,1:T(1,128)}, u32[]{:S(2)}) copy-start(f32[1,13,35,128]{3,0,2,1:T(1,128)} %param.26) | copy-start | bytes 698884
  9.9 16.2 %copy-start.13 = (f32[3,35,35,1]{2,1,3,0:T(8,128)S(1)}, f32[3,35,35,1]{2,1,3,0:T(8,128)}, u32[]{:S(2)}) copy-start(f32[3,35,35,1]{2,1,3,0:T(8,128)} %constant.74) | copy-start | bytes 44104
  13.6 13.3 %copy-start.47 = (f32[3,3,128]{2,1,0:T(4,128)S(1)}, f32[3,3,128]{2,1,0:T(4,128)}, u32[]{:S(2)}) copy-start(f32[3,3,128]{2,1,0:T(4,128)} %param.30) | copy-start | bytes 13828
  13.6 13.4 %copy-start = (f32[6,35,128]{2,1,0:T(8,128)S(1)}, f32[6,35,128]{2,1,0:T(8,128)}, u32[]{:S(2)}) copy-start(f32[6,35,128]{2,1,0:T(8,128)} %param.28) | copy-start | bytes 322564
  13.6 14.1 %copy-start.31 = (f32[1,2,13,35,128]{4,1,3,2,0:T(2,128)S(1)}, f32[1,2,13,35,128]{4,1,3,2,0:T(2,128)}, u32[]{:S(2)}) copy-start(f32[1,2,13,35,128]{4,1,3,2,0:T(2,128)} %param.27) | copy-start | bytes 1397764
  13.6 11.6 %copy-start.45 = (s32[1024]{0:T(1024)}, s32[1024]{0:T(1024)S(1)}, u32[]{:S(2)}) copy-start(s32[1024]{0:T(1024)S(1)} %pad_clamp_fusion.1) | copy-start | bytes 12292
  17.6 40.9 %collective-permute-start.1 = (f32[13,15,64]{1,0,2:T(8,128)}, f32[13,15,64]{1,0,2:T(8,128)}, u32[]{:S(2)}, u32[]{:S(2)}) collective-permute-start(f32[13,15,64]{1,0,2:T(8,128)} %get-tuple-element.21), channel_id=1, source_target_pairs={{1,0},{2,1},{3,2},{4,3},{5,4},{6,5},{7,6},{9,8},{10,9},{11,10},{12... | collective-permute-start | bytes 149768 | tf_op jit(solution)/shard_map/ppermute | solution.py:21
  18.9 40.9 %collective-permute-start = (f32[13,15,64]{1,0,2:T(8,128)}, f32[13,15,64]{1,0,2:T(8,128)}, u32[]{:S(2)}, u32[]{:S(2)}) collective-permute-start(f32[13,15,64]{1,0,2:T(8,128)} %get-tuple-element.20), channel_id=1, source_target_pairs={{0,1},{1,2},{2,3},{3,4},{4,5},{5,6},{6,7},{8,9},{9,10},{10,11},{11... | collective-permute-start | bytes 149768 | tf_op jit(solution)/shard_map/ppermute | solution.py:20
  27.0 4.6 %copy-start.37 = (f32[128]{0:T(128)}, f32[128]{0:T(128)S(1)}, u32[]{:S(2)}) copy-start(f32[128]{0:T(128)S(1)} %get-tuple-element.50) | copy-start | bytes 1540
  27.0 4.6 %copy-start.39 = (f32[128]{0:T(128)}, f32[128]{0:T(128)S(1)}, u32[]{:S(2)}) copy-start(f32[128]{0:T(128)S(1)} %get-tuple-element.51) | copy-start | bytes 1540
  27.0 4.6 %copy-start.40 = (f32[128]{0:T(128)}, f32[128]{0:T(128)S(1)}, u32[]{:S(2)}) copy-start(f32[128]{0:T(128)S(1)} %get-tuple-element.52) | copy-start | bytes 1540
  27.0 4.6 %copy-start.41 = (f32[128]{0:T(128)}, f32[128]{0:T(128)S(1)}, u32[]{:S(2)}) copy-start(f32[128]{0:T(128)S(1)} %get-tuple-element.53) | copy-start | bytes 1540
  27.0 4.6 %copy-start.42 = (f32[128]{0:T(128)}, f32[128]{0:T(128)S(1)}, u32[]{:S(2)}) copy-start(f32[128]{0:T(128)S(1)} %get-tuple-element.54) | copy-start | bytes 1540
  29.9 2.8 %copy-start.1 = (f32[5,6,35,128]{3,2,1,0:T(8,128)S(1)}, f32[5,6,35,128]{3,2,1,0:T(8,128)}, u32[]{:S(2)}) copy-start(f32[5,6,35,128]{3,2,1,0:T(8,128)} %param.36) | copy-start | bytes 1612804
  29.9 2.8 %copy-start.2 = (f32[5,6,35,128]{3,2,1,0:T(8,128)S(1)}, f32[5,6,35,128]{3,2,1,0:T(8,128)}, u32[]{:S(2)}) copy-start(f32[5,6,35,128]{3,2,1,0:T(8,128)} %param.37) | copy-start | bytes 1612804
  36.8 1.9 copy-start.4
  36.8 1.9 copy-start.17
  36.8 4.3 %copy-start.7 = (f32[1,13,35,128]{3,2,1,0:T(8,128)S(1)}, f32[1,13,35,128]{3,2,1,0:T(8,128)}, u32[]{:S(2)}) copy-start(f32[1,13,35,128]{3,2,1,0:T(8,128)} %get-tuple-element.25) | copy-start | bytes 698884
  36.8 4.3 %copy-start.8 = (f32[1,13,35,128]{3,2,1,0:T(8,128)S(1)}, f32[1,13,35,128]{3,2,1,0:T(8,128)}, u32[]{:S(2)}) copy-start(f32[1,13,35,128]{3,2,1,0:T(8,128)} %get-tuple-element.26) | copy-start | bytes 698884
  36.8 4.3 %copy-start.9 = (f32[1,13,35,128]{3,2,1,0:T(8,128)S(1)}, f32[1,13,35,128]{3,2,1,0:T(8,128)}, u32[]{:S(2)}) copy-start(f32[1,13,35,128]{3,2,1,0:T(8,128)} %get-tuple-element.27) | copy-start | bytes 698884
  37.5 4.6 %copy-start.10 = (f32[1,13,35,128]{3,2,1,0:T(8,128)S(1)}, f32[1,13,35,128]{3,2,1,0:T(8,128)}, u32[]{:S(2)}) copy-start(f32[1,13,35,128]{3,2,1,0:T(8,128)} %get-tuple-element.22) | copy-start | bytes 698884
  37.5 4.6 %copy-start.11 = (f32[1,13,35,128]{3,2,1,0:T(8,128)S(1)}, f32[1,13,35,128]{3,2,1,0:T(8,128)}, u32[]{:S(2)}) copy-start(f32[1,13,35,128]{3,2,1,0:T(8,128)} %get-tuple-element.23) | copy-start | bytes 698884
  37.5 4.6 %copy-start.12 = (f32[1,13,35,128]{3,2,1,0:T(8,128)S(1)}, f32[1,13,35,128]{3,2,1,0:T(8,128)}, u32[]{:S(2)}) copy-start(f32[1,13,35,128]{3,2,1,0:T(8,128)} %get-tuple-element.24) | copy-start | bytes 698884
  41.1 3.1 %copy-start.36 = (s32[7680]{0:T(1024)S(1)}, s32[7680]{0:T(1024)}, u32[]{:S(2)}) copy-start(s32[7680]{0:T(1024)} %fusion.40) | copy-start | bytes 92164
  43.1 2.8 %copy-start.46 = (f32[3,4,128]{2,1,0:T(4,128)S(1)}, f32[3,4,128]{2,1,0:T(4,128)}, u32[]{:S(2)}) copy-start(f32[3,4,128]{2,1,0:T(4,128)} %param.31) | copy-start | bytes 18436
  45.9 38.7 %copy-start.43 = (f32[3,4,128]{2,0,1:T(4,128)}, f32[3,4,128]{2,0,1:T(4,128)S(1)}, u32[]{:S(2)}) copy-start(f32[3,4,128]{2,0,1:T(4,128)S(1)} %copy.232) | copy-start | bytes 18436
  81.7 2.9 %copy-start.18 = (f32[3,6,13,13]{3,2,1,0:T(8,128)S(1)}, f32[3,6,13,13]{3,2,1,0:T(8,128)}, u32[]{:S(2)}) copy-start(f32[3,6,13,13]{3,2,1,0:T(8,128)} %param.29) | copy-start | bytes 36508
  84.6 3.8 %copy-start.6 = (f32[13,35,128]{2,0,1:T(8,128)S(1)}, f32[13,35,128]{2,0,1:T(8,128)}, u32[]{:S(2)}) copy-start(f32[13,35,128]{2,0,1:T(8,128)} %fusion.5) | copy-start | bytes 698884
  84.6 3.8 %copy-start.34 = (f32[4,35,15,1]{1,2,0,3:T(8,128)S(1)}, f32[4,35,15,1]{1,2,0,3:T(8,128)}, u32[]{:S(2)}) copy-start(f32[4,35,15,1]{1,2,0,3:T(8,128)} %constant.75) | copy-start | bytes 25204
  84.6 4.6 %copy-start.14 = (f32[3,35,35,1]{2,1,3,0:T(8,128)S(1)}, f32[3,35,35,1]{2,1,3,0:T(8,128)}, u32[]{:S(2)}) copy-start(f32[3,35,35,1]{2,1,3,0:T(8,128)} %constant.74) | copy-start | bytes 44104
  92.8 16.7 %copy-start.38 = (f32[128]{0:T(128)S(1)}, f32[128]{0:T(128)}, u32[]{:S(2)}) copy-start(f32[128]{0:T(128)} %copy-done.37) | copy-start | bytes 1540
  100.4 9.9 %copy-start.16 = (f32[3,13,35,128,1]{3,2,1,0,4:T(8,128)S(1)}, f32[3,13,35,128,1]{3,2,1,0,4:T(8,128)}, u32[]{:S(2)}) copy-start(f32[3,13,35,128,1]{3,2,1,0,4:T(8,128)} %maximum_bitcast_fusion.2) | copy-start | bytes 2096644
  100.4 9.9 %copy-start.19 = (f32[3,6,13,13]{3,2,1,0:T(8,128)S(1)}, f32[3,6,13,13]{3,2,1,0:T(8,128)}, u32[]{:S(2)}) copy-start(f32[3,6,13,13]{3,2,1,0:T(8,128)} %param.29) | copy-start | bytes 36508
  102.5 15.5 %collective-permute-start.3 = (f32[13,15,64]{1,0,2:T(8,128)S(1)}, f32[13,15,64]{1,0,2:T(8,128)}, u32[]{:S(2)}, u32[]{:S(2)}) collective-permute-start(f32[13,15,64]{1,0,2:T(8,128)S(1)} %get-tuple-element.19), channel_id=1, source_target_pairs={{1,0},{2,1},{3,2},{4,3},{5,4},{6,5},{7,6},{9,8},{10,9},{11,10},{12... | collective-permute-start | bytes 149768 | tf_op jit(solution)/shard_map/ppermute | solution.py:21
  103.8 8.9 %copy-start.5 = (f32[6,35,128]{2,0,1:T(8,128)S(1)}, f32[6,35,128]{2,0,1:T(8,128)}, u32[]{:S(2)}) copy-start(f32[6,35,128]{2,0,1:T(8,128)} %copy.228) | copy-start | bytes 322564
  103.8 25.6 %collective-permute-start.2 = (f32[13,15,64]{1,0,2:T(8,128)}, f32[13,15,64]{1,0,2:T(8,128)}, u32[]{:S(2)}, u32[]{:S(2)}) collective-permute-start(f32[13,15,64]{1,0,2:T(8,128)} %get-tuple-element.18), channel_id=1, source_target_pairs={{0,1},{1,2},{2,3},{3,4},{4,5},{5,6},{6,7},{8,9},{9,10},{10,11},{11... | collective-permute-start | bytes 149768 | tf_op jit(solution)/shard_map/ppermute | solution.py:20
  151.4 2.9 %copy-start.20 = (f32[3,6,13,13]{3,2,1,0:T(8,128)S(1)}, f32[3,6,13,13]{3,2,1,0:T(8,128)}, u32[]{:S(2)}) copy-start(f32[3,6,13,13]{3,2,1,0:T(8,128)} %param.29) | copy-start | bytes 36508
  151.4 2.9 %copy-start.32 = (f32[60,6,128]{2,1,0:T(8,128)S(1)}, f32[60,6,128]{2,1,0:T(8,128)}, u32[]{:S(2)}) copy-start(f32[60,6,128]{2,1,0:T(8,128)} %copy.298) | copy-start | bytes 552964
  151.4 2.9 %copy-start.44 = (f32[3,4,128]{2,0,1:T(4,128)S(1)}, f32[3,4,128]{2,0,1:T(4,128)}, u32[]{:S(2)}) copy-start(f32[3,4,128]{2,0,1:T(4,128)} %copy-done.43) | copy-start | bytes 18436
  154.3 2.8 %copy-start.35 = (f32[4,35,15,1]{1,2,0,3:T(8,128)S(1)}, f32[4,35,15,1]{1,2,0,3:T(8,128)}, u32[]{:S(2)}) copy-start(f32[4,35,15,1]{1,2,0,3:T(8,128)} %constant.75) | copy-start | bytes 25204
  154.3 3.6 %copy-start.15 = (f32[3,13,35,128,1]{3,2,1,0,4:T(8,128)S(1)}, f32[3,13,35,128,1]{3,2,1,0,4:T(8,128)}, u32[]{:S(2)}) copy-start(f32[3,13,35,128,1]{3,2,1,0,4:T(8,128)} %maximum_bitcast_fusion.3) | copy-start | bytes 2096644
  157.0 2.8 %copy-start.33 = (f32[6,35,128]{2,0,1:T(8,128)S(1)}, f32[6,35,128]{2,0,1:T(8,128)}, u32[]{:S(2)}) copy-start(f32[6,35,128]{2,0,1:T(8,128)} %fusion.3) | copy-start | bytes 322564
  157.9 3.3 %copy-start.50 = (f32[25]{0:T(128)S(1)}, f32[25]{0:T(128)}, u32[]{:S(2)}) copy-start(f32[25]{0:T(128)} %reshape.337) | copy-start | bytes 304
  157.9 3.3 %copy-start.51 = (f32[25]{0:T(128)S(1)}, f32[25]{0:T(128)}, u32[]{:S(2)}) copy-start(f32[25]{0:T(128)} %reshape.336) | copy-start | bytes 304
  158.0 91.1 %copy-start.21 = (f32[1,6,35,32]{2,1,3,0:T(8,128)S(1)}, f32[1,6,35,32]{2,1,3,0:T(8,128)}, u32[]{:S(2)}) copy-start(f32[1,6,35,32]{2,1,3,0:T(8,128)} %copy.329) | copy-start | bytes 80644
  158.0 91.1 %copy-start.22 = (f32[1,6,35,32]{2,1,3,0:T(8,128)S(1)}, f32[1,6,35,32]{2,1,3,0:T(8,128)}, u32[]{:S(2)}) copy-start(f32[1,6,35,32]{2,1,3,0:T(8,128)} %copy.328) | copy-start | bytes 80644
  158.0 91.1 %copy-start.23 = (f32[1,6,35,32]{2,1,3,0:T(8,128)S(1)}, f32[1,6,35,32]{2,1,3,0:T(8,128)}, u32[]{:S(2)}) copy-start(f32[1,6,35,32]{2,1,3,0:T(8,128)} %copy.327) | copy-start | bytes 80644
  158.0 91.1 %copy-start.24 = (f32[1,6,35,32]{2,1,3,0:T(8,128)S(1)}, f32[1,6,35,32]{2,1,3,0:T(8,128)}, u32[]{:S(2)}) copy-start(f32[1,6,35,32]{2,1,3,0:T(8,128)} %copy.326) | copy-start | bytes 80644
  158.0 91.1 %copy-start.25 = (f32[1,6,35,32]{2,1,3,0:T(8,128)S(1)}, f32[1,6,35,32]{2,1,3,0:T(8,128)}, u32[]{:S(2)}) copy-start(f32[1,6,35,32]{2,1,3,0:T(8,128)} %copy.325) | copy-start | bytes 80644
  158.0 91.1 %copy-start.26 = (f32[1,6,35,32]{2,1,3,0:T(8,128)S(1)}, f32[1,6,35,32]{2,1,3,0:T(8,128)}, u32[]{:S(2)}) copy-start(f32[1,6,35,32]{2,1,3,0:T(8,128)} %copy.324) | copy-start | bytes 80644
  158.1 91.1 %copy-start.27 = (f32[1,6,35,32]{2,1,3,0:T(8,128)S(1)}, f32[1,6,35,32]{2,1,3,0:T(8,128)}, u32[]{:S(2)}) copy-start(f32[1,6,35,32]{2,1,3,0:T(8,128)} %copy.323) | copy-start | bytes 80644
  159.9 89.4 %copy-start.28 = (f32[1,6,35,32]{2,1,3,0:T(8,128)S(1)}, f32[1,6,35,32]{2,1,3,0:T(8,128)}, u32[]{:S(2)}) copy-start(f32[1,6,35,32]{2,1,3,0:T(8,128)} %copy.322) | copy-start | bytes 80644
  159.9 89.4 %copy-start.29 = (f32[1,6,35,32]{2,1,3,0:T(8,128)S(1)}, f32[1,6,35,32]{2,1,3,0:T(8,128)}, u32[]{:S(2)}) copy-start(f32[1,6,35,32]{2,1,3,0:T(8,128)} %copy.321) | copy-start | bytes 80644
  159.9 89.4 %copy-start.30 = (f32[1,6,35,32]{2,1,3,0:T(8,128)S(1)}, f32[1,6,35,32]{2,1,3,0:T(8,128)}, u32[]{:S(2)}) copy-start(f32[1,6,35,32]{2,1,3,0:T(8,128)} %copy.320) | copy-start | bytes 80644
Sparse Core Ops, SparseCore 0:
  203.5 21.7 reduce-scatter.1

commit v2 on v1

--- a/solution.py
+++ b/solution.py
@@ -148,23 +148,19 @@
     )
 
 
-def search_direction(grad_share, local_grad, step_rows, change_rows, own_share, combine_sums):
+def search_direction(grad_share, local_grad, step_rows, change_rows, own_share, keep_gram, combine_sums):
     pairs = step_rows.shape[0]
-    step_share = own_share(step_rows)
-    change_share = own_share(change_rows)
-    step_grad = jnp.sum(step_rows * local_grad[None], axis=(1, 2, 3))
-    change_grad = jnp.sum(change_rows * local_grad[None], axis=(1, 2, 3))
-    step_change = jnp.sum(step_share[:, None] * change_share[None, :], axis=(2, 3, 4))
-    change_change = jnp.sum(change_share[:, None] * change_share[None, :], axis=(2, 3, 4))
-    summed = combine_sums(
-        jnp.concatenate(
-            [step_grad, change_grad, step_change.reshape(-1), change_change.reshape(-1)]
-        )
-    )
+    step_flat = step_rows.reshape(pairs, -1)
+    change_flat = change_rows.reshape(pairs, -1)
+    both_flat = jnp.concatenate([step_flat, change_flat], axis=0)
+    with_grad = jnp.dot(both_flat, local_grad.reshape(-1), precision=HIGH)
+    gram = jnp.dot(both_flat, change_flat.T, precision=HIGH) * keep_gram
+    summed = combine_sums(jnp.concatenate([with_grad, gram.reshape(-1)]))
     step_grad = summed[:pairs]
     change_grad = summed[pairs : 2 * pairs]
-    step_change = summed[2 * pairs : 2 * pairs + pairs * pairs].reshape(pairs, pairs)
-    change_change = summed[2 * pairs + pairs * pairs :].reshape(pairs, pairs)
+    gram = summed[2 * pairs :].reshape(2 * pairs, pairs)
+    step_change = gram[:pairs]
+    change_change = gram[pairs:]
     curvature = [step_change[slot, slot] for slot in range(pairs)]
     alphas = [None] * pairs
     for slot in reversed(range(pairs)):
@@ -183,6 +179,8 @@
             along = along + weights[earlier] * step_change[earlier, slot]
         beta_now = along / curvature[slot]
         weights[slot] = alphas[slot] - beta_now
+    step_share = own_share(step_rows)
+    change_share = own_share(change_rows)
     work = scaling * grad_share
     for slot in range(pairs):
         work = work - (scaling * alphas[slot]) * change_share[slot]
@@ -250,12 +248,17 @@
     def own_share(rows):
         return lax.dynamic_slice_in_dim(rows, share_start, share_width, rows.ndim - 1)
 
+    device_count = shot_count * lax.axis_size("mesh")
+
     def combine_sums(values):
-        return lax.psum(values, ("shot", "mesh"))
-
-    grad_share = lax.psum_scatter(gradient, "shot", scatter_dimension=2, tiled=True)
+        spread = jnp.broadcast_to(values[None], (device_count,) + values.shape)
+        return jnp.sum(lax.all_to_all(spread, ("shot", "mesh"), 0, 0, tiled=False), axis=0)
+
+    pieces = gradient.reshape(params, node_count, shot_count, share_width)
+    grad_share = jnp.sum(lax.all_to_all(pieces, "shot", 2, 2, tiled=False), axis=2)
+    keep_gram = (lax.axis_index("shot") == 0).astype(jnp.float32)
     result = search_direction(
-        grad_share, gradient, history_steps, history_changes, own_share, combine_sums
+        grad_share, gradient, history_steps, history_changes, own_share, keep_gram, combine_sums
     )
     return (adjoint[None], result)
 

time: 259 us -> 213 us (0.82)
  blocking collectives: 41.4 us -> 0 us
  between operations: 57.5 us -> 43.9 us
  local copies, waits for them, and re-layouts: 100 us -> 87.2 us
  starting transfers between devices: 14.5 us -> 23.8 us
  waiting for transfers between devices: 13.8 us -> 19.4 us
  matrix products: 19.2 us -> 24.4 us
    psum x1 -> x0, blocking collectives: 41.4 us -> none  [combine_sums(): return lax.psum(values, ('shot', 'mesh'))]
    unnamed x134 -> x139, local copies, waits for them, and re-layouts: 14.9 us -> 4.71 us
    all_to_all x0 -> x2, starting transfers between devices: none -> 9.14 us  [the longest x1 5.83 us: combine_sums(): lax.all_to_all(spread, ('shot', 'mesh'), 0, 0, tiled=False)]
    all_to_all x0 -> x2, waiting for transfers between devices: none -> 4.62 us  [the longest x1 4.62 us: combine_sums(): lax.all_to_all(spread, ('shot', 'mesh'), 0, 0, tiled=False)]
    dot_general x0 -> x2, matrix products: none -> 4.51 us  [the longest x1 2.27 us: search_direction(): with_grad = jnp.dot(both_flat, local_grad.reshape(-1), precision=HIGH)]
    dynamic_slice x3 -> x0, local copies, waits for them, and re-layouts: 4.12 us -> none  [own_share(): lax.dynamic_slice_in_dim(rows, share_start, share_width, rows.ndim - 1)]
  transfers between devices with their start and end apart: 5 -> 6, of which waited for: 2 -> 4; matrix products, arithmetic and copies ran while one was open for 17% -> 15% of each run, Pallas kernels for 0% -> 0%
where the time goes in v2:
time: 213 us; the launch traced here: 212 us
  local copies, waits for them, and re-layouts  87.2 us (41%)
  between operations  43.9 us (21%)
  matrix products  24.4 us (11%)
  starting transfers between devices  23.8 us (11%)
  waiting for transfers between devices  19.4 us (9%)
  other arithmetic  12.8 us (6%)
    gather x2, local copies, waits for them, and re-layouts, shards(): turned = ghosts.reshape(fields, face_width * slot_count)[:, flat_index]  34.5 us
    ppermute x2, starting transfers between devices, padded(): before = lax.ppermute(last, axis, up)  12.1 us
    ppermute x2, waiting for transfers between devices, padded(): before = lax.ppermute(last, axis, up)  10.5 us
    reshape x4, local copies, waits for them, and re-layouts, shards(): flat_trace = inner_trace.reshape(fields, face_width, 4 * elements)  8.71 us
    gather x2, local copies, waits for them, and re-layouts, shards(): sent_traces = flat_trace[:, :, send_faces]  6.91 us
    concatenate x2, local copies, waits for them, and re-layouts, shards(): jnp.concatenate([flat_trace, extended[:, :, :border], extended[:, :, 3 *...  6.52 us
    all_to_all x1, starting transfers between devices, combine_sums(): lax.all_to_all(spread, ('shot', 'mesh'), 0, 0, tiled=False)  5.83 us
    reshape x2, local copies, waits for them, and re-layouts, shards(): jump_trace = turned.reshape(fields, face_width, 4, elements) - inner_trace  5.56 us
  transfers between devices with their start and end apart: 6, of which 4 were waited for; matrix products, arithmetic and copies ran while one was open for 15% of the time, Pallas kernels for 0%

profile of v2, /device:TPU:0, one launch (start us, length us, event | category | flops | bytes accessed | tf_op | source)
XLA Modules:
  0.0 211.6 jit_solution(12440878787355908564)
XLA Ops:
  0.6 0.7 pad_clamp_fusion.2
  1.3 1.0 copy.433
  3.2 3.7 %copy.312 = f32[13,15,512]{1,0,2:T(8,128)} copy(f32[13,15,512]{2,1,0:T(8,128)S(1)} %reshape.342) | data formatting | bytes 798720 | tf_op jit(solution)/shard_map/reshape | solution.py:229
  7.1 3.0 %gather_fusion.2 = f32[128,13,15]{2,1,0:T(8,128)S(1)} fusion(f32[13,15,512]{1,0,2:T(8,128)} %copy.312, s32[1024]{0:T(1024)S(1)} %pad_clamp_fusion.1), kind=kCustom, calls=%fused_computation.2 | custom fusion | bytes 200192 | tf_op jit(solution)/shard_map/gather | solution.py:230
  10.1 1.0 fusion.68
  11.1 1.3 collective-permute-start.1
  12.4 6.3 %collective-permute-start = (f32[13,15,64]{1,0,2:T(8,128)}, f32[13,15,64]{1,0,2:T(8,128)}, u32[]{:S(2)}, u32[]{:S(2)}) collective-permute-start(f32[13,15,64]{1,0,2:T(8,128)} %get-tuple-element.20), channel_id=1, source_target_pairs={{0,1},{1,2},{2,3},{3,4},{4,5},{5,6},{6,7},{8,9},{9,10},{10,11},{11... | collective-permute-start | bytes 149768 | tf_op jit(solution)/shard_map/ppermute | solution.py:20
  18.9 0.7 fusion.64
  20.2 0.8 convolution_bitcast_fusion.3
  21.6 0.8 convolution_bitcast_fusion
  22.5 0.9 multiply_add_fusion.11
  23.4 1.0 multiply_add_fusion.2
  24.4 0.8 convolution_bitcast_fusion.1
  25.3 1.0 multiply_add_fusion.5
  26.4 1.3 reshape.348
  27.7 1.2 maximum_bitcast_fusion
  29.0 2.3 %fusion.7 = f32[13,35,128]{2,0,1:T(8,128)} fusion(f32[3,13,35,128,1]{3,2,1,0,4:T(8,128)S(1)} %maximum_bitcast_fusion, f32[6,35,128]{2,0,1:T(8,128)S(1)} %copy.305, f32[3,6,13,13]{3,2,1,0:T(8,128)S(1)} %copy-done.19), kind=kOutput, calls=%fused_computation.21 | convolution fusion | flops 164178560 | bytes 1051528 | tf_op jit(solution)/shard_map/dpfg,dfae->pgae/dot_general | solution.py:132
  31.3 1.0 maximum_bitcast_fusion.3
  32.3 1.0 maximum_bitcast_fusion.2
  33.3 2.2 %fusion.18 = f32[10,5]{0,1:T(8,128)S(1)} fusion(f32[5,26880]{1,0:T(8,128)S(1)} %reshape.349, f32[5,26880]{1,0:T(8,128)S(1)} %reshape.348, f32[]{:T(128)S(6)} %convert_element_type.75), kind=kOutput, calls=%fused_computation.38 | convolution fusion | flops 16396850 | bytes 1075404 | tf_op jit(solution)/shard_map/dot_general | solution.py:157
  35.5 0.6 pad_clamp_fusion
  36.2 0.8 gather_fusion
  37.0 0.8 copy.373
  38.0 1.3 copy.314
  39.6 1.9 copy.313
  41.5 1.0 pad_maximum_fusion.7
  42.5 3.2 %copy.315 = f32[13,15,640]{0,2,1:T(8,128)} copy(f32[13,15,640]{2,1,0:T(8,128)S(1)} %pad_maximum_fusion.7) | data formatting | bytes 998400 | tf_op jit(solution)/shard_map/concatenate | solution.py:232
  45.8 17.3 %gather_fusion.3 = f32[7680,13]{1,0:T(8,128)} fusion(f32[13,9600]{0,1:T(8,128)} %bitcast.326, s32[8192]{0:T(1024)S(1)} %copy-done.24), kind=kCustom, calls=%fused_computation.3 | custom fusion | bytes 829440 | tf_op jit(solution)/shard_map/gather | solution.py:235
  63.0 2.8 %copy.316 = f32[13,15,4,128]{3,0,2,1:T(8,128)S(1)} copy(f32[13,15,4,128]{0,3,2,1:T(8,128)} %bitcast.328) | data formatting | bytes 798720 | tf_op jit(solution)/shard_map/reshape | solution.py:236
  66.0 2.7 %fusion.1 = f32[13,15,4,128]{3,0,2,1:T(8,128)S(1)} fusion(f32[6,15,4,128]{3,0,2,1:T(8,128)S(1)} %bitcast.338, f32[13,15,4,128]{3,0,2,1:T(8,128)S(1)} %sub.149, f32[3,4,128]{2,0,1:T(4,128)S(1)} %copy.309, f32[3,6,13,13]{3,2,1,0:T(8,128)S(1)} %copy-done.20), kind=kOutput, calls=%fused_computation.10 | convolution fusion | flops 281748480 | bytes 1001352 | tf_op jit(solution)/shard_map/dpfg,dfnxe->pgnxe/dot_general | solution.py:144
  68.8 0.7 fusion.14
  69.6 1.7 convolution_bitcast_fusion.2
  72.0 0.9 copy.324
  72.9 1.2 reshape.345
  74.1 3.7 %copy.325 = f32[13,15,512]{1,0,2:T(8,128)} copy(f32[13,15,512]{2,1,0:T(8,128)S(1)} %reshape.345) | data formatting | bytes 798720 | tf_op jit(solution)/shard_map/reshape | solution.py:229
  77.8 3.9 %gather_fusion.5 = f32[128,13,15]{2,1,0:T(8,128)} fusion(f32[13,15,512]{1,0,2:T(8,128)} %copy.325, s32[1024]{0:T(1024)} %copy-done.53), kind=kCustom, calls=%fused_computation.5 | custom fusion | bytes 200192 | tf_op jit(solution)/shard_map/gather | solution.py:230
  81.8 2.2 %fusion.67 = (f32[13,15,64]{1,0,2:T(8,128)}, f32[13,15,64]{1,0,2:T(8,128)S(1)}) fusion(f32[13,15,128]{1,0,2:T(8,128)} %bitcast.336), kind=kLoop, calls=%fused_computation.147 | loop fusion | bytes 199680 | tf_op jit(solution)/shard_map/slice | solution.py:18
  84.0 1.3 collective-permute-start.3
  85.2 5.8 %collective-permute-start.2 = (f32[13,15,64]{1,0,2:T(8,128)}, f32[13,15,64]{1,0,2:T(8,128)}, u32[]{:S(2)}, u32[]{:S(2)}) collective-permute-start(f32[13,15,64]{1,0,2:T(8,128)} %get-tuple-element.18), channel_id=1, source_target_pairs={{0,1},{1,2},{2,3},{3,4},{4,5},{5,6},{6,7},{8,9},{9,10},{10,11},{11... | collective-permute-start | bytes 149768 | tf_op jit(solution)/shard_map/ppermute | solution.py:20
  91.3 2.4 %fusion.5 = f32[6,35,128]{2,0,1:T(8,128)} fusion(f32[3,13,35,128,1]{3,2,1,0,4:T(8,128)S(1)} %copy-done.18, f32[13,35,128]{2,0,1:T(8,128)S(1)} %copy.323, f32[3,6,13,13]{3,2,1,0:T(8,128)S(1)} %copy-done.21), kind=kOutput, calls=%fused_computation.17 | convolution fusion | flops 164209920 | bytes 1051528 | tf_op jit(solution)/shard_map/dpfg,dgae->pfae/dot_general | solution.py:138
  93.8 2.3 %fusion.6 = f32[13,35,128]{2,0,1:T(8,128)} fusion(f32[3,13,35,128,1]{3,2,1,0,4:T(8,128)S(1)} %maximum_bitcast_fusion.1, f32[6,35,128]{2,0,1:T(8,128)S(1)} %copy-done.7, f32[3,6,13,13]{3,2,1,0:T(8,128)S(1)} %copy-done.21), kind=kOutput, calls=%fused_computation.19 | convolution fusion | flops 164178560 | bytes 1051528 | tf_op jit(solution)/shard_map/dpfg,dfae->pgae/dot_general | solution.py:132
  96.2 4.3 %collective-permute-done.3 = f32[13,15,64]{1,0,2:T(8,128)} collective-permute-done((f32[13,15,64]{1,0,2:T(8,128)S(1)}, f32[13,15,64]{1,0,2:T(8,128)}, u32[]{:S(2)}, u32[]{:S(2)}) %collective-permute-start.3) | collective-permute-done | bytes 49952 | tf_op jit(solution)/shard_map/ppermute | solution.py:21
  100.5 1.3 copy.327
  101.8 10.1 %collective-permute-done.2 = f32[13,15,64]{1,0,2:T(8,128)} collective-permute-done((f32[13,15,64]{1,0,2:T(8,128)}, f32[13,15,64]{1,0,2:T(8,128)}, u32[]{:S(2)}, u32[]{:S(2)}) %collective-permute-start.2) | collective-permute-done | bytes 49952 | tf_op jit(solution)/shard_map/ppermute | solution.py:20
  111.9 1.9 copy.326
  113.8 1.0 pad_maximum_fusion.8
  114.8 3.3 %copy.328 = f32[13,15,640]{0,2,1:T(8,128)} copy(f32[13,15,640]{2,1,0:T(8,128)S(1)} %pad_maximum_fusion.8) | data formatting | bytes 998400 | tf_op jit(solution)/shard_map/concatenate | solution.py:232
  118.1 17.3 %gather_fusion.6 = f32[7680,13]{1,0:T(8,128)} fusion(f32[13,9600]{0,1:T(8,128)} %bitcast.325, s32[8192]{0:T(1024)S(1)} %copy-done.25), kind=kCustom, calls=%fused_computation.6 | custom fusion | bytes 829440 | tf_op jit(solution)/shard_map/gather | solution.py:235
  135.4 2.8 %copy.329 = f32[13,15,4,128]{3,0,2,1:T(8,128)S(1)} copy(f32[13,15,4,128]{0,3,2,1:T(8,128)} %bitcast.327) | data formatting | bytes 798720 | tf_op jit(solution)/shard_map/reshape | solution.py:236
  138.3 2.7 %fusion = f32[13,15,4,128]{3,0,2,1:T(8,128)S(1)} fusion(f32[6,15,4,128]{3,0,2,1:T(8,128)S(1)} %bitcast.339, f32[13,15,4,128]{3,0,2,1:T(8,128)S(1)} %sub.150, f32[3,4,128]{2,0,1:T(4,128)S(1)} %copy-done.52, f32[3,6,13,13]{3,2,1,0:T(8,128)S(1)} %copy-done.22), kind=kOutput, calls=%fused_computation.8 | convolution fusion | flops 281748480 | bytes 1001352 | tf_op jit(solution)/shard_map/dpfg,dfnxe->pgnxe/dot_general | solution.py:144
  141.1 0.7 fusion.17
  142.1 1.8 fusion.4
  144.1 2.3 %fusion.19 = f32[10]{0:T(128)S(1)} fusion(f32[26880,1]{0,1:T(1,128)S(1)} %reshape.449, f32[5,26880]{1,0:T(8,128)S(1)} %reshape.349, f32[5,26880]{1,0:T(8,128)S(1)} %reshape.348), kind=kOutput, calls=%fused_computation.39 | convolution fusion | flops 3494400 | bytes 1182760 | tf_op jit(solution)/shard_map/dot_general | solution.py:156
  147.1 5.8 %all-to-all-start = ((f32[32,1,60]{2,1,0:T(1,128)}), f32[32,1,60]{2,1,0:T(1,128)S(1)}, u32[]{:S(2)}, u32[]{:S(2)}) async-start(f32[32,1,60]{2,1,0:T(1,128)} %broadcast_in_dim.17), calls=%async_computation | async-start | bytes 32768 | tf_op jit(solution)/shard_map/all_to_all | solution.py:255
  153.1 0.9 copy.347
  154.3 1.0 reshape.454
  155.3 4.6 %all-to-all-done = f32[32,1,60]{2,1,0:T(1,128)S(1)} async-done(((f32[32,1,60]{2,1,0:T(1,128)}), f32[32,1,60]{2,1,0:T(1,128)S(1)}, u32[]{:S(2)}, u32[]{:S(2)}) %all-to-all-start) | async-done | bytes 7712 | tf_op jit(solution)/shard_map/all_to_all | solution.py:255
  160.0 3.3 %all-to-all-start.1 = ((f32[4,1,6720]{2,1,0:T(1,128)}), f32[4,1,6720]{2,1,0:T(1,128)S(1)}, u32[]{:S(2)}, u32[]{:S(2)}) async-start(f32[4,1,6720]{2,1,0:T(1,128)} %reshape.454), calls=%async_computation.1 | async-start | bytes 217088 | tf_op jit(solution)/shard_map/all_to_all | solution.py:258
  163.3 0.7 fusion.73
  164.2 0.7 fusion.72
  164.9 0.7 fusion.71
  186.5 0.7 fusion.70
  209.0 0.9 reduce.3
  210.9 0.8 copy.348
  (173 shorter events, 7.5 us)
Async XLA Ops:
  3.2 3.7 %copy-start.64 = (s32[128]{0:T(128)S(1)}, s32[128]{0:T(128)}, u32[]{:S(2)}) copy-start(s32[128]{0:T(128)} %param.35) | copy-start | bytes 1540
  6.9 11.8 %copy-start.56 = (s32[4,128]{1,0:T(4,128)S(1)}, s32[4,128]{1,0:T(4,128)}, u32[]{:S(2)}) copy-start(s32[4,128]{1,0:T(4,128)} %param.34) | copy-start | bytes 6148
  6.9 11.8 %copy-start.57 = (s32[4,128]{1,0:T(4,128)S(1)}, s32[4,128]{1,0:T(4,128)}, u32[]{:S(2)}) copy-start(s32[4,128]{1,0:T(4,128)} %param.33) | copy-start | bytes 6148
  6.9 11.8 %copy-start.59 = (s32[15]{0:T(128)S(1)}, s32[15]{0:T(128)}, u32[]{:S(2)}) copy-start(s32[15]{0:T(128)} %constant.67.clone) | copy-start | bytes 184
  7.0 11.8 %copy-start.60 = (s32[15]{0:T(128)S(1)}, s32[15]{0:T(128)}, u32[]{:S(2)}) copy-start(s32[15]{0:T(128)} %constant.66.clone) | copy-start | bytes 184
  7.0 11.8 %copy-start.61 = (s32[15]{0:T(128)S(1)}, s32[15]{0:T(128)}, u32[]{:S(2)}) copy-start(s32[15]{0:T(128)} %constant.65.clone) | copy-start | bytes 184
  7.0 11.8 %copy-start.62 = (s32[15]{0:T(128)S(1)}, s32[15]{0:T(128)}, u32[]{:S(2)}) copy-start(s32[15]{0:T(128)} %constant.64.clone) | copy-start | bytes 184
  7.0 11.8 %copy-start.63 = (s32[15]{0:T(128)S(1)}, s32[15]{0:T(128)}, u32[]{:S(2)}) copy-start(s32[15]{0:T(128)} %constant.63.clone) | copy-start | bytes 184
  7.0 12.6 %copy-start.58 = (f32[4,128]{1,0:T(4,128)S(1)}, f32[4,128]{1,0:T(4,128)}, u32[]{:S(2)}) copy-start(f32[4,128]{1,0:T(4,128)} %param.32) | copy-start | bytes 6148
  7.0 13.2 %copy-start.2 = (f32[1,13,35,128]{3,0,2,1:T(1,128)S(1)}, f32[1,13,35,128]{3,0,2,1:T(1,128)}, u32[]{:S(2)}) copy-start(f32[1,13,35,128]{3,0,2,1:T(1,128)} %param.26) | copy-start | bytes 698884
  7.0 13.2 %copy-start.15 = (f32[3,35,35,1]{2,1,3,0:T(8,128)S(1)}, f32[3,35,35,1]{2,1,3,0:T(8,128)}, u32[]{:S(2)}) copy-start(f32[3,35,35,1]{2,1,3,0:T(8,128)} %constant.74) | copy-start | bytes 44104
  7.1 11.7 %copy-start.53 = (s32[1024]{0:T(1024)}, s32[1024]{0:T(1024)S(1)}, u32[]{:S(2)}) copy-start(s32[1024]{0:T(1024)S(1)} %pad_clamp_fusion.1) | copy-start | bytes 12292
  10.0 11.0 %copy-start.55 = (f32[3,3,128]{2,1,0:T(4,128)S(1)}, f32[3,3,128]{2,1,0:T(4,128)}, u32[]{:S(2)}) copy-start(f32[3,3,128]{2,1,0:T(4,128)} %param.30) | copy-start | bytes 13828
  10.1 11.0 %copy-start = (f32[6,35,128]{2,1,0:T(8,128)S(1)}, f32[6,35,128]{2,1,0:T(8,128)}, u32[]{:S(2)}) copy-start(f32[6,35,128]{2,1,0:T(8,128)} %param.28) | copy-start | bytes 322564
  10.1 11.2 %copy-start.23 = (f32[1,2,13,35,128]{4,1,3,2,0:T(2,128)S(1)}, f32[1,2,13,35,128]{4,1,3,2,0:T(2,128)}, u32[]{:S(2)}) copy-start(f32[1,2,13,35,128]{4,1,3,2,0:T(2,128)} %param.27) | copy-start | bytes 1397764
  11.1 26.9 %collective-permute-start.1 = (f32[13,15,64]{1,0,2:T(8,128)}, f32[13,15,64]{1,0,2:T(8,128)}, u32[]{:S(2)}, u32[]{:S(2)}) collective-permute-start(f32[13,15,64]{1,0,2:T(8,128)} %get-tuple-element.21), channel_id=1, source_target_pairs={{1,0},{2,1},{3,2},{4,3},{5,4},{6,5},{7,6},{9,8},{10,9},{11,10},{12... | collective-permute-start | bytes 149768 | tf_op jit(solution)/shard_map/ppermute | solution.py:21
  12.4 27.2 %collective-permute-start = (f32[13,15,64]{1,0,2:T(8,128)}, f32[13,15,64]{1,0,2:T(8,128)}, u32[]{:S(2)}, u32[]{:S(2)}) collective-permute-start(f32[13,15,64]{1,0,2:T(8,128)} %get-tuple-element.20), channel_id=1, source_target_pairs={{0,1},{1,2},{2,3},{3,4},{4,5},{5,6},{6,7},{8,9},{9,10},{10,11},{11... | collective-permute-start | bytes 149768 | tf_op jit(solution)/shard_map/ppermute | solution.py:20
  21.1 4.1 %copy-start.33 = (f32[128]{0:T(128)}, f32[128]{0:T(128)S(1)}, u32[]{:S(2)}) copy-start(f32[128]{0:T(128)S(1)} %get-tuple-element.36) | copy-start | bytes 1540
  21.1 4.1 %copy-start.35 = (f32[128]{0:T(128)}, f32[128]{0:T(128)S(1)}, u32[]{:S(2)}) copy-start(f32[128]{0:T(128)S(1)} %get-tuple-element.37) | copy-start | bytes 1540
  21.1 4.1 %copy-start.37 = (f32[128]{0:T(128)}, f32[128]{0:T(128)S(1)}, u32[]{:S(2)}) copy-start(f32[128]{0:T(128)S(1)} %get-tuple-element.38) | copy-start | bytes 1540
  21.1 4.1 %copy-start.39 = (f32[128]{0:T(128)}, f32[128]{0:T(128)S(1)}, u32[]{:S(2)}) copy-start(f32[128]{0:T(128)S(1)} %get-tuple-element.39) | copy-start | bytes 1540
  21.1 4.1 %copy-start.41 = (f32[128]{0:T(128)}, f32[128]{0:T(128)S(1)}, u32[]{:S(2)}) copy-start(f32[128]{0:T(128)S(1)} %get-tuple-element.40) | copy-start | bytes 1540
  21.2 4.1 %copy-start.43 = (f32[128]{0:T(128)}, f32[128]{0:T(128)S(1)}, u32[]{:S(2)}) copy-start(f32[128]{0:T(128)S(1)} %get-tuple-element.41) | copy-start | bytes 1540
  21.2 4.1 %copy-start.45 = (f32[128]{0:T(128)}, f32[128]{0:T(128)S(1)}, u32[]{:S(2)}) copy-start(f32[128]{0:T(128)S(1)} %get-tuple-element.42) | copy-start | bytes 1540
  21.2 4.1 %copy-start.47 = (f32[128]{0:T(128)}, f32[128]{0:T(128)S(1)}, u32[]{:S(2)}) copy-start(f32[128]{0:T(128)S(1)} %get-tuple-element.43) | copy-start | bytes 1540
  21.2 4.1 %copy-start.49 = (f32[128]{0:T(128)}, f32[128]{0:T(128)S(1)}, u32[]{:S(2)}) copy-start(f32[128]{0:T(128)S(1)} %get-tuple-element.44) | copy-start | bytes 1540
  21.2 7.7 %copy-start.6 = (f32[6,35,128]{2,0,1:T(8,128)}, f32[6,35,128]{2,0,1:T(8,128)S(1)}, u32[]{:S(2)}) copy-start(f32[6,35,128]{2,0,1:T(8,128)S(1)} %copy.305) | copy-start | bytes 322564
  27.7 3.6 %copy-start.10 = (f32[1,13,35,128]{3,2,1,0:T(8,128)S(1)}, f32[1,13,35,128]{3,2,1,0:T(8,128)}, u32[]{:S(2)}) copy-start(f32[1,13,35,128]{3,2,1,0:T(8,128)} %get-tuple-element.26) | copy-start | bytes 698884
  27.7 3.6 %copy-start.11 = (f32[1,13,35,128]{3,2,1,0:T(8,128)S(1)}, f32[1,13,35,128]{3,2,1,0:T(8,128)}, u32[]{:S(2)}) copy-start(f32[1,13,35,128]{3,2,1,0:T(8,128)} %get-tuple-element.27) | copy-start | bytes 698884
  29.0 3.3 %copy-start.12 = (f32[1,13,35,128]{3,2,1,0:T(8,128)S(1)}, f32[1,13,35,128]{3,2,1,0:T(8,128)}, u32[]{:S(2)}) copy-start(f32[1,13,35,128]{3,2,1,0:T(8,128)} %get-tuple-element.22) | copy-start | bytes 698884
  29.0 3.3 %copy-start.13 = (f32[1,13,35,128]{3,2,1,0:T(8,128)S(1)}, f32[1,13,35,128]{3,2,1,0:T(8,128)}, u32[]{:S(2)}) copy-start(f32[1,13,35,128]{3,2,1,0:T(8,128)} %get-tuple-element.23) | copy-start | bytes 698884
  29.0 3.3 %copy-start.14 = (f32[1,13,35,128]{3,2,1,0:T(8,128)S(1)}, f32[1,13,35,128]{3,2,1,0:T(8,128)}, u32[]{:S(2)}) copy-start(f32[1,13,35,128]{3,2,1,0:T(8,128)} %get-tuple-element.24) | copy-start | bytes 698884
  32.3 3.2 %copy-start.31 = (s32[7680]{0:T(1024)S(1)}, s32[7680]{0:T(1024)}, u32[]{:S(2)}) copy-start(s32[7680]{0:T(1024)} %fusion.64) | copy-start | bytes 92164
  33.3 4.5 %copy-start.54 = (f32[3,4,128]{2,1,0:T(4,128)S(1)}, f32[3,4,128]{2,1,0:T(4,128)}, u32[]{:S(2)}) copy-start(f32[3,4,128]{2,1,0:T(4,128)} %param.31) | copy-start | bytes 18436
  37.8 28.1 %copy-start.51 = (f32[3,4,128]{2,0,1:T(4,128)}, f32[3,4,128]{2,0,1:T(4,128)S(1)}, u32[]{:S(2)}) copy-start(f32[3,4,128]{2,0,1:T(4,128)S(1)} %copy.309) | copy-start | bytes 18436
  42.5 3.3 %copy-start.24 = (s32[8192]{0:T(1024)S(1)}, s32[8192]{0:T(1024)}, u32[]{:S(2)}) copy-start(s32[8192]{0:T(1024)} %pad_clamp_fusion) | copy-start | bytes 98308
  63.0 2.9 %copy-start.20 = (f32[3,6,13,13]{3,2,1,0:T(8,128)S(1)}, f32[3,6,13,13]{3,2,1,0:T(8,128)}, u32[]{:S(2)}) copy-start(f32[3,6,13,13]{3,2,1,0:T(8,128)} %param.29) | copy-start | bytes 36508
  63.0 2.9 %copy-start.26 = (f32[60,6,128]{2,1,0:T(8,128)S(1)}, f32[60,6,128]{2,1,0:T(8,128)}, u32[]{:S(2)}) copy-start(f32[60,6,128]{2,1,0:T(8,128)} %copy.373) | copy-start | bytes 552964
  65.9 2.8 %copy-start.8 = (f32[13,35,128]{2,0,1:T(8,128)S(1)}, f32[13,35,128]{2,0,1:T(8,128)}, u32[]{:S(2)}) copy-start(f32[13,35,128]{2,0,1:T(8,128)} %fusion.7) | copy-start | bytes 698884
  65.9 2.8 %copy-start.29 = (f32[4,35,15,1]{1,2,0,3:T(8,128)S(1)}, f32[4,35,15,1]{1,2,0,3:T(8,128)}, u32[]{:S(2)}) copy-start(f32[4,35,15,1]{1,2,0,3:T(8,128)} %constant.75) | copy-start | bytes 25204
  77.7 13.3 %copy-start.34 = (f32[128]{0:T(128)S(1)}, f32[128]{0:T(128)}, u32[]{:S(2)}) copy-start(f32[128]{0:T(128)} %copy-done.33) | copy-start | bytes 1540
  77.7 13.3 %copy-start.36 = (f32[128]{0:T(128)S(1)}, f32[128]{0:T(128)}, u32[]{:S(2)}) copy-start(f32[128]{0:T(128)} %copy-done.35) | copy-start | bytes 1540
  77.8 13.3 %copy-start.38 = (f32[128]{0:T(128)S(1)}, f32[128]{0:T(128)}, u32[]{:S(2)}) copy-start(f32[128]{0:T(128)} %copy-done.37) | copy-start | bytes 1540
  77.8 13.3 %copy-start.40 = (f32[128]{0:T(128)S(1)}, f32[128]{0:T(128)}, u32[]{:S(2)}) copy-start(f32[128]{0:T(128)} %copy-done.39) | copy-start | bytes 1540
  77.8 13.3 %copy-start.42 = (f32[128]{0:T(128)S(1)}, f32[128]{0:T(128)}, u32[]{:S(2)}) copy-start(f32[128]{0:T(128)} %copy-done.41) | copy-start | bytes 1540
  77.8 13.3 %copy-start.44 = (f32[128]{0:T(128)S(1)}, f32[128]{0:T(128)}, u32[]{:S(2)}) copy-start(f32[128]{0:T(128)} %copy-done.43) | copy-start | bytes 1540
  77.8 13.3 %copy-start.46 = (f32[128]{0:T(128)S(1)}, f32[128]{0:T(128)}, u32[]{:S(2)}) copy-start(f32[128]{0:T(128)} %copy-done.45) | copy-start | bytes 1540
  77.8 13.3 %copy-start.48 = (f32[128]{0:T(128)S(1)}, f32[128]{0:T(128)}, u32[]{:S(2)}) copy-start(f32[128]{0:T(128)} %copy-done.47) | copy-start | bytes 1540
  77.8 13.3 %copy-start.50 = (f32[128]{0:T(128)S(1)}, f32[128]{0:T(128)}, u32[]{:S(2)}) copy-start(f32[128]{0:T(128)} %copy-done.49) | copy-start | bytes 1540
  81.8 9.4 %copy-start.1 = (f32[3,13,35,128]{3,2,1,0:T(8,128)S(1)}, f32[3,13,35,128]{3,2,1,0:T(8,128)}, u32[]{:S(2)}) copy-start(f32[3,13,35,128]{3,2,1,0:T(8,128)} %convolution_bitcast_fusion.2) | copy-start | bytes 2096644
  81.8 9.5 %copy-start.18 = (f32[3,13,35,128,1]{3,2,1,0,4:T(8,128)S(1)}, f32[3,13,35,128,1]{3,2,1,0,4:T(8,128)}, u32[]{:S(2)}) copy-start(f32[3,13,35,128,1]{3,2,1,0,4:T(8,128)} %maximum_bitcast_fusion.2) | copy-start | bytes 2096644
  81.8 9.5 %copy-start.21 = (f32[3,6,13,13]{3,2,1,0:T(8,128)S(1)}, f32[3,6,13,13]{3,2,1,0:T(8,128)}, u32[]{:S(2)}) copy-start(f32[3,6,13,13]{3,2,1,0:T(8,128)} %param.29) | copy-start | bytes 36508
  84.0 16.6 %collective-permute-start.3 = (f32[13,15,64]{1,0,2:T(8,128)S(1)}, f32[13,15,64]{1,0,2:T(8,128)}, u32[]{:S(2)}, u32[]{:S(2)}) collective-permute-start(f32[13,15,64]{1,0,2:T(8,128)S(1)} %get-tuple-element.19), channel_id=1, source_target_pairs={{1,0},{2,1},{3,2},{4,3},{5,4},{6,5},{7,6},{9,8},{10,9},{11,10},{12... | collective-permute-start | bytes 149768 | tf_op jit(solution)/shard_map/ppermute | solution.py:21
  85.2 26.7 %collective-permute-start.2 = (f32[13,15,64]{1,0,2:T(8,128)}, f32[13,15,64]{1,0,2:T(8,128)}, u32[]{:S(2)}, u32[]{:S(2)}) collective-permute-start(f32[13,15,64]{1,0,2:T(8,128)} %get-tuple-element.18), channel_id=1, source_target_pairs={{0,1},{1,2},{2,3},{3,4},{4,5},{5,6},{6,7},{8,9},{9,10},{10,11},{11... | collective-permute-start | bytes 149768 | tf_op jit(solution)/shard_map/ppermute | solution.py:20
  114.8 3.3 %copy-start.25 = (s32[8192]{0:T(1024)S(1)}, s32[8192]{0:T(1024)}, u32[]{:S(2)}) copy-start(s32[8192]{0:T(1024)} %pad_clamp_fusion) | copy-start | bytes 98308
  135.4 2.9 %copy-start.22 = (f32[3,6,13,13]{3,2,1,0:T(8,128)S(1)}, f32[3,6,13,13]{3,2,1,0:T(8,128)}, u32[]{:S(2)}) copy-start(f32[3,6,13,13]{3,2,1,0:T(8,128)} %param.29) | copy-start | bytes 36508
  135.4 2.9 %copy-start.27 = (f32[60,6,128]{2,1,0:T(8,128)S(1)}, f32[60,6,128]{2,1,0:T(8,128)}, u32[]{:S(2)}) copy-start(f32[60,6,128]{2,1,0:T(8,128)} %copy.373) | copy-start | bytes 552964
  135.4 2.9 %copy-start.52 = (f32[3,4,128]{2,0,1:T(4,128)S(1)}, f32[3,4,128]{2,0,1:T(4,128)}, u32[]{:S(2)}) copy-start(f32[3,4,128]{2,0,1:T(4,128)} %copy-done.51) | copy-start | bytes 18436
  138.3 2.8 %copy-start.9 = (f32[13,35,128]{2,0,1:T(8,128)S(1)}, f32[13,35,128]{2,0,1:T(8,128)}, u32[]{:S(2)}) copy-start(f32[13,35,128]{2,0,1:T(8,128)} %fusion.6) | copy-start | bytes 698884
  138.3 2.8 %copy-start.30 = (f32[4,35,15,1]{1,2,0,3:T(8,128)S(1)}, f32[4,35,15,1]{1,2,0,3:T(8,128)}, u32[]{:S(2)}) copy-start(f32[4,35,15,1]{1,2,0,3:T(8,128)} %constant.75) | copy-start | bytes 25204
  147.1 12.9 %all-to-all-start = ((f32[32,1,60]{2,1,0:T(1,128)}), f32[32,1,60]{2,1,0:T(1,128)S(1)}, u32[]{:S(2)}, u32[]{:S(2)}) async-start(f32[32,1,60]{2,1,0:T(1,128)} %broadcast_in_dim.17), calls=%async_computation | async-start | bytes 32768 | tf_op jit(solution)/shard_map/all_to_all | solution.py:255
  154.1 56.4 %copy-start.3 = (f32[5,6,35,128]{3,2,1,0:T(8,128)S(1)}, f32[5,6,35,128]{3,2,1,0:T(8,128)}, u32[]{:S(2)}) copy-start(f32[5,6,35,128]{3,2,1,0:T(8,128)} %param.36) | copy-start | bytes 1612804
  154.1 56.4 %copy-start.5 = (f32[5,6,35,128]{3,2,1,0:T(8,128)S(1)}, f32[5,6,35,128]{3,2,1,0:T(8,128)}, u32[]{:S(2)}) copy-start(f32[5,6,35,128]{3,2,1,0:T(8,128)} %param.37) | copy-start | bytes 1612804
  160.0 48.5 %all-to-all-start.1 = ((f32[4,1,6720]{2,1,0:T(1,128)}), f32[4,1,6720]{2,1,0:T(1,128)S(1)}, u32[]{:S(2)}, u32[]{:S(2)}) async-start(f32[4,1,6720]{2,1,0:T(1,128)} %reshape.454), calls=%async_computation.1 | async-start | bytes 217088 | tf_op jit(solution)/shard_map/all_to_all | solution.py:258
  (7 other events, 14.6 us)

commit v3 on v2

--- a/solution.py
+++ b/solution.py
@@ -146,6 +146,23 @@
     return jnp.einsum(
         "xan,fnxe->fae", lift_tables, face_flux * face_scale[None, None], precision=HIGH
     )
+
+
+def halving_sum(values, axis, count):
+    position = lax.axis_index(axis)
+    work = values
+    bit = count // 2
+    while bit >= 1:
+        width = work.shape[-1] // 2
+        upper = (position & bit) != 0
+        low = work[..., :width]
+        high = work[..., width:]
+        sent = lax.ppermute(
+            jnp.where(upper, low, high), axis, [(i, i ^ bit) for i in range(count)]
+        )
+        work = jnp.where(upper, high, low) + sent
+        bit //= 2
+    return work
 
 
 def search_direction(grad_share, local_grad, step_rows, change_rows, own_share, keep_gram, combine_sums):
@@ -254,8 +271,7 @@
         spread = jnp.broadcast_to(values[None], (device_count,) + values.shape)
         return jnp.sum(lax.all_to_all(spread, ("shot", "mesh"), 0, 0, tiled=False), axis=0)
 
-    pieces = gradient.reshape(params, node_count, shot_count, share_width)
-    grad_share = jnp.sum(lax.all_to_all(pieces, "shot", 2, 2, tiled=False), axis=2)
+    grad_share = halving_sum(gradient, "shot", shot_count)
     keep_gram = (lax.axis_index("shot") == 0).astype(jnp.float32)
     result = search_direction(
         grad_share, gradient, history_steps, history_changes, own_share, keep_gram, combine_sums

time: 213 us -> 209 us (0.981)
    all_to_all x1 -> x0, starting transfers between devices: 3.31 us -> none  [shards(): lax.all_to_all(pieces, 'shot', 2, 2, tiled=False)]
    unnamed x139 -> x156, local copies, waits for them, and re-layouts: 4.71 us -> 3.26 us
  transfers between devices with their start and end apart: 6 -> 7, of which waited for: 4 -> 3; matrix products, arithmetic and copies ran while one was open for 15% -> 15% of each run, Pallas kernels for 0% -> 0%
where the time goes in v3:
time: 209 us; the launch traced here: 208 us
  local copies, waits for them, and re-layouts  86.6 us (41%)
  between operations  44.3 us (21%)
  matrix products  24.4 us (12%)
  starting transfers between devices  22.4 us (11%)
  waiting for transfers between devices  18 us (9%)
  other arithmetic  12 us (6%)
    gather x2, local copies, waits for them, and re-layouts, shards(): turned = ghosts.reshape(fields, face_width * slot_count)[:, flat_index]  34.8 us
    ppermute x2, starting transfers between devices, padded(): before = lax.ppermute(last, axis, up)  11.8 us
    ppermute x2, waiting for transfers between devices, padded(): before = lax.ppermute(last, axis, up)  10.1 us
    reshape x4, local copies, waits for them, and re-layouts, shards(): flat_trace = inner_trace.reshape(fields, face_width, 4 * elements)  8.65 us
    gather x2, local copies, waits for them, and re-layouts, shards(): sent_traces = flat_trace[:, :, send_faces]  6.92 us
    concatenate x2, local copies, waits for them, and re-layouts, shards(): jnp.concatenate([flat_trace, extended[:, :, :border], extended[:, :, 3 *...  6.54 us
    all_to_all x1, starting transfers between devices, combine_sums(): lax.all_to_all(spread, ('shot', 'mesh'), 0, 0, tiled=False)  6.16 us
    reshape x2, local copies, waits for them, and re-layouts, shards(): jump_trace = turned.reshape(fields, face_width, 4, elements) - inner_trace  5.56 us
  transfers between devices with their start and end apart: 7, of which 3 were waited for; matrix products, arithmetic and copies ran while one was open for 15% of the time, Pallas kernels for 0%

profile of v3, /device:TPU:0, one launch (start us, length us, event | category | flops | bytes accessed | tf_op | source)
XLA Modules:
  0.0 207.7 jit_solution(11403323831153791259)
XLA Ops:
  0.6 0.7 pad_clamp_fusion.2
  1.3 1.0 copy.419
  2.3 0.6 gather_fusion.1
  3.2 3.7 %copy.222 = f32[13,15,512]{1,0,2:T(8,128)} copy(f32[13,15,512]{2,1,0:T(8,128)S(1)} %reshape.334) | data formatting | bytes 798720 | tf_op jit(solution)/shard_map/reshape | solution.py:246
  7.0 3.0 %gather_fusion.2 = f32[128,13,15]{2,1,0:T(8,128)S(1)} fusion(f32[13,15,512]{1,0,2:T(8,128)} %copy.222, s32[1024]{0:T(1024)S(1)} %pad_clamp_fusion.1), kind=kCustom, calls=%fused_computation.2 | custom fusion | bytes 200192 | tf_op jit(solution)/shard_map/gather | solution.py:247
  10.1 1.1 fusion.67
  11.2 1.3 collective-permute-start.1
  12.4 6.3 %collective-permute-start = (f32[13,15,64]{1,0,2:T(8,128)}, f32[13,15,64]{1,0,2:T(8,128)}, u32[]{:S(2)}, u32[]{:S(2)}) collective-permute-start(f32[13,15,64]{1,0,2:T(8,128)} %get-tuple-element.16), channel_id=1, source_target_pairs={{0,1},{1,2},{2,3},{3,4},{4,5},{5,6},{6,7},{8,9},{9,10},{10,11},{11... | collective-permute-start | bytes 149768 | tf_op jit(solution)/shard_map/ppermute | solution.py:20
  19.0 0.7 fusion.63
  20.3 0.8 convolution_bitcast_fusion.3
  21.6 0.8 convolution_bitcast_fusion.1
  22.5 1.0 multiply_add_fusion.11
  23.4 0.9 multiply_add_fusion.5
  24.4 0.8 convolution_bitcast_fusion
  25.3 1.0 multiply_add_fusion.2
  26.4 1.3 reshape.340
  27.7 1.2 maximum_bitcast_fusion
  29.0 2.3 %fusion.7 = f32[13,35,128]{2,0,1:T(8,128)} fusion(f32[3,13,35,128,1]{3,2,1,0,4:T(8,128)S(1)} %maximum_bitcast_fusion, f32[6,35,128]{2,0,1:T(8,128)S(1)} %copy.215, f32[3,6,13,13]{3,2,1,0:T(8,128)S(1)} %copy-done.19), kind=kOutput, calls=%fused_computation.21 | convolution fusion | flops 164178560 | bytes 1051528 | tf_op jit(solution)/shard_map/dpfg,dfae->pgae/dot_general | solution.py:132
  31.3 1.0 maximum_bitcast_fusion.2
  32.3 1.0 maximum_bitcast_fusion.3
  33.3 2.2 %fusion.18 = f32[10,5]{0,1:T(8,128)S(1)} fusion(f32[5,26880]{1,0:T(8,128)S(1)} %reshape.341, f32[5,26880]{1,0:T(8,128)S(1)} %reshape.340, f32[]{:T(128)S(6)} %convert_element_type.75), kind=kOutput, calls=%fused_computation.38 | convolution fusion | flops 16396850 | bytes 1075404 | tf_op jit(solution)/shard_map/dot_general | solution.py:174
  35.6 1.5 constant_dynamic-slice_fusion.2
  37.7 0.8 gather_fusion
  38.6 0.8 copy.282
  39.5 1.3 copy.224
  40.8 1.9 copy.223
  42.7 1.0 pad_maximum_fusion.7
  43.7 3.2 %copy.225 = f32[13,15,640]{0,2,1:T(8,128)} copy(f32[13,15,640]{2,1,0:T(8,128)S(1)} %pad_maximum_fusion.7) | data formatting | bytes 998400 | tf_op jit(solution)/shard_map/concatenate | solution.py:249
  47.0 17.4 %gather_fusion.3 = f32[7680,13]{1,0:T(8,128)} fusion(f32[13,9600]{0,1:T(8,128)} %bitcast.323, s32[8192]{0:T(1024)S(1)} %copy-done.34), kind=kCustom, calls=%fused_computation.3 | custom fusion | bytes 829440 | tf_op jit(solution)/shard_map/gather | solution.py:252
  64.4 2.8 %copy.226 = f32[13,15,4,128]{3,0,2,1:T(8,128)S(1)} copy(f32[13,15,4,128]{0,3,2,1:T(8,128)} %bitcast.325) | data formatting | bytes 798720 | tf_op jit(solution)/shard_map/reshape | solution.py:253
  67.3 2.7 %fusion.1 = f32[13,15,4,128]{3,0,2,1:T(8,128)S(1)} fusion(f32[6,15,4,128]{3,0,2,1:T(8,128)S(1)} %bitcast.334, f32[13,15,4,128]{3,0,2,1:T(8,128)S(1)} %sub.149, f32[3,4,128]{2,0,1:T(4,128)S(1)} %copy.219, f32[3,6,13,13]{3,2,1,0:T(8,128)S(1)} %copy-done.20), kind=kOutput, calls=%fused_computation.10 | convolution fusion | flops 281748480 | bytes 1001352 | tf_op jit(solution)/shard_map/dpfg,dfnxe->pgnxe/dot_general | solution.py:144
  70.1 0.7 fusion.14
  71.0 1.7 convolution_bitcast_fusion.2
  73.3 0.9 copy.234
  74.2 1.2 reshape.337
  75.4 3.7 %copy.235 = f32[13,15,512]{1,0,2:T(8,128)} copy(f32[13,15,512]{2,1,0:T(8,128)S(1)} %reshape.337) | data formatting | bytes 798720 | tf_op jit(solution)/shard_map/reshape | solution.py:246
  79.1 4.0 %gather_fusion.5 = f32[128,13,15]{2,1,0:T(8,128)} fusion(f32[13,15,512]{1,0,2:T(8,128)} %copy.235, s32[1024]{0:T(1024)} %copy-done.63), kind=kCustom, calls=%fused_computation.5 | custom fusion | bytes 200192 | tf_op jit(solution)/shard_map/gather | solution.py:247
  83.1 2.2 %fusion.66 = (f32[13,15,64]{1,0,2:T(8,128)}, f32[13,15,64]{1,0,2:T(8,128)S(1)}) fusion(f32[13,15,128]{1,0,2:T(8,128)} %bitcast.332), kind=kLoop, calls=%fused_computation.159 | loop fusion | bytes 199680 | tf_op jit(solution)/shard_map/slice | solution.py:18
  85.3 1.3 collective-permute-start.3
  86.5 5.5 %collective-permute-start.2 = (f32[13,15,64]{1,0,2:T(8,128)}, f32[13,15,64]{1,0,2:T(8,128)}, u32[]{:S(2)}, u32[]{:S(2)}) collective-permute-start(f32[13,15,64]{1,0,2:T(8,128)} %get-tuple-element.14), channel_id=1, source_target_pairs={{0,1},{1,2},{2,3},{3,4},{4,5},{5,6},{6,7},{8,9},{9,10},{10,11},{11... | collective-permute-start | bytes 149768 | tf_op jit(solution)/shard_map/ppermute | solution.py:20
  92.3 2.4 %fusion.5 = f32[6,35,128]{2,0,1:T(8,128)} fusion(f32[3,13,35,128,1]{3,2,1,0,4:T(8,128)S(1)} %copy-done.18, f32[13,35,128]{2,0,1:T(8,128)S(1)} %copy.233, f32[3,6,13,13]{3,2,1,0:T(8,128)S(1)} %copy-done.21), kind=kOutput, calls=%fused_computation.17 | convolution fusion | flops 164209920 | bytes 1051528 | tf_op jit(solution)/shard_map/dpfg,dgae->pfae/dot_general | solution.py:138
  94.8 2.3 %fusion.6 = f32[13,35,128]{2,0,1:T(8,128)} fusion(f32[3,13,35,128,1]{3,2,1,0,4:T(8,128)S(1)} %maximum_bitcast_fusion.1, f32[6,35,128]{2,0,1:T(8,128)S(1)} %copy-done.7, f32[3,6,13,13]{3,2,1,0:T(8,128)S(1)} %copy-done.21), kind=kOutput, calls=%fused_computation.19 | convolution fusion | flops 164178560 | bytes 1051528 | tf_op jit(solution)/shard_map/dpfg,dfae->pgae/dot_general | solution.py:132
  97.1 3.6 %collective-permute-done.3 = f32[13,15,64]{1,0,2:T(8,128)} collective-permute-done((f32[13,15,64]{1,0,2:T(8,128)S(1)}, f32[13,15,64]{1,0,2:T(8,128)}, u32[]{:S(2)}, u32[]{:S(2)}) %collective-permute-start.3) | collective-permute-done | bytes 49952 | tf_op jit(solution)/shard_map/ppermute | solution.py:21
  100.8 1.3 copy.237
  102.0 10.1 %collective-permute-done.2 = f32[13,15,64]{1,0,2:T(8,128)} collective-permute-done((f32[13,15,64]{1,0,2:T(8,128)}, f32[13,15,64]{1,0,2:T(8,128)}, u32[]{:S(2)}, u32[]{:S(2)}) %collective-permute-start.2) | collective-permute-done | bytes 49952 | tf_op jit(solution)/shard_map/ppermute | solution.py:20
  112.2 1.9 copy.236
  114.1 1.0 pad_maximum_fusion.8
  115.1 3.3 %copy.238 = f32[13,15,640]{0,2,1:T(8,128)} copy(f32[13,15,640]{2,1,0:T(8,128)S(1)} %pad_maximum_fusion.8) | data formatting | bytes 998400 | tf_op jit(solution)/shard_map/concatenate | solution.py:249
  118.4 17.4 %gather_fusion.6 = f32[7680,13]{1,0:T(8,128)} fusion(f32[13,9600]{0,1:T(8,128)} %bitcast.322, s32[8192]{0:T(1024)S(1)} %copy-done.35), kind=kCustom, calls=%fused_computation.6 | custom fusion | bytes 829440 | tf_op jit(solution)/shard_map/gather | solution.py:252
  135.7 2.8 %copy.239 = f32[13,15,4,128]{3,0,2,1:T(8,128)S(1)} copy(f32[13,15,4,128]{0,3,2,1:T(8,128)} %bitcast.324) | data formatting | bytes 798720 | tf_op jit(solution)/shard_map/reshape | solution.py:253
  138.7 2.7 %fusion = f32[13,15,4,128]{3,0,2,1:T(8,128)S(1)} fusion(f32[6,15,4,128]{3,0,2,1:T(8,128)S(1)} %bitcast.335, f32[13,15,4,128]{3,0,2,1:T(8,128)S(1)} %sub.150, f32[3,4,128]{2,0,1:T(4,128)S(1)} %copy-done.62, f32[3,6,13,13]{3,2,1,0:T(8,128)S(1)} %copy-done.22), kind=kOutput, calls=%fused_computation.8 | convolution fusion | flops 281748480 | bytes 1001352 | tf_op jit(solution)/shard_map/dpfg,dfnxe->pgnxe/dot_general | solution.py:144
  141.5 0.7 fusion.17
  142.5 1.8 fusion.4
  144.6 2.3 %fusion.19 = f32[10]{0:T(128)S(1)} fusion(f32[26880,1]{0,1:T(1,128)S(1)} %reshape.441, f32[5,26880]{1,0:T(8,128)S(1)} %reshape.341, f32[5,26880]{1,0:T(8,128)S(1)} %reshape.340), kind=kOutput, calls=%fused_computation.39 | convolution fusion | flops 3494400 | bytes 1182760 | tf_op jit(solution)/shard_map/dot_general | solution.py:173
  146.9 0.6 broadcast_in_dim.17
  147.5 6.2 %all-to-all-start = ((f32[32,1,60]{2,1,0:T(1,128)}), f32[32,1,60]{2,1,0:T(1,128)S(1)}, u32[]{:S(2)}, u32[]{:S(2)}) async-start(f32[32,1,60]{2,1,0:T(1,128)} %broadcast_in_dim.17), calls=%async_computation | async-start | bytes 32768 | tf_op jit(solution)/shard_map/all_to_all | solution.py:272
  153.8 0.9 copy.256
  154.7 1.8 collective-permute-start.4
  156.5 4.3 %all-to-all-done = f32[32,1,60]{2,1,0:T(1,128)S(1)} async-done(((f32[32,1,60]{2,1,0:T(1,128)}), f32[32,1,60]{2,1,0:T(1,128)S(1)}, u32[]{:S(2)}, u32[]{:S(2)}) %all-to-all-start) | async-done | bytes 7712 | tf_op jit(solution)/shard_map/all_to_all | solution.py:272
  161.0 0.7 fusion.71
  161.8 0.7 fusion.69
  162.5 0.7 fusion.72
  163.5 0.7 fusion.70
  206.9 0.8 copy.257
  (192 shorter events, 5.4 us)
Async XLA Ops:
  3.2 3.7 %copy-start.74 = (s32[128]{0:T(128)S(1)}, s32[128]{0:T(128)}, u32[]{:S(2)}) copy-start(s32[128]{0:T(128)} %param.35) | copy-start | bytes 1540
  6.9 11.8 %copy-start.66 = (s32[4,128]{1,0:T(4,128)S(1)}, s32[4,128]{1,0:T(4,128)}, u32[]{:S(2)}) copy-start(s32[4,128]{1,0:T(4,128)} %param.34) | copy-start | bytes 6148
  6.9 11.9 %copy-start.67 = (s32[4,128]{1,0:T(4,128)S(1)}, s32[4,128]{1,0:T(4,128)}, u32[]{:S(2)}) copy-start(s32[4,128]{1,0:T(4,128)} %param.33) | copy-start | bytes 6148
  6.9 11.9 %copy-start.69 = (s32[15]{0:T(128)S(1)}, s32[15]{0:T(128)}, u32[]{:S(2)}) copy-start(s32[15]{0:T(128)} %constant.69.clone) | copy-start | bytes 184
  6.9 11.9 %copy-start.70 = (s32[15]{0:T(128)S(1)}, s32[15]{0:T(128)}, u32[]{:S(2)}) copy-start(s32[15]{0:T(128)} %constant.68.clone) | copy-start | bytes 184
  6.9 11.9 %copy-start.71 = (s32[15]{0:T(128)S(1)}, s32[15]{0:T(128)}, u32[]{:S(2)}) copy-start(s32[15]{0:T(128)} %constant.67.clone) | copy-start | bytes 184
  6.9 11.9 %copy-start.72 = (s32[15]{0:T(128)S(1)}, s32[15]{0:T(128)}, u32[]{:S(2)}) copy-start(s32[15]{0:T(128)} %constant.66.clone) | copy-start | bytes 184
  7.0 11.9 %copy-start.73 = (s32[15]{0:T(128)S(1)}, s32[15]{0:T(128)}, u32[]{:S(2)}) copy-start(s32[15]{0:T(128)} %constant.24.clone) | copy-start | bytes 184
  7.0 12.7 %copy-start.68 = (f32[4,128]{1,0:T(4,128)S(1)}, f32[4,128]{1,0:T(4,128)}, u32[]{:S(2)}) copy-start(f32[4,128]{1,0:T(4,128)} %param.32) | copy-start | bytes 6148
  7.0 13.3 %copy-start.2 = (f32[1,13,35,128]{3,0,2,1:T(1,128)S(1)}, f32[1,13,35,128]{3,0,2,1:T(1,128)}, u32[]{:S(2)}) copy-start(f32[1,13,35,128]{3,0,2,1:T(1,128)} %param.26) | copy-start | bytes 698884
  7.0 13.3 %copy-start.15 = (f32[3,35,35,1]{2,1,3,0:T(8,128)S(1)}, f32[3,35,35,1]{2,1,3,0:T(8,128)}, u32[]{:S(2)}) copy-start(f32[3,35,35,1]{2,1,3,0:T(8,128)} %constant.76) | copy-start | bytes 44104
  7.0 11.7 %copy-start.63 = (s32[1024]{0:T(1024)}, s32[1024]{0:T(1024)S(1)}, u32[]{:S(2)}) copy-start(s32[1024]{0:T(1024)S(1)} %pad_clamp_fusion.1) | copy-start | bytes 12292
  10.0 11.1 %copy-start.65 = (f32[3,3,128]{2,1,0:T(4,128)S(1)}, f32[3,3,128]{2,1,0:T(4,128)}, u32[]{:S(2)}) copy-start(f32[3,3,128]{2,1,0:T(4,128)} %param.30) | copy-start | bytes 13828
  10.0 11.1 %copy-start = (f32[6,35,128]{2,1,0:T(8,128)S(1)}, f32[6,35,128]{2,1,0:T(8,128)}, u32[]{:S(2)}) copy-start(f32[6,35,128]{2,1,0:T(8,128)} %param.28) | copy-start | bytes 322564
  10.0 11.2 %copy-start.33 = (f32[1,2,13,35,128]{4,1,3,2,0:T(2,128)S(1)}, f32[1,2,13,35,128]{4,1,3,2,0:T(2,128)}, u32[]{:S(2)}) copy-start(f32[1,2,13,35,128]{4,1,3,2,0:T(2,128)} %param.27) | copy-start | bytes 1397764
  11.2 28.4 %collective-permute-start.1 = (f32[13,15,64]{1,0,2:T(8,128)}, f32[13,15,64]{1,0,2:T(8,128)}, u32[]{:S(2)}, u32[]{:S(2)}) collective-permute-start(f32[13,15,64]{1,0,2:T(8,128)} %get-tuple-element.17), channel_id=1, source_target_pairs={{1,0},{2,1},{3,2},{4,3},{5,4},{6,5},{7,6},{9,8},{10,9},{11,10},{12... | collective-permute-start | bytes 149768 | tf_op jit(solution)/shard_map/ppermute | solution.py:21
  12.4 28.4 %collective-permute-start = (f32[13,15,64]{1,0,2:T(8,128)}, f32[13,15,64]{1,0,2:T(8,128)}, u32[]{:S(2)}, u32[]{:S(2)}) collective-permute-start(f32[13,15,64]{1,0,2:T(8,128)} %get-tuple-element.16), channel_id=1, source_target_pairs={{0,1},{1,2},{2,3},{3,4},{4,5},{5,6},{6,7},{8,9},{9,10},{10,11},{11... | collective-permute-start | bytes 149768 | tf_op jit(solution)/shard_map/ppermute | solution.py:20
  21.1 4.1 %copy-start.43 = (f32[128]{0:T(128)}, f32[128]{0:T(128)S(1)}, u32[]{:S(2)}) copy-start(f32[128]{0:T(128)S(1)} %get-tuple-element.42) | copy-start | bytes 1540
  21.1 4.1 %copy-start.45 = (f32[128]{0:T(128)}, f32[128]{0:T(128)S(1)}, u32[]{:S(2)}) copy-start(f32[128]{0:T(128)S(1)} %get-tuple-element.43) | copy-start | bytes 1540
  21.1 4.1 %copy-start.47 = (f32[128]{0:T(128)}, f32[128]{0:T(128)S(1)}, u32[]{:S(2)}) copy-start(f32[128]{0:T(128)S(1)} %get-tuple-element.44) | copy-start | bytes 1540
  21.1 4.1 %copy-start.49 = (f32[128]{0:T(128)}, f32[128]{0:T(128)S(1)}, u32[]{:S(2)}) copy-start(f32[128]{0:T(128)S(1)} %get-tuple-element.45) | copy-start | bytes 1540
  21.1 4.1 %copy-start.51 = (f32[128]{0:T(128)}, f32[128]{0:T(128)S(1)}, u32[]{:S(2)}) copy-start(f32[128]{0:T(128)S(1)} %get-tuple-element.46) | copy-start | bytes 1540
  21.2 4.1 %copy-start.53 = (f32[128]{0:T(128)}, f32[128]{0:T(128)S(1)}, u32[]{:S(2)}) copy-start(f32[128]{0:T(128)S(1)} %get-tuple-element.47) | copy-start | bytes 1540
  21.2 4.1 %copy-start.55 = (f32[128]{0:T(128)}, f32[128]{0:T(128)S(1)}, u32[]{:S(2)}) copy-start(f32[128]{0:T(128)S(1)} %get-tuple-element.48) | copy-start | bytes 1540
  21.2 4.1 %copy-start.57 = (f32[128]{0:T(128)}, f32[128]{0:T(128)S(1)}, u32[]{:S(2)}) copy-start(f32[128]{0:T(128)S(1)} %get-tuple-element.49) | copy-start | bytes 1540
  21.2 4.1 %copy-start.59 = (f32[128]{0:T(128)}, f32[128]{0:T(128)S(1)}, u32[]{:S(2)}) copy-start(f32[128]{0:T(128)S(1)} %get-tuple-element.50) | copy-start | bytes 1540
  21.2 7.7 %copy-start.6 = (f32[6,35,128]{2,0,1:T(8,128)}, f32[6,35,128]{2,0,1:T(8,128)S(1)}, u32[]{:S(2)}) copy-start(f32[6,35,128]{2,0,1:T(8,128)S(1)} %copy.215) | copy-start | bytes 322564
  27.7 3.6 %copy-start.10 = (f32[1,13,35,128]{3,2,1,0:T(8,128)S(1)}, f32[1,13,35,128]{3,2,1,0:T(8,128)}, u32[]{:S(2)}) copy-start(f32[1,13,35,128]{3,2,1,0:T(8,128)} %get-tuple-element.22) | copy-start | bytes 698884
  27.7 3.6 %copy-start.11 = (f32[1,13,35,128]{3,2,1,0:T(8,128)S(1)}, f32[1,13,35,128]{3,2,1,0:T(8,128)}, u32[]{:S(2)}) copy-start(f32[1,13,35,128]{3,2,1,0:T(8,128)} %get-tuple-element.23) | copy-start | bytes 698884
  28.9 3.4 %copy-start.12 = (f32[1,13,35,128]{3,2,1,0:T(8,128)S(1)}, f32[1,13,35,128]{3,2,1,0:T(8,128)}, u32[]{:S(2)}) copy-start(f32[1,13,35,128]{3,2,1,0:T(8,128)} %get-tuple-element.18) | copy-start | bytes 698884
  29.0 3.3 %copy-start.13 = (f32[1,13,35,128]{3,2,1,0:T(8,128)S(1)}, f32[1,13,35,128]{3,2,1,0:T(8,128)}, u32[]{:S(2)}) copy-start(f32[1,13,35,128]{3,2,1,0:T(8,128)} %get-tuple-element.19) | copy-start | bytes 698884
  29.0 3.3 %copy-start.14 = (f32[1,13,35,128]{3,2,1,0:T(8,128)S(1)}, f32[1,13,35,128]{3,2,1,0:T(8,128)}, u32[]{:S(2)}) copy-start(f32[1,13,35,128]{3,2,1,0:T(8,128)} %get-tuple-element.20) | copy-start | bytes 698884
  33.3 3.8 %copy-start.41 = (s32[7680]{0:T(1024)S(1)}, s32[7680]{0:T(1024)}, u32[]{:S(2)}) copy-start(s32[7680]{0:T(1024)} %fusion.63) | copy-start | bytes 92164
  35.6 3.8 %copy-start.64 = (f32[3,4,128]{2,1,0:T(4,128)S(1)}, f32[3,4,128]{2,1,0:T(4,128)}, u32[]{:S(2)}) copy-start(f32[3,4,128]{2,1,0:T(4,128)} %param.31) | copy-start | bytes 18436
  39.4 27.9 %copy-start.61 = (f32[3,4,128]{2,0,1:T(4,128)}, f32[3,4,128]{2,0,1:T(4,128)S(1)}, u32[]{:S(2)}) copy-start(f32[3,4,128]{2,0,1:T(4,128)S(1)} %copy.219) | copy-start | bytes 18436
  43.7 3.3 %copy-start.34 = (s32[8192]{0:T(1024)S(1)}, s32[8192]{0:T(1024)}, u32[]{:S(2)}) copy-start(s32[8192]{0:T(1024)} %pad_clamp_fusion) | copy-start | bytes 98308
  79.1 13.0 %copy-start.44 = (f32[128]{0:T(128)S(1)}, f32[128]{0:T(128)}, u32[]{:S(2)}) copy-start(f32[128]{0:T(128)} %copy-done.43) | copy-start | bytes 1540
  79.1 13.0 %copy-start.46 = (f32[128]{0:T(128)S(1)}, f32[128]{0:T(128)}, u32[]{:S(2)}) copy-start(f32[128]{0:T(128)} %copy-done.45) | copy-start | bytes 1540
  79.1 13.0 %copy-start.48 = (f32[128]{0:T(128)S(1)}, f32[128]{0:T(128)}, u32[]{:S(2)}) copy-start(f32[128]{0:T(128)} %copy-done.47) | copy-start | bytes 1540
  79.1 13.0 %copy-start.50 = (f32[128]{0:T(128)S(1)}, f32[128]{0:T(128)}, u32[]{:S(2)}) copy-start(f32[128]{0:T(128)} %copy-done.49) | copy-start | bytes 1540
  79.1 13.0 %copy-start.52 = (f32[128]{0:T(128)S(1)}, f32[128]{0:T(128)}, u32[]{:S(2)}) copy-start(f32[128]{0:T(128)} %copy-done.51) | copy-start | bytes 1540
  79.1 13.0 %copy-start.54 = (f32[128]{0:T(128)S(1)}, f32[128]{0:T(128)}, u32[]{:S(2)}) copy-start(f32[128]{0:T(128)} %copy-done.53) | copy-start | bytes 1540
  79.1 13.0 %copy-start.56 = (f32[128]{0:T(128)S(1)}, f32[128]{0:T(128)}, u32[]{:S(2)}) copy-start(f32[128]{0:T(128)} %copy-done.55) | copy-start | bytes 1540
  79.1 13.0 %copy-start.58 = (f32[128]{0:T(128)S(1)}, f32[128]{0:T(128)}, u32[]{:S(2)}) copy-start(f32[128]{0:T(128)} %copy-done.57) | copy-start | bytes 1540
  79.1 13.0 %copy-start.60 = (f32[128]{0:T(128)S(1)}, f32[128]{0:T(128)}, u32[]{:S(2)}) copy-start(f32[128]{0:T(128)} %copy-done.59) | copy-start | bytes 1540
  83.1 9.0 %copy-start.1 = (f32[3,13,35,128]{3,2,1,0:T(8,128)S(1)}, f32[3,13,35,128]{3,2,1,0:T(8,128)}, u32[]{:S(2)}) copy-start(f32[3,13,35,128]{3,2,1,0:T(8,128)} %convolution_bitcast_fusion.2) | copy-start | bytes 2096644
  83.1 9.2 %copy-start.18 = (f32[3,13,35,128,1]{3,2,1,0,4:T(8,128)S(1)}, f32[3,13,35,128,1]{3,2,1,0,4:T(8,128)}, u32[]{:S(2)}) copy-start(f32[3,13,35,128,1]{3,2,1,0,4:T(8,128)} %maximum_bitcast_fusion.2) | copy-start | bytes 2096644
  83.1 9.2 %copy-start.21 = (f32[3,6,13,13]{3,2,1,0:T(8,128)S(1)}, f32[3,6,13,13]{3,2,1,0:T(8,128)}, u32[]{:S(2)}) copy-start(f32[3,6,13,13]{3,2,1,0:T(8,128)} %param.29) | copy-start | bytes 36508
  85.3 15.5 %collective-permute-start.3 = (f32[13,15,64]{1,0,2:T(8,128)S(1)}, f32[13,15,64]{1,0,2:T(8,128)}, u32[]{:S(2)}, u32[]{:S(2)}) collective-permute-start(f32[13,15,64]{1,0,2:T(8,128)S(1)} %get-tuple-element.15), channel_id=1, source_target_pairs={{1,0},{2,1},{3,2},{4,3},{5,4},{6,5},{7,6},{9,8},{10,9},{11,10},{12... | collective-permute-start | bytes 149768 | tf_op jit(solution)/shard_map/ppermute | solution.py:21
  86.5 25.6 %collective-permute-start.2 = (f32[13,15,64]{1,0,2:T(8,128)}, f32[13,15,64]{1,0,2:T(8,128)}, u32[]{:S(2)}, u32[]{:S(2)}) collective-permute-start(f32[13,15,64]{1,0,2:T(8,128)} %get-tuple-element.14), channel_id=1, source_target_pairs={{0,1},{1,2},{2,3},{3,4},{4,5},{5,6},{6,7},{8,9},{9,10},{10,11},{11... | collective-permute-start | bytes 149768 | tf_op jit(solution)/shard_map/ppermute | solution.py:20
  115.0 3.3 %copy-start.35 = (s32[8192]{0:T(1024)S(1)}, s32[8192]{0:T(1024)}, u32[]{:S(2)}) copy-start(s32[8192]{0:T(1024)} %pad_clamp_fusion) | copy-start | bytes 98308
  144.5 62.1 %copy-start.23 = (f32[1,6,35,32]{3,2,1,0:T(8,128)S(1)}, f32[1,6,35,32]{3,2,1,0:T(8,128)}, u32[]{:S(2)}) copy-start(f32[1,6,35,32]{3,2,1,0:T(8,128)} %get-tuple-element.35) | copy-start | bytes 80644
  144.5 62.1 %copy-start.24 = (f32[1,6,35,32]{3,2,1,0:T(8,128)S(1)}, f32[1,6,35,32]{3,2,1,0:T(8,128)}, u32[]{:S(2)}) copy-start(f32[1,6,35,32]{3,2,1,0:T(8,128)} %get-tuple-element.36) | copy-start | bytes 80644
  144.5 62.1 %copy-start.25 = (f32[1,6,35,32]{3,2,1,0:T(8,128)S(1)}, f32[1,6,35,32]{3,2,1,0:T(8,128)}, u32[]{:S(2)}) copy-start(f32[1,6,35,32]{3,2,1,0:T(8,128)} %get-tuple-element.37) | copy-start | bytes 80644
  144.5 62.1 %copy-start.26 = (f32[1,6,35,32]{3,2,1,0:T(8,128)S(1)}, f32[1,6,35,32]{3,2,1,0:T(8,128)}, u32[]{:S(2)}) copy-start(f32[1,6,35,32]{3,2,1,0:T(8,128)} %get-tuple-element.38) | copy-start | bytes 80644
  144.5 62.1 %copy-start.27 = (f32[1,6,35,32]{3,2,1,0:T(8,128)S(1)}, f32[1,6,35,32]{3,2,1,0:T(8,128)}, u32[]{:S(2)}) copy-start(f32[1,6,35,32]{3,2,1,0:T(8,128)} %get-tuple-element.39) | copy-start | bytes 80644
  144.5 62.1 %copy-start.28 = (f32[1,6,35,32]{3,2,1,0:T(8,128)S(1)}, f32[1,6,35,32]{3,2,1,0:T(8,128)}, u32[]{:S(2)}) copy-start(f32[1,6,35,32]{3,2,1,0:T(8,128)} %get-tuple-element.109) | copy-start | bytes 80644
  144.5 62.1 %copy-start.29 = (f32[1,6,35,32]{3,2,1,0:T(8,128)S(1)}, f32[1,6,35,32]{3,2,1,0:T(8,128)}, u32[]{:S(2)}) copy-start(f32[1,6,35,32]{3,2,1,0:T(8,128)} %get-tuple-element.110) | copy-start | bytes 80644
  144.5 62.1 %copy-start.30 = (f32[1,6,35,32]{3,2,1,0:T(8,128)S(1)}, f32[1,6,35,32]{3,2,1,0:T(8,128)}, u32[]{:S(2)}) copy-start(f32[1,6,35,32]{3,2,1,0:T(8,128)} %get-tuple-element.111) | copy-start | bytes 80644
  144.5 62.1 %copy-start.31 = (f32[1,6,35,32]{3,2,1,0:T(8,128)S(1)}, f32[1,6,35,32]{3,2,1,0:T(8,128)}, u32[]{:S(2)}) copy-start(f32[1,6,35,32]{3,2,1,0:T(8,128)} %get-tuple-element.112) | copy-start | bytes 80644
  144.5 62.1 %copy-start.32 = (f32[1,6,35,32]{3,2,1,0:T(8,128)S(1)}, f32[1,6,35,32]{3,2,1,0:T(8,128)}, u32[]{:S(2)}) copy-start(f32[1,6,35,32]{3,2,1,0:T(8,128)} %get-tuple-element.113) | copy-start | bytes 80644
  147.5 13.2 %all-to-all-start = ((f32[32,1,60]{2,1,0:T(1,128)}), f32[32,1,60]{2,1,0:T(1,128)S(1)}, u32[]{:S(2)}, u32[]{:S(2)}) async-start(f32[32,1,60]{2,1,0:T(1,128)} %broadcast_in_dim.17), calls=%async_computation | async-start | bytes 32768 | tf_op jit(solution)/shard_map/all_to_all | solution.py:272
  154.7 8.4 %collective-permute-start.4 = (f32[6,35,64]{2,0,1:T(8,128)S(1)}, f32[6,35,64]{2,0,1:T(8,128)S(1)}, u32[]{:S(2)}, u32[]{:S(2)}) collective-permute-start(f32[6,35,64]{2,0,1:T(8,128)S(1)} %slice_select_fusion.1), channel_id=1, source_target_pairs={{0,16},{8,24},{16,0},{24,8},{1,17},{9,25},{17,1},{25,9},{2,18},{10... | collective-permute-start | bytes 161288 | tf_op jit(solution)/shard_map/ppermute | solution.py:160
  163.4 43.2 %collective-permute-start.5 = (f32[6,35,32]{2,0,1:T(8,128)S(1)}, f32[6,35,32]{2,0,1:T(8,128)S(1)}, u32[]{:S(2)}, u32[]{:S(2)}) collective-permute-start(f32[6,35,32]{2,0,1:T(8,128)S(1)} %slice_select_fusion), channel_id=1, source_target_pairs={{0,8},{8,0},{16,24},{24,16},{1,9},{9,1},{17,25},{25,17},{2,10},{10... | collective-permute-start | bytes 80648 | tf_op jit(solution)/shard_map/ppermute | solution.py:160
  (18 other events, 46.9 us)

commit v4 on v3

--- a/solution.py
+++ b/solution.py
@@ -196,13 +196,12 @@
             along = along + weights[earlier] * step_change[earlier, slot]
         beta_now = along / curvature[slot]
         weights[slot] = alphas[slot] - beta_now
-    step_share = own_share(step_rows)
-    change_share = own_share(change_rows)
-    work = scaling * grad_share
+    combined = (-scaling * alphas[0]) * change_rows[0]
+    for slot in range(1, pairs):
+        combined = combined - (scaling * alphas[slot]) * change_rows[slot]
     for slot in range(pairs):
-        work = work - (scaling * alphas[slot]) * change_share[slot]
-    for slot in range(pairs):
-        work = work + weights[slot] * step_share[slot]
+        combined = combined + weights[slot] * step_rows[slot]
+    work = scaling * grad_share + own_share(combined)
     return -work
 
 

time: 209 us -> 213 us (1.019)
  other arithmetic: 12 us -> 7.32 us
  local copies, waits for them, and re-layouts: 86.6 us -> 90.7 us
  waiting for transfers between devices: 18 us -> 21.2 us
    add x4, other arithmetic: 3.02 us -> 0.56 us  [spatial_of(): total = total + metric[2, direction_axis] * reference_grads[2]]
    unnamed x156 -> x114, local copies, waits for them, and re-layouts: 3.26 us -> 4.45 us
  transfers between devices with their start and end apart: 7 -> 7, of which waited for: 3 -> 5; matrix products, arithmetic and copies ran while one was open for 15% -> 14% of each run, Pallas kernels for 0% -> 0%
where the time goes in v4:
time: 213 us; the launch traced here: 211 us
  local copies, waits for them, and re-layouts  90.7 us (43%)
  between operations  43.8 us (21%)
  matrix products  26 us (12%)
  starting transfers between devices  22.4 us (11%)
  waiting for transfers between devices  21.2 us (10%)
  other arithmetic  7.32 us (3%)
    gather x2, local copies, waits for them, and re-layouts, shards(): turned = ghosts.reshape(fields, face_width * slot_count)[:, flat_index]  34.6 us
    ppermute x2, starting transfers between devices, padded(): before = lax.ppermute(last, axis, up)  12.1 us
    ppermute x2, waiting for transfers between devices, padded(): before = lax.ppermute(last, axis, up)  11.5 us
    reshape x4, local copies, waits for them, and re-layouts, shards(): flat_trace = inner_trace.reshape(fields, face_width, 4 * elements)  8.68 us
    gather x2, local copies, waits for them, and re-layouts, shards(): sent_traces = flat_trace[:, :, send_faces]  7.91 us
    concatenate x2, local copies, waits for them, and re-layouts, shards(): jnp.concatenate([flat_trace, extended[:, :, :border], extended[:, :, 3 *...  7.2 us
    all_to_all x1, starting transfers between devices, combine_sums(): lax.all_to_all(spread, ('shot', 'mesh'), 0, 0, tiled=False)  5.83 us
    reshape x2, local copies, waits for them, and re-layouts, shards(): jump_trace = turned.reshape(fields, face_width, 4, elements) - inner_trace  5.55 us
  transfers between devices with their start and end apart: 7, of which 5 were waited for; matrix products, arithmetic and copies ran while one was open for 14% of the time, Pallas kernels for 0%

profile of v4, /device:TPU:0, one launch (start us, length us, event | category | flops | bytes accessed | tf_op | source)
XLA Modules:
  0.0 211.4 jit_solution(4718631249992912141)
XLA Ops:
  0.6 0.7 pad_clamp_fusion.2
  1.3 1.0 copy.332
  2.3 0.6 gather_fusion.1
  3.2 3.7 %copy.217 = f32[13,15,512]{1,0,2:T(8,128)} copy(f32[13,15,512]{2,1,0:T(8,128)S(1)} %reshape.337) | data formatting | bytes 798720 | tf_op jit(solution)/shard_map/reshape | solution.py:245
  7.1 4.0 %gather_fusion.2 = f32[128,13,15]{2,1,0:T(8,128)} fusion(f32[13,15,512]{1,0,2:T(8,128)} %copy.217, s32[1024]{0:T(1024)S(1)} %pad_clamp_fusion.1), kind=kCustom, calls=%fused_computation.2 | custom fusion | bytes 200192 | tf_op jit(solution)/shard_map/gather | solution.py:246
  11.0 2.3 %fusion.52 = (f32[13,15,64]{1,0,2:T(8,128)}, f32[13,15,64]{1,0,2:T(8,128)}) fusion(f32[13,15,128]{1,0,2:T(8,128)} %bitcast.277), kind=kLoop, calls=%fused_computation.134 | loop fusion | bytes 199680 | tf_op jit(solution)/shard_map/slice | solution.py:18
  13.3 1.3 collective-permute-start.1
  14.6 6.3 %collective-permute-start = (f32[13,15,64]{1,0,2:T(8,128)}, f32[13,15,64]{1,0,2:T(8,128)}, u32[]{:S(2)}, u32[]{:S(2)}) collective-permute-start(f32[13,15,64]{1,0,2:T(8,128)} %get-tuple-element.16), channel_id=1, source_target_pairs={{0,1},{1,2},{2,3},{3,4},{4,5},{5,6},{6,7},{8,9},{9,10},{10,11},{11... | collective-permute-start | bytes 149768 | tf_op jit(solution)/shard_map/ppermute | solution.py:20
  21.3 1.7 convolution_bitcast_fusion.3
  23.3 1.2 reshape.343
  24.6 1.6 fusion.54
  26.2 0.8 convolution_bitcast_fusion.1
  27.3 0.8 convolution_bitcast_fusion
  28.5 0.7 copy-done.15
  29.1 2.3 %fusion.7 = f32[13,35,128]{2,0,1:T(8,128)} fusion(f32[3,13,35,128,1]{3,2,1,0,4:T(8,128)S(1)} %maximum_bitcast_fusion, f32[6,35,128]{2,0,1:T(8,128)S(1)} %copy.210, f32[3,6,13,13]{3,2,1,0:T(8,128)S(1)} %copy-done.15), kind=kOutput, calls=%fused_computation.21 | convolution fusion | flops 164178560 | bytes 1051528 | tf_op jit(solution)/shard_map/dpfg,dfae->pgae/dot_general | solution.py:132
  31.4 2.2 %fusion.18 = f32[10,5]{0,1:T(8,128)S(1)} fusion(f32[5,26880]{1,0:T(8,128)S(1)} %reshape.344, f32[5,26880]{1,0:T(8,128)S(1)} %reshape.343, f32[]{:T(128)S(6)} %convert_element_type.75), kind=kOutput, calls=%fused_computation.38 | convolution fusion | flops 16396850 | bytes 1075404 | tf_op jit(solution)/shard_map/dot_general | solution.py:174
  33.7 1.0 maximum_bitcast_fusion.2
  34.7 1.0 maximum_bitcast_fusion.3
  35.6 0.6 pad_clamp_fusion
  36.3 0.8 gather_fusion
  37.1 0.8 copy.276
  39.2 1.3 copy.219
  40.4 1.4 collective-permute-done
  41.8 1.9 copy.218
  43.7 1.0 pad_maximum_fusion.7
  44.7 3.2 %copy.220 = f32[13,15,640]{0,2,1:T(8,128)} copy(f32[13,15,640]{2,1,0:T(8,128)S(1)} %pad_maximum_fusion.7) | data formatting | bytes 998400 | tf_op jit(solution)/shard_map/concatenate | solution.py:248
  48.0 17.3 %gather_fusion.3 = f32[7680,13]{1,0:T(8,128)} fusion(f32[13,9600]{0,1:T(8,128)} %bitcast.267, s32[8192]{0:T(1024)S(1)} %copy-done.18), kind=kCustom, calls=%fused_computation.3 | custom fusion | bytes 829440 | tf_op jit(solution)/shard_map/gather | solution.py:251
  65.3 2.8 %copy.221 = f32[13,15,4,128]{3,0,2,1:T(8,128)S(1)} copy(f32[13,15,4,128]{0,3,2,1:T(8,128)} %bitcast.269) | data formatting | bytes 798720 | tf_op jit(solution)/shard_map/reshape | solution.py:252
  68.2 2.7 %fusion.1 = f32[13,15,4,128]{3,0,2,1:T(8,128)S(1)} fusion(f32[6,15,4,128]{3,0,2,1:T(8,128)S(1)} %bitcast.278, f32[13,15,4,128]{3,0,2,1:T(8,128)S(1)} %sub.151, f32[3,4,128]{2,0,1:T(4,128)S(1)} %copy-done.39, f32[3,6,13,13]{3,2,1,0:T(8,128)S(1)} %copy-done.16), kind=kOutput, calls=%fused_computation.10 | convolution fusion | flops 281748480 | bytes 1001352 | tf_op jit(solution)/shard_map/dpfg,dfnxe->pgnxe/dot_general | solution.py:144
  71.0 0.7 fusion.14
  71.8 1.7 convolution_bitcast_fusion.2
  74.2 0.9 copy.229
  75.1 1.2 reshape.340
  76.3 3.7 %copy.230 = f32[13,15,512]{1,0,2:T(8,128)} copy(f32[13,15,512]{2,1,0:T(8,128)S(1)} %reshape.340) | data formatting | bytes 798720 | tf_op jit(solution)/shard_map/reshape | solution.py:245
  80.0 3.9 %gather_fusion.5 = f32[128,13,15]{2,1,0:T(8,128)} fusion(f32[13,15,512]{1,0,2:T(8,128)} %copy.230, s32[1024]{0:T(1024)} %copy-done.41), kind=kCustom, calls=%fused_computation.5 | custom fusion | bytes 200192 | tf_op jit(solution)/shard_map/gather | solution.py:246
  83.9 2.2 %fusion.51 = (f32[13,15,64]{1,0,2:T(8,128)}, f32[13,15,64]{1,0,2:T(8,128)S(1)}) fusion(f32[13,15,128]{1,0,2:T(8,128)} %bitcast.276), kind=kLoop, calls=%fused_computation.133 | loop fusion | bytes 199680 | tf_op jit(solution)/shard_map/slice | solution.py:18
  86.1 1.3 collective-permute-start.3
  87.4 5.8 %collective-permute-start.2 = (f32[13,15,64]{1,0,2:T(8,128)}, f32[13,15,64]{1,0,2:T(8,128)}, u32[]{:S(2)}, u32[]{:S(2)}) collective-permute-start(f32[13,15,64]{1,0,2:T(8,128)} %get-tuple-element.14), channel_id=1, source_target_pairs={{0,1},{1,2},{2,3},{3,4},{4,5},{5,6},{6,7},{8,9},{9,10},{10,11},{11... | collective-permute-start | bytes 149768 | tf_op jit(solution)/shard_map/ppermute | solution.py:20
  93.5 2.4 %fusion.5 = f32[6,35,128]{2,0,1:T(8,128)} fusion(f32[3,13,35,128,1]{3,2,1,0,4:T(8,128)S(1)} %copy-done.14, f32[13,35,128]{2,0,1:T(8,128)S(1)} %copy.228, f32[3,6,13,13]{3,2,1,0:T(8,128)S(1)} %copy-done.17), kind=kOutput, calls=%fused_computation.17 | convolution fusion | flops 164209920 | bytes 1051528 | tf_op jit(solution)/shard_map/dpfg,dgae->pfae/dot_general | solution.py:138
  96.0 2.4 %fusion.6 = f32[13,35,128]{2,0,1:T(8,128)} fusion(f32[3,13,35,128,1]{3,2,1,0,4:T(8,128)S(1)} %maximum_bitcast_fusion.1, f32[6,35,128]{2,0,1:T(8,128)S(1)} %copy-done.8, f32[3,6,13,13]{3,2,1,0:T(8,128)S(1)} %copy-done.17), kind=kOutput, calls=%fused_computation.19 | convolution fusion | flops 164178560 | bytes 1051528 | tf_op jit(solution)/shard_map/dpfg,dfae->pgae/dot_general | solution.py:132
  98.3 4.4 %collective-permute-done.3 = f32[13,15,64]{1,0,2:T(8,128)} collective-permute-done((f32[13,15,64]{1,0,2:T(8,128)S(1)}, f32[13,15,64]{1,0,2:T(8,128)}, u32[]{:S(2)}, u32[]{:S(2)}) %collective-permute-start.3) | collective-permute-done | bytes 49952 | tf_op jit(solution)/shard_map/ppermute | solution.py:21
  102.7 1.3 copy.232
  104.0 10.1 %collective-permute-done.2 = f32[13,15,64]{1,0,2:T(8,128)} collective-permute-done((f32[13,15,64]{1,0,2:T(8,128)}, f32[13,15,64]{1,0,2:T(8,128)}, u32[]{:S(2)}, u32[]{:S(2)}) %collective-permute-start.2) | collective-permute-done | bytes 49952 | tf_op jit(solution)/shard_map/ppermute | solution.py:20
  114.1 1.3 copy.231
  115.4 0.9 pad_maximum_fusion.8
  116.3 4.0 %copy.233 = f32[13,15,640]{0,2,1:T(8,128)} copy(f32[13,15,640]{2,1,0:T(8,128)} %pad_maximum_fusion.8) | data formatting | bytes 998400 | tf_op jit(solution)/shard_map/concatenate | solution.py:248
  120.2 17.3 %gather_fusion.6 = f32[7680,13]{1,0:T(8,128)} fusion(f32[13,9600]{0,1:T(8,128)} %bitcast.266, s32[8192]{0:T(1024)S(1)} %copy-done.18), kind=kCustom, calls=%fused_computation.6 | custom fusion | bytes 829440 | tf_op jit(solution)/shard_map/gather | solution.py:251
  137.5 2.8 %copy.234 = f32[13,15,4,128]{3,0,2,1:T(8,128)S(1)} copy(f32[13,15,4,128]{0,3,2,1:T(8,128)} %bitcast.268) | data formatting | bytes 798720 | tf_op jit(solution)/shard_map/reshape | solution.py:252
  140.4 2.6 %fusion = f32[13,15,4,128]{3,0,2,1:T(8,128)S(1)} fusion(f32[6,15,4,128]{3,0,2,1:T(8,128)S(1)} %bitcast.279, f32[13,15,4,128]{3,0,2,1:T(8,128)S(1)} %sub.152, f32[3,4,128]{2,0,1:T(4,128)S(1)} %copy-done.40, f32[3,6,13,13]{3,2,1,0:T(8,128)S(1)} %copy-done.17), kind=kOutput, calls=%fused_computation.8 | convolution fusion | flops 281748480 | bytes 1001352 | tf_op jit(solution)/shard_map/dpfg,dfnxe->pgnxe/dot_general | solution.py:144
  143.2 0.7 fusion.17
  144.2 1.8 fusion.4
  146.1 0.7 reshape.451
  146.8 3.1 %fusion.19 = f32[10]{0:T(128)S(1)} fusion(f32[26880,1]{0,1:T(1,128)} %reshape.451, f32[5,26880]{1,0:T(8,128)S(1)} %reshape.344, f32[5,26880]{1,0:T(8,128)S(1)} %reshape.343), kind=kOutput, calls=%fused_computation.39 | convolution fusion | flops 3494400 | bytes 1182760 | tf_op jit(solution)/shard_map/dot_general | solution.py:173
  150.0 0.6 broadcast_in_dim.17
  150.6 5.8 %all-to-all-start = ((f32[32,1,60]{2,1,0:T(1,128)}), f32[32,1,60]{2,1,0:T(1,128)S(1)}, u32[]{:S(2)}, u32[]{:S(2)}) async-start(f32[32,1,60]{2,1,0:T(1,128)} %broadcast_in_dim.17), calls=%async_computation | async-start | bytes 32768 | tf_op jit(solution)/shard_map/all_to_all | solution.py:271
  156.6 0.9 copy.250
  157.5 1.8 collective-permute-start.4
  159.3 4.3 %all-to-all-done = f32[32,1,60]{2,1,0:T(1,128)S(1)} async-done(((f32[32,1,60]{2,1,0:T(1,128)}), f32[32,1,60]{2,1,0:T(1,128)S(1)}, u32[]{:S(2)}, u32[]{:S(2)}) %all-to-all-start) | async-done | bytes 7712 | tf_op jit(solution)/shard_map/all_to_all | solution.py:271
  163.7 0.7 fusion.58
  164.4 0.7 fusion.57
  165.2 0.7 fusion.56
  179.9 0.7 fusion.55
  209.5 1.0 collective-permute-done.5
  210.6 0.8 copy.251
  (151 shorter events, 5.5 us)
Async XLA Ops:
  3.2 3.7 %copy-start.53 = (s32[128]{0:T(128)S(1)}, s32[128]{0:T(128)}, u32[]{:S(2)}) copy-start(s32[128]{0:T(128)} %param.35) | copy-start | bytes 1540
  6.9 14.0 %copy-start.44 = (s32[4,128]{1,0:T(4,128)S(1)}, s32[4,128]{1,0:T(4,128)}, u32[]{:S(2)}) copy-start(s32[4,128]{1,0:T(4,128)} %param.34) | copy-start | bytes 6148
  6.9 14.0 %copy-start.45 = (s32[4,128]{1,0:T(4,128)S(1)}, s32[4,128]{1,0:T(4,128)}, u32[]{:S(2)}) copy-start(s32[4,128]{1,0:T(4,128)} %param.33) | copy-start | bytes 6148
  6.9 14.1 %copy-start.47 = (s32[15]{0:T(128)S(1)}, s32[15]{0:T(128)}, u32[]{:S(2)}) copy-start(s32[15]{0:T(128)} %constant.69.clone) | copy-start | bytes 184
  6.9 14.1 %copy-start.48 = (s32[15]{0:T(128)S(1)}, s32[15]{0:T(128)}, u32[]{:S(2)}) copy-start(s32[15]{0:T(128)} %constant.68.clone) | copy-start | bytes 184
  6.9 14.1 %copy-start.49 = (s32[15]{0:T(128)S(1)}, s32[15]{0:T(128)}, u32[]{:S(2)}) copy-start(s32[15]{0:T(128)} %constant.67.clone) | copy-start | bytes 184
  7.0 14.0 %copy-start.50 = (s32[15]{0:T(128)S(1)}, s32[15]{0:T(128)}, u32[]{:S(2)}) copy-start(s32[15]{0:T(128)} %constant.66.clone) | copy-start | bytes 184
  7.0 14.0 %copy-start.51 = (s32[15]{0:T(128)S(1)}, s32[15]{0:T(128)}, u32[]{:S(2)}) copy-start(s32[15]{0:T(128)} %constant.24.clone) | copy-start | bytes 184
  7.0 14.3 %copy-start.46 = (f32[4,128]{1,0:T(4,128)S(1)}, f32[4,128]{1,0:T(4,128)}, u32[]{:S(2)}) copy-start(f32[4,128]{1,0:T(4,128)} %param.32) | copy-start | bytes 6148
  7.0 14.3 %copy-start.3 = (f32[1,13,35,128]{3,0,2,1:T(1,128)S(1)}, f32[1,13,35,128]{3,0,2,1:T(1,128)}, u32[]{:S(2)}) copy-start(f32[1,13,35,128]{3,0,2,1:T(1,128)} %param.26) | copy-start | bytes 698884
  7.0 14.3 %copy-start.11 = (f32[3,35,35,1]{2,1,3,0:T(8,128)S(1)}, f32[3,35,35,1]{2,1,3,0:T(8,128)}, u32[]{:S(2)}) copy-start(f32[3,35,35,1]{2,1,3,0:T(8,128)} %constant.77) | copy-start | bytes 44104
  7.0 13.9 %copy-start.41 = (s32[1024]{0:T(1024)}, s32[1024]{0:T(1024)S(1)}, u32[]{:S(2)}) copy-start(s32[1024]{0:T(1024)S(1)} %pad_clamp_fusion.1) | copy-start | bytes 12292
  11.0 12.0 %copy-start.43 = (f32[3,3,128]{2,1,0:T(4,128)S(1)}, f32[3,3,128]{2,1,0:T(4,128)}, u32[]{:S(2)}) copy-start(f32[3,3,128]{2,1,0:T(4,128)} %param.30) | copy-start | bytes 13828
  11.0 12.0 %copy-start = (f32[6,35,128]{2,1,0:T(8,128)S(1)}, f32[6,35,128]{2,1,0:T(8,128)}, u32[]{:S(2)}) copy-start(f32[6,35,128]{2,1,0:T(8,128)} %param.28) | copy-start | bytes 322564
  11.0 12.1 %copy-start.4 = (f32[5,6,35,128]{3,2,1,0:T(8,128)S(1)}, f32[5,6,35,128]{3,2,1,0:T(8,128)}, u32[]{:S(2)}) copy-start(f32[5,6,35,128]{3,2,1,0:T(8,128)} %param.37) | copy-start | bytes 1612804
  13.3 25.8 %collective-permute-start.1 = (f32[13,15,64]{1,0,2:T(8,128)}, f32[13,15,64]{1,0,2:T(8,128)}, u32[]{:S(2)}, u32[]{:S(2)}) collective-permute-start(f32[13,15,64]{1,0,2:T(8,128)} %get-tuple-element.17), channel_id=1, source_target_pairs={{1,0},{2,1},{3,2},{4,3},{5,4},{6,5},{7,6},{9,8},{10,9},{11,10},{12... | collective-permute-start | bytes 149768 | tf_op jit(solution)/shard_map/ppermute | solution.py:21
  14.6 27.2 %collective-permute-start = (f32[13,15,64]{1,0,2:T(8,128)}, f32[13,15,64]{1,0,2:T(8,128)}, u32[]{:S(2)}, u32[]{:S(2)}) collective-permute-start(f32[13,15,64]{1,0,2:T(8,128)} %get-tuple-element.16), channel_id=1, source_target_pairs={{0,1},{1,2},{2,3},{3,4},{4,5},{5,6},{6,7},{8,9},{9,10},{10,11},{11... | collective-permute-start | bytes 149768 | tf_op jit(solution)/shard_map/ppermute | solution.py:20
  23.0 5.1 %copy-start.23 = (f32[128]{0:T(128)}, f32[128]{0:T(128)S(1)}, u32[]{:S(2)}) copy-start(f32[128]{0:T(128)S(1)} %get-tuple-element.40) | copy-start | bytes 1540
  23.0 5.1 %copy-start.25 = (f32[128]{0:T(128)}, f32[128]{0:T(128)S(1)}, u32[]{:S(2)}) copy-start(f32[128]{0:T(128)S(1)} %get-tuple-element.41) | copy-start | bytes 1540
  23.1 5.1 %copy-start.27 = (f32[128]{0:T(128)}, f32[128]{0:T(128)S(1)}, u32[]{:S(2)}) copy-start(f32[128]{0:T(128)S(1)} %get-tuple-element.42) | copy-start | bytes 1540
  23.1 5.1 %copy-start.29 = (f32[128]{0:T(128)}, f32[128]{0:T(128)S(1)}, u32[]{:S(2)}) copy-start(f32[128]{0:T(128)S(1)} %get-tuple-element.43) | copy-start | bytes 1540
  23.1 5.1 %copy-start.31 = (f32[128]{0:T(128)}, f32[128]{0:T(128)S(1)}, u32[]{:S(2)}) copy-start(f32[128]{0:T(128)S(1)} %get-tuple-element.44) | copy-start | bytes 1540
  23.1 5.1 %copy-start.33 = (f32[128]{0:T(128)}, f32[128]{0:T(128)S(1)}, u32[]{:S(2)}) copy-start(f32[128]{0:T(128)S(1)} %get-tuple-element.45) | copy-start | bytes 1540
  23.1 5.1 %copy-start.35 = (f32[128]{0:T(128)}, f32[128]{0:T(128)S(1)}, u32[]{:S(2)}) copy-start(f32[128]{0:T(128)S(1)} %get-tuple-element.46) | copy-start | bytes 1540
  23.1 5.1 %copy-start.37 = (f32[128]{0:T(128)}, f32[128]{0:T(128)S(1)}, u32[]{:S(2)}) copy-start(f32[128]{0:T(128)S(1)} %get-tuple-element.47) | copy-start | bytes 1540
  23.2 5.3 %copy-start.7 = (f32[6,35,128]{2,0,1:T(8,128)}, f32[6,35,128]{2,0,1:T(8,128)S(1)}, u32[]{:S(2)}) copy-start(f32[6,35,128]{2,0,1:T(8,128)S(1)} %copy.210) | copy-start | bytes 322564
  24.6 2.5 %copy-start.2 = (f32[3,13,35,128]{3,2,1,0:T(8,128)S(1)}, f32[3,13,35,128]{3,2,1,0:T(8,128)}, u32[]{:S(2)}) copy-start(f32[3,13,35,128]{3,2,1,0:T(8,128)} %convolution_bitcast_fusion.3) | copy-start | bytes 2096644
  28.2 0.9 copy-start.15
  34.7 3.3 %copy-start.42 = (f32[3,4,128]{2,1,0:T(4,128)S(1)}, f32[3,4,128]{2,1,0:T(4,128)}, u32[]{:S(2)}) copy-start(f32[3,4,128]{2,1,0:T(4,128)} %param.31) | copy-start | bytes 18436
  44.7 3.3 %copy-start.18 = (s32[8192]{0:T(1024)S(1)}, s32[8192]{0:T(1024)}, u32[]{:S(2)}) copy-start(s32[8192]{0:T(1024)} %pad_clamp_fusion) | copy-start | bytes 98308
  65.3 2.9 %copy-start.16 = (f32[3,6,13,13]{3,2,1,0:T(8,128)S(1)}, f32[3,6,13,13]{3,2,1,0:T(8,128)}, u32[]{:S(2)}) copy-start(f32[3,6,13,13]{3,2,1,0:T(8,128)} %param.29) | copy-start | bytes 36508
  65.3 2.9 %copy-start.19 = (f32[60,6,128]{2,1,0:T(8,128)S(1)}, f32[60,6,128]{2,1,0:T(8,128)}, u32[]{:S(2)}) copy-start(f32[60,6,128]{2,1,0:T(8,128)} %copy.276) | copy-start | bytes 552964
  65.3 2.9 %copy-start.39 = (f32[3,4,128]{2,0,1:T(4,128)S(1)}, f32[3,4,128]{2,0,1:T(4,128)}, u32[]{:S(2)}) copy-start(f32[3,4,128]{2,0,1:T(4,128)} %copy.214) | copy-start | bytes 18436
  68.2 2.8 %copy-start.9 = (f32[13,35,128]{2,0,1:T(8,128)S(1)}, f32[13,35,128]{2,0,1:T(8,128)}, u32[]{:S(2)}) copy-start(f32[13,35,128]{2,0,1:T(8,128)} %fusion.7) | copy-start | bytes 698884
  68.2 2.8 %copy-start.22 = (f32[4,35,15,1]{1,2,0,3:T(8,128)S(1)}, f32[4,35,15,1]{1,2,0,3:T(8,128)}, u32[]{:S(2)}) copy-start(f32[4,35,15,1]{1,2,0,3:T(8,128)} %constant.78) | copy-start | bytes 25204
  70.9 0.9 copy-start.12
  79.9 13.3 %copy-start.24 = (f32[128]{0:T(128)S(1)}, f32[128]{0:T(128)}, u32[]{:S(2)}) copy-start(f32[128]{0:T(128)} %copy-done.23) | copy-start | bytes 1540
  79.9 13.3 %copy-start.26 = (f32[128]{0:T(128)S(1)}, f32[128]{0:T(128)}, u32[]{:S(2)}) copy-start(f32[128]{0:T(128)} %copy-done.25) | copy-start | bytes 1540
  79.9 13.3 %copy-start.28 = (f32[128]{0:T(128)S(1)}, f32[128]{0:T(128)}, u32[]{:S(2)}) copy-start(f32[128]{0:T(128)} %copy-done.27) | copy-start | bytes 1540
  79.9 13.3 %copy-start.30 = (f32[128]{0:T(128)S(1)}, f32[128]{0:T(128)}, u32[]{:S(2)}) copy-start(f32[128]{0:T(128)} %copy-done.29) | copy-start | bytes 1540
  79.9 13.3 %copy-start.32 = (f32[128]{0:T(128)S(1)}, f32[128]{0:T(128)}, u32[]{:S(2)}) copy-start(f32[128]{0:T(128)} %copy-done.31) | copy-start | bytes 1540
  80.0 13.3 %copy-start.34 = (f32[128]{0:T(128)S(1)}, f32[128]{0:T(128)}, u32[]{:S(2)}) copy-start(f32[128]{0:T(128)} %copy-done.33) | copy-start | bytes 1540
  80.0 13.3 %copy-start.36 = (f32[128]{0:T(128)S(1)}, f32[128]{0:T(128)}, u32[]{:S(2)}) copy-start(f32[128]{0:T(128)} %copy-done.35) | copy-start | bytes 1540
  80.0 13.3 %copy-start.38 = (f32[128]{0:T(128)S(1)}, f32[128]{0:T(128)}, u32[]{:S(2)}) copy-start(f32[128]{0:T(128)} %copy-done.37) | copy-start | bytes 1540
  83.9 9.4 %copy-start.1 = (f32[3,13,35,128]{3,2,1,0:T(8,128)S(1)}, f32[3,13,35,128]{3,2,1,0:T(8,128)}, u32[]{:S(2)}) copy-start(f32[3,13,35,128]{3,2,1,0:T(8,128)} %convolution_bitcast_fusion.2) | copy-start | bytes 2096644
  83.9 9.5 %copy-start.14 = (f32[3,13,35,128,1]{3,2,1,0,4:T(8,128)S(1)}, f32[3,13,35,128,1]{3,2,1,0,4:T(8,128)}, u32[]{:S(2)}) copy-start(f32[3,13,35,128,1]{3,2,1,0,4:T(8,128)} %maximum_bitcast_fusion.2) | copy-start | bytes 2096644
  83.9 9.5 %copy-start.17 = (f32[3,6,13,13]{3,2,1,0:T(8,128)S(1)}, f32[3,6,13,13]{3,2,1,0:T(8,128)}, u32[]{:S(2)}) copy-start(f32[3,6,13,13]{3,2,1,0:T(8,128)} %param.29) | copy-start | bytes 36508
  86.1 16.6 %collective-permute-start.3 = (f32[13,15,64]{1,0,2:T(8,128)S(1)}, f32[13,15,64]{1,0,2:T(8,128)}, u32[]{:S(2)}, u32[]{:S(2)}) collective-permute-start(f32[13,15,64]{1,0,2:T(8,128)S(1)} %get-tuple-element.15), channel_id=1, source_target_pairs={{1,0},{2,1},{3,2},{4,3},{5,4},{6,5},{7,6},{9,8},{10,9},{11,10},{12... | collective-permute-start | bytes 149768 | tf_op jit(solution)/shard_map/ppermute | solution.py:21
  87.4 26.7 %collective-permute-start.2 = (f32[13,15,64]{1,0,2:T(8,128)}, f32[13,15,64]{1,0,2:T(8,128)}, u32[]{:S(2)}, u32[]{:S(2)}) collective-permute-start(f32[13,15,64]{1,0,2:T(8,128)} %get-tuple-element.14), channel_id=1, source_target_pairs={{0,1},{1,2},{2,3},{3,4},{4,5},{5,6},{6,7},{8,9},{9,10},{10,11},{11... | collective-permute-start | bytes 149768 | tf_op jit(solution)/shard_map/ppermute | solution.py:20
  93.5 2.5 %copy-start.8 = (f32[6,35,128]{2,0,1:T(8,128)S(1)}, f32[6,35,128]{2,0,1:T(8,128)}, u32[]{:S(2)}) copy-start(f32[6,35,128]{2,0,1:T(8,128)} %copy-done.7) | copy-start | bytes 322564
  137.5 2.9 %copy-start.20 = (f32[60,6,128]{2,1,0:T(8,128)S(1)}, f32[60,6,128]{2,1,0:T(8,128)}, u32[]{:S(2)}) copy-start(f32[60,6,128]{2,1,0:T(8,128)} %copy.276) | copy-start | bytes 552964
  137.5 2.9 %copy-start.40 = (f32[3,4,128]{2,0,1:T(4,128)S(1)}, f32[3,4,128]{2,0,1:T(4,128)}, u32[]{:S(2)}) copy-start(f32[3,4,128]{2,0,1:T(4,128)} %copy.214) | copy-start | bytes 18436
  140.4 2.7 %copy-start.10 = (f32[13,35,128]{2,0,1:T(8,128)S(1)}, f32[13,35,128]{2,0,1:T(8,128)}, u32[]{:S(2)}) copy-start(f32[13,35,128]{2,0,1:T(8,128)} %fusion.6) | copy-start | bytes 698884
  143.0 1.1 copy-start.13
  143.1 2.8 %copy-start.21 = (f32[6,35,128]{2,0,1:T(8,128)S(1)}, f32[6,35,128]{2,0,1:T(8,128)}, u32[]{:S(2)}) copy-start(f32[6,35,128]{2,0,1:T(8,128)} %fusion.5) | copy-start | bytes 322564
  146.0 3.9 %copy-start.52 = (f32[50]{0:T(128)S(1)}, f32[50]{0:T(128)}, u32[]{:S(2)}) copy-start(f32[50]{0:T(128)} %reshape.345) | copy-start | bytes 604
  146.0 33.7 %copy-start.5 = (f32[5,6,35,128]{3,2,1,0:T(8,128)S(1)}, f32[5,6,35,128]{3,2,1,0:T(8,128)}, u32[]{:S(2)}) copy-start(f32[5,6,35,128]{3,2,1,0:T(8,128)} %param.37) | copy-start | bytes 1612804
  146.0 33.7 %copy-start.6 = (f32[5,6,35,128]{3,2,1,0:T(8,128)S(1)}, f32[5,6,35,128]{3,2,1,0:T(8,128)}, u32[]{:S(2)}) copy-start(f32[5,6,35,128]{3,2,1,0:T(8,128)} %param.36) | copy-start | bytes 1612804
  150.6 12.9 %all-to-all-start = ((f32[32,1,60]{2,1,0:T(1,128)}), f32[32,1,60]{2,1,0:T(1,128)S(1)}, u32[]{:S(2)}, u32[]{:S(2)}) async-start(f32[32,1,60]{2,1,0:T(1,128)} %broadcast_in_dim.17), calls=%async_computation | async-start | bytes 32768 | tf_op jit(solution)/shard_map/all_to_all | solution.py:271
  157.5 51.3 %collective-permute-start.4 = (f32[6,35,64]{2,0,1:T(8,128)S(1)}, f32[6,35,64]{2,0,1:T(8,128)S(1)}, u32[]{:S(2)}, u32[]{:S(2)}) collective-permute-start(f32[6,35,64]{2,0,1:T(8,128)S(1)} %slice_select_fusion.1), channel_id=1, source_target_pairs={{0,16},{8,24},{16,0},{24,8},{1,17},{9,25},{17,1},{25,9},{2,18},{10... | collective-permute-start | bytes 161288 | tf_op jit(solution)/shard_map/ppermute | solution.py:160
  209.1 1.4 collective-permute-start.5

commit v5 on v3

--- a/solution.py
+++ b/solution.py
@@ -165,13 +165,10 @@
     return work
 
 
-def search_direction(grad_share, local_grad, step_rows, change_rows, own_share, keep_gram, combine_sums):
-    pairs = step_rows.shape[0]
-    step_flat = step_rows.reshape(pairs, -1)
-    change_flat = change_rows.reshape(pairs, -1)
-    both_flat = jnp.concatenate([step_flat, change_flat], axis=0)
-    with_grad = jnp.dot(both_flat, local_grad.reshape(-1), precision=HIGH)
-    gram = jnp.dot(both_flat, change_flat.T, precision=HIGH) * keep_gram
+def search_direction(grad_share, step_share, change_share, gram, combine_sums):
+    pairs = step_share.shape[0]
+    both_share = jnp.concatenate([step_share, change_share], axis=0)
+    with_grad = jnp.sum(both_share * grad_share[None], axis=(1, 2, 3))
     summed = combine_sums(jnp.concatenate([with_grad, gram.reshape(-1)]))
     step_grad = summed[:pairs]
     change_grad = summed[pairs : 2 * pairs]
@@ -196,8 +193,6 @@
             along = along + weights[earlier] * step_change[earlier, slot]
         beta_now = along / curvature[slot]
         weights[slot] = alphas[slot] - beta_now
-    step_share = own_share(step_rows)
-    change_share = own_share(change_rows)
     work = scaling * grad_share
     for slot in range(pairs):
         work = work - (scaling * alphas[slot]) * change_share[slot]
@@ -240,6 +235,20 @@
             * jnp.asarray(turn_nodes[option], jnp.int32)[:, None]
         )
     flat_index = (node_pick * slot_count + neighbours[None, :]).reshape(-1)
+    shot_count = lax.axis_size("shot")
+    share_width = elements // shot_count
+    share_start = lax.axis_index("shot") * share_width
+
+    def own_share(rows):
+        return lax.dynamic_slice_in_dim(rows, share_start, share_width, rows.ndim - 1)
+
+    step_share = own_share(history_steps)
+    change_share = own_share(history_changes)
+    both_share = jnp.concatenate([step_share, change_share], axis=0)
+    gram = jnp.sum(both_share[:, None] * change_share[None, :], axis=(2, 3, 4))
+    step_share, change_share, gram, adjoint = lax.optimization_barrier(
+        (step_share, change_share, gram, adjoint)
+    )
     gradient = jnp.zeros((params, node_count, elements), jnp.float32)
     for step_index in range(forward_states.shape[1]):
         inner_trace = adjoint[:, face_nodes.T, :]
@@ -258,13 +267,6 @@
         gradient = gradient + STEP_SIZE * kernel_term(
             adjoint, forward_states[0, step_index], coupling, metric, derivs
         )
-    shot_count = lax.axis_size("shot")
-    share_width = elements // shot_count
-    share_start = lax.axis_index("shot") * share_width
-
-    def own_share(rows):
-        return lax.dynamic_slice_in_dim(rows, share_start, share_width, rows.ndim - 1)
-
     device_count = shot_count * lax.axis_size("mesh")
 
     def combine_sums(values):
@@ -272,10 +274,7 @@
         return jnp.sum(lax.all_to_all(spread, ("shot", "mesh"), 0, 0, tiled=False), axis=0)
 
     grad_share = halving_sum(gradient, "shot", shot_count)
-    keep_gram = (lax.axis_index("shot") == 0).astype(jnp.float32)
-    result = search_direction(
-        grad_share, gradient, history_steps, history_changes, own_share, keep_gram, combine_sums
-    )
+    result = search_direction(grad_share, step_share, change_share, gram, combine_sums)
     return (adjoint[None], result)
 
 

time: 209 us -> 218 us (1.043)
  waiting for transfers between devices: 18 us -> 36 us
  matrix products: 24.4 us -> 19.1 us
  other arithmetic: 12 us -> 7.36 us
    ppermute x2, waiting for transfers between devices: 10.1 us -> 19.3 us  [padded(): before = lax.ppermute(last, axis, up)]
    ppermute x2, waiting for transfers between devices: 0.01 us -> 5.44 us  [halving_sum(): lax.ppermute(jnp.where(upper, low, high), axis, [(i, i ^ bit) for i in ra...]
    dot_general x2 -> x0, matrix products: 4.51 us -> none  [the longest x1 2.27 us: search_direction(): with_grad = jnp.dot(both_flat, local_grad.reshape(-1), precision=HIGH)]
    add x4, other arithmetic: 3.02 us -> 0.56 us  [spatial_of(): total = total + metric[2, direction_axis] * reference_grads[2]]
    reduce_sum x0 -> x2, other arithmetic: none -> 2.21 us  [the longest x1 1.82 us: shards(): gram = jnp.sum(both_share[:, None] * change_share[None, :], axis=(2, 3, 4))]
  transfers between devices with their start and end apart: 7 -> 7, of which waited for: 3 -> 6; matrix products, arithmetic and copies ran while one was open for 15% -> 8% of each run, Pallas kernels for 0% -> 0%
where the time goes in v5:
time: 218 us; the launch traced here: 217 us
  local copies, waits for them, and re-layouts  88.6 us (41%)
  between operations  43.6 us (20%)
  waiting for transfers between devices  36 us (17%)
  starting transfers between devices  22.2 us (10%)
  matrix products  19.1 us (9%)
  other arithmetic  7.36 us (3%)
    gather x2, local copies, waits for them, and re-layouts, shards(): turned = ghosts.reshape(fields, face_width * slot_count)[:, flat_index]  34.5 us
    ppermute x2, waiting for transfers between devices, padded(): before = lax.ppermute(last, axis, up)  19.3 us
    ppermute x2, starting transfers between devices, padded(): before = lax.ppermute(last, axis, up)  12.1 us
    reshape x4, local copies, waits for them, and re-layouts, shards(): flat_trace = inner_trace.reshape(fields, face_width, 4 * elements)  8.56 us
    gather x2, local copies, waits for them, and re-layouts, shards(): sent_traces = flat_trace[:, :, send_faces]  7.7 us
    concatenate x2, local copies, waits for them, and re-layouts, shards(): jnp.concatenate([flat_trace, extended[:, :, :border], extended[:, :, 3 *...  6.47 us
    dot_general x2, matrix products, surface_term(): mixing = jnp.einsum('dpfg,dfnxe->pgnxe', coupling, weighted, precision=HIGH)  6.26 us
    all_to_all x1, waiting for transfers between devices, combine_sums(): lax.all_to_all(spread, ('shot', 'mesh'), 0, 0, tiled=False)  6.14 us
  transfers between devices with their start and end apart: 7, of which 6 were waited for; matrix products, arithmetic and copies ran while one was open for 8% of the time, Pallas kernels for 0%

profile of v5, /device:TPU:0, one launch (start us, length us, event | category | flops | bytes accessed | tf_op | source)
XLA Modules:
  0.0 216.8 jit_solution(4595474724682552826)
XLA Ops:
  0.6 1.6 constant_dynamic-slice_fusion
  2.4 0.3 copy.224
  3.0 1.5 copy.223
  4.5 1.0 copy.344
  5.5 1.8 multiply_reduce_fusion
  7.4 0.6 gather_fusion.1
  8.4 3.6 %copy.232 = f32[13,15,512]{1,0,2:T(8,128)} copy(f32[13,15,512]{2,1,0:T(8,128)S(1)} %reshape.323) | data formatting | bytes 798720 | tf_op jit(solution)/shard_map/reshape | solution.py:255
  12.1 3.9 %gather_fusion.2 = f32[128,13,15]{2,1,0:T(8,128)} fusion(f32[13,15,512]{1,0,2:T(8,128)} %copy.232, s32[1024]{0:T(1024)S(1)} %pad_clamp_fusion.1), kind=kCustom, calls=%fused_computation.2 | custom fusion | bytes 200192 | tf_op jit(solution)/shard_map/gather | solution.py:256
  16.0 2.3 %fusion.43 = (f32[13,15,64]{1,0,2:T(8,128)}, f32[13,15,64]{1,0,2:T(8,128)}) fusion(f32[13,15,128]{1,0,2:T(8,128)} %bitcast.313), kind=kLoop, calls=%fused_computation.129 | loop fusion | bytes 199680 | tf_op jit(solution)/shard_map/slice | solution.py:18
  18.3 1.3 collective-permute-start.1
  19.6 6.3 %collective-permute-start = (f32[13,15,64]{1,0,2:T(8,128)}, f32[13,15,64]{1,0,2:T(8,128)}, u32[]{:S(2)}, u32[]{:S(2)}) collective-permute-start(f32[13,15,64]{1,0,2:T(8,128)} %get-tuple-element.24), channel_id=1, source_target_pairs={{0,1},{1,2},{2,3},{3,4},{4,5},{5,6},{6,7},{8,9},{9,10},{10,11},{11... | collective-permute-start | bytes 149768 | tf_op jit(solution)/shard_map/ppermute | solution.py:20
  26.2 0.8 convolution_bitcast_fusion.3
  27.1 0.4 fusion.44
  27.5 0.8 convolution_bitcast_fusion.1
  28.6 0.8 convolution_bitcast_fusion
  29.7 0.7 copy-done.9
  30.4 2.3 %fusion.5 = f32[13,35,128]{2,0,1:T(8,128)} fusion(f32[3,13,35,128,1]{3,2,0,1,4:T(8,128)S(1)} %maximum_bitcast_fusion, f32[6,35,128]{2,0,1:T(8,128)S(1)} %copy.225, f32[3,6,13,13]{3,2,1,0:T(8,128)S(1)} %copy-done.9), kind=kOutput, calls=%fused_computation.19 | convolution fusion | flops 164178560 | bytes 1051528 | tf_op jit(solution)/shard_map/dpfg,dfae->pgae/dot_general | solution.py:132
  32.6 1.0 maximum_bitcast_fusion.2
  33.6 1.0 maximum_bitcast_fusion.3
  34.6 0.8 gather_fusion
  35.5 0.8 copy.293
  36.3 1.3 copy.234
  37.6 9.2 %collective-permute-done = f32[13,15,64]{1,0,2:T(8,128)} collective-permute-done((f32[13,15,64]{1,0,2:T(8,128)}, f32[13,15,64]{1,0,2:T(8,128)}, u32[]{:S(2)}, u32[]{:S(2)}) %collective-permute-start) | collective-permute-done | bytes 49952 | tf_op jit(solution)/shard_map/ppermute | solution.py:20
  46.8 1.3 copy.233
  48.1 3.2 %copy.235 = f32[13,15,640]{0,2,1:T(8,128)} copy(f32[13,15,640]{2,1,0:T(8,128)S(1)} %pad_maximum_fusion.1) | data formatting | bytes 998400 | tf_op jit(solution)/shard_map/concatenate | solution.py:258
  51.3 17.3 %gather_fusion.3 = f32[7680,13]{1,0:T(8,128)} fusion(f32[13,9600]{0,1:T(8,128)} %bitcast.301, s32[8192]{0:T(1024)S(1)} %pad_clamp_fusion), kind=kCustom, calls=%fused_computation.3 | custom fusion | bytes 829440 | tf_op jit(solution)/shard_map/gather | solution.py:261
  68.6 2.8 %copy.236 = f32[13,15,4,128]{3,0,2,1:T(8,128)S(1)} copy(f32[13,15,4,128]{0,3,2,1:T(8,128)} %bitcast.303) | data formatting | bytes 798720 | tf_op jit(solution)/shard_map/reshape | solution.py:262
  71.5 2.6 %fusion.1 = f32[13,15,4,128]{3,0,2,1:T(8,128)S(1)} fusion(f32[6,15,4,128]{3,0,2,1:T(8,128)S(1)} %bitcast.315, f32[13,15,4,128]{3,0,2,1:T(8,128)S(1)} %sub.149, f32[3,4,128]{2,0,1:T(4,128)S(1)} %copy.229, f32[3,6,13,13]{3,2,1,0:T(8,128)S(1)} %copy-done.10), kind=kOutput, calls=%fused_computation.11 | convolution fusion | flops 281748480 | bytes 1001352 | tf_op jit(solution)/shard_map/dpfg,dfnxe->pgnxe/dot_general | solution.py:144
  74.3 0.7 fusion.13
  75.1 0.8 convolution_bitcast_fusion.2
  75.9 0.6 gather_fusion.4
  76.6 0.9 copy.243
  77.5 1.2 reshape.326
  78.7 3.6 %copy.244 = f32[13,15,512]{1,0,2:T(8,128)} copy(f32[13,15,512]{2,1,0:T(8,128)S(1)} %reshape.326) | data formatting | bytes 798720 | tf_op jit(solution)/shard_map/reshape | solution.py:255
  82.3 3.8 %gather_fusion.5 = f32[128,13,15]{2,1,0:T(8,128)} fusion(f32[13,15,512]{1,0,2:T(8,128)} %copy.244, s32[1024]{0:T(1024)S(1)} %pad_clamp_fusion.1), kind=kCustom, calls=%fused_computation.5 | custom fusion | bytes 200192 | tf_op jit(solution)/shard_map/gather | solution.py:256
  86.1 2.2 fusion.42
  88.3 1.3 collective-permute-start.3
  89.6 5.8 %collective-permute-start.2 = (f32[13,15,64]{1,0,2:T(8,128)}, f32[13,15,64]{1,0,2:T(8,128)}, u32[]{:S(2)}, u32[]{:S(2)}) collective-permute-start(f32[13,15,64]{1,0,2:T(8,128)} %get-tuple-element.22), channel_id=1, source_target_pairs={{0,1},{1,2},{2,3},{3,4},{4,5},{5,6},{6,7},{8,9},{9,10},{10,11},{11... | collective-permute-start | bytes 149768 | tf_op jit(solution)/shard_map/ppermute | solution.py:20
  95.6 2.4 %fusion.3 = f32[6,35,128]{2,0,1:T(8,128)} fusion(f32[3,13,35,128,1]{3,2,0,1,4:T(8,128)S(1)} %copy-done.8, f32[13,35,128]{2,0,1:T(8,128)S(1)} %copy-done.2, f32[3,6,13,13]{3,2,1,0:T(8,128)S(1)} %copy-done.11), kind=kOutput, calls=%fused_computation.15 | convolution fusion | flops 164209920 | bytes 1051528 | tf_op jit(solution)/shard_map/dpfg,dgae->pfae/dot_general | solution.py:138
  98.1 1.6 fusion.4
  99.7 5.1 %collective-permute-done.3 = f32[13,15,64]{1,0,2:T(8,128)} collective-permute-done((f32[13,15,64]{1,0,2:T(8,128)S(1)}, f32[13,15,64]{1,0,2:T(8,128)}, u32[]{:S(2)}, u32[]{:S(2)}) %collective-permute-start.3) | collective-permute-done | bytes 49952 | tf_op jit(solution)/shard_map/ppermute | solution.py:21
  104.9 1.3 copy.246
  106.1 10.1 %collective-permute-done.2 = f32[13,15,64]{1,0,2:T(8,128)} collective-permute-done((f32[13,15,64]{1,0,2:T(8,128)}, f32[13,15,64]{1,0,2:T(8,128)}, u32[]{:S(2)}, u32[]{:S(2)}) %collective-permute-start.2) | collective-permute-done | bytes 49952 | tf_op jit(solution)/shard_map/ppermute | solution.py:20
  116.2 1.9 copy.245
  118.1 1.0 pad_maximum_fusion.2
  119.1 3.3 %copy.247 = f32[13,15,640]{0,2,1:T(8,128)} copy(f32[13,15,640]{2,1,0:T(8,128)S(1)} %pad_maximum_fusion.2) | data formatting | bytes 998400 | tf_op jit(solution)/shard_map/concatenate | solution.py:258
  122.4 17.3 %gather_fusion.6 = f32[7680,13]{1,0:T(8,128)} fusion(f32[13,9600]{0,1:T(8,128)} %bitcast.300, s32[8192]{0:T(1024)S(1)} %copy-done.15), kind=kCustom, calls=%fused_computation.6 | custom fusion | bytes 829440 | tf_op jit(solution)/shard_map/gather | solution.py:261
  139.7 2.8 %copy.248 = f32[13,15,4,128]{3,0,2,1:T(8,128)S(1)} copy(f32[13,15,4,128]{0,3,2,1:T(8,128)} %bitcast.302) | data formatting | bytes 798720 | tf_op jit(solution)/shard_map/reshape | solution.py:262
  142.6 3.6 %fusion = f32[13,15,4,128]{3,0,2,1:T(8,128)S(1)} fusion(f32[6,15,4,128]{3,0,2,1:T(8,128)} %bitcast.314, f32[13,15,4,128]{3,0,2,1:T(8,128)S(1)} %sub.150, f32[3,4,128]{2,0,1:T(4,128)S(1)} %copy-done.21, f32[3,6,13,13]{3,2,1,0:T(8,128)S(1)} %copy-done.12), kind=kOutput, calls=%fused_computation.9 | convolution fusion | flops 281748480 | bytes 1001352 | tf_op jit(solution)/shard_map/dpfg,dfnxe->pgnxe/dot_general | solution.py:144
  146.3 0.8 fusion.16
  147.3 1.8 fusion.2
  149.2 1.6 collective-permute-start.4
  150.8 4.2 %collective-permute-done.4 = f32[6,35,64]{2,0,1:T(8,128)S(1)} collective-permute-done((f32[6,35,64]{2,0,1:T(8,128)S(1)}, f32[6,35,64]{2,0,1:T(8,128)S(1)}, u32[]{:S(2)}, u32[]{:S(2)}) %collective-permute-start.4) | collective-permute-done | bytes 53792 | tf_op jit(solution)/shard_map/ppermute | solution.py:160
  155.4 1.3 collective-permute-done.5
  156.8 0.4 fusion.10
  157.2 0.6 broadcast_in_dim.17
  157.9 5.8 %all-to-all-start = ((f32[32,1,60]{2,1,0:T(1,128)}), f32[32,1,60]{2,1,0:T(1,128)S(1)}, u32[]{:S(2)}, u32[]{:S(2)}) async-start(f32[32,1,60]{2,1,0:T(1,128)} %broadcast_in_dim.17), calls=%async_computation | async-start | bytes 32768 | tf_op jit(solution)/shard_map/all_to_all | solution.py:274
  163.7 0.9 copy.263
  164.6 6.1 %all-to-all-done = f32[32,1,60]{2,1,0:T(1,128)S(1)} async-done(((f32[32,1,60]{2,1,0:T(1,128)}), f32[32,1,60]{2,1,0:T(1,128)S(1)}, u32[]{:S(2)}, u32[]{:S(2)}) %all-to-all-start) | async-done | bytes 7712 | tf_op jit(solution)/shard_map/all_to_all | solution.py:274
  170.8 0.7 fusion.48
  171.6 0.7 fusion.46
  172.3 0.7 fusion.45
  173.1 0.7 fusion.47
  216.1 0.8 copy.264
  (112 shorter events, 3.8 us)
Async XLA Ops:
  3.0 4.3 %copy-start.32 = (s32[60]{0:T(128)S(1)}, s32[60]{0:T(128)}, u32[]{:S(2)}) copy-start(s32[60]{0:T(128)} %constant.73) | copy-start | bytes 724
  8.3 3.6 %copy-start.33 = (s32[128]{0:T(128)S(1)}, s32[128]{0:T(128)}, u32[]{:S(2)}) copy-start(s32[128]{0:T(128)} %param.35) | copy-start | bytes 1540
  12.0 13.9 %copy-start.24 = (s32[4,128]{1,0:T(4,128)S(1)}, s32[4,128]{1,0:T(4,128)}, u32[]{:S(2)}) copy-start(s32[4,128]{1,0:T(4,128)} %param.34) | copy-start | bytes 6148
  12.0 13.9 %copy-start.25 = (s32[4,128]{1,0:T(4,128)S(1)}, s32[4,128]{1,0:T(4,128)}, u32[]{:S(2)}) copy-start(s32[4,128]{1,0:T(4,128)} %param.33) | copy-start | bytes 6148
  12.0 13.9 %copy-start.27 = (s32[15]{0:T(128)S(1)}, s32[15]{0:T(128)}, u32[]{:S(2)}) copy-start(s32[15]{0:T(128)} %constant.69.clone) | copy-start | bytes 184
  12.0 13.9 %copy-start.28 = (s32[15]{0:T(128)S(1)}, s32[15]{0:T(128)}, u32[]{:S(2)}) copy-start(s32[15]{0:T(128)} %constant.68.clone) | copy-start | bytes 184
  12.0 13.9 %copy-start.29 = (s32[15]{0:T(128)S(1)}, s32[15]{0:T(128)}, u32[]{:S(2)}) copy-start(s32[15]{0:T(128)} %constant.67.clone) | copy-start | bytes 184
  12.0 13.9 %copy-start.30 = (s32[15]{0:T(128)S(1)}, s32[15]{0:T(128)}, u32[]{:S(2)}) copy-start(s32[15]{0:T(128)} %constant.66.clone) | copy-start | bytes 184
  12.0 13.9 %copy-start.31 = (s32[15]{0:T(128)S(1)}, s32[15]{0:T(128)}, u32[]{:S(2)}) copy-start(s32[15]{0:T(128)} %constant.24.clone) | copy-start | bytes 184
  12.0 14.1 %copy-start.26 = (f32[4,128]{1,0:T(4,128)S(1)}, f32[4,128]{1,0:T(4,128)}, u32[]{:S(2)}) copy-start(f32[4,128]{1,0:T(4,128)} %param.32) | copy-start | bytes 6148
  12.1 14.1 %copy-start.6 = (f32[3,35,35,1]{2,1,0,3:T(8,128)S(1)}, f32[3,35,35,1]{2,1,0,3:T(8,128)}, u32[]{:S(2)}) copy-start(f32[3,35,35,1]{2,1,0,3:T(8,128)} %constant.76) | copy-start | bytes 44104
  16.0 11.1 %copy-start.23 = (f32[3,3,128]{2,1,0:T(4,128)S(1)}, f32[3,3,128]{2,1,0:T(4,128)}, u32[]{:S(2)}) copy-start(f32[3,3,128]{2,1,0:T(4,128)} %param.30) | copy-start | bytes 13828
  16.0 11.1 %copy-start = (f32[6,35,128]{2,1,0:T(8,128)S(1)}, f32[6,35,128]{2,1,0:T(8,128)}, u32[]{:S(2)}) copy-start(f32[6,35,128]{2,1,0:T(8,128)} %param.28) | copy-start | bytes 322564
  16.0 11.1 %copy-start.13 = (f32[1,2,13,35,128]{4,1,3,2,0:T(2,128)S(1)}, f32[1,2,13,35,128]{4,1,3,2,0:T(2,128)}, u32[]{:S(2)}) copy-start(f32[1,2,13,35,128]{4,1,3,2,0:T(2,128)} %param.27) | copy-start | bytes 1397764
  18.3 18.0 %collective-permute-start.1 = (f32[13,15,64]{1,0,2:T(8,128)}, f32[13,15,64]{1,0,2:T(8,128)}, u32[]{:S(2)}, u32[]{:S(2)}) collective-permute-start(f32[13,15,64]{1,0,2:T(8,128)} %get-tuple-element.25), channel_id=1, source_target_pairs={{1,0},{2,1},{3,2},{4,3},{5,4},{6,5},{7,6},{9,8},{10,9},{11,10},{12... | collective-permute-start | bytes 149768 | tf_op jit(solution)/shard_map/ppermute | solution.py:21
  19.6 27.2 %collective-permute-start = (f32[13,15,64]{1,0,2:T(8,128)}, f32[13,15,64]{1,0,2:T(8,128)}, u32[]{:S(2)}, u32[]{:S(2)}) collective-permute-start(f32[13,15,64]{1,0,2:T(8,128)} %get-tuple-element.24), channel_id=1, source_target_pairs={{0,1},{1,2},{2,3},{3,4},{4,5},{5,6},{6,7},{8,9},{9,10},{10,11},{11... | collective-permute-start | bytes 149768 | tf_op jit(solution)/shard_map/ppermute | solution.py:20
  27.1 2.6 %copy-start.3 = (f32[6,35,128]{2,0,1:T(8,128)}, f32[6,35,128]{2,0,1:T(8,128)S(1)}, u32[]{:S(2)}) copy-start(f32[6,35,128]{2,0,1:T(8,128)S(1)} %copy.225) | copy-start | bytes 322564
  29.4 0.9 copy-start.9
  33.6 2.7 %copy-start.22 = (f32[3,4,128]{2,1,0:T(4,128)S(1)}, f32[3,4,128]{2,1,0:T(4,128)}, u32[]{:S(2)}) copy-start(f32[3,4,128]{2,1,0:T(4,128)} %param.31) | copy-start | bytes 18436
  34.6 16.7 %copy-start.14 = (s32[8192]{0:T(1024)}, s32[8192]{0:T(1024)S(1)}, u32[]{:S(2)}) copy-start(s32[8192]{0:T(1024)S(1)} %pad_clamp_fusion) | copy-start | bytes 98308
  36.3 35.2 %copy-start.20 = (f32[3,4,128]{2,0,1:T(4,128)}, f32[3,4,128]{2,0,1:T(4,128)S(1)}, u32[]{:S(2)}) copy-start(f32[3,4,128]{2,0,1:T(4,128)S(1)} %copy.229) | copy-start | bytes 18436
  68.6 2.9 %copy-start.10 = (f32[3,6,13,13]{3,2,1,0:T(8,128)S(1)}, f32[3,6,13,13]{3,2,1,0:T(8,128)}, u32[]{:S(2)}) copy-start(f32[3,6,13,13]{3,2,1,0:T(8,128)} %param.29) | copy-start | bytes 36508
  68.6 2.9 %copy-start.16 = (f32[60,6,128]{2,1,0:T(8,128)S(1)}, f32[60,6,128]{2,1,0:T(8,128)}, u32[]{:S(2)}) copy-start(f32[60,6,128]{2,1,0:T(8,128)} %copy.293) | copy-start | bytes 552964
  71.5 2.8 %copy-start.5 = (f32[13,35,128]{2,0,1:T(8,128)S(1)}, f32[13,35,128]{2,0,1:T(8,128)}, u32[]{:S(2)}) copy-start(f32[13,35,128]{2,0,1:T(8,128)} %fusion.5) | copy-start | bytes 698884
  71.5 2.8 %copy-start.18 = (f32[4,35,15,1]{1,2,0,3:T(8,128)S(1)}, f32[4,35,15,1]{1,2,0,3:T(8,128)}, u32[]{:S(2)}) copy-start(f32[4,35,15,1]{1,2,0,3:T(8,128)} %constant.77) | copy-start | bytes 25204
  75.1 1.5 copy-start.1
  86.1 9.4 %copy-start.2 = (f32[13,35,128]{2,0,1:T(8,128)S(1)}, f32[13,35,128]{2,0,1:T(8,128)}, u32[]{:S(2)}) copy-start(f32[13,35,128]{2,0,1:T(8,128)} %copy-done.1) | copy-start | bytes 698884
  86.1 9.4 %copy-start.8 = (f32[3,13,35,128,1]{3,2,0,1,4:T(8,128)S(1)}, f32[3,13,35,128,1]{3,2,0,1,4:T(8,128)}, u32[]{:S(2)}) copy-start(f32[3,13,35,128,1]{3,2,0,1,4:T(8,128)} %maximum_bitcast_fusion.2) | copy-start | bytes 2096644
  86.1 9.4 %copy-start.11 = (f32[3,6,13,13]{3,2,1,0:T(8,128)S(1)}, f32[3,6,13,13]{3,2,1,0:T(8,128)}, u32[]{:S(2)}) copy-start(f32[3,6,13,13]{3,2,1,0:T(8,128)} %param.29) | copy-start | bytes 36508
  88.3 16.6 %collective-permute-start.3 = (f32[13,15,64]{1,0,2:T(8,128)S(1)}, f32[13,15,64]{1,0,2:T(8,128)}, u32[]{:S(2)}, u32[]{:S(2)}) collective-permute-start(f32[13,15,64]{1,0,2:T(8,128)S(1)} %get-tuple-element.23), channel_id=1, source_target_pairs={{1,0},{2,1},{3,2},{4,3},{5,4},{6,5},{7,6},{9,8},{10,9},{11,10},{12... | collective-permute-start | bytes 149768 | tf_op jit(solution)/shard_map/ppermute | solution.py:21
  89.6 26.7 %collective-permute-start.2 = (f32[13,15,64]{1,0,2:T(8,128)}, f32[13,15,64]{1,0,2:T(8,128)}, u32[]{:S(2)}, u32[]{:S(2)}) collective-permute-start(f32[13,15,64]{1,0,2:T(8,128)} %get-tuple-element.22), channel_id=1, source_target_pairs={{0,1},{1,2},{2,3},{3,4},{4,5},{5,6},{6,7},{8,9},{9,10},{10,11},{11... | collective-permute-start | bytes 149768 | tf_op jit(solution)/shard_map/ppermute | solution.py:20
  95.6 2.5 %copy-start.4 = (f32[6,35,128]{2,0,1:T(8,128)S(1)}, f32[6,35,128]{2,0,1:T(8,128)}, u32[]{:S(2)}) copy-start(f32[6,35,128]{2,0,1:T(8,128)} %copy-done.3) | copy-start | bytes 322564
  119.1 3.3 %copy-start.15 = (s32[8192]{0:T(1024)S(1)}, s32[8192]{0:T(1024)}, u32[]{:S(2)}) copy-start(s32[8192]{0:T(1024)} %copy-done.14) | copy-start | bytes 98308
  139.7 2.9 %copy-start.12 = (f32[3,6,13,13]{3,2,1,0:T(8,128)S(1)}, f32[3,6,13,13]{3,2,1,0:T(8,128)}, u32[]{:S(2)}) copy-start(f32[3,6,13,13]{3,2,1,0:T(8,128)} %param.29) | copy-start | bytes 36508
  139.7 2.9 %copy-start.21 = (f32[3,4,128]{2,0,1:T(4,128)S(1)}, f32[3,4,128]{2,0,1:T(4,128)}, u32[]{:S(2)}) copy-start(f32[3,4,128]{2,0,1:T(4,128)} %copy-done.20) | copy-start | bytes 18436
  142.5 3.7 %copy-start.19 = (f32[4,35,15,1]{1,2,0,3:T(8,128)S(1)}, f32[4,35,15,1]{1,2,0,3:T(8,128)}, u32[]{:S(2)}) copy-start(f32[4,35,15,1]{1,2,0,3:T(8,128)} %constant.77) | copy-start | bytes 25204
  146.2 1.1 copy-start.7
  146.3 2.8 %copy-start.17 = (f32[6,35,128]{2,0,1:T(8,128)S(1)}, f32[6,35,128]{2,0,1:T(8,128)}, u32[]{:S(2)}) copy-start(f32[6,35,128]{2,0,1:T(8,128)} %fusion.3) | copy-start | bytes 322564
  149.2 5.8 %collective-permute-start.4 = (f32[6,35,64]{2,0,1:T(8,128)S(1)}, f32[6,35,64]{2,0,1:T(8,128)S(1)}, u32[]{:S(2)}, u32[]{:S(2)}) collective-permute-start(f32[6,35,64]{2,0,1:T(8,128)S(1)} %slice_select_fusion.1), channel_id=1, source_target_pairs={{0,16},{8,24},{16,0},{24,8},{1,17},{9,25},{17,1},{25,9},{2,18},{10... | collective-permute-start | bytes 161288 | tf_op jit(solution)/shard_map/ppermute | solution.py:160
  155.2 1.4 collective-permute-start.5
  157.9 12.9 %all-to-all-start = ((f32[32,1,60]{2,1,0:T(1,128)}), f32[32,1,60]{2,1,0:T(1,128)S(1)}, u32[]{:S(2)}, u32[]{:S(2)}) async-start(f32[32,1,60]{2,1,0:T(1,128)} %broadcast_in_dim.17), calls=%async_computation | async-start | bytes 32768 | tf_op jit(solution)/shard_map/all_to_all | solution.py:274

commit v6 on v5

--- a/solution.py
+++ b/solution.py
@@ -170,9 +170,11 @@
     both_share = jnp.concatenate([step_share, change_share], axis=0)
     with_grad = jnp.sum(both_share * grad_share[None], axis=(1, 2, 3))
     summed = combine_sums(jnp.concatenate([with_grad, gram.reshape(-1)]))
+    lanes = 0.0 * step_share[0, 0, :8, :]
+    summed = summed[:, None, None] + lanes[None]
     step_grad = summed[:pairs]
     change_grad = summed[pairs : 2 * pairs]
-    gram = summed[2 * pairs :].reshape(2 * pairs, pairs)
+    gram = summed[2 * pairs :].reshape((2 * pairs, pairs) + summed.shape[1:])
     step_change = gram[:pairs]
     change_change = gram[pairs:]
     curvature = [step_change[slot, slot] for slot in range(pairs)]
@@ -193,11 +195,13 @@
             along = along + weights[earlier] * step_change[earlier, slot]
         beta_now = along / curvature[slot]
         weights[slot] = alphas[slot] - beta_now
-    work = scaling * grad_share
-    for slot in range(pairs):
-        work = work - (scaling * alphas[slot]) * change_share[slot]
-    for slot in range(pairs):
-        work = work + weights[slot] * step_share[slot]
+    coefficients = jnp.stack(
+        [weights[slot] for slot in range(pairs)]
+        + [-scaling * alphas[slot] for slot in range(pairs)]
+        + [scaling]
+    )[:, 0, 0]
+    rows = jnp.concatenate([both_share, grad_share[None]], axis=0)
+    work = jnp.sum(coefficients[:, None, None, None] * rows, axis=0)
     return -work
 
 

time: 218 us -> 170 us (0.78)
  between operations: 43.6 us -> 1.64 us
  local copies, waits for them, and re-layouts: 88.6 us -> 85 us
    slice x6 -> x1, local copies, waits for them, and re-layouts: 2.93 us -> 0.17 us  [search_direction(): jnp.stack([weights[slot] for slot in range(pairs)] + [-scaling * alphas[s...]
  transfers between devices with their start and end apart: 7 -> 7, of which waited for: 6 -> 6; matrix products, arithmetic and copies ran while one was open for 8% -> 10% of each run, Pallas kernels for 0% -> 0%
where the time goes in v6:
time: 170 us; the launch traced here: 169 us
  local copies, waits for them, and re-layouts  85 us (50%)
  waiting for transfers between devices  36.5 us (21%)
  starting transfers between devices  22.2 us (13%)
  matrix products  17.5 us (10%)
  other arithmetic  6.63 us (4%)
    gather x2, local copies, waits for them, and re-layouts, shards(): turned = ghosts.reshape(fields, face_width * slot_count)[:, flat_index]  34.6 us
    ppermute x2, waiting for transfers between devices, padded(): before = lax.ppermute(last, axis, up)  19.8 us
    ppermute x2, starting transfers between devices, padded(): before = lax.ppermute(last, axis, up)  12.2 us
    reshape x4, local copies, waits for them, and re-layouts, shards(): flat_trace = inner_trace.reshape(fields, face_width, 4 * elements)  8.6 us
    gather x2, local copies, waits for them, and re-layouts, shards(): sent_traces = flat_trace[:, :, send_faces]  7.89 us
    concatenate x2, local copies, waits for them, and re-layouts, shards(): jnp.concatenate([flat_trace, extended[:, :, :border], extended[:, :, 3 *...  6.45 us
    all_to_all x1, waiting for transfers between devices, combine_sums(): lax.all_to_all(spread, ('shot', 'mesh'), 0, 0, tiled=False)  6.1 us
    all_to_all x1, starting transfers between devices, combine_sums(): lax.all_to_all(spread, ('shot', 'mesh'), 0, 0, tiled=False)  5.82 us
  transfers between devices with their start and end apart: 7, of which 6 were waited for; matrix products, arithmetic and copies ran while one was open for 10% of the time, Pallas kernels for 0%

profile of v6, /device:TPU:0, one launch (start us, length us, event | category | flops | bytes accessed | tf_op | source)
XLA Modules:
  0.0 169.5 jit_solution(8201138267207277505)
XLA Ops:
  0.6 1.6 constant_dynamic-slice_fusion
  2.3 1.1 copy.234
  3.5 0.5 copy.233
  4.0 1.0 copy.353
  4.9 1.6 multiply_reduce_fusion
  6.7 0.6 gather_fusion.1
  7.3 0.2 copy.241
  7.5 0.2 reshape.516
  7.6 3.6 %copy.242 = f32[13,15,512]{1,0,2:T(8,128)} copy(f32[13,15,512]{2,1,0:T(8,128)S(1)} %reshape.516) | data formatting | bytes 798720 | tf_op jit(solution)/shard_map/reshape | solution.py:259
  11.4 3.9 %gather_fusion.2 = f32[128,13,15]{2,1,0:T(8,128)} fusion(f32[13,15,512]{1,0,2:T(8,128)} %copy.242, s32[1024]{0:T(1024)S(1)} %get-tuple-element.65), kind=kCustom, calls=%fused_computation.2 | custom fusion | bytes 200192 | tf_op jit(solution)/shard_map/gather | solution.py:260
  15.3 2.3 %fusion.132 = (f32[13,15,64]{1,0,2:T(8,128)}, f32[13,15,64]{1,0,2:T(8,128)}) fusion(f32[13,15,128]{1,0,2:T(8,128)} %bitcast.782), kind=kLoop, calls=%fused_computation.264 | loop fusion | bytes 199680 | tf_op jit(solution)/shard_map/slice | solution.py:18
  17.6 1.3 collective-permute-start.1
  18.9 6.3 %collective-permute-start = (f32[13,15,64]{1,0,2:T(8,128)}, f32[13,15,64]{1,0,2:T(8,128)}, u32[]{:S(2)}, u32[]{:S(2)}) collective-permute-start(f32[13,15,64]{1,0,2:T(8,128)} %get-tuple-element.30), channel_id=1, source_target_pairs={{0,1},{1,2},{2,3},{3,4},{4,5},{5,6},{6,7},{8,9},{9,10},{10,11},{11... | collective-permute-start | bytes 149768 | tf_op jit(solution)/shard_map/ppermute | solution.py:20
  25.6 0.8 convolution_bitcast_fusion.3
  26.6 0.4 fusion.133
  26.9 0.8 convolution_bitcast_fusion.1
  28.0 0.8 convolution_bitcast_fusion
  29.2 0.7 copy-done.7
  29.8 1.6 fusion.5
  31.5 1.0 maximum_bitcast_fusion.2
  32.5 1.0 maximum_bitcast_fusion.3
  33.5 0.8 gather_fusion
  34.3 0.8 copy.305
  35.1 1.3 copy.244
  36.4 9.7 %collective-permute-done = f32[13,15,64]{1,0,2:T(8,128)} collective-permute-done((f32[13,15,64]{1,0,2:T(8,128)}, f32[13,15,64]{1,0,2:T(8,128)}, u32[]{:S(2)}, u32[]{:S(2)}) %collective-permute-start) | collective-permute-done | bytes 49952 | tf_op jit(solution)/shard_map/ppermute | solution.py:20
  46.1 1.3 copy.243
  47.5 3.2 %copy.245 = f32[13,15,640]{0,2,1:T(8,128)} copy(f32[13,15,640]{2,1,0:T(8,128)S(1)} %pad_maximum_fusion.1) | data formatting | bytes 998400 | tf_op jit(solution)/shard_map/concatenate | solution.py:262
  50.7 17.3 %gather_fusion.3 = f32[7680,13]{1,0:T(8,128)} fusion(f32[13,9600]{0,1:T(8,128)} %bitcast.764, s32[8192]{0:T(1024)S(1)} %pad_clamp_fusion), kind=kCustom, calls=%fused_computation.3 | custom fusion | bytes 829440 | tf_op jit(solution)/shard_map/gather | solution.py:265
  68.0 2.8 %copy.246 = f32[13,15,4,128]{3,0,2,1:T(8,128)S(1)} copy(f32[13,15,4,128]{0,3,2,1:T(8,128)} %bitcast.766) | data formatting | bytes 798720 | tf_op jit(solution)/shard_map/reshape | solution.py:266
  70.9 2.7 %fusion.1 = f32[13,15,4,128]{3,0,2,1:T(8,128)S(1)} fusion(f32[6,15,4,128]{3,0,2,1:T(8,128)S(1)} %bitcast.789, f32[13,15,4,128]{3,0,2,1:T(8,128)S(1)} %sub.294, f32[3,4,128]{2,0,1:T(4,128)S(1)} %copy.239, f32[3,6,13,13]{3,2,1,0:T(8,128)S(1)} %copy-done.8), kind=kOutput, calls=%fused_computation.11 | convolution fusion | flops 281748480 | bytes 1001352 | tf_op jit(solution)/shard_map/dpfg,dfnxe->pgnxe/dot_general | solution.py:144
  73.7 0.7 fusion.14
  74.5 0.8 convolution_bitcast_fusion.2
  75.3 0.6 gather_fusion.4
  76.0 0.9 copy.253
  76.9 1.2 reshape.519
  78.0 3.6 %copy.254 = f32[13,15,512]{1,0,2:T(8,128)} copy(f32[13,15,512]{2,1,0:T(8,128)S(1)} %reshape.519) | data formatting | bytes 798720 | tf_op jit(solution)/shard_map/reshape | solution.py:259
  81.7 4.0 %gather_fusion.5 = f32[128,13,15]{2,1,0:T(8,128)} fusion(f32[13,15,512]{1,0,2:T(8,128)} %copy.254, s32[1024]{0:T(1024)} %copy-done.33), kind=kCustom, calls=%fused_computation.5 | custom fusion | bytes 200192 | tf_op jit(solution)/shard_map/gather | solution.py:260
  85.7 2.2 %fusion.131 = (f32[13,15,64]{1,0,2:T(8,128)}, f32[13,15,64]{1,0,2:T(8,128)S(1)}) fusion(f32[13,15,128]{1,0,2:T(8,128)} %bitcast.781), kind=kLoop, calls=%fused_computation.263 | loop fusion | bytes 199680 | tf_op jit(solution)/shard_map/slice | solution.py:18
  87.9 1.3 collective-permute-start.3
  89.1 5.8 %collective-permute-start.2 = (f32[13,15,64]{1,0,2:T(8,128)}, f32[13,15,64]{1,0,2:T(8,128)}, u32[]{:S(2)}, u32[]{:S(2)}) collective-permute-start(f32[13,15,64]{1,0,2:T(8,128)} %get-tuple-element.28), channel_id=1, source_target_pairs={{0,1},{1,2},{2,3},{3,4},{4,5},{5,6},{6,7},{8,9},{9,10},{10,11},{11... | collective-permute-start | bytes 149768 | tf_op jit(solution)/shard_map/ppermute | solution.py:20
  95.2 2.4 %fusion.3 = f32[6,35,128]{2,0,1:T(8,128)} fusion(f32[3,13,35,128,1]{3,2,0,1,4:T(8,128)S(1)} %copy-done.6, f32[13,35,128]{2,0,1:T(8,128)S(1)} %copy.252, f32[3,6,13,13]{3,2,1,0:T(8,128)S(1)} %copy-done.9), kind=kOutput, calls=%fused_computation.15 | convolution fusion | flops 164209920 | bytes 1051528 | tf_op jit(solution)/shard_map/dpfg,dgae->pfae/dot_general | solution.py:138
  97.7 1.6 fusion.4
  99.3 5.1 %collective-permute-done.3 = f32[13,15,64]{1,0,2:T(8,128)} collective-permute-done((f32[13,15,64]{1,0,2:T(8,128)S(1)}, f32[13,15,64]{1,0,2:T(8,128)}, u32[]{:S(2)}, u32[]{:S(2)}) %collective-permute-start.3) | collective-permute-done | bytes 49952 | tf_op jit(solution)/shard_map/ppermute | solution.py:21
  104.4 1.3 copy.256
  105.7 10.1 %collective-permute-done.2 = f32[13,15,64]{1,0,2:T(8,128)} collective-permute-done((f32[13,15,64]{1,0,2:T(8,128)}, f32[13,15,64]{1,0,2:T(8,128)}, u32[]{:S(2)}, u32[]{:S(2)}) %collective-permute-start.2) | collective-permute-done | bytes 49952 | tf_op jit(solution)/shard_map/ppermute | solution.py:20
  115.8 1.3 copy.255
  117.2 3.2 %copy.257 = f32[13,15,640]{0,2,1:T(8,128)} copy(f32[13,15,640]{2,1,0:T(8,128)S(1)} %pad_maximum_fusion.2) | data formatting | bytes 998400 | tf_op jit(solution)/shard_map/concatenate | solution.py:262
  120.4 17.3 %gather_fusion.6 = f32[7680,13]{1,0:T(8,128)} fusion(f32[13,9600]{0,1:T(8,128)} %bitcast.763, s32[8192]{0:T(1024)S(1)} %pad_clamp_fusion), kind=kCustom, calls=%fused_computation.6 | custom fusion | bytes 829440 | tf_op jit(solution)/shard_map/gather | solution.py:265
  137.7 2.8 %copy.258 = f32[13,15,4,128]{3,0,2,1:T(8,128)S(1)} copy(f32[13,15,4,128]{0,3,2,1:T(8,128)} %bitcast.765) | data formatting | bytes 798720 | tf_op jit(solution)/shard_map/reshape | solution.py:266
  140.6 2.7 %fusion = f32[13,15,4,128]{3,0,2,1:T(8,128)S(1)} fusion(f32[6,15,4,128]{3,0,2,1:T(8,128)S(1)} %bitcast.790, f32[13,15,4,128]{3,0,2,1:T(8,128)S(1)} %sub.295, f32[3,4,128]{2,0,1:T(4,128)S(1)} %copy-done.32, f32[3,6,13,13]{3,2,1,0:T(8,128)S(1)} %copy-done.10), kind=kOutput, calls=%fused_computation.9 | convolution fusion | flops 281748480 | bytes 1001352 | tf_op jit(solution)/shard_map/dpfg,dfnxe->pgnxe/dot_general | solution.py:144
  143.5 0.7 fusion.17
  144.3 0.2 copy-done.5
  144.5 1.8 %fusion.2 = f32[6,35,128]{2,0,1:T(8,128)S(1)} fusion(f32[3,13,35,128,1]{3,2,0,1,4:T(8,128)S(1)} %copy-done.5, f32[13,35,128]{2,0,1:T(8,128)S(1)} %copy.271, f32[3,6,13,13]{3,2,1,0:T(8,128)S(1)} %copy-done.10), kind=kOutput, calls=%fused_computation.13 | convolution fusion | flops 164209920 | bytes 1051528 | tf_op jit(solution)/shard_map/dpfg,dgae->pfae/dot_general | solution.py:138
  146.4 1.6 collective-permute-start.4
  148.0 4.2 %collective-permute-done.4 = f32[6,35,64]{2,0,1:T(8,128)S(1)} collective-permute-done((f32[6,35,64]{2,0,1:T(8,128)S(1)}, f32[6,35,64]{2,0,1:T(8,128)S(1)}, u32[]{:S(2)}, u32[]{:S(2)}) %collective-permute-start.4) | collective-permute-done | bytes 53792 | tf_op jit(solution)/shard_map/ppermute | solution.py:160
  152.5 1.3 collective-permute-done.5
  154.0 0.3 fusion.11
  154.3 0.6 broadcast_in_dim.19
  154.9 5.8 %all-to-all-start = ((f32[32,1,60]{2,1,0:T(1,128)}), f32[32,1,60]{2,1,0:T(1,128)S(1)}, u32[]{:S(2)}, u32[]{:S(2)}) async-start(f32[32,1,60]{2,1,0:T(1,128)} %broadcast_in_dim.19), calls=%async_computation | async-start | bytes 32768 | tf_op jit(solution)/shard_map/all_to_all | solution.py:278
  160.8 0.9 copy.275
  161.7 6.1 %all-to-all-done = f32[32,1,60]{2,1,0:T(1,128)S(1)} async-done(((f32[32,1,60]{2,1,0:T(1,128)}), f32[32,1,60]{2,1,0:T(1,128)S(1)}, u32[]{:S(2)}, u32[]{:S(2)}) %all-to-all-start) | async-done | bytes 7712 | tf_op jit(solution)/shard_map/all_to_all | solution.py:278
  168.3 0.2 slice_reduce_fusion
  168.4 0.2 fusion.10
  168.7 0.8 copy.276
  (144 shorter events, 3.1 us)
Async XLA Ops:
  3.5 3.1 %copy-start.45 = (s32[128]{0:T(128)S(1)}, s32[128]{0:T(128)}, u32[]{:S(2)}) copy-start(s32[128]{0:T(128)} %param.35) | copy-start | bytes 1540
  4.0 2.7 %copy-start.44 = (s32[60]{0:T(128)S(1)}, s32[60]{0:T(128)}, u32[]{:S(2)}) copy-start(s32[60]{0:T(128)} %constant.74) | copy-start | bytes 724
  6.7 4.7 %copy-start.33 = (s32[1024]{0:T(1024)}, s32[1024]{0:T(1024)S(1)}, u32[]{:S(2)}) copy-start(s32[1024]{0:T(1024)S(1)} %get-tuple-element.65) | copy-start | bytes 12292
  11.3 14.0 %copy-start.36 = (s32[4,128]{1,0:T(4,128)S(1)}, s32[4,128]{1,0:T(4,128)}, u32[]{:S(2)}) copy-start(s32[4,128]{1,0:T(4,128)} %param.34) | copy-start | bytes 6148
  11.3 14.0 %copy-start.37 = (s32[4,128]{1,0:T(4,128)S(1)}, s32[4,128]{1,0:T(4,128)}, u32[]{:S(2)}) copy-start(s32[4,128]{1,0:T(4,128)} %param.33) | copy-start | bytes 6148
  11.3 14.0 %copy-start.39 = (s32[15]{0:T(128)S(1)}, s32[15]{0:T(128)}, u32[]{:S(2)}) copy-start(s32[15]{0:T(128)} %constant.70.clone) | copy-start | bytes 184
  11.3 14.0 %copy-start.40 = (s32[15]{0:T(128)S(1)}, s32[15]{0:T(128)}, u32[]{:S(2)}) copy-start(s32[15]{0:T(128)} %constant.69.clone) | copy-start | bytes 184
  11.3 14.0 %copy-start.41 = (s32[15]{0:T(128)S(1)}, s32[15]{0:T(128)}, u32[]{:S(2)}) copy-start(s32[15]{0:T(128)} %constant.68.clone) | copy-start | bytes 184
  11.3 14.0 %copy-start.42 = (s32[15]{0:T(128)S(1)}, s32[15]{0:T(128)}, u32[]{:S(2)}) copy-start(s32[15]{0:T(128)} %constant.24.clone) | copy-start | bytes 184
  11.3 14.0 %copy-start.43 = (s32[15]{0:T(128)S(1)}, s32[15]{0:T(128)}, u32[]{:S(2)}) copy-start(s32[15]{0:T(128)} %constant.23.clone) | copy-start | bytes 184
  11.3 14.2 %copy-start.38 = (f32[4,128]{1,0:T(4,128)S(1)}, f32[4,128]{1,0:T(4,128)}, u32[]{:S(2)}) copy-start(f32[4,128]{1,0:T(4,128)} %param.32) | copy-start | bytes 6148
  11.3 14.2 %copy-start.3 = (f32[3,35,35,1]{2,1,0,3:T(8,128)S(1)}, f32[3,35,35,1]{2,1,0,3:T(8,128)}, u32[]{:S(2)}) copy-start(f32[3,35,35,1]{2,1,0,3:T(8,128)} %constant.77) | copy-start | bytes 44104
  15.3 11.1 %copy-start.35 = (f32[3,3,128]{2,1,0:T(4,128)S(1)}, f32[3,3,128]{2,1,0:T(4,128)}, u32[]{:S(2)}) copy-start(f32[3,3,128]{2,1,0:T(4,128)} %param.30) | copy-start | bytes 13828
  15.3 11.1 %copy-start = (f32[6,35,128]{2,1,0:T(8,128)S(1)}, f32[6,35,128]{2,1,0:T(8,128)}, u32[]{:S(2)}) copy-start(f32[6,35,128]{2,1,0:T(8,128)} %param.28) | copy-start | bytes 322564
  15.3 11.2 %copy-start.11 = (f32[1,2,13,35,128]{4,1,3,2,0:T(2,128)S(1)}, f32[1,2,13,35,128]{4,1,3,2,0:T(2,128)}, u32[]{:S(2)}) copy-start(f32[1,2,13,35,128]{4,1,3,2,0:T(2,128)} %param.27) | copy-start | bytes 1397764
  17.6 17.5 %collective-permute-start.1 = (f32[13,15,64]{1,0,2:T(8,128)}, f32[13,15,64]{1,0,2:T(8,128)}, u32[]{:S(2)}, u32[]{:S(2)}) collective-permute-start(f32[13,15,64]{1,0,2:T(8,128)} %get-tuple-element.31), channel_id=1, source_target_pairs={{1,0},{2,1},{3,2},{4,3},{5,4},{6,5},{7,6},{9,8},{10,9},{11,10},{12... | collective-permute-start | bytes 149768 | tf_op jit(solution)/shard_map/ppermute | solution.py:21
  18.9 27.2 %collective-permute-start = (f32[13,15,64]{1,0,2:T(8,128)}, f32[13,15,64]{1,0,2:T(8,128)}, u32[]{:S(2)}, u32[]{:S(2)}) collective-permute-start(f32[13,15,64]{1,0,2:T(8,128)} %get-tuple-element.30), channel_id=1, source_target_pairs={{0,1},{1,2},{2,3},{3,4},{4,5},{5,6},{6,7},{8,9},{9,10},{10,11},{11... | collective-permute-start | bytes 149768 | tf_op jit(solution)/shard_map/ppermute | solution.py:20
  26.4 2.4 %copy-start.17 = (f32[128]{0:T(128)}, f32[128]{0:T(128)S(1)}, u32[]{:S(2)}) copy-start(f32[128]{0:T(128)S(1)} %get-tuple-element.50) | copy-start | bytes 1540
  26.4 2.4 %copy-start.19 = (f32[128]{0:T(128)}, f32[128]{0:T(128)S(1)}, u32[]{:S(2)}) copy-start(f32[128]{0:T(128)S(1)} %get-tuple-element.51) | copy-start | bytes 1540
  26.4 2.4 %copy-start.21 = (f32[128]{0:T(128)}, f32[128]{0:T(128)S(1)}, u32[]{:S(2)}) copy-start(f32[128]{0:T(128)S(1)} %get-tuple-element.52) | copy-start | bytes 1540
  26.5 2.4 %copy-start.23 = (f32[128]{0:T(128)}, f32[128]{0:T(128)S(1)}, u32[]{:S(2)}) copy-start(f32[128]{0:T(128)S(1)} %get-tuple-element.53) | copy-start | bytes 1540
  26.5 2.4 %copy-start.25 = (f32[128]{0:T(128)}, f32[128]{0:T(128)S(1)}, u32[]{:S(2)}) copy-start(f32[128]{0:T(128)S(1)} %get-tuple-element.54) | copy-start | bytes 1540
  26.5 2.4 %copy-start.27 = (f32[128]{0:T(128)}, f32[128]{0:T(128)S(1)}, u32[]{:S(2)}) copy-start(f32[128]{0:T(128)S(1)} %get-tuple-element.55) | copy-start | bytes 1540
  26.5 2.4 %copy-start.29 = (f32[128]{0:T(128)}, f32[128]{0:T(128)S(1)}, u32[]{:S(2)}) copy-start(f32[128]{0:T(128)S(1)} %get-tuple-element.56) | copy-start | bytes 1540
  26.5 2.6 %copy-start.1 = (f32[6,35,128]{2,0,1:T(8,128)}, f32[6,35,128]{2,0,1:T(8,128)S(1)}, u32[]{:S(2)}) copy-start(f32[6,35,128]{2,0,1:T(8,128)S(1)} %copy.235) | copy-start | bytes 322564
  28.9 0.9 copy-start.7
  32.5 2.7 %copy-start.34 = (f32[3,4,128]{2,1,0:T(4,128)S(1)}, f32[3,4,128]{2,1,0:T(4,128)}, u32[]{:S(2)}) copy-start(f32[3,4,128]{2,1,0:T(4,128)} %param.31) | copy-start | bytes 18436
  35.1 35.7 %copy-start.31 = (f32[3,4,128]{2,0,1:T(4,128)}, f32[3,4,128]{2,0,1:T(4,128)S(1)}, u32[]{:S(2)}) copy-start(f32[3,4,128]{2,0,1:T(4,128)S(1)} %copy.239) | copy-start | bytes 18436
  68.0 2.9 %copy-start.8 = (f32[3,6,13,13]{3,2,1,0:T(8,128)S(1)}, f32[3,6,13,13]{3,2,1,0:T(8,128)}, u32[]{:S(2)}) copy-start(f32[3,6,13,13]{3,2,1,0:T(8,128)} %param.29) | copy-start | bytes 36508
  68.0 2.9 %copy-start.12 = (f32[60,6,128]{2,1,0:T(8,128)S(1)}, f32[60,6,128]{2,1,0:T(8,128)}, u32[]{:S(2)}) copy-start(f32[60,6,128]{2,1,0:T(8,128)} %copy.305) | copy-start | bytes 552964
  70.9 2.8 %copy-start.15 = (f32[4,35,15,1]{1,2,0,3:T(8,128)S(1)}, f32[4,35,15,1]{1,2,0,3:T(8,128)}, u32[]{:S(2)}) copy-start(f32[4,35,15,1]{1,2,0,3:T(8,128)} %constant.78) | copy-start | bytes 25204
  73.6 0.9 copy-start.4
  81.7 13.3 %copy-start.18 = (f32[128]{0:T(128)S(1)}, f32[128]{0:T(128)}, u32[]{:S(2)}) copy-start(f32[128]{0:T(128)} %copy-done.17) | copy-start | bytes 1540
  85.6 9.3 %copy-start.20 = (f32[128]{0:T(128)S(1)}, f32[128]{0:T(128)}, u32[]{:S(2)}) copy-start(f32[128]{0:T(128)} %copy-done.19) | copy-start | bytes 1540
  85.6 9.3 %copy-start.22 = (f32[128]{0:T(128)S(1)}, f32[128]{0:T(128)}, u32[]{:S(2)}) copy-start(f32[128]{0:T(128)} %copy-done.21) | copy-start | bytes 1540
  85.7 9.3 %copy-start.24 = (f32[128]{0:T(128)S(1)}, f32[128]{0:T(128)}, u32[]{:S(2)}) copy-start(f32[128]{0:T(128)} %copy-done.23) | copy-start | bytes 1540
  85.7 9.3 %copy-start.26 = (f32[128]{0:T(128)S(1)}, f32[128]{0:T(128)}, u32[]{:S(2)}) copy-start(f32[128]{0:T(128)} %copy-done.25) | copy-start | bytes 1540
  85.7 9.3 %copy-start.28 = (f32[128]{0:T(128)S(1)}, f32[128]{0:T(128)}, u32[]{:S(2)}) copy-start(f32[128]{0:T(128)} %copy-done.27) | copy-start | bytes 1540
  85.7 9.3 %copy-start.30 = (f32[128]{0:T(128)S(1)}, f32[128]{0:T(128)}, u32[]{:S(2)}) copy-start(f32[128]{0:T(128)} %copy-done.29) | copy-start | bytes 1540
  85.7 9.5 %copy-start.6 = (f32[3,13,35,128,1]{3,2,0,1,4:T(8,128)S(1)}, f32[3,13,35,128,1]{3,2,0,1,4:T(8,128)}, u32[]{:S(2)}) copy-start(f32[3,13,35,128,1]{3,2,0,1,4:T(8,128)} %maximum_bitcast_fusion.2) | copy-start | bytes 2096644
  85.7 9.5 %copy-start.9 = (f32[3,6,13,13]{3,2,1,0:T(8,128)S(1)}, f32[3,6,13,13]{3,2,1,0:T(8,128)}, u32[]{:S(2)}) copy-start(f32[3,6,13,13]{3,2,1,0:T(8,128)} %param.29) | copy-start | bytes 36508
  87.9 16.6 %collective-permute-start.3 = (f32[13,15,64]{1,0,2:T(8,128)S(1)}, f32[13,15,64]{1,0,2:T(8,128)}, u32[]{:S(2)}, u32[]{:S(2)}) collective-permute-start(f32[13,15,64]{1,0,2:T(8,128)S(1)} %get-tuple-element.29), channel_id=1, source_target_pairs={{1,0},{2,1},{3,2},{4,3},{5,4},{6,5},{7,6},{9,8},{10,9},{11,10},{12... | collective-permute-start | bytes 149768 | tf_op jit(solution)/shard_map/ppermute | solution.py:21
  89.1 26.7 %collective-permute-start.2 = (f32[13,15,64]{1,0,2:T(8,128)}, f32[13,15,64]{1,0,2:T(8,128)}, u32[]{:S(2)}, u32[]{:S(2)}) collective-permute-start(f32[13,15,64]{1,0,2:T(8,128)} %get-tuple-element.28), channel_id=1, source_target_pairs={{0,1},{1,2},{2,3},{3,4},{4,5},{5,6},{6,7},{8,9},{9,10},{10,11},{11... | collective-permute-start | bytes 149768 | tf_op jit(solution)/shard_map/ppermute | solution.py:20
  95.2 2.5 %copy-start.2 = (f32[6,35,128]{2,0,1:T(8,128)S(1)}, f32[6,35,128]{2,0,1:T(8,128)}, u32[]{:S(2)}) copy-start(f32[6,35,128]{2,0,1:T(8,128)} %copy-done.1) | copy-start | bytes 322564
  137.7 2.9 %copy-start.10 = (f32[3,6,13,13]{3,2,1,0:T(8,128)S(1)}, f32[3,6,13,13]{3,2,1,0:T(8,128)}, u32[]{:S(2)}) copy-start(f32[3,6,13,13]{3,2,1,0:T(8,128)} %param.29) | copy-start | bytes 36508
  137.7 2.9 %copy-start.13 = (f32[60,6,128]{2,1,0:T(8,128)S(1)}, f32[60,6,128]{2,1,0:T(8,128)}, u32[]{:S(2)}) copy-start(f32[60,6,128]{2,1,0:T(8,128)} %copy.305) | copy-start | bytes 552964
  137.7 2.9 %copy-start.32 = (f32[3,4,128]{2,0,1:T(4,128)S(1)}, f32[3,4,128]{2,0,1:T(4,128)}, u32[]{:S(2)}) copy-start(f32[3,4,128]{2,0,1:T(4,128)} %copy-done.31) | copy-start | bytes 18436
  140.6 2.8 %copy-start.16 = (f32[4,35,15,1]{1,2,0,3:T(8,128)S(1)}, f32[4,35,15,1]{1,2,0,3:T(8,128)}, u32[]{:S(2)}) copy-start(f32[4,35,15,1]{1,2,0,3:T(8,128)} %constant.78) | copy-start | bytes 25204
  143.3 1.1 copy-start.5
  143.4 2.8 %copy-start.14 = (f32[6,35,128]{2,0,1:T(8,128)S(1)}, f32[6,35,128]{2,0,1:T(8,128)}, u32[]{:S(2)}) copy-start(f32[6,35,128]{2,0,1:T(8,128)} %fusion.3) | copy-start | bytes 322564
  146.4 5.8 %collective-permute-start.4 = (f32[6,35,64]{2,0,1:T(8,128)S(1)}, f32[6,35,64]{2,0,1:T(8,128)S(1)}, u32[]{:S(2)}, u32[]{:S(2)}) collective-permute-start(f32[6,35,64]{2,0,1:T(8,128)S(1)} %slice_select_fusion.1), channel_id=1, source_target_pairs={{0,16},{8,24},{16,0},{24,8},{1,17},{9,25},{17,1},{25,9},{2,18},{10... | collective-permute-start | bytes 161288 | tf_op jit(solution)/shard_map/ppermute | solution.py:160
  152.4 1.4 collective-permute-start.5
  154.9 12.9 %all-to-all-start = ((f32[32,1,60]{2,1,0:T(1,128)}), f32[32,1,60]{2,1,0:T(1,128)S(1)}, u32[]{:S(2)}, u32[]{:S(2)}) async-start(f32[32,1,60]{2,1,0:T(1,128)} %broadcast_in_dim.19), calls=%async_computation | async-start | bytes 32768 | tf_op jit(solution)/shard_map/all_to_all | solution.py:278

commit v7 on v6

--- a/solution.py
+++ b/solution.py
@@ -231,14 +231,16 @@
     face_material = material[:, face_nodes.T, :]
     neighbours = face_neighbours.reshape(-1)
     orient = face_orientation.reshape(-1)
-    node_pick = jnp.zeros((face_width, 4 * elements), jnp.int32)
-    for option in range(turn_nodes.shape[0]):
-        node_pick = (
-            node_pick
-            + (orient == option).astype(jnp.int32)[None, :]
-            * jnp.asarray(turn_nodes[option], jnp.int32)[:, None]
-        )
-    flat_index = (node_pick * slot_count + neighbours[None, :]).reshape(-1)
+    face_total = 4 * elements
+    slot_pick = (
+        neighbours[None, :] == jnp.arange(slot_count, dtype=jnp.int32)[:, None]
+    ).astype(jnp.float32)
+    local_pick = slot_pick[:face_total]
+    below_pick = slot_pick[face_total : face_total + border]
+    above_pick = slot_pick[face_total + border :]
+    send_pick = (
+        send_faces[None, :] == jnp.arange(face_total, dtype=jnp.int32)[:, None]
+    ).astype(jnp.float32)
     shot_count = lax.axis_size("shot")
     share_width = elements // shot_count
     share_start = lax.axis_index("shot") * share_width
@@ -257,12 +259,20 @@
     for step_index in range(forward_states.shape[1]):
         inner_trace = adjoint[:, face_nodes.T, :]
         flat_trace = inner_trace.reshape(fields, face_width, 4 * elements)
-        sent_traces = flat_trace[:, :, send_faces]
+        sent_traces = jnp.einsum("fns,sj->fnj", flat_trace, send_pick, precision=HIGH)
         extended = padded(sent_traces, (("mesh", 2),), border)
-        ghosts = jnp.concatenate(
-            [flat_trace, extended[:, :, :border], extended[:, :, 3 * border :]], axis=2
-        )
-        turned = ghosts.reshape(fields, face_width * slot_count)[:, flat_index]
+        gathered = jnp.einsum("fns,sj->fnj", flat_trace, local_pick, precision=HIGH)
+        gathered = gathered + jnp.einsum(
+            "fns,sj->fnj", extended[:, :, :border], below_pick, precision=HIGH
+        )
+        gathered = gathered + jnp.einsum(
+            "fns,sj->fnj", extended[:, :, 3 * border :], above_pick, precision=HIGH
+        )
+        turned = gathered
+        for option in range(turn_nodes.shape[0]):
+            turned = jnp.where(
+                (orient == option)[None, None, :], gathered[:, turn_nodes[option], :], turned
+            )
         jump_trace = turned.reshape(fields, face_width, 4, elements) - inner_trace
         change = volume_term(adjoint, material, coupling, metric, derivs) + surface_term(
             jump_trace, face_material, face_normals, face_scale, coupling, lift_tables

time: 170 us -> 110 us (0.65)
  local copies, waits for them, and re-layouts: 85 us -> 36.5 us
  waiting for transfers between devices: 36.5 us -> 11 us
  matrix products: 17.5 us -> 24.9 us
  other arithmetic: 6.63 us -> 12.7 us
    gather x4 -> x12, local copies, waits for them, and re-layouts: 42.5 us -> 17.1 us  [shards(): gathered[:, turn_nodes[option], :]]
    ppermute x2, waiting for transfers between devices: 19.8 us -> 0.01 us  [padded(): before = lax.ppermute(last, axis, up)]
    reshape x4 -> x2, local copies, waits for them, and re-layouts: 8.6 us -> 1.33 us  [shards(): flat_trace = inner_trace.reshape(fields, face_width, 4 * elements)]
    concatenate x2 -> x0, local copies, waits for them, and re-layouts: 6.45 us -> none  [shards(): jnp.concatenate([flat_trace, extended[:, :, :border], extended[:, :, 3 *...]
    select_n x2, other arithmetic: 0.1 us -> 6.24 us  [shards(): jnp.where((orient == option)[None, None, :], gathered[:, turn_nodes[optio...]
    dot_general x0 -> x8, matrix products: none -> 5.76 us  [the longest x2 1.95 us: shards(): gathered = jnp.einsum('fns,sj->fnj', flat_trace, local_pick, precision=HIGH)]
    reshape x2, local copies, waits for them, and re-layouts: 5.56 us -> 0.29 us  [shards(): jump_trace = turned.reshape(fields, face_width, 4, elements) - inner_trace]
    ppermute x2, waiting for transfers between devices: 5.11 us -> 0.01 us  [padded(): after = lax.ppermute(first, axis, down)]
  transfers between devices with their start and end apart: 7 -> 7, of which waited for: 6 -> 3; matrix products, arithmetic and copies ran while one was open for 10% -> 17% of each run, Pallas kernels for 0% -> 0%
where the time goes in v7:
time: 110 us; the launch traced here: 109 us
  local copies, waits for them, and re-layouts  36.5 us (33%)
  matrix products  24.9 us (23%)
  starting transfers between devices  21.9 us (20%)
  other arithmetic  12.7 us (12%)
  waiting for transfers between devices  11 us (10%)
  between operations  1.96 us (2%)
    gather x12, local copies, waits for them, and re-layouts, shards(): gathered[:, turn_nodes[option], :]  17.1 us
    ppermute x2, starting transfers between devices, padded(): before = lax.ppermute(last, axis, up)  10.2 us
    unnamed x135, local copies, waits for them, and re-layouts  7.92 us
    all_to_all x1, starting transfers between devices, combine_sums(): lax.all_to_all(spread, ('shot', 'mesh'), 0, 0, tiled=False)  7.24 us
    select_n x2, other arithmetic, shards(): jnp.where((orient == option)[None, None, :], gathered[:, turn_nodes[optio...  6.24 us
    all_to_all x1, waiting for transfers between devices, combine_sums(): lax.all_to_all(spread, ('shot', 'mesh'), 0, 0, tiled=False)  6.1 us
    dot_general x2, matrix products, surface_term(): mixing = jnp.einsum('dpfg,dfnxe->pgnxe', coupling, weighted, precision=HIGH)  5.3 us
    ppermute x2, waiting for transfers between devices, halving_sum(): lax.ppermute(jnp.where(upper, low, high), axis, [(i, i ^ bit) for i in ra...  4.85 us
  transfers between devices with their start and end apart: 7, of which 3 were waited for; matrix products, arithmetic and copies ran while one was open for 17% of the time, Pallas kernels for 0%

profile of v7, /device:TPU:0, one launch (start us, length us, event | category | flops | bytes accessed | tf_op | source)
XLA Modules:
  0.0 108.8 jit_solution(15899716992513097425)
XLA Ops:
  0.6 1.6 %constant_dynamic-slice_fusion = (f32[5,6,35,32]{3,2,1,0:T(8,128)S(1)}, f32[5,6,35,32]{3,2,1,0:T(8,128)S(1)}) fusion(f32[5,6,35,128]{3,2,1,0:T(8,128)} %param.55, s32[]{:T(128)S(6)} %select_n.110, f32[5,6,35,128]{3,2,1,0:T(8,128)} %param.54), kind=kLoop, calls=%fused_computation.293 | loop fusion | bytes 537604 | tf_op jit(solution)/shard_map/dynamic_slice | solution.py:249
  2.3 1.1 copy.312
  3.4 0.5 copy.311
  3.9 1.0 copy.460
  4.9 1.6 %multiply_reduce_fusion = f32[10,5]{1,0:T(8,128)S(1)} fusion(f32[5,6,35,32]{2,3,1,0:T(8,128)} %copy.312, f32[10,6,35,32]{2,3,1,0:T(8,128)S(1)} %copy.311), kind=kLoop, calls=%fused_computation.15 | loop fusion | flops 671950 | bytes 403400 | tf_op jit(solution)/shard_map/reduce_sum | solution.py:254
  6.6 0.6 gather_fusion.1
  7.7 0.4 fusion.45
  8.0 0.6 fusion.149
  8.7 5.5 %collective-permute-start = (f32[13,15,64]{2,1,0:T(8,128)S(1)}, f32[13,15,64]{2,1,0:T(8,128)}, u32[]{:S(2)}, u32[]{:S(2)}) collective-permute-start(f32[13,15,64]{2,1,0:T(8,128)S(1)} %get-tuple-element.47), channel_id=1, source_target_pairs={{0,1},{1,2},{2,3},{3,4},{4,5},{5,6},{6,7},{8,9},{9,10},{10,11},{11... | collective-permute-start | bytes 149768 | tf_op jit(solution)/shard_map/ppermute | solution.py:20
  14.2 1.5 %collective-permute-start.1 = (f32[13,15,64]{2,1,0:T(8,128)}, f32[13,15,64]{2,1,0:T(8,128)}, u32[]{:S(2)}, u32[]{:S(2)}) collective-permute-start(f32[13,15,64]{2,1,0:T(8,128)} %get-tuple-element.46), channel_id=1, source_target_pairs={{1,0},{2,1},{3,2},{4,3},{5,4},{6,5},{7,6},{9,8},{10,9},{11,10},{12... | collective-permute-start | bytes 149768 | tf_op jit(solution)/shard_map/ppermute | solution.py:21
  15.9 1.4 %fusion.27 = f32[13,15,512]{2,1,0:T(8,128)} fusion(f32[13,15,512]{2,1,0:T(8,128)S(1)} %reshape.325, pred[640,512]{1,0:T(32,128)(4,1)S(1)} %iota_compare_fusion), kind=kOutput, calls=%fused_computation.68 | convolution fusion | flops 613416960 | bytes 1087488 | tf_op jit(solution)/shard_map/fns,sj->fnj/dot_general | solution.py:264
  17.4 0.8 convolution_bitcast_fusion.3
  18.4 0.4 fusion.146
  18.7 0.8 convolution_bitcast_fusion.1
  19.9 0.8 convolution_bitcast_fusion
  21.1 0.6 copy-done.12
  21.7 2.3 %fusion.5 = f32[13,35,128]{2,0,1:T(8,128)} fusion(f32[3,13,35,128,1]{3,2,0,1,4:T(8,128)S(1)} %maximum_bitcast_fusion, f32[6,35,128]{2,0,1:T(8,128)S(1)} %copy.313, f32[3,6,13,13]{3,2,1,0:T(8,128)S(1)} %copy-done.12), kind=kOutput, calls=%fused_computation.27 | convolution fusion | flops 164178560 | bytes 1051528 | tf_op jit(solution)/shard_map/dpfg,dfae->pgae/dot_general | solution.py:132
  24.0 1.0 maximum_bitcast_fusion.2
  25.0 1.0 maximum_bitcast_fusion.3
  26.0 0.8 gather_fusion
  26.9 0.8 copy.399
  27.7 1.2 %convolution_add_fusion.3 = f32[13,15,512]{2,1,0:T(8,128)S(1)} fusion(f32[13,15,512]{2,1,0:T(8,128)S(1)} %copy-done.1, f32[13,15,64]{2,1,0:T(8,128)} %collective-permute-done, pred[640,512]{1,0:T(32,128)(4,1)S(1)} %iota_compare_fusion), kind=kOutput, calls=%fused_computation.45 | convolution fusion | flops 76776960 | bytes 908032 | tf_op jit(solution)/shard_map/fns,sj->fnj/dot_general | solution.py:265
  29.0 1.2 %convolution_add_fusion.2 = f32[13,15,512]{2,1,0:T(8,128)S(1)} fusion(f32[13,15,512]{2,1,0:T(8,128)S(1)} %convolution_add_fusion.3, f32[13,15,64]{2,1,0:T(8,128)} %collective-permute-done.1, pred[640,512]{1,0:T(32,128)(4,1)S(1)} %iota_compare_fusion), kind=kOutput, calls=%fused_computation.44 | convolution fusion | flops 76776960 | bytes 908032 | tf_op jit(solution)/shard_map/fns,sj->fnj/dot_general | solution.py:268
  30.5 1.4 %gather_fusion.7 = f32[15,13,512]{2,1,0:T(8,128)} fusion(f32[13,15,512]{2,0,1:T(8,128)S(1)} %copy.320, s32[1024]{0:T(1024)S(1)} %get-tuple-element.65), kind=kCustom, calls=%fused_computation.7 | custom fusion | bytes 798780 | tf_op jit(solution)/shard_map/gather | solution.py:274
  31.8 1.4 %gather_fusion.6 = f32[15,13,512]{2,1,0:T(8,128)} fusion(f32[13,15,512]{2,0,1:T(8,128)S(1)} %copy.320, s32[1024]{0:T(1024)S(1)} %get-tuple-element.66), kind=kCustom, calls=%fused_computation.6 | custom fusion | bytes 798780 | tf_op jit(solution)/shard_map/gather | solution.py:274
  33.2 1.4 %gather_fusion.5 = f32[15,13,512]{2,1,0:T(8,128)} fusion(f32[13,15,512]{2,0,1:T(8,128)S(1)} %copy.320, s32[1024]{0:T(1024)S(1)} %get-tuple-element.67), kind=kCustom, calls=%fused_computation.5 | custom fusion | bytes 798780 | tf_op jit(solution)/shard_map/gather | solution.py:274
  34.5 1.4 %gather_fusion.4 = f32[15,13,512]{2,1,0:T(8,128)} fusion(f32[13,15,512]{2,0,1:T(8,128)S(1)} %copy.320, s32[1024]{0:T(1024)S(1)} %get-tuple-element.68), kind=kCustom, calls=%fused_computation.4 | custom fusion | bytes 798780 | tf_op jit(solution)/shard_map/gather | solution.py:274
  35.9 1.4 %gather_fusion.3 = f32[15,13,512]{2,1,0:T(8,128)} fusion(f32[13,15,512]{2,0,1:T(8,128)S(1)} %copy.320, s32[1024]{0:T(1024)S(1)} %get-tuple-element.69), kind=kCustom, calls=%fused_computation.3 | custom fusion | bytes 798780 | tf_op jit(solution)/shard_map/gather | solution.py:274
  37.3 1.4 %gather_fusion.2 = f32[15,13,512]{2,1,0:T(8,128)} fusion(f32[13,15,512]{2,0,1:T(8,128)S(1)} %copy.320, s32[1024]{0:T(1024)S(1)} %get-tuple-element.70), kind=kCustom, calls=%fused_computation.2 | custom fusion | bytes 798780 | tf_op jit(solution)/shard_map/gather | solution.py:274
  38.7 3.1 %fusion.37 = f32[13,15,512]{2,1,0:T(8,128)S(1)} fusion(f32[13,15,512]{2,1,0:T(8,128)S(1)} %convolution_add_fusion.2, f32[15,13,512]{2,1,0:T(8,128)} %gather_fusion.7, f32[15,13,512]{2,1,0:T(8,128)} %gather_fusion.6, f32[15,13,512]{2,1,0:T(8,128)} %gather_fusion.5, f32[15,13,512]{2,1,0:T(8,128)} %gather_fusion.4, f32[15,13,512]{2,1,0:T(8,128)} %gather_fusion.3, ...), kind=kLoop, calls=%fused_computation.84 | loop fusion | flops 599040 | bytes 3197952 | tf_op jit(solution)/shard_map/jit(_where)/select_n | solution.py:273
  42.1 0.7 copy-done.13
  42.9 2.7 %fusion.1 = f32[13,15,4,128]{3,0,2,1:T(8,128)S(1)} fusion(f32[6,15,4,128]{3,0,2,1:T(8,128)S(1)} %bitcast.836, f32[13,15,4,128]{3,0,2,1:T(8,128)S(1)} %copy_subtract_fusion.1, f32[3,4,128]{2,0,1:T(4,128)S(1)} %copy.317, f32[3,6,13,13]{3,2,1,0:T(8,128)S(1)} %copy-done.13), kind=kOutput, calls=%fused_computation.19 | convolution fusion | flops 281748480 | bytes 1001352 | tf_op jit(solution)/shard_map/dpfg,dfnxe->pgnxe/dot_general | solution.py:144
  45.8 0.8 copy-done.6
  46.6 1.0 fusion.14
  47.6 0.6 gather_fusion.8
  48.3 0.9 copy.339
  49.2 1.2 %reshape.327 = f32[13,15,512]{2,1,0:T(8,128)S(1)} reshape(f32[13,15,4,128]{3,2,1,0:T(4,128)} %copy.339) | data formatting | bytes 798720 | tf_op jit(solution)/shard_map/reshape | solution.py:261
  50.4 0.6 fusion.26
  51.4 0.8 convolution_bitcast_fusion.2
  52.4 4.7 %collective-permute-start.2 = (f32[13,15,64]{2,1,0:T(8,128)S(1)}, f32[13,15,64]{2,1,0:T(8,128)S(1)}, u32[]{:S(2)}, u32[]{:S(2)}) collective-permute-start(f32[13,15,64]{2,1,0:T(8,128)S(1)} %get-tuple-element.45), channel_id=1, source_target_pairs={{0,1},{1,2},{2,3},{3,4},{4,5},{5,6},{6,7},{8,9},{9,10},{10,11},{11... | collective-permute-start | bytes 149768 | tf_op jit(solution)/shard_map/ppermute | solution.py:20
  57.1 1.3 %collective-permute-start.3 = (f32[13,15,64]{2,1,0:T(8,128)S(1)}, f32[13,15,64]{2,1,0:T(8,128)S(1)}, u32[]{:S(2)}, u32[]{:S(2)}) collective-permute-start(f32[13,15,64]{2,1,0:T(8,128)S(1)} %get-tuple-element.44), channel_id=1, source_target_pairs={{1,0},{2,1},{3,2},{4,3},{5,4},{6,5},{7,6},{9,8},{10,9},{11,10},{12... | collective-permute-start | bytes 149768 | tf_op jit(solution)/shard_map/ppermute | solution.py:21
  58.6 2.4 %fusion.3 = f32[6,35,128]{2,0,1:T(8,128)} fusion(f32[3,13,35,128,1]{3,2,0,1,4:T(8,128)S(1)} %copy-done.11, f32[13,35,128]{2,0,1:T(8,128)S(1)} %copy-done.3, f32[3,6,13,13]{3,2,1,0:T(8,128)S(1)} %copy-done.14), kind=kOutput, calls=%fused_computation.23 | convolution fusion | flops 164209920 | bytes 1051528 | tf_op jit(solution)/shard_map/dpfg,dgae->pfae/dot_general | solution.py:138
  61.1 0.8 copy-done.5
  61.9 2.3 %fusion.4 = f32[13,35,128]{2,0,1:T(8,128)} fusion(f32[3,13,35,128,1]{3,2,0,1,4:T(8,128)S(1)} %maximum_bitcast_fusion.1, f32[6,35,128]{2,0,1:T(8,128)S(1)} %copy-done.5, f32[3,6,13,13]{3,2,1,0:T(8,128)S(1)} %copy-done.14), kind=kOutput, calls=%fused_computation.25 | convolution fusion | flops 164178560 | bytes 1051528 | tf_op jit(solution)/shard_map/dpfg,dfae->pgae/dot_general | solution.py:132
  65.2 1.5 %gather_fusion.14 = f32[15,13,512]{2,1,0:T(8,128)} fusion(f32[13,15,512]{2,0,1:T(8,128)S(1)} %copy.340, s32[1024]{0:T(1024)} %copy-done.35), kind=kCustom, calls=%fused_computation.14 | custom fusion | bytes 798780 | tf_op jit(solution)/shard_map/gather | solution.py:274
  66.7 1.5 %gather_fusion.13 = f32[15,13,512]{2,1,0:T(8,128)} fusion(f32[13,15,512]{2,0,1:T(8,128)S(1)} %copy.340, s32[1024]{0:T(1024)} %copy-done.34), kind=kCustom, calls=%fused_computation.13 | custom fusion | bytes 798780 | tf_op jit(solution)/shard_map/gather | solution.py:274
  68.2 1.5 %gather_fusion.12 = f32[15,13,512]{2,1,0:T(8,128)} fusion(f32[13,15,512]{2,0,1:T(8,128)S(1)} %copy.340, s32[1024]{0:T(1024)} %copy-done.37), kind=kCustom, calls=%fused_computation.12 | custom fusion | bytes 798780 | tf_op jit(solution)/shard_map/gather | solution.py:274
  69.7 1.5 %gather_fusion.11 = f32[15,13,512]{2,1,0:T(8,128)} fusion(f32[13,15,512]{2,0,1:T(8,128)S(1)} %copy.340, s32[1024]{0:T(1024)} %copy-done.36), kind=kCustom, calls=%fused_computation.11 | custom fusion | bytes 798780 | tf_op jit(solution)/shard_map/gather | solution.py:274
  71.2 1.5 %gather_fusion.10 = f32[15,13,512]{2,1,0:T(8,128)} fusion(f32[13,15,512]{2,0,1:T(8,128)S(1)} %copy.340, s32[1024]{0:T(1024)} %copy-done.39), kind=kCustom, calls=%fused_computation.10 | custom fusion | bytes 798780 | tf_op jit(solution)/shard_map/gather | solution.py:274
  72.7 1.5 %gather_fusion.9 = f32[15,13,512]{2,1,0:T(8,128)} fusion(f32[13,15,512]{2,0,1:T(8,128)S(1)} %copy.340, s32[1024]{0:T(1024)} %copy-done.38), kind=kCustom, calls=%fused_computation.9 | custom fusion | bytes 798780 | tf_op jit(solution)/shard_map/gather | solution.py:274
  74.2 3.1 %fusion.32 = f32[13,15,512]{2,1,0:T(8,128)S(1)} fusion(f32[13,15,512]{2,1,0:T(8,128)S(1)} %convolution_add_fusion, f32[15,13,512]{2,1,0:T(8,128)} %gather_fusion.14, f32[15,13,512]{2,1,0:T(8,128)} %gather_fusion.13, f32[15,13,512]{2,1,0:T(8,128)} %gather_fusion.12, f32[15,13,512]{2,1,0:T(8,128)} %gather_fusion.11, f32[15,13,512]{2,1,0:T(8,128)} %gather_fusion.10, ...), kind=kLoop, calls=%fused_computation.78 | loop fusion | flops 599040 | bytes 3197952 | tf_op jit(solution)/shard_map/jit(_where)/select_n | solution.py:273
  77.6 0.7 copy-done.17
  78.3 2.6 %fusion = f32[13,15,4,128]{3,0,2,1:T(8,128)S(1)} fusion(f32[6,15,4,128]{3,0,2,1:T(8,128)S(1)} %bitcast.837, f32[13,15,4,128]{3,0,2,1:T(8,128)S(1)} %copy_subtract_fusion, f32[3,4,128]{2,0,1:T(4,128)S(1)} %copy-done.33, f32[3,6,13,13]{3,2,1,0:T(8,128)S(1)} %copy-done.14), kind=kOutput, calls=%fused_computation.17 | convolution fusion | flops 281748480 | bytes 1001352 | tf_op jit(solution)/shard_map/dpfg,dfnxe->pgnxe/dot_general | solution.py:144
  81.0 0.9 copy-done.7
  81.9 0.7 fusion.17
  83.0 1.8 %fusion.2 = f32[6,35,128]{2,0,1:T(8,128)S(1)} fusion(f32[3,13,35,128,1]{3,2,0,1,4:T(8,128)S(1)} %copy-done.10, f32[13,35,128]{2,0,1:T(8,128)S(1)} %copy.365, f32[3,6,13,13]{3,2,1,0:T(8,128)S(1)} %copy-done.14), kind=kOutput, calls=%fused_computation.21 | convolution fusion | flops 164209920 | bytes 1051528 | tf_op jit(solution)/shard_map/dpfg,dgae->pfae/dot_general | solution.py:138
  84.9 1.6 %collective-permute-start.4 = (f32[6,35,64]{2,0,1:T(8,128)S(1)}, f32[6,35,64]{2,0,1:T(8,128)S(1)}, u32[]{:S(2)}, u32[]{:S(2)}) collective-permute-start(f32[6,35,64]{2,0,1:T(8,128)S(1)} %slice_select_fusion.1), channel_id=1, source_target_pairs={{0,16},{8,24},{16,0},{24,8},{1,17},{9,25},{17,1},{25,9},{2,18},{10... | collective-permute-start | bytes 161288 | tf_op jit(solution)/shard_map/ppermute | solution.py:160
  86.5 3.6 %collective-permute-done.4 = f32[6,35,64]{2,0,1:T(8,128)S(1)} collective-permute-done((f32[6,35,64]{2,0,1:T(8,128)S(1)}, f32[6,35,64]{2,0,1:T(8,128)S(1)}, u32[]{:S(2)}, u32[]{:S(2)}) %collective-permute-start.4) | collective-permute-done | bytes 53792 | tf_op jit(solution)/shard_map/ppermute | solution.py:160
  90.5 1.3 %collective-permute-done.5 = f32[6,35,32]{2,0,1:T(8,128)S(1)} collective-permute-done((f32[6,35,32]{2,0,1:T(8,128)S(1)}, f32[6,35,32]{2,0,1:T(8,128)S(1)}, u32[]{:S(2)}, u32[]{:S(2)}) %collective-permute-start.5) | collective-permute-done | bytes 26912 | tf_op jit(solution)/shard_map/ppermute | solution.py:160
  92.3 0.6 broadcast_in_dim.162
  92.9 7.2 %all-to-all-start = ((f32[32,1,60]{2,1,0:T(1,128)}), f32[32,1,60]{2,1,0:T(1,128)S(1)}, u32[]{:S(2)}, u32[]{:S(2)}) async-start(f32[32,1,60]{2,1,0:T(1,128)} %broadcast_in_dim.162), calls=%async_computation | async-start | bytes 32768 | tf_op jit(solution)/shard_map/all_to_all | solution.py:288
  100.1 0.9 copy.369
  101.1 6.1 %all-to-all-done = f32[32,1,60]{2,1,0:T(1,128)S(1)} async-done(((f32[32,1,60]{2,1,0:T(1,128)}), f32[32,1,60]{2,1,0:T(1,128)S(1)}, u32[]{:S(2)}, u32[]{:S(2)}) %all-to-all-start) | async-done | bytes 7712 | tf_op jit(solution)/shard_map/all_to_all | solution.py:288
  108.1 0.8 copy.370
  (192 shorter events, 6.4 us)
Async XLA Ops:
  3.9 2.6 %copy-start.64 = (s32[60]{0:T(128)S(1)}, s32[60]{0:T(128)}, u32[]{:S(2)}) copy-start(s32[60]{0:T(128)} %constant.75) | copy-start | bytes 724
  6.6 1.0 copy-start.55
  7.3 8.4 %copy-start.54 = (s32[4,128]{1,0:T(4,128)S(1)}, s32[4,128]{1,0:T(4,128)}, u32[]{:S(2)}) copy-start(s32[4,128]{1,0:T(4,128)} %param.51) | copy-start | bytes 6148
  7.6 9.6 %copy-start.57 = (s32[4,128]{1,0:T(4,128)S(1)}, s32[4,128]{1,0:T(4,128)}, u32[]{:S(2)}) copy-start(s32[4,128]{1,0:T(4,128)} %param.52) | copy-start | bytes 6148
  7.6 9.6 %copy-start.58 = (f32[4,128]{1,0:T(4,128)S(1)}, f32[4,128]{1,0:T(4,128)}, u32[]{:S(2)}) copy-start(f32[4,128]{1,0:T(4,128)} %param.50) | copy-start | bytes 6148
  7.7 9.7 %copy-start.8 = (f32[3,35,35,1]{2,1,0,3:T(8,128)S(1)}, f32[3,35,35,1]{2,1,0,3:T(8,128)}, u32[]{:S(2)}) copy-start(f32[3,35,35,1]{2,1,0,3:T(8,128)} %constant.88) | copy-start | bytes 44104
  8.7 19.0 %collective-permute-start = (f32[13,15,64]{2,1,0:T(8,128)S(1)}, f32[13,15,64]{2,1,0:T(8,128)}, u32[]{:S(2)}, u32[]{:S(2)}) collective-permute-start(f32[13,15,64]{2,1,0:T(8,128)S(1)} %get-tuple-element.47), channel_id=1, source_target_pairs={{0,1},{1,2},{2,3},{3,4},{4,5},{5,6},{6,7},{8,9},{9,10},{10,11},{11... | collective-permute-start | bytes 149768 | tf_op jit(solution)/shard_map/ppermute | solution.py:20
  14.2 14.8 %collective-permute-start.1 = (f32[13,15,64]{2,1,0:T(8,128)}, f32[13,15,64]{2,1,0:T(8,128)}, u32[]{:S(2)}, u32[]{:S(2)}) collective-permute-start(f32[13,15,64]{2,1,0:T(8,128)} %get-tuple-element.46), channel_id=1, source_target_pairs={{1,0},{2,1},{3,2},{4,3},{5,4},{6,5},{7,6},{9,8},{10,9},{11,10},{12... | collective-permute-start | bytes 149768 | tf_op jit(solution)/shard_map/ppermute | solution.py:21
  15.7 2.5 %copy-start.53 = (f32[3,3,128]{2,1,0:T(4,128)S(1)}, f32[3,3,128]{2,1,0:T(4,128)}, u32[]{:S(2)}) copy-start(f32[3,3,128]{2,1,0:T(4,128)} %param.48) | copy-start | bytes 13828
  15.7 2.6 %copy-start = (f32[6,35,128]{2,1,0:T(8,128)S(1)}, f32[6,35,128]{2,1,0:T(8,128)}, u32[]{:S(2)}) copy-start(f32[6,35,128]{2,1,0:T(8,128)} %param.46) | copy-start | bytes 322564
  15.9 2.4 %copy-start.15 = (f32[1,2,13,35,128]{4,1,3,2,0:T(2,128)S(1)}, f32[1,2,13,35,128]{4,1,3,2,0:T(2,128)}, u32[]{:S(2)}) copy-start(f32[1,2,13,35,128]{4,1,3,2,0:T(2,128)} %param.45) | copy-start | bytes 1397764
  17.3 21.4 %copy-start.41 = (pred[512]{0:T(512)(128)(4,1)}, pred[512]{0:T(512)(128)(4,1)S(1)}, u32[]{:S(2)}) copy-start(pred[512]{0:T(512)(128)(4,1)S(1)} %get-tuple-element.57) | copy-start | bytes 1540
  17.3 21.3 %copy-start.43 = (pred[512]{0:T(512)(128)(4,1)}, pred[512]{0:T(512)(128)(4,1)S(1)}, u32[]{:S(2)}) copy-start(pred[512]{0:T(512)(128)(4,1)S(1)} %get-tuple-element.58) | copy-start | bytes 1540
  17.3 21.3 %copy-start.45 = (pred[512]{0:T(512)(128)(4,1)}, pred[512]{0:T(512)(128)(4,1)S(1)}, u32[]{:S(2)}) copy-start(pred[512]{0:T(512)(128)(4,1)S(1)} %get-tuple-element.59) | copy-start | bytes 1540
  17.3 21.3 %copy-start.47 = (pred[512]{0:T(512)(128)(4,1)}, pred[512]{0:T(512)(128)(4,1)S(1)}, u32[]{:S(2)}) copy-start(pred[512]{0:T(512)(128)(4,1)S(1)} %get-tuple-element.60) | copy-start | bytes 1540
  17.3 21.3 %copy-start.49 = (pred[512]{0:T(512)(128)(4,1)}, pred[512]{0:T(512)(128)(4,1)S(1)}, u32[]{:S(2)}) copy-start(pred[512]{0:T(512)(128)(4,1)S(1)} %get-tuple-element.61) | copy-start | bytes 1540
  17.3 21.3 %copy-start.51 = (pred[512]{0:T(512)(128)(4,1)}, pred[512]{0:T(512)(128)(4,1)S(1)}, u32[]{:S(2)}) copy-start(pred[512]{0:T(512)(128)(4,1)S(1)} %get-tuple-element.62) | copy-start | bytes 1540
  18.2 2.5 %copy-start.20 = (f32[128]{0:T(128)}, f32[128]{0:T(128)S(1)}, u32[]{:S(2)}) copy-start(f32[128]{0:T(128)S(1)} %get-tuple-element.51) | copy-start | bytes 1540
  18.3 2.5 %copy-start.22 = (f32[128]{0:T(128)}, f32[128]{0:T(128)S(1)}, u32[]{:S(2)}) copy-start(f32[128]{0:T(128)S(1)} %get-tuple-element.52) | copy-start | bytes 1540
  18.3 2.5 %copy-start.24 = (f32[128]{0:T(128)}, f32[128]{0:T(128)S(1)}, u32[]{:S(2)}) copy-start(f32[128]{0:T(128)S(1)} %get-tuple-element.53) | copy-start | bytes 1540
  18.3 2.5 %copy-start.26 = (f32[128]{0:T(128)}, f32[128]{0:T(128)S(1)}, u32[]{:S(2)}) copy-start(f32[128]{0:T(128)S(1)} %get-tuple-element.54) | copy-start | bytes 1540
  18.3 2.5 %copy-start.28 = (f32[128]{0:T(128)}, f32[128]{0:T(128)S(1)}, u32[]{:S(2)}) copy-start(f32[128]{0:T(128)S(1)} %get-tuple-element.55) | copy-start | bytes 1540
  18.3 2.5 %copy-start.30 = (f32[128]{0:T(128)}, f32[128]{0:T(128)S(1)}, u32[]{:S(2)}) copy-start(f32[128]{0:T(128)S(1)} %get-tuple-element.56) | copy-start | bytes 1540
  18.3 2.8 %copy-start.4 = (f32[6,35,128]{2,0,1:T(8,128)}, f32[6,35,128]{2,0,1:T(8,128)S(1)}, u32[]{:S(2)}) copy-start(f32[6,35,128]{2,0,1:T(8,128)S(1)} %copy.313) | copy-start | bytes 322564
  19.8 1.1 %copy-start.63 = (s32[15]{0:T(128)S(1)}, s32[15]{0:T(128)}, u32[]{:S(2)}) copy-start(s32[15]{0:T(128)} %constant.81) | copy-start | bytes 184
  19.9 1.1 %copy-start.61 = (s32[15]{0:T(128)S(1)}, s32[15]{0:T(128)}, u32[]{:S(2)}) copy-start(s32[15]{0:T(128)} %constant.80) | copy-start | bytes 184
  19.9 1.1 %copy-start.62 = (s32[15]{0:T(128)S(1)}, s32[15]{0:T(128)}, u32[]{:S(2)}) copy-start(s32[15]{0:T(128)} %constant.79) | copy-start | bytes 184
  21.0 9.5 %copy-start.35 = (s32[1024]{0:T(1024)}, s32[1024]{0:T(1024)S(1)}, u32[]{:S(2)}) copy-start(s32[1024]{0:T(1024)S(1)} %get-tuple-element.65) | copy-start | bytes 12292
  21.0 10.8 %copy-start.34 = (s32[1024]{0:T(1024)}, s32[1024]{0:T(1024)S(1)}, u32[]{:S(2)}) copy-start(s32[1024]{0:T(1024)S(1)} %get-tuple-element.66) | copy-start | bytes 12292
  21.0 12.2 %copy-start.37 = (s32[1024]{0:T(1024)}, s32[1024]{0:T(1024)S(1)}, u32[]{:S(2)}) copy-start(s32[1024]{0:T(1024)S(1)} %get-tuple-element.67) | copy-start | bytes 12292
  21.0 13.5 %copy-start.36 = (s32[1024]{0:T(1024)}, s32[1024]{0:T(1024)S(1)}, u32[]{:S(2)}) copy-start(s32[1024]{0:T(1024)S(1)} %get-tuple-element.68) | copy-start | bytes 12292
  24.0 2.0 %copy-start.59 = (s32[15]{0:T(128)S(1)}, s32[15]{0:T(128)}, u32[]{:S(2)}) copy-start(s32[15]{0:T(128)} %constant.78) | copy-start | bytes 184
  24.0 2.0 %copy-start.60 = (s32[15]{0:T(128)S(1)}, s32[15]{0:T(128)}, u32[]{:S(2)}) copy-start(s32[15]{0:T(128)} %constant.77) | copy-start | bytes 184
  26.0 1.7 %copy-start.40 = (f32[3,4,128]{2,1,0:T(4,128)S(1)}, f32[3,4,128]{2,1,0:T(4,128)}, u32[]{:S(2)}) copy-start(f32[3,4,128]{2,1,0:T(4,128)} %param.49) | copy-start | bytes 18436
  26.0 1.7 %copy-start.1 = (f32[13,15,512]{2,1,0:T(8,128)S(1)}, f32[13,15,512]{2,1,0:T(8,128)}, u32[]{:S(2)}) copy-start(f32[13,15,512]{2,1,0:T(8,128)} %fusion.27) | copy-start | bytes 1198084
  26.0 9.9 %copy-start.39 = (s32[1024]{0:T(1024)}, s32[1024]{0:T(1024)S(1)}, u32[]{:S(2)}) copy-start(s32[1024]{0:T(1024)S(1)} %get-tuple-element.69) | copy-start | bytes 12292
  26.0 11.3 %copy-start.38 = (s32[1024]{0:T(1024)}, s32[1024]{0:T(1024)S(1)}, u32[]{:S(2)}) copy-start(s32[1024]{0:T(1024)S(1)} %get-tuple-element.70) | copy-start | bytes 12292
  27.7 14.4 %copy-start.32 = (f32[3,4,128]{2,0,1:T(4,128)}, f32[3,4,128]{2,0,1:T(4,128)S(1)}, u32[]{:S(2)}) copy-start(f32[3,4,128]{2,0,1:T(4,128)S(1)} %copy.317) | copy-start | bytes 18436
  42.0 1.0 copy-start.16
  47.6 1.6 %copy-start.2 = (f32[13,35,128]{2,0,1:T(8,128)}, f32[13,35,128]{2,0,1:T(8,128)S(1)}, u32[]{:S(2)}) copy-start(f32[13,35,128]{2,0,1:T(8,128)S(1)} %copy.338) | copy-start | bytes 698884
  48.3 2.7 %copy-start.56 = (s32[128]{0:T(128)S(1)}, s32[128]{0:T(128)}, u32[]{:S(2)}) copy-start(s32[128]{0:T(128)} %param.53) | copy-start | bytes 1540
  49.2 2.2 %copy-start.9 = (f32[3,35,35,1]{2,1,0,3:T(8,128)S(1)}, f32[3,35,35,1]{2,1,0,3:T(8,128)}, u32[]{:S(2)}) copy-start(f32[3,35,35,1]{2,1,0,3:T(8,128)} %constant.88) | copy-start | bytes 44104
  51.0 7.4 %copy-start.21 = (f32[128]{0:T(128)S(1)}, f32[128]{0:T(128)}, u32[]{:S(2)}) copy-start(f32[128]{0:T(128)} %copy-done.20) | copy-start | bytes 1540
  51.0 7.4 %copy-start.23 = (f32[128]{0:T(128)S(1)}, f32[128]{0:T(128)}, u32[]{:S(2)}) copy-start(f32[128]{0:T(128)} %copy-done.22) | copy-start | bytes 1540
  51.0 7.4 %copy-start.25 = (f32[128]{0:T(128)S(1)}, f32[128]{0:T(128)}, u32[]{:S(2)}) copy-start(f32[128]{0:T(128)} %copy-done.24) | copy-start | bytes 1540
  51.0 7.4 %copy-start.27 = (f32[128]{0:T(128)S(1)}, f32[128]{0:T(128)}, u32[]{:S(2)}) copy-start(f32[128]{0:T(128)} %copy-done.26) | copy-start | bytes 1540
  51.0 7.4 %copy-start.29 = (f32[128]{0:T(128)S(1)}, f32[128]{0:T(128)}, u32[]{:S(2)}) copy-start(f32[128]{0:T(128)} %copy-done.28) | copy-start | bytes 1540
  51.0 7.4 %copy-start.31 = (f32[128]{0:T(128)S(1)}, f32[128]{0:T(128)}, u32[]{:S(2)}) copy-start(f32[128]{0:T(128)} %copy-done.30) | copy-start | bytes 1540
  52.2 6.3 %copy-start.3 = (f32[13,35,128]{2,0,1:T(8,128)S(1)}, f32[13,35,128]{2,0,1:T(8,128)}, u32[]{:S(2)}) copy-start(f32[13,35,128]{2,0,1:T(8,128)} %copy-done.2) | copy-start | bytes 698884
  52.2 6.3 %copy-start.11 = (f32[3,13,35,128,1]{3,2,0,1,4:T(8,128)S(1)}, f32[3,13,35,128,1]{3,2,0,1,4:T(8,128)}, u32[]{:S(2)}) copy-start(f32[3,13,35,128,1]{3,2,0,1,4:T(8,128)} %maximum_bitcast_fusion.2) | copy-start | bytes 2096644
  52.3 6.3 %copy-start.14 = (f32[3,6,13,13]{3,2,1,0:T(8,128)S(1)}, f32[3,6,13,13]{3,2,1,0:T(8,128)}, u32[]{:S(2)}) copy-start(f32[3,6,13,13]{3,2,1,0:T(8,128)} %param.47) | copy-start | bytes 36508
  52.4 11.9 %collective-permute-start.2 = (f32[13,15,64]{2,1,0:T(8,128)S(1)}, f32[13,15,64]{2,1,0:T(8,128)S(1)}, u32[]{:S(2)}, u32[]{:S(2)}) collective-permute-start(f32[13,15,64]{2,1,0:T(8,128)S(1)} %get-tuple-element.45), channel_id=1, source_target_pairs={{0,1},{1,2},{2,3},{3,4},{4,5},{5,6},{6,7},{8,9},{9,10},{10,11},{11... | collective-permute-start | bytes 149768 | tf_op jit(solution)/shard_map/ppermute | solution.py:20
  57.1 7.6 %collective-permute-start.3 = (f32[13,15,64]{2,1,0:T(8,128)S(1)}, f32[13,15,64]{2,1,0:T(8,128)S(1)}, u32[]{:S(2)}, u32[]{:S(2)}) collective-permute-start(f32[13,15,64]{2,1,0:T(8,128)S(1)} %get-tuple-element.44), channel_id=1, source_target_pairs={{1,0},{2,1},{3,2},{4,3},{5,4},{6,5},{7,6},{9,8},{10,9},{11,10},{12... | collective-permute-start | bytes 149768 | tf_op jit(solution)/shard_map/ppermute | solution.py:21
  69.7 4.5 %copy-start.42 = (pred[512]{0:T(512)(128)(4,1)S(1)}, pred[512]{0:T(512)(128)(4,1)}, u32[]{:S(2)}) copy-start(pred[512]{0:T(512)(128)(4,1)} %copy-done.41) | copy-start | bytes 1540
  69.7 4.5 %copy-start.44 = (pred[512]{0:T(512)(128)(4,1)S(1)}, pred[512]{0:T(512)(128)(4,1)}, u32[]{:S(2)}) copy-start(pred[512]{0:T(512)(128)(4,1)} %copy-done.43) | copy-start | bytes 1540
  69.7 4.5 %copy-start.46 = (pred[512]{0:T(512)(128)(4,1)S(1)}, pred[512]{0:T(512)(128)(4,1)}, u32[]{:S(2)}) copy-start(pred[512]{0:T(512)(128)(4,1)} %copy-done.45) | copy-start | bytes 1540
  69.7 4.5 %copy-start.48 = (pred[512]{0:T(512)(128)(4,1)S(1)}, pred[512]{0:T(512)(128)(4,1)}, u32[]{:S(2)}) copy-start(pred[512]{0:T(512)(128)(4,1)} %copy-done.47) | copy-start | bytes 1540
  69.7 4.5 %copy-start.50 = (pred[512]{0:T(512)(128)(4,1)S(1)}, pred[512]{0:T(512)(128)(4,1)}, u32[]{:S(2)}) copy-start(pred[512]{0:T(512)(128)(4,1)} %copy-done.49) | copy-start | bytes 1540
  69.7 4.5 %copy-start.52 = (pred[512]{0:T(512)(128)(4,1)S(1)}, pred[512]{0:T(512)(128)(4,1)}, u32[]{:S(2)}) copy-start(pred[512]{0:T(512)(128)(4,1)} %copy-done.51) | copy-start | bytes 1540
  81.9 1.1 %copy-start.10 = (f32[3,13,35,128,1]{3,2,0,1,4:T(8,128)S(1)}, f32[3,13,35,128,1]{3,2,0,1,4:T(8,128)}, u32[]{:S(2)}) copy-start(f32[3,13,35,128,1]{3,2,0,1,4:T(8,128)} %maximum_bitcast_fusion.3) | copy-start | bytes 2096644
  82.6 2.2 %copy-start.18 = (f32[6,35,128]{2,0,1:T(8,128)S(1)}, f32[6,35,128]{2,0,1:T(8,128)}, u32[]{:S(2)}) copy-start(f32[6,35,128]{2,0,1:T(8,128)} %fusion.3) | copy-start | bytes 322564
  84.9 5.2 %collective-permute-start.4 = (f32[6,35,64]{2,0,1:T(8,128)S(1)}, f32[6,35,64]{2,0,1:T(8,128)S(1)}, u32[]{:S(2)}, u32[]{:S(2)}) collective-permute-start(f32[6,35,64]{2,0,1:T(8,128)S(1)} %slice_select_fusion.1), channel_id=1, source_target_pairs={{0,16},{8,24},{16,0},{24,8},{1,17},{9,25},{17,1},{25,9},{2,18},{10... | collective-permute-start | bytes 161288 | tf_op jit(solution)/shard_map/ppermute | solution.py:160
  90.3 1.4 %collective-permute-start.5 = (f32[6,35,32]{2,0,1:T(8,128)S(1)}, f32[6,35,32]{2,0,1:T(8,128)S(1)}, u32[]{:S(2)}, u32[]{:S(2)}) collective-permute-start(f32[6,35,32]{2,0,1:T(8,128)S(1)} %slice_select_fusion), channel_id=1, source_target_pairs={{0,8},{8,0},{16,24},{24,16},{1,9},{9,1},{17,25},{25,17},{2,10},{10... | collective-permute-start | bytes 80648 | tf_op jit(solution)/shard_map/ppermute | solution.py:160
  92.9 14.3 %all-to-all-start = ((f32[32,1,60]{2,1,0:T(1,128)}), f32[32,1,60]{2,1,0:T(1,128)S(1)}, u32[]{:S(2)}, u32[]{:S(2)}) async-start(f32[32,1,60]{2,1,0:T(1,128)} %broadcast_in_dim.162), calls=%async_computation | async-start | bytes 32768 | tf_op jit(solution)/shard_map/all_to_all | solution.py:288
  (8 other events, 7.5 us)

commit v8 on v7

--- a/solution.py
+++ b/solution.py
@@ -238,6 +238,11 @@
     local_pick = slot_pick[:face_total]
     below_pick = slot_pick[face_total : face_total + border]
     above_pick = slot_pick[face_total + border :]
+    node_turn = jnp.zeros((face_width, face_width, face_total), jnp.float32)
+    for option in range(turn_nodes.shape[0]):
+        node_turn = node_turn + (orient == option).astype(jnp.float32)[None, None, :] * jnp.asarray(
+            np.eye(face_width, dtype=np.float32)[turn_nodes[option]].T
+        )[:, :, None]
     send_pick = (
         send_faces[None, :] == jnp.arange(face_total, dtype=jnp.int32)[:, None]
     ).astype(jnp.float32)
@@ -268,11 +273,7 @@
         gathered = gathered + jnp.einsum(
             "fns,sj->fnj", extended[:, :, 3 * border :], above_pick, precision=HIGH
         )
-        turned = gathered
-        for option in range(turn_nodes.shape[0]):
-            turned = jnp.where(
-                (orient == option)[None, None, :], gathered[:, turn_nodes[option], :], turned
-            )
+        turned = jnp.sum(gathered[:, :, None, :] * node_turn[None], axis=1)
         jump_trace = turned.reshape(fields, face_width, 4, elements) - inner_trace
         change = volume_term(adjoint, material, coupling, metric, derivs) + surface_term(
             jump_trace, face_material, face_normals, face_scale, coupling, lift_tables

time: 110 us -> 88.9 us (0.81)
  local copies, waits for them, and re-layouts: 36.5 us -> 20.6 us
  other arithmetic: 12.7 us -> 8.98 us
    gather x12 -> x0, local copies, waits for them, and re-layouts: 17.1 us -> none  [shards(): gathered[:, turn_nodes[option], :]]
    select_n x2 -> x0, other arithmetic: 6.24 us -> none  [shards(): jnp.where((orient == option)[None, None, :], gathered[:, turn_nodes[optio...]
    gather x2, local copies, waits for them, and re-layouts: 1.66 us -> 3.23 us  [shards(): face_material = material[:, face_nodes.T, :]]
    reduce_sum x0 -> x2, other arithmetic: none -> 1.23 us  [shards(): turned = jnp.sum(gathered[:, :, None, :] * node_turn[None], axis=1)]
    unnamed x135 -> x105, local copies, waits for them, and re-layouts: 7.92 us -> 7.23 us
  transfers between devices with their start and end apart: 7 -> 7, of which waited for: 3 -> 3; matrix products, arithmetic and copies ran while one was open for 17% -> 22% of each run, Pallas kernels for 0% -> 0%
where the time goes in v8:
time: 88.9 us; the launch traced here: 88.4 us
  matrix products  24.2 us (27%)
  starting transfers between devices  21.9 us (25%)
  local copies, waits for them, and re-layouts  20.6 us (23%)
  waiting for transfers between devices  11 us (12%)
  other arithmetic  8.98 us (10%)
  between operations  1.77 us (2%)
    ppermute x2, starting transfers between devices, padded(): before = lax.ppermute(last, axis, up)  10.2 us
    all_to_all x1, starting transfers between devices, combine_sums(): lax.all_to_all(spread, ('shot', 'mesh'), 0, 0, tiled=False)  7.25 us
    unnamed x105, local copies, waits for them, and re-layouts  7.23 us
    all_to_all x1, waiting for transfers between devices, combine_sums(): lax.all_to_all(spread, ('shot', 'mesh'), 0, 0, tiled=False)  6.1 us
    dot_general x2, matrix products, surface_term(): mixing = jnp.einsum('dpfg,dfnxe->pgnxe', coupling, weighted, precision=HIGH)  5.35 us
    ppermute x2, waiting for transfers between devices, halving_sum(): lax.ppermute(jnp.where(upper, low, high), axis, [(i, i ^ bit) for i in ra...  4.84 us
    dot_general x2, matrix products, volume_term(): mixing = jnp.einsum('dpfg,dfae->pgae', coupling, spatial, precision=HIGH)  4.68 us
    dot_general x2, matrix products, kernel_term(): mixing = jnp.einsum('dpfg,dgae->pfae', coupling, spatial, precision=HIGH)  4.18 us
  transfers between devices with their start and end apart: 7, of which 3 were waited for; matrix products, arithmetic and copies ran while one was open for 22% of the time, Pallas kernels for 0%

profile of v8, /device:TPU:0, one launch (start us, length us, event | category | flops | bytes accessed | tf_op | source)
XLA Modules:
  0.0 88.4 jit_solution(9005400013312478026)
XLA Ops:
  0.6 1.6 %constant_dynamic-slice_fusion = (f32[5,6,35,32]{3,2,1,0:T(8,128)S(1)}, f32[5,6,35,32]{3,2,1,0:T(8,128)S(1)}) fusion(f32[5,6,35,128]{3,2,1,0:T(8,128)} %param.37, s32[]{:T(128)S(6)} %select_n.37, f32[5,6,35,128]{3,2,1,0:T(8,128)} %param.36), kind=kLoop, calls=%fused_computation.266 | loop fusion | bytes 537604 | tf_op jit(solution)/shard_map/dynamic_slice | solution.py:254
  2.3 1.1 %copy.196 = f32[5,6,35,32]{2,3,1,0:T(8,128)} copy(f32[5,6,35,32]{3,2,1,0:T(8,128)S(1)} %get-tuple-element.8) | data formatting | bytes 268800 | tf_op jit(solution)/shard_map/dynamic_slice | solution.py:254
  3.5 0.5 copy.195
  4.0 1.0 %copy.308 = f32[1,13,35,128]{3,2,0,1:T(8,128)S(1)} copy(f32[1,13,35,128]{3,0,2,1:T(1,128)} %param.26) | data formatting | bytes 465920
  4.9 1.6 %multiply_reduce_fusion.2 = f32[10,5]{1,0:T(8,128)S(1)} fusion(f32[5,6,35,32]{2,3,1,0:T(8,128)} %copy.196, f32[10,6,35,32]{2,3,1,0:T(8,128)S(1)} %copy.195), kind=kLoop, calls=%fused_computation.5 | loop fusion | flops 671950 | bytes 403400 | tf_op jit(solution)/shard_map/reduce_sum | solution.py:259
  6.7 0.6 gather_fusion.1
  7.3 0.2 copy.203
  7.5 0.2 reshape.362
  7.7 0.4 fusion.35
  8.0 0.7 fusion.139
  8.8 5.5 %collective-permute-start = (f32[13,15,64]{2,1,0:T(8,128)}, f32[13,15,64]{2,1,0:T(8,128)}, u32[]{:S(2)}, u32[]{:S(2)}) collective-permute-start(f32[13,15,64]{2,1,0:T(8,128)} %get-tuple-element.47), channel_id=1, source_target_pairs={{0,1},{1,2},{2,3},{3,4},{4,5},{5,6},{6,7},{8,9},{9,10},{10,11},{11... | collective-permute-start | bytes 149768 | tf_op jit(solution)/shard_map/ppermute | solution.py:20
  14.3 1.5 %collective-permute-start.1 = (f32[13,15,64]{2,1,0:T(8,128)}, f32[13,15,64]{2,1,0:T(8,128)}, u32[]{:S(2)}, u32[]{:S(2)}) collective-permute-start(f32[13,15,64]{2,1,0:T(8,128)} %get-tuple-element.46), channel_id=1, source_target_pairs={{1,0},{2,1},{3,2},{4,3},{5,4},{6,5},{7,6},{9,8},{10,9},{11,10},{12... | collective-permute-start | bytes 149768 | tf_op jit(solution)/shard_map/ppermute | solution.py:21
  15.8 0.2 iota_compare_fusion
  16.1 0.6 fusion.27
  16.7 0.8 convolution_bitcast_fusion.3
  17.7 0.4 fusion.136
  18.1 0.8 convolution_bitcast_fusion.1
  19.2 0.8 convolution_bitcast_fusion
  20.3 0.7 copy-done.11
  21.0 2.4 %fusion.5 = f32[13,35,128]{2,0,1:T(8,128)} fusion(f32[3,13,35,128,1]{3,2,0,1,4:T(8,128)S(1)} %maximum_bitcast_fusion, f32[6,35,128]{2,0,1:T(8,128)S(1)} %copy.197, f32[3,6,13,13]{3,2,1,0:T(8,128)S(1)} %copy-done.11), kind=kOutput, calls=%fused_computation.17 | convolution fusion | flops 164178560 | bytes 1051528 | tf_op jit(solution)/shard_map/dpfg,dfae->pgae/dot_general | solution.py:132
  23.4 1.0 %maximum_bitcast_fusion.2 = f32[3,13,35,128,1]{3,2,0,1,4:T(8,128)} fusion(f32[1,13,35,128]{3,2,0,1:T(8,128)S(1)} %get-tuple-element.33, f32[1,13,35,128]{3,2,0,1:T(8,128)S(1)} %get-tuple-element.32, f32[1,13,35,128]{3,2,0,1:T(8,128)S(1)} %get-tuple-element.31), kind=kLoop, calls=%fused_computation.51 | loop fusion | flops 349440 | bytes 1397760 | tf_op jit(solution)/shard_map/stack | solution.py:127
  24.4 0.3 multiply_add_fusion
  24.6 1.0 %maximum_bitcast_fusion.3 = f32[3,13,35,128,1]{3,2,0,1,4:T(8,128)} fusion(f32[1,13,35,128]{3,2,0,1:T(8,128)S(1)} %get-tuple-element.30, f32[1,13,35,128]{3,2,0,1:T(8,128)S(1)} %get-tuple-element.29, f32[1,13,35,128]{3,2,0,1:T(8,128)S(1)} %get-tuple-element.28), kind=kLoop, calls=%fused_computation.52 | loop fusion | flops 349440 | bytes 1397760 | tf_op jit(solution)/shard_map/stack | solution.py:127
  25.6 1.5 %gather_fusion = f32[60,6,128]{2,0,1:T(8,128)} fusion(f32[6,35,128]{2,1,0:T(8,128)S(1)} %copy-done, s32[1024]{0:T(1024)S(1)} %pad_clamp_fusion), kind=kCustom, calls=%fused_computation | custom fusion | bytes 368880 | tf_op jit(solution)/shard_map/gather | solution.py:231
  27.1 1.7 %copy.259 = f32[60,6,128]{2,1,0:T(8,128)} copy(f32[60,6,128]{2,0,1:T(8,128)} %gather_fusion) | data formatting | bytes 368640 | tf_op jit(solution)/shard_map/gather | solution.py:231
  28.9 1.2 %convolution_add_fusion.3 = f32[13,15,512]{2,1,0:T(8,128)S(1)} fusion(f32[13,15,512]{2,1,0:T(8,128)S(1)} %fusion.27, f32[13,15,64]{2,1,0:T(8,128)} %collective-permute-done, pred[640,512]{1,0:T(32,128)(4,1)S(1)} %iota_compare_fusion), kind=kOutput, calls=%fused_computation.35 | convolution fusion | flops 76776960 | bytes 908032 | tf_op jit(solution)/shard_map/fns,sj->fnj/dot_general | solution.py:270
  30.1 1.2 %convolution_add_fusion.2 = f32[13,15,512]{2,1,0:T(8,128)S(1)} fusion(f32[13,15,512]{2,1,0:T(8,128)S(1)} %convolution_add_fusion.3, f32[13,15,64]{2,1,0:T(8,128)} %collective-permute-done.1, pred[640,512]{1,0:T(32,128)(4,1)S(1)} %iota_compare_fusion), kind=kOutput, calls=%fused_computation.34 | convolution fusion | flops 76776960 | bytes 908032 | tf_op jit(solution)/shard_map/fns,sj->fnj/dot_general | solution.py:273
  31.4 0.6 multiply_reduce_fusion.1
  32.0 0.9 %reshape.363 = f32[13,15,4,128]{3,2,1,0:T(4,128)} reshape(f32[13,15,512]{2,1,0:T(8,128)S(1)} %multiply_reduce_fusion.1) | data formatting | bytes 798720 | tf_op jit(solution)/shard_map/reshape | solution.py:277
  32.9 1.1 %copy_subtract_fusion.1 = f32[13,15,4,128]{3,0,2,1:T(8,128)S(1)} fusion(f32[13,15,4,128]{3,0,2,1:T(8,128)S(1)} %bitcast.776, f32[13,15,4,128]{3,2,1,0:T(4,128)} %reshape.363), kind=kLoop, calls=%fused_computation.60 | loop fusion | flops 99840 | bytes 1198080 | tf_op jit(solution)/shard_map/sub | solution.py:277
  34.1 2.7 %fusion.1 = f32[13,15,4,128]{3,0,2,1:T(8,128)S(1)} fusion(f32[6,15,4,128]{3,0,2,1:T(8,128)S(1)} %bitcast.792, f32[13,15,4,128]{3,0,2,1:T(8,128)S(1)} %copy_subtract_fusion.1, f32[3,4,128]{2,0,1:T(4,128)S(1)} %copy.201, f32[3,6,13,13]{3,2,1,0:T(8,128)S(1)} %copy-done.12), kind=kOutput, calls=%fused_computation.9 | convolution fusion | flops 281748480 | bytes 1001352 | tf_op jit(solution)/shard_map/dpfg,dfnxe->pgnxe/dot_general | solution.py:144
  36.8 0.9 copy-done.5
  37.7 0.7 fusion.14
  38.5 0.6 gather_fusion.2
  39.2 0.9 %copy.211 = f32[13,15,4,128]{3,2,1,0:T(4,128)} copy(f32[13,15,4,128]{3,0,2,1:T(8,128)S(1)} %bitcast.777) | data formatting | bytes 798720 | tf_op jit(solution)/shard_map/gather | solution.py:265
  40.1 1.2 %reshape.364 = f32[13,15,512]{2,1,0:T(8,128)S(1)} reshape(f32[13,15,4,128]{3,2,1,0:T(4,128)} %copy.211) | data formatting | bytes 798720 | tf_op jit(solution)/shard_map/reshape | solution.py:266
  41.3 0.8 fusion.26
  42.2 0.4 fusion.33
  42.6 0.8 convolution_bitcast_fusion.2
  43.5 4.7 %collective-permute-start.2 = (f32[13,15,64]{2,1,0:T(8,128)S(1)}, f32[13,15,64]{2,1,0:T(8,128)S(1)}, u32[]{:S(2)}, u32[]{:S(2)}) collective-permute-start(f32[13,15,64]{2,1,0:T(8,128)S(1)} %get-tuple-element.45), channel_id=1, source_target_pairs={{0,1},{1,2},{2,3},{3,4},{4,5},{5,6},{6,7},{8,9},{9,10},{10,11},{11... | collective-permute-start | bytes 149768 | tf_op jit(solution)/shard_map/ppermute | solution.py:20
  48.2 1.3 %collective-permute-start.3 = (f32[13,15,64]{2,1,0:T(8,128)S(1)}, f32[13,15,64]{2,1,0:T(8,128)S(1)}, u32[]{:S(2)}, u32[]{:S(2)}) collective-permute-start(f32[13,15,64]{2,1,0:T(8,128)S(1)} %get-tuple-element.44), channel_id=1, source_target_pairs={{1,0},{2,1},{3,2},{4,3},{5,4},{6,5},{7,6},{9,8},{10,9},{11,10},{12... | collective-permute-start | bytes 149768 | tf_op jit(solution)/shard_map/ppermute | solution.py:21
  49.8 2.4 %fusion.3 = f32[6,35,128]{2,0,1:T(8,128)} fusion(f32[3,13,35,128,1]{3,2,0,1,4:T(8,128)S(1)} %copy-done.10, f32[13,35,128]{2,0,1:T(8,128)S(1)} %copy-done.2, f32[3,6,13,13]{3,2,1,0:T(8,128)S(1)} %copy-done.13), kind=kOutput, calls=%fused_computation.13 | convolution fusion | flops 164209920 | bytes 1051528 | tf_op jit(solution)/shard_map/dpfg,dgae->pfae/dot_general | solution.py:138
  52.3 0.8 copy-done.4
  53.1 2.3 %fusion.4 = f32[13,35,128]{2,0,1:T(8,128)} fusion(f32[3,13,35,128,1]{3,2,0,1,4:T(8,128)S(1)} %maximum_bitcast_fusion.1, f32[6,35,128]{2,0,1:T(8,128)S(1)} %copy-done.4, f32[3,6,13,13]{3,2,1,0:T(8,128)S(1)} %copy-done.13), kind=kOutput, calls=%fused_computation.15 | convolution fusion | flops 164178560 | bytes 1051528 | tf_op jit(solution)/shard_map/dpfg,dfae->pgae/dot_general | solution.py:132
  55.4 0.3 convolution_add_fusion.1
  55.8 0.3 convolution_add_fusion
  56.1 0.6 multiply_reduce_fusion
  57.0 0.6 copy-done.14
  57.8 2.7 %fusion = f32[13,15,4,128]{3,0,2,1:T(8,128)S(1)} fusion(f32[6,15,4,128]{3,0,2,1:T(8,128)S(1)} %bitcast.793, f32[13,15,4,128]{3,0,2,1:T(8,128)S(1)} %copy_subtract_fusion, f32[3,4,128]{2,0,1:T(4,128)S(1)} %copy-done.41, f32[3,6,13,13]{3,2,1,0:T(8,128)S(1)} %copy-done.14), kind=kOutput, calls=%fused_computation.7 | convolution fusion | flops 281748480 | bytes 1001352 | tf_op jit(solution)/shard_map/dpfg,dfnxe->pgnxe/dot_general | solution.py:144
  60.6 0.9 copy-done.6
  61.4 0.7 fusion.17
  62.2 0.3 copy-done.9
  62.5 1.8 %fusion.2 = f32[6,35,128]{2,0,1:T(8,128)S(1)} fusion(f32[3,13,35,128,1]{3,2,0,1,4:T(8,128)S(1)} %copy-done.9, f32[13,35,128]{2,0,1:T(8,128)S(1)} %copy.225, f32[3,6,13,13]{3,2,1,0:T(8,128)S(1)} %copy-done.14), kind=kOutput, calls=%fused_computation.11 | convolution fusion | flops 164209920 | bytes 1051528 | tf_op jit(solution)/shard_map/dpfg,dgae->pfae/dot_general | solution.py:138
  64.5 1.6 %collective-permute-start.4 = (f32[6,35,64]{2,0,1:T(8,128)S(1)}, f32[6,35,64]{2,0,1:T(8,128)S(1)}, u32[]{:S(2)}, u32[]{:S(2)}) collective-permute-start(f32[6,35,64]{2,0,1:T(8,128)S(1)} %slice_select_fusion.1), channel_id=1, source_target_pairs={{0,16},{8,24},{16,0},{24,8},{1,17},{9,25},{17,1},{25,9},{2,18},{10... | collective-permute-start | bytes 161288 | tf_op jit(solution)/shard_map/ppermute | solution.py:160
  66.1 3.6 %collective-permute-done.4 = f32[6,35,64]{2,0,1:T(8,128)S(1)} collective-permute-done((f32[6,35,64]{2,0,1:T(8,128)S(1)}, f32[6,35,64]{2,0,1:T(8,128)S(1)}, u32[]{:S(2)}, u32[]{:S(2)}) %collective-permute-start.4) | collective-permute-done | bytes 53792 | tf_op jit(solution)/shard_map/ppermute | solution.py:160
  70.0 1.3 %collective-permute-done.5 = f32[6,35,32]{2,0,1:T(8,128)S(1)} collective-permute-done((f32[6,35,32]{2,0,1:T(8,128)S(1)}, f32[6,35,32]{2,0,1:T(8,128)S(1)}, u32[]{:S(2)}, u32[]{:S(2)}) %collective-permute-start.5) | collective-permute-done | bytes 26912 | tf_op jit(solution)/shard_map/ppermute | solution.py:160
  71.4 0.3 fusion.11
  71.8 0.6 broadcast_in_dim.16
  72.4 7.2 %all-to-all-start = ((f32[32,1,60]{2,1,0:T(1,128)}), f32[32,1,60]{2,1,0:T(1,128)S(1)}, u32[]{:S(2)}, u32[]{:S(2)}) async-start(f32[32,1,60]{2,1,0:T(1,128)} %broadcast_in_dim.16), calls=%async_computation | async-start | bytes 32768 | tf_op jit(solution)/shard_map/all_to_all | solution.py:289
  79.7 0.9 %copy.229 = f32[1,13,35,128]{3,0,2,1:T(1,128)} copy(f32[1,13,35,128]{3,2,1,0:T(8,128)S(1)} %bitcast.779) | data formatting | bytes 465920
  80.6 6.1 %all-to-all-done = f32[32,1,60]{2,1,0:T(1,128)S(1)} async-done(((f32[32,1,60]{2,1,0:T(1,128)}), f32[32,1,60]{2,1,0:T(1,128)S(1)}, u32[]{:S(2)}, u32[]{:S(2)}) %all-to-all-start) | async-done | bytes 7712 | tf_op jit(solution)/shard_map/all_to_all | solution.py:289
  87.2 0.2 slice_reduce_fusion
  87.3 0.2 fusion.10
  87.6 0.8 copy.230
  (145 shorter events, 3.0 us)
Async XLA Ops:
  3.9 2.6 %copy-start.49 = (s32[60]{0:T(128)S(1)}, s32[60]{0:T(128)}, u32[]{:S(2)}) copy-start(s32[60]{0:T(128)} %constant.67) | copy-start | bytes 724
  6.6 1.0 %copy-start.45 = (s32[128]{0:T(128)S(1)}, s32[128]{0:T(128)}, u32[]{:S(2)}) copy-start(s32[128]{0:T(128)} %param.35) | copy-start | bytes 1540
  7.3 8.5 %copy-start.47 = (s32[4,128]{1,0:T(4,128)S(1)}, s32[4,128]{1,0:T(4,128)}, u32[]{:S(2)}) copy-start(s32[4,128]{1,0:T(4,128)} %param.34) | copy-start | bytes 6148
  7.3 8.5 %copy-start.44 = (s32[4,128]{1,0:T(4,128)S(1)}, s32[4,128]{1,0:T(4,128)}, u32[]{:S(2)}) copy-start(s32[4,128]{1,0:T(4,128)} %param.33) | copy-start | bytes 6148
  7.7 9.0 %copy-start.48 = (f32[4,128]{1,0:T(4,128)S(1)}, f32[4,128]{1,0:T(4,128)}, u32[]{:S(2)}) copy-start(f32[4,128]{1,0:T(4,128)} %param.32) | copy-start | bytes 6148
  7.7 9.0 %copy-start.7 = (f32[3,35,35,1]{2,1,0,3:T(8,128)S(1)}, f32[3,35,35,1]{2,1,0,3:T(8,128)}, u32[]{:S(2)}) copy-start(f32[3,35,35,1]{2,1,0,3:T(8,128)} %constant.70) | copy-start | bytes 44104
  8.8 20.1 %collective-permute-start = (f32[13,15,64]{2,1,0:T(8,128)}, f32[13,15,64]{2,1,0:T(8,128)}, u32[]{:S(2)}, u32[]{:S(2)}) collective-permute-start(f32[13,15,64]{2,1,0:T(8,128)} %get-tuple-element.47), channel_id=1, source_target_pairs={{0,1},{1,2},{2,3},{3,4},{4,5},{5,6},{6,7},{8,9},{9,10},{10,11},{11... | collective-permute-start | bytes 149768 | tf_op jit(solution)/shard_map/ppermute | solution.py:20
  14.3 15.8 %collective-permute-start.1 = (f32[13,15,64]{2,1,0:T(8,128)}, f32[13,15,64]{2,1,0:T(8,128)}, u32[]{:S(2)}, u32[]{:S(2)}) collective-permute-start(f32[13,15,64]{2,1,0:T(8,128)} %get-tuple-element.46), channel_id=1, source_target_pairs={{1,0},{2,1},{3,2},{4,3},{5,4},{6,5},{7,6},{9,8},{10,9},{11,10},{12... | collective-permute-start | bytes 149768 | tf_op jit(solution)/shard_map/ppermute | solution.py:21
  15.8 1.7 %copy-start.43 = (f32[3,3,128]{2,1,0:T(4,128)S(1)}, f32[3,3,128]{2,1,0:T(4,128)}, u32[]{:S(2)}) copy-start(f32[3,3,128]{2,1,0:T(4,128)} %param.30) | copy-start | bytes 13828
  15.8 1.7 %copy-start = (f32[6,35,128]{2,1,0:T(8,128)S(1)}, f32[6,35,128]{2,1,0:T(8,128)}, u32[]{:S(2)}) copy-start(f32[6,35,128]{2,1,0:T(8,128)} %param.28) | copy-start | bytes 322564
  16.0 1.6 %copy-start.15 = (f32[1,2,13,35,128]{4,1,3,2,0:T(2,128)S(1)}, f32[1,2,13,35,128]{4,1,3,2,0:T(2,128)}, u32[]{:S(2)}) copy-start(f32[1,2,13,35,128]{4,1,3,2,0:T(2,128)} %param.27) | copy-start | bytes 1397764
  17.6 2.4 %copy-start.20 = (f32[128]{0:T(128)}, f32[128]{0:T(128)S(1)}, u32[]{:S(2)}) copy-start(f32[128]{0:T(128)S(1)} %get-tuple-element.50) | copy-start | bytes 1540
  17.6 2.4 %copy-start.22 = (f32[128]{0:T(128)}, f32[128]{0:T(128)S(1)}, u32[]{:S(2)}) copy-start(f32[128]{0:T(128)S(1)} %get-tuple-element.51) | copy-start | bytes 1540
  17.6 2.4 %copy-start.24 = (f32[128]{0:T(128)}, f32[128]{0:T(128)S(1)}, u32[]{:S(2)}) copy-start(f32[128]{0:T(128)S(1)} %get-tuple-element.52) | copy-start | bytes 1540
  17.6 2.4 %copy-start.26 = (f32[128]{0:T(128)}, f32[128]{0:T(128)S(1)}, u32[]{:S(2)}) copy-start(f32[128]{0:T(128)S(1)} %get-tuple-element.53) | copy-start | bytes 1540
  17.6 2.4 %copy-start.28 = (f32[128]{0:T(128)}, f32[128]{0:T(128)S(1)}, u32[]{:S(2)}) copy-start(f32[128]{0:T(128)S(1)} %get-tuple-element.54) | copy-start | bytes 1540
  17.6 2.4 %copy-start.30 = (f32[128]{0:T(128)}, f32[128]{0:T(128)S(1)}, u32[]{:S(2)}) copy-start(f32[128]{0:T(128)S(1)} %get-tuple-element.55) | copy-start | bytes 1540
  17.6 2.4 %copy-start.32 = (f32[128]{0:T(128)}, f32[128]{0:T(128)S(1)}, u32[]{:S(2)}) copy-start(f32[128]{0:T(128)S(1)} %get-tuple-element.56) | copy-start | bytes 1540
  17.7 2.6 %copy-start.3 = (f32[6,35,128]{2,0,1:T(8,128)}, f32[6,35,128]{2,0,1:T(8,128)S(1)}, u32[]{:S(2)}) copy-start(f32[6,35,128]{2,0,1:T(8,128)S(1)} %copy.197) | copy-start | bytes 322564
  20.1 0.9 %copy-start.11 = (f32[3,6,13,13]{3,2,1,0:T(8,128)S(1)}, f32[3,6,13,13]{3,2,1,0:T(8,128)}, u32[]{:S(2)}) copy-start(f32[3,6,13,13]{3,2,1,0:T(8,128)} %param.29) | copy-start | bytes 36508
  21.0 3.4 %copy-start.34 = (f32[15,15]{1,0:T(8,128)S(1)}, f32[15,15]{1,0:T(8,128)}, u32[]{:S(2)}) copy-start(f32[15,15]{1,0:T(8,128)} %constant.63.clone) | copy-start | bytes 2704
  21.0 3.4 %copy-start.35 = (f32[15,15]{1,0:T(8,128)S(1)}, f32[15,15]{1,0:T(8,128)}, u32[]{:S(2)}) copy-start(f32[15,15]{1,0:T(8,128)} %constant.62.clone) | copy-start | bytes 2704
  21.0 3.4 %copy-start.36 = (f32[15,15]{1,0:T(8,128)S(1)}, f32[15,15]{1,0:T(8,128)}, u32[]{:S(2)}) copy-start(f32[15,15]{1,0:T(8,128)} %constant.61.clone) | copy-start | bytes 2704
  21.0 3.4 %copy-start.37 = (f32[15,15]{1,0:T(8,128)S(1)}, f32[15,15]{1,0:T(8,128)}, u32[]{:S(2)}) copy-start(f32[15,15]{1,0:T(8,128)} %constant.60.clone) | copy-start | bytes 2704
  21.0 3.4 %copy-start.38 = (f32[15,15]{1,0:T(8,128)S(1)}, f32[15,15]{1,0:T(8,128)}, u32[]{:S(2)}) copy-start(f32[15,15]{1,0:T(8,128)} %constant.59.clone) | copy-start | bytes 2704
  21.0 3.4 %copy-start.39 = (f32[15,15]{1,0:T(8,128)S(1)}, f32[15,15]{1,0:T(8,128)}, u32[]{:S(2)}) copy-start(f32[15,15]{1,0:T(8,128)} %constant.58.clone) | copy-start | bytes 2704
  25.6 3.2 %copy-start.42 = (f32[3,4,128]{2,1,0:T(4,128)S(1)}, f32[3,4,128]{2,1,0:T(4,128)}, u32[]{:S(2)}) copy-start(f32[3,4,128]{2,1,0:T(4,128)} %param.31) | copy-start | bytes 18436
  28.9 5.2 %copy-start.40 = (f32[3,4,128]{2,0,1:T(4,128)}, f32[3,4,128]{2,0,1:T(4,128)S(1)}, u32[]{:S(2)}) copy-start(f32[3,4,128]{2,0,1:T(4,128)S(1)} %copy.201) | copy-start | bytes 18436
  32.9 1.2 %copy-start.12 = (f32[3,6,13,13]{3,2,1,0:T(8,128)S(1)}, f32[3,6,13,13]{3,2,1,0:T(8,128)}, u32[]{:S(2)}) copy-start(f32[3,6,13,13]{3,2,1,0:T(8,128)} %param.29) | copy-start | bytes 36508
  32.9 1.2 %copy-start.16 = (f32[60,6,128]{2,1,0:T(8,128)S(1)}, f32[60,6,128]{2,1,0:T(8,128)}, u32[]{:S(2)}) copy-start(f32[60,6,128]{2,1,0:T(8,128)} %copy.259) | copy-start | bytes 552964
  36.7 1.0 %copy-start.5 = (f32[13,35,128]{2,0,1:T(8,128)S(1)}, f32[13,35,128]{2,0,1:T(8,128)}, u32[]{:S(2)}) copy-start(f32[13,35,128]{2,0,1:T(8,128)} %fusion.5) | copy-start | bytes 698884
  36.7 1.0 %copy-start.19 = (f32[4,35,15,1]{1,2,0,3:T(8,128)S(1)}, f32[4,35,15,1]{1,2,0,3:T(8,128)}, u32[]{:S(2)}) copy-start(f32[4,35,15,1]{1,2,0,3:T(8,128)} %constant.71) | copy-start | bytes 25204
  38.5 0.7 copy-start.1
  39.2 2.9 %copy-start.46 = (s32[128]{0:T(128)S(1)}, s32[128]{0:T(128)}, u32[]{:S(2)}) copy-start(s32[128]{0:T(128)} %param.35) | copy-start | bytes 1540
  40.1 2.4 %copy-start.8 = (f32[3,35,35,1]{2,1,0,3:T(8,128)S(1)}, f32[3,35,35,1]{2,1,0,3:T(8,128)}, u32[]{:S(2)}) copy-start(f32[3,35,35,1]{2,1,0,3:T(8,128)} %constant.70) | copy-start | bytes 44104
  42.1 7.4 %copy-start.21 = (f32[128]{0:T(128)S(1)}, f32[128]{0:T(128)}, u32[]{:S(2)}) copy-start(f32[128]{0:T(128)} %copy-done.20) | copy-start | bytes 1540
  42.1 7.4 %copy-start.23 = (f32[128]{0:T(128)S(1)}, f32[128]{0:T(128)}, u32[]{:S(2)}) copy-start(f32[128]{0:T(128)} %copy-done.22) | copy-start | bytes 1540
  42.2 7.4 %copy-start.25 = (f32[128]{0:T(128)S(1)}, f32[128]{0:T(128)}, u32[]{:S(2)}) copy-start(f32[128]{0:T(128)} %copy-done.24) | copy-start | bytes 1540
  42.2 7.4 %copy-start.27 = (f32[128]{0:T(128)S(1)}, f32[128]{0:T(128)}, u32[]{:S(2)}) copy-start(f32[128]{0:T(128)} %copy-done.26) | copy-start | bytes 1540
  42.2 7.4 %copy-start.29 = (f32[128]{0:T(128)S(1)}, f32[128]{0:T(128)}, u32[]{:S(2)}) copy-start(f32[128]{0:T(128)} %copy-done.28) | copy-start | bytes 1540
  42.2 7.4 %copy-start.31 = (f32[128]{0:T(128)S(1)}, f32[128]{0:T(128)}, u32[]{:S(2)}) copy-start(f32[128]{0:T(128)} %copy-done.30) | copy-start | bytes 1540
  42.2 7.4 %copy-start.33 = (f32[128]{0:T(128)S(1)}, f32[128]{0:T(128)}, u32[]{:S(2)}) copy-start(f32[128]{0:T(128)} %copy-done.32) | copy-start | bytes 1540
  43.4 6.3 %copy-start.2 = (f32[13,35,128]{2,0,1:T(8,128)S(1)}, f32[13,35,128]{2,0,1:T(8,128)}, u32[]{:S(2)}) copy-start(f32[13,35,128]{2,0,1:T(8,128)} %copy-done.1) | copy-start | bytes 698884
  43.4 6.3 %copy-start.10 = (f32[3,13,35,128,1]{3,2,0,1,4:T(8,128)S(1)}, f32[3,13,35,128,1]{3,2,0,1,4:T(8,128)}, u32[]{:S(2)}) copy-start(f32[3,13,35,128,1]{3,2,0,1,4:T(8,128)} %maximum_bitcast_fusion.2) | copy-start | bytes 2096644
  43.4 6.3 %copy-start.13 = (f32[3,6,13,13]{3,2,1,0:T(8,128)S(1)}, f32[3,6,13,13]{3,2,1,0:T(8,128)}, u32[]{:S(2)}) copy-start(f32[3,6,13,13]{3,2,1,0:T(8,128)} %param.29) | copy-start | bytes 36508
  43.5 11.9 %collective-permute-start.2 = (f32[13,15,64]{2,1,0:T(8,128)S(1)}, f32[13,15,64]{2,1,0:T(8,128)S(1)}, u32[]{:S(2)}, u32[]{:S(2)}) collective-permute-start(f32[13,15,64]{2,1,0:T(8,128)S(1)} %get-tuple-element.45), channel_id=1, source_target_pairs={{0,1},{1,2},{2,3},{3,4},{4,5},{5,6},{6,7},{8,9},{9,10},{10,11},{11... | collective-permute-start | bytes 149768 | tf_op jit(solution)/shard_map/ppermute | solution.py:20
  48.2 7.6 %collective-permute-start.3 = (f32[13,15,64]{2,1,0:T(8,128)S(1)}, f32[13,15,64]{2,1,0:T(8,128)S(1)}, u32[]{:S(2)}, u32[]{:S(2)}) collective-permute-start(f32[13,15,64]{2,1,0:T(8,128)S(1)} %get-tuple-element.44), channel_id=1, source_target_pairs={{1,0},{2,1},{3,2},{4,3},{5,4},{6,5},{7,6},{9,8},{10,9},{11,10},{12... | collective-permute-start | bytes 149768 | tf_op jit(solution)/shard_map/ppermute | solution.py:21
  52.2 0.9 %copy-start.4 = (f32[6,35,128]{2,0,1:T(8,128)S(1)}, f32[6,35,128]{2,0,1:T(8,128)}, u32[]{:S(2)}) copy-start(f32[6,35,128]{2,0,1:T(8,128)} %copy-done.3) | copy-start | bytes 322564
  56.7 0.9 %copy-start.14 = (f32[3,6,13,13]{3,2,1,0:T(8,128)S(1)}, f32[3,6,13,13]{3,2,1,0:T(8,128)}, u32[]{:S(2)}) copy-start(f32[3,6,13,13]{3,2,1,0:T(8,128)} %param.29) | copy-start | bytes 36508
  56.8 1.0 %copy-start.17 = (f32[60,6,128]{2,1,0:T(8,128)S(1)}, f32[60,6,128]{2,1,0:T(8,128)}, u32[]{:S(2)}) copy-start(f32[60,6,128]{2,1,0:T(8,128)} %copy.259) | copy-start | bytes 552964
  56.8 1.0 %copy-start.41 = (f32[3,4,128]{2,0,1:T(4,128)S(1)}, f32[3,4,128]{2,0,1:T(4,128)}, u32[]{:S(2)}) copy-start(f32[3,4,128]{2,0,1:T(4,128)} %copy-done.40) | copy-start | bytes 18436
  60.5 1.0 %copy-start.6 = (f32[13,35,128]{2,0,1:T(8,128)S(1)}, f32[13,35,128]{2,0,1:T(8,128)}, u32[]{:S(2)}) copy-start(f32[13,35,128]{2,0,1:T(8,128)} %fusion.4) | copy-start | bytes 698884
  61.4 1.1 %copy-start.9 = (f32[3,13,35,128,1]{3,2,0,1,4:T(8,128)S(1)}, f32[3,13,35,128,1]{3,2,0,1,4:T(8,128)}, u32[]{:S(2)}) copy-start(f32[3,13,35,128,1]{3,2,0,1,4:T(8,128)} %maximum_bitcast_fusion.3) | copy-start | bytes 2096644
  62.2 2.2 %copy-start.18 = (f32[6,35,128]{2,0,1:T(8,128)S(1)}, f32[6,35,128]{2,0,1:T(8,128)}, u32[]{:S(2)}) copy-start(f32[6,35,128]{2,0,1:T(8,128)} %fusion.3) | copy-start | bytes 322564
  64.5 5.2 %collective-permute-start.4 = (f32[6,35,64]{2,0,1:T(8,128)S(1)}, f32[6,35,64]{2,0,1:T(8,128)S(1)}, u32[]{:S(2)}, u32[]{:S(2)}) collective-permute-start(f32[6,35,64]{2,0,1:T(8,128)S(1)} %slice_select_fusion.1), channel_id=1, source_target_pairs={{0,16},{8,24},{16,0},{24,8},{1,17},{9,25},{17,1},{25,9},{2,18},{10... | collective-permute-start | bytes 161288 | tf_op jit(solution)/shard_map/ppermute | solution.py:160
  69.9 1.4 %collective-permute-start.5 = (f32[6,35,32]{2,0,1:T(8,128)S(1)}, f32[6,35,32]{2,0,1:T(8,128)S(1)}, u32[]{:S(2)}, u32[]{:S(2)}) collective-permute-start(f32[6,35,32]{2,0,1:T(8,128)S(1)} %slice_select_fusion), channel_id=1, source_target_pairs={{0,8},{8,0},{16,24},{24,16},{1,9},{9,1},{17,25},{25,17},{2,10},{10... | collective-permute-start | bytes 80648 | tf_op jit(solution)/shard_map/ppermute | solution.py:160
  72.4 14.3 %all-to-all-start = ((f32[32,1,60]{2,1,0:T(1,128)}), f32[32,1,60]{2,1,0:T(1,128)S(1)}, u32[]{:S(2)}, u32[]{:S(2)}) async-start(f32[32,1,60]{2,1,0:T(1,128)} %broadcast_in_dim.16), calls=%async_computation | async-start | bytes 32768 | tf_op jit(solution)/shard_map/all_to_all | solution.py:289

commit v9 on v8

--- a/solution.py
+++ b/solution.py
@@ -165,10 +165,10 @@
     return work
 
 
-def search_direction(grad_share, step_share, change_share, gram, combine_sums):
+def search_direction(grad_share, local_grad, both_rows, step_share, change_share, gram, combine_sums):
     pairs = step_share.shape[0]
     both_share = jnp.concatenate([step_share, change_share], axis=0)
-    with_grad = jnp.sum(both_share * grad_share[None], axis=(1, 2, 3))
+    with_grad = jnp.sum(both_rows * local_grad[None], axis=(1, 2, 3))
     summed = combine_sums(jnp.concatenate([with_grad, gram.reshape(-1)]))
     lanes = 0.0 * step_share[0, 0, :8, :]
     summed = summed[:, None, None] + lanes[None]
@@ -257,8 +257,9 @@
     change_share = own_share(history_changes)
     both_share = jnp.concatenate([step_share, change_share], axis=0)
     gram = jnp.sum(both_share[:, None] * change_share[None, :], axis=(2, 3, 4))
-    step_share, change_share, gram, adjoint = lax.optimization_barrier(
-        (step_share, change_share, gram, adjoint)
+    both_rows = jnp.concatenate([history_steps, history_changes], axis=0)
+    both_rows, step_share, change_share, gram, adjoint = lax.optimization_barrier(
+        (both_rows, step_share, change_share, gram, adjoint)
     )
     gradient = jnp.zeros((params, node_count, elements), jnp.float32)
     for step_index in range(forward_states.shape[1]):
@@ -289,7 +290,9 @@
         return jnp.sum(lax.all_to_all(spread, ("shot", "mesh"), 0, 0, tiled=False), axis=0)
 
     grad_share = halving_sum(gradient, "shot", shot_count)
-    result = search_direction(grad_share, step_share, change_share, gram, combine_sums)
+    result = search_direction(
+        grad_share, gradient, both_rows, step_share, change_share, gram, combine_sums
+    )
     return (adjoint[None], result)
 
 

time: 88.9 us -> 103 us (1.16)
  local copies, waits for them, and re-layouts: 20.6 us -> 30.7 us
  waiting for transfers between devices: 11 us -> 5.46 us
  other arithmetic: 8.98 us -> 14.3 us
  matrix products: 24.2 us -> 27.9 us
    ppermute x2, waiting for transfers between devices: 4.84 us -> 1.19 us  [halving_sum(): lax.ppermute(jnp.where(upper, low, high), axis, [(i, i ^ bit) for i in ra...]
    gather x4, local copies, waits for them, and re-layouts: 2.32 us -> 5.87 us  [shards(): inner_trace = adjoint[:, face_nodes.T, :]]
    reshape x2, local copies, waits for them, and re-layouts: 1.03 us -> 3.85 us  [shards(): jump_trace = turned.reshape(fields, face_width, 4, elements) - inner_trace]
    reshape x2, local copies, waits for them, and re-layouts: 1.33 us -> 3.84 us  [shards(): flat_trace = inner_trace.reshape(fields, face_width, 4 * elements)]
    concatenate x1, local copies, waits for them, and re-layouts: 0.47 us -> 2.77 us  [shards(): both_share = jnp.concatenate([step_share, change_share], axis=0)]
    all_to_all x1, waiting for transfers between devices: 6.1 us -> 4.26 us  [combine_sums(): lax.all_to_all(spread, ('shot', 'mesh'), 0, 0, tiled=False)]
    dot_general x2, matrix products: 1.41 us -> 3.24 us  [shards(): gathered = jnp.einsum('fns,sj->fnj', flat_trace, local_pick, precision=HIGH)]
    dot_general x2, matrix products: 0.71 us -> 2.44 us  [shards(): jnp.einsum('fns,sj->fnj', flat_trace, send_pick, precision=HIGH)]
  transfers between devices with their start and end apart: 7 -> 7, of which waited for: 3 -> 2; matrix products, arithmetic and copies ran while one was open for 22% -> 21% of each run, Pallas kernels for 0% -> 0%
where the time goes in v9:
time: 103 us; the launch traced here: 102 us
  local copies, waits for them, and re-layouts  30.7 us (30%)
  matrix products  27.9 us (27%)
  starting transfers between devices  22 us (21%)
  other arithmetic  14.3 us (14%)
  waiting for transfers between devices  5.46 us (5%)
  between operations  1.81 us (2%)
    ppermute x2, starting transfers between devices, padded(): before = lax.ppermute(last, axis, up)  10.2 us
    all_to_all x1, starting transfers between devices, combine_sums(): lax.all_to_all(spread, ('shot', 'mesh'), 0, 0, tiled=False)  7.24 us
    unnamed x133, local copies, waits for them, and re-layouts  5.93 us
    gather x4, local copies, waits for them, and re-layouts, shards(): inner_trace = adjoint[:, face_nodes.T, :]  5.87 us
    dot_general x2, matrix products, surface_term(): mixing = jnp.einsum('dpfg,dfnxe->pgnxe', coupling, weighted, precision=HIGH)  5.36 us
    dot_general x2, matrix products, volume_term(): mixing = jnp.einsum('dpfg,dfae->pgae', coupling, spatial, precision=HIGH)  4.62 us
    all_to_all x1, waiting for transfers between devices, combine_sums(): lax.all_to_all(spread, ('shot', 'mesh'), 0, 0, tiled=False)  4.26 us
    dot_general x2, matrix products, kernel_term(): mixing = jnp.einsum('dpfg,dgae->pfae', coupling, spatial, precision=HIGH)  4.19 us
  transfers between devices with their start and end apart: 7, of which 2 were waited for; matrix products, arithmetic and copies ran while one was open for 21% of the time, Pallas kernels for 0%

profile of v9, /device:TPU:0, one launch (start us, length us, event | category | flops | bytes accessed | tf_op | source)
XLA Modules:
  0.0 102.2 jit_solution(14720853838207795058)
XLA Ops:
  0.6 1.4 %pad_maximum_fusion = f32[10,6,35,128]{3,2,1,0:T(8,128)S(1)} fusion(f32[5,6,35,128]{3,2,1,0:T(8,128)} %param.37, f32[5,6,35,128]{3,2,1,0:T(8,128)} %param.36), kind=kLoop, calls=%fused_computation.29 | loop fusion | flops 268800 | bytes 2150400 | tf_op jit(solution)/shard_map/concatenate | solution.py:260
  2.1 1.5 %constant_dynamic-slice_fusion = (f32[5,6,35,32]{3,2,1,0:T(8,128)S(1)}, f32[5,6,35,32]{3,2,1,0:T(8,128)S(1)}) fusion(f32[5,6,35,128]{3,2,1,0:T(8,128)S(1)} %copy-done.9, s32[]{:T(128)S(6)} %select_n.37, f32[5,6,35,128]{3,2,1,0:T(8,128)} %param.36), kind=kLoop, calls=%fused_computation.266 | loop fusion | bytes 537604 | tf_op jit(solution)/shard_map/dynamic_slice | solution.py:254
  3.5 0.3 copy.196
  3.8 1.2 %pad_maximum_fusion.1 = f32[10,6,35,32]{3,2,1,0:T(8,128)} fusion(f32[5,6,35,32]{3,2,1,0:T(8,128)S(1)} %get-tuple-element.11, f32[5,6,35,32]{3,2,1,0:T(8,128)S(1)} %get-tuple-element.10), kind=kLoop, calls=%fused_computation.30 | loop fusion | flops 67200 | bytes 537600 | tf_op jit(solution)/shard_map/concatenate | solution.py:258
  5.0 2.8 %copy.195 = f32[10,6,35,32]{2,3,1,0:T(8,128)} copy(f32[10,6,35,32]{3,2,1,0:T(8,128)} %pad_maximum_fusion.1) | data formatting | bytes 537600 | tf_op jit(solution)/shard_map/concatenate | solution.py:258
  7.8 1.9 %multiply_reduce_fusion.2 = f32[10,5]{1,0:T(8,128)S(1)} fusion(f32[5,6,35,32]{2,3,1,0:T(8,128)S(1)} %copy.196, f32[10,6,35,32]{2,3,1,0:T(8,128)} %copy.195), kind=kLoop, calls=%fused_computation.5 | loop fusion | flops 671950 | bytes 403400 | tf_op jit(solution)/shard_map/reduce_sum | solution.py:259
  9.8 0.6 gather_fusion.1
  10.5 0.9 copy.203
  11.4 1.9 %reshape.368 = f32[13,15,512]{2,1,0:T(8,128)} reshape(f32[13,15,4,128]{3,2,1,0:T(4,128)} %copy.203) | data formatting | bytes 798720 | tf_op jit(solution)/shard_map/reshape | solution.py:267
  13.3 1.4 %fusion.34 = f32[13,15,128]{2,1,0:T(8,128)S(1)} fusion(f32[13,15,512]{2,1,0:T(8,128)} %reshape.368, s32[128]{0:T(128)S(1)} %copy-done.59), kind=kOutput, calls=%fused_computation.86 | convolution fusion | flops 153419776 | bytes 499712 | tf_op jit(solution)/shard_map/fns,sj->fnj/dot_general | solution.py:268
  14.8 0.7 fusion.138
  15.5 5.5 %collective-permute-start = (f32[13,15,64]{2,1,0:T(8,128)}, f32[13,15,64]{2,1,0:T(8,128)}, u32[]{:S(2)}, u32[]{:S(2)}) collective-permute-start(f32[13,15,64]{2,1,0:T(8,128)} %get-tuple-element.49), channel_id=1, source_target_pairs={{0,1},{1,2},{2,3},{3,4},{4,5},{5,6},{6,7},{8,9},{9,10},{10,11},{11... | collective-permute-start | bytes 149768 | tf_op jit(solution)/shard_map/ppermute | solution.py:20
  21.0 1.5 %collective-permute-start.1 = (f32[13,15,64]{2,1,0:T(8,128)S(1)}, f32[13,15,64]{2,1,0:T(8,128)}, u32[]{:S(2)}, u32[]{:S(2)}) collective-permute-start(f32[13,15,64]{2,1,0:T(8,128)S(1)} %get-tuple-element.48), channel_id=1, source_target_pairs={{1,0},{2,1},{3,2},{4,3},{5,4},{6,5},{7,6},{9,8},{10,9},{11,10},{12... | collective-permute-start | bytes 149768 | tf_op jit(solution)/shard_map/ppermute | solution.py:21
  22.8 1.4 %fusion.26 = f32[13,15,512]{2,1,0:T(8,128)} fusion(f32[13,15,512]{2,1,0:T(8,128)S(1)} %copy-done.5, pred[640,512]{1,0:T(32,128)(4,1)S(1)} %iota_compare_fusion), kind=kOutput, calls=%fused_computation.58 | convolution fusion | flops 613416960 | bytes 1087488 | tf_op jit(solution)/shard_map/fns,sj->fnj/dot_general | solution.py:270
  24.2 0.8 convolution_bitcast_fusion.3
  25.2 0.4 fusion.135
  25.6 0.8 convolution_bitcast_fusion.1
  26.7 0.8 convolution_bitcast_fusion
  27.9 0.6 copy-done.19
  28.5 2.3 %fusion.5 = f32[13,35,128]{2,0,1:T(8,128)} fusion(f32[3,13,35,128,1]{3,2,0,1,4:T(8,128)S(1)} %maximum_bitcast_fusion, f32[6,35,128]{2,0,1:T(8,128)S(1)} %copy.197, f32[3,6,13,13]{3,2,1,0:T(8,128)S(1)} %copy-done.19), kind=kOutput, calls=%fused_computation.17 | convolution fusion | flops 164178560 | bytes 1051528 | tf_op jit(solution)/shard_map/dpfg,dfae->pgae/dot_general | solution.py:132
  30.8 1.0 maximum_bitcast_fusion.2
  31.8 0.3 multiply_add_fusion
  32.1 1.0 maximum_bitcast_fusion.3
  33.1 1.5 %gather_fusion = f32[60,6,128]{2,0,1:T(8,128)} fusion(f32[6,35,128]{2,1,0:T(8,128)S(1)} %copy-done, s32[1024]{0:T(1024)S(1)} %pad_clamp_fusion), kind=kCustom, calls=%fused_computation | custom fusion | bytes 368880 | tf_op jit(solution)/shard_map/gather | solution.py:231
  34.6 1.7 %copy.259 = f32[60,6,128]{2,1,0:T(8,128)} copy(f32[60,6,128]{2,0,1:T(8,128)} %gather_fusion) | data formatting | bytes 368640 | tf_op jit(solution)/shard_map/gather | solution.py:231
  36.3 0.6 reshape.372
  37.0 1.4 %convolution_add_fusion.3 = f32[13,15,512]{2,1,0:T(8,128)S(1)} fusion(f32[13,15,512]{2,1,0:T(8,128)} %fusion.26, f32[13,15,64]{2,1,0:T(8,128)} %collective-permute-done, pred[640,512]{1,0:T(32,128)(4,1)S(1)} %iota_compare_fusion), kind=kOutput, calls=%fused_computation.35 | convolution fusion | flops 76776960 | bytes 881408 | tf_op jit(solution)/shard_map/fns,sj->fnj/dot_general | solution.py:271
  38.4 1.2 %convolution_add_fusion.2 = f32[13,15,512]{2,1,0:T(8,128)S(1)} fusion(f32[13,15,512]{2,1,0:T(8,128)S(1)} %convolution_add_fusion.3, f32[13,15,64]{2,1,0:T(8,128)} %collective-permute-done.1, pred[640,512]{1,0:T(32,128)(4,1)S(1)} %iota_compare_fusion), kind=kOutput, calls=%fused_computation.34 | convolution fusion | flops 76776960 | bytes 908032 | tf_op jit(solution)/shard_map/fns,sj->fnj/dot_general | solution.py:274
  39.6 1.4 %multiply_reduce_fusion.1 = f32[13,15,512]{2,1,0:T(8,128)} fusion(f32[15,15,512]{2,1,0:T(8,128)S(1)} %multiply_add_fusion, f32[13,15,512]{2,1,0:T(8,128)S(1)} %convolution_add_fusion.2), kind=kLoop, calls=%fused_computation.4 | loop fusion | flops 2895360 | bytes 1259520 | tf_op jit(solution)/shard_map/reduce_sum | solution.py:277
  41.0 1.9 %reshape.369 = f32[13,15,4,128]{3,2,1,0:T(4,128)} reshape(f32[13,15,512]{2,1,0:T(8,128)} %multiply_reduce_fusion.1) | data formatting | bytes 798720 | tf_op jit(solution)/shard_map/reshape | solution.py:278
  42.9 1.1 %copy_subtract_fusion.1 = f32[13,15,4,128]{3,0,2,1:T(8,128)S(1)} fusion(f32[13,15,4,128]{3,0,2,1:T(8,128)S(1)} %bitcast.777, f32[13,15,4,128]{3,2,1,0:T(4,128)} %reshape.369), kind=kLoop, calls=%fused_computation.60 | loop fusion | flops 99840 | bytes 1198080 | tf_op jit(solution)/shard_map/sub | solution.py:278
  44.1 2.7 %fusion.1 = f32[13,15,4,128]{3,0,2,1:T(8,128)S(1)} fusion(f32[6,15,4,128]{3,0,2,1:T(8,128)S(1)} %bitcast.792, f32[13,15,4,128]{3,0,2,1:T(8,128)S(1)} %copy_subtract_fusion.1, f32[3,4,128]{2,0,1:T(4,128)S(1)} %copy.201, f32[3,6,13,13]{3,2,1,0:T(8,128)S(1)} %copy-done.20), kind=kOutput, calls=%fused_computation.9 | convolution fusion | flops 281748480 | bytes 1001352 | tf_op jit(solution)/shard_map/dpfg,dfnxe->pgnxe/dot_general | solution.py:144
  46.9 0.8 copy-done.2
  47.8 0.7 fusion.13
  48.6 0.8 copy.210
  49.3 2.4 %gather_fusion.2 = f32[60,13,128]{2,1,0:T(8,128)} fusion(f32[13,35,128]{2,0,1:T(8,128)} %copy.210, s32[1024]{0:T(1024)S(1)} %pad_clamp_fusion), kind=kCustom, calls=%fused_computation.2 | custom fusion | bytes 798960 | tf_op jit(solution)/shard_map/gather | solution.py:266
  51.7 1.9 %copy.211 = f32[13,15,4,128]{3,2,1,0:T(4,128)} copy(f32[13,15,4,128]{3,0,2,1:T(8,128)} %bitcast.778) | data formatting | bytes 798720 | tf_op jit(solution)/shard_map/gather | solution.py:266
  53.6 1.9 %reshape.370 = f32[13,15,512]{2,1,0:T(8,128)} reshape(f32[13,15,4,128]{3,2,1,0:T(4,128)} %copy.211) | data formatting | bytes 798720 | tf_op jit(solution)/shard_map/reshape | solution.py:267
  55.6 1.9 %fusion.25 = f32[13,15,512]{2,1,0:T(8,128)S(1)} fusion(f32[13,15,512]{2,1,0:T(8,128)} %reshape.370, pred[640,512]{1,0:T(32,128)(4,1)S(1)} %copy-done.8), kind=kOutput, calls=%fused_computation.57 | convolution fusion | flops 613416960 | bytes 1060864 | tf_op jit(solution)/shard_map/fns,sj->fnj/dot_general | solution.py:270
  57.5 1.0 fusion.32
  58.6 0.8 convolution_bitcast_fusion.2
  59.5 4.7 %collective-permute-start.2 = (f32[13,15,64]{2,1,0:T(8,128)S(1)}, f32[13,15,64]{2,1,0:T(8,128)S(1)}, u32[]{:S(2)}, u32[]{:S(2)}) collective-permute-start(f32[13,15,64]{2,1,0:T(8,128)S(1)} %get-tuple-element.47), channel_id=1, source_target_pairs={{0,1},{1,2},{2,3},{3,4},{4,5},{5,6},{6,7},{8,9},{9,10},{10,11},{11... | collective-permute-start | bytes 149768 | tf_op jit(solution)/shard_map/ppermute | solution.py:20
  64.2 1.3 %collective-permute-start.3 = (f32[13,15,64]{2,1,0:T(8,128)S(1)}, f32[13,15,64]{2,1,0:T(8,128)S(1)}, u32[]{:S(2)}, u32[]{:S(2)}) collective-permute-start(f32[13,15,64]{2,1,0:T(8,128)S(1)} %get-tuple-element.46), channel_id=1, source_target_pairs={{1,0},{2,1},{3,2},{4,3},{5,4},{6,5},{7,6},{9,8},{10,9},{11,10},{12... | collective-permute-start | bytes 149768 | tf_op jit(solution)/shard_map/ppermute | solution.py:21
  65.8 2.4 %fusion.3 = f32[6,35,128]{2,0,1:T(8,128)} fusion(f32[3,13,35,128,1]{3,2,0,1,4:T(8,128)S(1)} %copy-done.18, f32[13,35,128]{2,0,1:T(8,128)S(1)} %copy-done.10, f32[3,6,13,13]{3,2,1,0:T(8,128)S(1)} %copy-done.21), kind=kOutput, calls=%fused_computation.13 | convolution fusion | flops 164209920 | bytes 1051528 | tf_op jit(solution)/shard_map/dpfg,dgae->pfae/dot_general | solution.py:138
  68.3 0.8 copy-done.12
  69.1 2.3 %fusion.4 = f32[13,35,128]{2,0,1:T(8,128)} fusion(f32[3,13,35,128,1]{3,2,0,1,4:T(8,128)S(1)} %maximum_bitcast_fusion.1, f32[6,35,128]{2,0,1:T(8,128)S(1)} %copy-done.12, f32[3,6,13,13]{3,2,1,0:T(8,128)S(1)} %copy-done.21), kind=kOutput, calls=%fused_computation.15 | convolution fusion | flops 164178560 | bytes 1051528 | tf_op jit(solution)/shard_map/dpfg,dfae->pgae/dot_general | solution.py:132
  71.4 0.3 convolution_add_fusion.1
  71.8 0.3 convolution_add_fusion
  72.1 1.4 %multiply_reduce_fusion = f32[13,15,512]{2,1,0:T(8,128)} fusion(f32[13,15,512]{2,1,0:T(8,128)S(1)} %convolution_add_fusion, f32[15,15,512]{2,1,0:T(8,128)S(1)} %multiply_add_fusion), kind=kLoop, calls=%fused_computation.3 | loop fusion | flops 2895360 | bytes 1259520 | tf_op jit(solution)/shard_map/reduce_sum | solution.py:277
  73.5 2.0 %reshape.371 = f32[13,15,4,128]{3,2,1,0:T(4,128)} reshape(f32[13,15,512]{2,1,0:T(8,128)} %multiply_reduce_fusion) | data formatting | bytes 798720 | tf_op jit(solution)/shard_map/reshape | solution.py:278
  75.5 1.3 %copy_subtract_fusion = f32[13,15,4,128]{3,0,2,1:T(8,128)S(1)} fusion(f32[13,15,4,128]{3,0,2,1:T(8,128)} %bitcast.779, f32[13,15,4,128]{3,2,1,0:T(4,128)} %reshape.371), kind=kLoop, calls=%fused_computation.59 | loop fusion | flops 99840 | bytes 1198080 | tf_op jit(solution)/shard_map/sub | solution.py:278
  76.8 2.7 %fusion = f32[13,15,4,128]{3,0,2,1:T(8,128)S(1)} fusion(f32[6,15,4,128]{3,0,2,1:T(8,128)S(1)} %bitcast.793, f32[13,15,4,128]{3,0,2,1:T(8,128)S(1)} %copy_subtract_fusion, f32[3,4,128]{2,0,1:T(4,128)S(1)} %copy-done.55, f32[3,6,13,13]{3,2,1,0:T(8,128)S(1)} %copy-done.22), kind=kOutput, calls=%fused_computation.7 | convolution fusion | flops 281748480 | bytes 1001352 | tf_op jit(solution)/shard_map/dpfg,dfnxe->pgnxe/dot_general | solution.py:144
  79.6 0.9 copy-done.14
  80.4 0.7 fusion.16
  81.2 0.3 copy-done.17
  81.5 1.8 %fusion.2 = f32[6,35,128]{2,0,1:T(8,128)S(1)} fusion(f32[3,13,35,128,1]{3,2,0,1,4:T(8,128)S(1)} %copy-done.17, f32[13,35,128]{2,0,1:T(8,128)S(1)} %copy.225, f32[3,6,13,13]{3,2,1,0:T(8,128)S(1)} %copy-done.22), kind=kOutput, calls=%fused_computation.11 | convolution fusion | flops 164209920 | bytes 1051528 | tf_op jit(solution)/shard_map/dpfg,dgae->pfae/dot_general | solution.py:138
  83.6 0.3 copy-done.62
  84.0 0.6 broadcast_in_dim.16
  84.6 7.2 %all-to-all-start = ((f32[32,1,60]{2,1,0:T(1,128)}), f32[32,1,60]{2,1,0:T(1,128)S(1)}, u32[]{:S(2)}, u32[]{:S(2)}) async-start(f32[32,1,60]{2,1,0:T(1,128)} %broadcast_in_dim.16), calls=%async_computation | async-start | bytes 32768 | tf_op jit(solution)/shard_map/all_to_all | solution.py:290
  92.0 0.9 copy.229
  92.9 1.8 %collective-permute-start.4 = (f32[6,35,64]{2,0,1:T(8,128)S(1)}, f32[6,35,64]{2,0,1:T(8,128)S(1)}, u32[]{:S(2)}, u32[]{:S(2)}) collective-permute-start(f32[6,35,64]{2,0,1:T(8,128)S(1)} %slice_select_fusion.1), channel_id=1, source_target_pairs={{0,16},{8,24},{16,0},{24,8},{1,17},{9,25},{17,1},{25,9},{2,18},{10... | collective-permute-start | bytes 161288 | tf_op jit(solution)/shard_map/ppermute | solution.py:160
  94.7 4.3 %all-to-all-done = f32[32,1,60]{2,1,0:T(1,128)S(1)} async-done(((f32[32,1,60]{2,1,0:T(1,128)}), f32[32,1,60]{2,1,0:T(1,128)S(1)}, u32[]{:S(2)}, u32[]{:S(2)}) %all-to-all-start) | async-done | bytes 7712 | tf_op jit(solution)/shard_map/all_to_all | solution.py:290
  99.9 1.2 %collective-permute-done.5 = f32[6,35,32]{2,0,1:T(8,128)S(1)} collective-permute-done((f32[6,35,32]{2,0,1:T(8,128)S(1)}, f32[6,35,32]{2,0,1:T(8,128)S(1)}, u32[]{:S(2)}, u32[]{:S(2)}) %collective-permute-start.5) | collective-permute-done | bytes 26912 | tf_op jit(solution)/shard_map/ppermute | solution.py:160
  101.5 0.8 copy.230
  (174 shorter events, 3.4 us)
Async XLA Ops:
  0.6 1.4 %copy-start.9 = (f32[5,6,35,128]{3,2,1,0:T(8,128)S(1)}, f32[5,6,35,128]{3,2,1,0:T(8,128)}, u32[]{:S(2)}) copy-start(f32[5,6,35,128]{3,2,1,0:T(8,128)} %param.37) | copy-start | bytes 1612804
  5.0 2.8 %copy-start.26 = (f32[1,13,35,128]{3,0,2,1:T(1,128)S(1)}, f32[1,13,35,128]{3,0,2,1:T(1,128)}, u32[]{:S(2)}) copy-start(f32[1,13,35,128]{3,0,2,1:T(1,128)} %param.26) | copy-start | bytes 698884
  7.7 2.0 %copy-start.63 = (s32[60]{0:T(128)S(1)}, s32[60]{0:T(128)}, u32[]{:S(2)}) copy-start(s32[60]{0:T(128)} %constant.67) | copy-start | bytes 724
  7.8 16.4 %copy-start.1 = (f32[1,13,35,128]{3,2,0,1:T(8,128)}, f32[1,13,35,128]{3,2,0,1:T(8,128)S(1)}, u32[]{:S(2)}) copy-start(f32[1,13,35,128]{3,2,0,1:T(8,128)S(1)} %copy.308) | copy-start | bytes 698884
  9.8 3.5 %copy-start.59 = (s32[128]{0:T(128)S(1)}, s32[128]{0:T(128)}, u32[]{:S(2)}) copy-start(s32[128]{0:T(128)} %param.35) | copy-start | bytes 1540
  10.4 5.1 %copy-start.3 = (f32[60,13,128]{2,1,0:T(8,128)}, f32[60,13,128]{2,1,0:T(8,128)S(1)}, u32[]{:S(2)}) copy-start(f32[60,13,128]{2,1,0:T(8,128)S(1)} %gather_fusion.1) | copy-start | bytes 1198084
  10.5 12.0 %copy-start.60 = (s32[4,128]{1,0:T(4,128)S(1)}, s32[4,128]{1,0:T(4,128)}, u32[]{:S(2)}) copy-start(s32[4,128]{1,0:T(4,128)} %param.34) | copy-start | bytes 6148
  10.5 12.0 %copy-start.58 = (s32[4,128]{1,0:T(4,128)S(1)}, s32[4,128]{1,0:T(4,128)}, u32[]{:S(2)}) copy-start(s32[4,128]{1,0:T(4,128)} %param.33) | copy-start | bytes 6148
  13.3 9.4 %copy-start.5 = (f32[13,15,512]{2,1,0:T(8,128)S(1)}, f32[13,15,512]{2,1,0:T(8,128)}, u32[]{:S(2)}) copy-start(f32[13,15,512]{2,1,0:T(8,128)} %reshape.368) | copy-start | bytes 1198084
  13.3 10.9 %copy-start.61 = (f32[4,128]{1,0:T(4,128)S(1)}, f32[4,128]{1,0:T(4,128)}, u32[]{:S(2)}) copy-start(f32[4,128]{1,0:T(4,128)} %param.32) | copy-start | bytes 6148
  13.3 10.9 %copy-start.15 = (f32[3,35,35,1]{2,1,0,3:T(8,128)S(1)}, f32[3,35,35,1]{2,1,0,3:T(8,128)}, u32[]{:S(2)}) copy-start(f32[3,35,35,1]{2,1,0,3:T(8,128)} %constant.70) | copy-start | bytes 44104
  15.5 21.4 %collective-permute-start = (f32[13,15,64]{2,1,0:T(8,128)}, f32[13,15,64]{2,1,0:T(8,128)}, u32[]{:S(2)}, u32[]{:S(2)}) collective-permute-start(f32[13,15,64]{2,1,0:T(8,128)} %get-tuple-element.49), channel_id=1, source_target_pairs={{0,1},{1,2},{2,3},{3,4},{4,5},{5,6},{6,7},{8,9},{9,10},{10,11},{11... | collective-permute-start | bytes 149768 | tf_op jit(solution)/shard_map/ppermute | solution.py:20
  21.0 17.3 %collective-permute-start.1 = (f32[13,15,64]{2,1,0:T(8,128)S(1)}, f32[13,15,64]{2,1,0:T(8,128)}, u32[]{:S(2)}, u32[]{:S(2)}) collective-permute-start(f32[13,15,64]{2,1,0:T(8,128)S(1)} %get-tuple-element.48), channel_id=1, source_target_pairs={{1,0},{2,1},{3,2},{4,3},{5,4},{6,5},{7,6},{9,8},{10,9},{11,10},{12... | collective-permute-start | bytes 149768 | tf_op jit(solution)/shard_map/ppermute | solution.py:21
  22.5 2.5 %copy-start.57 = (f32[3,3,128]{2,1,0:T(4,128)S(1)}, f32[3,3,128]{2,1,0:T(4,128)}, u32[]{:S(2)}) copy-start(f32[3,3,128]{2,1,0:T(4,128)} %param.30) | copy-start | bytes 13828
  22.5 2.5 %copy-start = (f32[6,35,128]{2,1,0:T(8,128)S(1)}, f32[6,35,128]{2,1,0:T(8,128)}, u32[]{:S(2)}) copy-start(f32[6,35,128]{2,1,0:T(8,128)} %param.28) | copy-start | bytes 322564
  22.8 15.6 %copy-start.7 = (pred[640,512]{1,0:T(32,128)(4,1)}, pred[640,512]{1,0:T(32,128)(4,1)S(1)}, u32[]{:S(2)}) copy-start(pred[640,512]{1,0:T(32,128)(4,1)S(1)} %iota_compare_fusion) | copy-start | bytes 983044
  22.8 2.4 %copy-start.23 = (f32[1,2,13,35,128]{4,1,3,2,0:T(2,128)S(1)}, f32[1,2,13,35,128]{4,1,3,2,0:T(2,128)}, u32[]{:S(2)}) copy-start(f32[1,2,13,35,128]{4,1,3,2,0:T(2,128)} %param.27) | copy-start | bytes 1397764
  25.1 2.4 %copy-start.30 = (f32[128]{0:T(128)}, f32[128]{0:T(128)S(1)}, u32[]{:S(2)}) copy-start(f32[128]{0:T(128)S(1)} %get-tuple-element.50) | copy-start | bytes 1540
  25.1 2.4 %copy-start.32 = (f32[128]{0:T(128)}, f32[128]{0:T(128)S(1)}, u32[]{:S(2)}) copy-start(f32[128]{0:T(128)S(1)} %get-tuple-element.51) | copy-start | bytes 1540
  25.1 2.4 %copy-start.34 = (f32[128]{0:T(128)}, f32[128]{0:T(128)S(1)}, u32[]{:S(2)}) copy-start(f32[128]{0:T(128)S(1)} %get-tuple-element.52) | copy-start | bytes 1540
  25.1 2.4 %copy-start.36 = (f32[128]{0:T(128)}, f32[128]{0:T(128)S(1)}, u32[]{:S(2)}) copy-start(f32[128]{0:T(128)S(1)} %get-tuple-element.53) | copy-start | bytes 1540
  25.1 2.4 %copy-start.38 = (f32[128]{0:T(128)}, f32[128]{0:T(128)S(1)}, u32[]{:S(2)}) copy-start(f32[128]{0:T(128)S(1)} %get-tuple-element.54) | copy-start | bytes 1540
  25.1 2.4 %copy-start.40 = (f32[128]{0:T(128)}, f32[128]{0:T(128)S(1)}, u32[]{:S(2)}) copy-start(f32[128]{0:T(128)S(1)} %get-tuple-element.55) | copy-start | bytes 1540
  25.1 2.4 %copy-start.42 = (f32[128]{0:T(128)}, f32[128]{0:T(128)S(1)}, u32[]{:S(2)}) copy-start(f32[128]{0:T(128)S(1)} %get-tuple-element.56) | copy-start | bytes 1540
  25.1 2.4 %copy-start.44 = (f32[128]{0:T(128)}, f32[128]{0:T(128)S(1)}, u32[]{:S(2)}) copy-start(f32[128]{0:T(128)S(1)} %get-tuple-element.57) | copy-start | bytes 1540
  25.1 2.4 %copy-start.46 = (f32[128]{0:T(128)}, f32[128]{0:T(128)S(1)}, u32[]{:S(2)}) copy-start(f32[128]{0:T(128)S(1)} %get-tuple-element.58) | copy-start | bytes 1540
  25.2 2.7 %copy-start.11 = (f32[6,35,128]{2,0,1:T(8,128)}, f32[6,35,128]{2,0,1:T(8,128)S(1)}, u32[]{:S(2)}) copy-start(f32[6,35,128]{2,0,1:T(8,128)S(1)} %copy.197) | copy-start | bytes 322564
  28.5 3.3 %copy-start.48 = (f32[15,15]{1,0:T(8,128)S(1)}, f32[15,15]{1,0:T(8,128)}, u32[]{:S(2)}) copy-start(f32[15,15]{1,0:T(8,128)} %constant.63.clone) | copy-start | bytes 2704
  28.5 3.3 %copy-start.49 = (f32[15,15]{1,0:T(8,128)S(1)}, f32[15,15]{1,0:T(8,128)}, u32[]{:S(2)}) copy-start(f32[15,15]{1,0:T(8,128)} %constant.62.clone) | copy-start | bytes 2704
  28.5 3.3 %copy-start.50 = (f32[15,15]{1,0:T(8,128)S(1)}, f32[15,15]{1,0:T(8,128)}, u32[]{:S(2)}) copy-start(f32[15,15]{1,0:T(8,128)} %constant.61.clone) | copy-start | bytes 2704
  28.5 3.3 %copy-start.51 = (f32[15,15]{1,0:T(8,128)S(1)}, f32[15,15]{1,0:T(8,128)}, u32[]{:S(2)}) copy-start(f32[15,15]{1,0:T(8,128)} %constant.60.clone) | copy-start | bytes 2704
  28.5 3.3 %copy-start.52 = (f32[15,15]{1,0:T(8,128)S(1)}, f32[15,15]{1,0:T(8,128)}, u32[]{:S(2)}) copy-start(f32[15,15]{1,0:T(8,128)} %constant.59.clone) | copy-start | bytes 2704
  28.5 3.3 %copy-start.53 = (f32[15,15]{1,0:T(8,128)S(1)}, f32[15,15]{1,0:T(8,128)}, u32[]{:S(2)}) copy-start(f32[15,15]{1,0:T(8,128)} %constant.58.clone) | copy-start | bytes 2704
  33.1 3.2 %copy-start.56 = (f32[3,4,128]{2,1,0:T(4,128)S(1)}, f32[3,4,128]{2,1,0:T(4,128)}, u32[]{:S(2)}) copy-start(f32[3,4,128]{2,1,0:T(4,128)} %param.31) | copy-start | bytes 18436
  36.3 7.7 %copy-start.54 = (f32[3,4,128]{2,0,1:T(4,128)}, f32[3,4,128]{2,0,1:T(4,128)S(1)}, u32[]{:S(2)}) copy-start(f32[3,4,128]{2,0,1:T(4,128)S(1)} %copy.201) | copy-start | bytes 18436
  39.6 3.3 %copy-start.4 = (f32[60,13,128]{2,1,0:T(8,128)S(1)}, f32[60,13,128]{2,1,0:T(8,128)}, u32[]{:S(2)}) copy-start(f32[60,13,128]{2,1,0:T(8,128)} %copy-done.3) | copy-start | bytes 1198084
  42.9 1.1 %copy-start.20 = (f32[3,6,13,13]{3,2,1,0:T(8,128)S(1)}, f32[3,6,13,13]{3,2,1,0:T(8,128)}, u32[]{:S(2)}) copy-start(f32[3,6,13,13]{3,2,1,0:T(8,128)} %param.29) | copy-start | bytes 36508
  42.9 1.1 %copy-start.24 = (f32[60,6,128]{2,1,0:T(8,128)S(1)}, f32[60,6,128]{2,1,0:T(8,128)}, u32[]{:S(2)}) copy-start(f32[60,6,128]{2,1,0:T(8,128)} %copy.259) | copy-start | bytes 552964
  46.8 1.0 %copy-start.13 = (f32[13,35,128]{2,0,1:T(8,128)S(1)}, f32[13,35,128]{2,0,1:T(8,128)}, u32[]{:S(2)}) copy-start(f32[13,35,128]{2,0,1:T(8,128)} %fusion.5) | copy-start | bytes 698884
  49.3 6.2 %copy-start.8 = (pred[640,512]{1,0:T(32,128)(4,1)S(1)}, pred[640,512]{1,0:T(32,128)(4,1)}, u32[]{:S(2)}) copy-start(pred[640,512]{1,0:T(32,128)(4,1)} %copy-done.7) | copy-start | bytes 983044
  55.6 1.9 %copy-start.6 = (f32[13,15,512]{2,1,0:T(8,128)S(1)}, f32[13,15,512]{2,1,0:T(8,128)}, u32[]{:S(2)}) copy-start(f32[13,15,512]{2,1,0:T(8,128)} %reshape.370) | copy-start | bytes 1198084
  55.6 3.0 %copy-start.16 = (f32[3,35,35,1]{2,1,0,3:T(8,128)S(1)}, f32[3,35,35,1]{2,1,0,3:T(8,128)}, u32[]{:S(2)}) copy-start(f32[3,35,35,1]{2,1,0,3:T(8,128)} %constant.70) | copy-start | bytes 44104
  57.5 8.1 %copy-start.31 = (f32[128]{0:T(128)S(1)}, f32[128]{0:T(128)}, u32[]{:S(2)}) copy-start(f32[128]{0:T(128)} %copy-done.30) | copy-start | bytes 1540
  57.5 8.1 %copy-start.33 = (f32[128]{0:T(128)S(1)}, f32[128]{0:T(128)}, u32[]{:S(2)}) copy-start(f32[128]{0:T(128)} %copy-done.32) | copy-start | bytes 1540
  57.5 8.1 %copy-start.35 = (f32[128]{0:T(128)S(1)}, f32[128]{0:T(128)}, u32[]{:S(2)}) copy-start(f32[128]{0:T(128)} %copy-done.34) | copy-start | bytes 1540
  57.5 8.1 %copy-start.37 = (f32[128]{0:T(128)S(1)}, f32[128]{0:T(128)}, u32[]{:S(2)}) copy-start(f32[128]{0:T(128)} %copy-done.36) | copy-start | bytes 1540
  57.5 8.1 %copy-start.39 = (f32[128]{0:T(128)S(1)}, f32[128]{0:T(128)}, u32[]{:S(2)}) copy-start(f32[128]{0:T(128)} %copy-done.38) | copy-start | bytes 1540
  57.5 8.1 %copy-start.41 = (f32[128]{0:T(128)S(1)}, f32[128]{0:T(128)}, u32[]{:S(2)}) copy-start(f32[128]{0:T(128)} %copy-done.40) | copy-start | bytes 1540
  57.5 8.1 %copy-start.43 = (f32[128]{0:T(128)S(1)}, f32[128]{0:T(128)}, u32[]{:S(2)}) copy-start(f32[128]{0:T(128)} %copy-done.42) | copy-start | bytes 1540
  57.5 8.1 %copy-start.45 = (f32[128]{0:T(128)S(1)}, f32[128]{0:T(128)}, u32[]{:S(2)}) copy-start(f32[128]{0:T(128)} %copy-done.44) | copy-start | bytes 1540
  57.5 8.1 %copy-start.47 = (f32[128]{0:T(128)S(1)}, f32[128]{0:T(128)}, u32[]{:S(2)}) copy-start(f32[128]{0:T(128)} %copy-done.46) | copy-start | bytes 1540
  59.4 6.4 %copy-start.10 = (f32[13,35,128]{2,0,1:T(8,128)S(1)}, f32[13,35,128]{2,0,1:T(8,128)}, u32[]{:S(2)}) copy-start(f32[13,35,128]{2,0,1:T(8,128)} %copy.210) | copy-start | bytes 698884
  59.4 6.4 %copy-start.18 = (f32[3,13,35,128,1]{3,2,0,1,4:T(8,128)S(1)}, f32[3,13,35,128,1]{3,2,0,1,4:T(8,128)}, u32[]{:S(2)}) copy-start(f32[3,13,35,128,1]{3,2,0,1,4:T(8,128)} %maximum_bitcast_fusion.2) | copy-start | bytes 2096644
  59.4 6.4 %copy-start.21 = (f32[3,6,13,13]{3,2,1,0:T(8,128)S(1)}, f32[3,6,13,13]{3,2,1,0:T(8,128)}, u32[]{:S(2)}) copy-start(f32[3,6,13,13]{3,2,1,0:T(8,128)} %param.29) | copy-start | bytes 36508
  59.5 11.9 %collective-permute-start.2 = (f32[13,15,64]{2,1,0:T(8,128)S(1)}, f32[13,15,64]{2,1,0:T(8,128)S(1)}, u32[]{:S(2)}, u32[]{:S(2)}) collective-permute-start(f32[13,15,64]{2,1,0:T(8,128)S(1)} %get-tuple-element.47), channel_id=1, source_target_pairs={{0,1},{1,2},{2,3},{3,4},{4,5},{5,6},{6,7},{8,9},{9,10},{10,11},{11... | collective-permute-start | bytes 149768 | tf_op jit(solution)/shard_map/ppermute | solution.py:20
  64.2 7.6 %collective-permute-start.3 = (f32[13,15,64]{2,1,0:T(8,128)S(1)}, f32[13,15,64]{2,1,0:T(8,128)S(1)}, u32[]{:S(2)}, u32[]{:S(2)}) collective-permute-start(f32[13,15,64]{2,1,0:T(8,128)S(1)} %get-tuple-element.46), channel_id=1, source_target_pairs={{1,0},{2,1},{3,2},{4,3},{5,4},{6,5},{7,6},{9,8},{10,9},{11,10},{12... | collective-permute-start | bytes 149768 | tf_op jit(solution)/shard_map/ppermute | solution.py:21
  73.5 3.2 %copy-start.22 = (f32[3,6,13,13]{3,2,1,0:T(8,128)S(1)}, f32[3,6,13,13]{3,2,1,0:T(8,128)}, u32[]{:S(2)}) copy-start(f32[3,6,13,13]{3,2,1,0:T(8,128)} %param.29) | copy-start | bytes 36508
  73.5 3.2 %copy-start.55 = (f32[3,4,128]{2,0,1:T(4,128)S(1)}, f32[3,4,128]{2,0,1:T(4,128)}, u32[]{:S(2)}) copy-start(f32[3,4,128]{2,0,1:T(4,128)} %copy-done.54) | copy-start | bytes 18436
  75.5 1.3 %copy-start.25 = (f32[60,6,128]{2,1,0:T(8,128)S(1)}, f32[60,6,128]{2,1,0:T(8,128)}, u32[]{:S(2)}) copy-start(f32[60,6,128]{2,1,0:T(8,128)} %copy.259) | copy-start | bytes 552964
  80.4 1.1 %copy-start.17 = (f32[3,13,35,128,1]{3,2,0,1,4:T(8,128)S(1)}, f32[3,13,35,128,1]{3,2,0,1,4:T(8,128)}, u32[]{:S(2)}) copy-start(f32[3,13,35,128,1]{3,2,0,1,4:T(8,128)} %maximum_bitcast_fusion.3) | copy-start | bytes 2096644
  81.2 2.2 %copy-start.27 = (f32[6,35,128]{2,0,1:T(8,128)S(1)}, f32[6,35,128]{2,0,1:T(8,128)}, u32[]{:S(2)}) copy-start(f32[6,35,128]{2,0,1:T(8,128)} %fusion.3) | copy-start | bytes 322564
  84.6 14.3 %all-to-all-start = ((f32[32,1,60]{2,1,0:T(1,128)}), f32[32,1,60]{2,1,0:T(1,128)S(1)}, u32[]{:S(2)}, u32[]{:S(2)}) async-start(f32[32,1,60]{2,1,0:T(1,128)} %broadcast_in_dim.16), calls=%async_computation | async-start | bytes 32768 | tf_op jit(solution)/shard_map/all_to_all | solution.py:290
  92.9 6.5 %collective-permute-start.4 = (f32[6,35,64]{2,0,1:T(8,128)S(1)}, f32[6,35,64]{2,0,1:T(8,128)S(1)}, u32[]{:S(2)}, u32[]{:S(2)}) collective-permute-start(f32[6,35,64]{2,0,1:T(8,128)S(1)} %slice_select_fusion.1), channel_id=1, source_target_pairs={{0,16},{8,24},{16,0},{24,8},{1,17},{9,25},{17,1},{25,9},{2,18},{10... | collective-permute-start | bytes 161288 | tf_op jit(solution)/shard_map/ppermute | solution.py:160
  99.6 1.4 %collective-permute-start.5 = (f32[6,35,32]{2,0,1:T(8,128)S(1)}, f32[6,35,32]{2,0,1:T(8,128)S(1)}, u32[]{:S(2)}, u32[]{:S(2)}) collective-permute-start(f32[6,35,32]{2,0,1:T(8,128)S(1)} %slice_select_fusion), channel_id=1, source_target_pairs={{0,8},{8,0},{16,24},{24,16},{1,9},{9,1},{17,25},{25,17},{2,10},{10... | collective-permute-start | bytes 80648 | tf_op jit(solution)/shard_map/ppermute | solution.py:160
  (7 other events, 6.3 us)

commit v10 on v8

--- a/solution.py
+++ b/solution.py
@@ -7,6 +7,7 @@
 from jax.sharding import PartitionSpec as P
 
 HIGH = lax.Precision.HIGHEST
+MIX = lax.Precision.HIGH
 STEP_SIZE = 0.02
 
 
@@ -117,7 +118,7 @@
 
 
 def spatial_of(field, metric, derivs):
-    reference_grads = jnp.einsum("rab,fbe->rfae", derivs, field, precision=HIGH)
+    reference_grads = jnp.einsum("rab,fbe->rfae", derivs, field, precision=MIX)
     rows = []
     for direction_axis in range(3):
         total = metric[0, direction_axis] * reference_grads[0]
@@ -129,22 +130,22 @@
 
 def volume_term(adjoint, material, coupling, metric, derivs):
     spatial = spatial_of(adjoint, metric, derivs)
-    mixing = jnp.einsum("dpfg,dfae->pgae", coupling, spatial, precision=HIGH)
+    mixing = jnp.einsum("dpfg,dfae->pgae", coupling, spatial, precision=MIX)
     return jnp.sum(material[:, None] * mixing, axis=0)
 
 
 def kernel_term(adjoint, forward, coupling, metric, derivs):
     spatial = spatial_of(forward, metric, derivs)
-    mixing = jnp.einsum("dpfg,dgae->pfae", coupling, spatial, precision=HIGH)
+    mixing = jnp.einsum("dpfg,dgae->pfae", coupling, spatial, precision=MIX)
     return jnp.sum(mixing * adjoint[None], axis=1)
 
 
 def surface_term(jump_trace, face_material, face_normals, face_scale, coupling, lift_tables):
     weighted = face_normals[:, None, None] * jump_trace[None]
-    mixing = jnp.einsum("dpfg,dfnxe->pgnxe", coupling, weighted, precision=HIGH)
+    mixing = jnp.einsum("dpfg,dfnxe->pgnxe", coupling, weighted, precision=MIX)
     face_flux = 0.5 * jnp.sum(face_material[:, None] * mixing, axis=0) + 0.5 * jump_trace
     return jnp.einsum(
-        "xan,fnxe->fae", lift_tables, face_flux * face_scale[None, None], precision=HIGH
+        "xan,fnxe->fae", lift_tables, face_flux * face_scale[None, None], precision=MIX
     )
 
 

time: 88.9 us -> 82.4 us (0.927)
  matrix products: 24.2 us -> 17.3 us
    dot_general x10, matrix products: 17.5 us -> 11.1 us  [the longest x2 3.32 us: volume_term(): mixing = jnp.einsum('dpfg,dfae->pgae', coupling, spatial, precision=MIX)]
  transfers between devices with their start and end apart: 7 -> 7, of which waited for: 3 -> 4; matrix products, arithmetic and copies ran while one was open for 22% -> 20% of each run, Pallas kernels for 0% -> 0%
where the time goes in v10:
time: 82.4 us; the launch traced here: 81.8 us
  starting transfers between devices  21.9 us (27%)
  local copies, waits for them, and re-layouts  20.8 us (25%)
  matrix products  17.3 us (21%)
  waiting for transfers between devices  11.1 us (13%)
  other arithmetic  8.98 us (11%)
  between operations  1.76 us (2%)
    ppermute x2, starting transfers between devices, padded(): before = lax.ppermute(last, axis, up)  10.2 us
    unnamed x105, local copies, waits for them, and re-layouts  7.38 us
    all_to_all x1, starting transfers between devices, combine_sums(): lax.all_to_all(spread, ('shot', 'mesh'), 0, 0, tiled=False)  7.1 us
    all_to_all x1, waiting for transfers between devices, combine_sums(): lax.all_to_all(spread, ('shot', 'mesh'), 0, 0, tiled=False)  6.1 us
    ppermute x2, waiting for transfers between devices, halving_sum(): lax.ppermute(jnp.where(upper, low, high), axis, [(i, i ^ bit) for i in ra...  4.85 us
    dot_general x2, matrix products, volume_term(): mixing = jnp.einsum('dpfg,dfae->pgae', coupling, spatial, precision=MIX)  3.32 us
    gather x2, local copies, waits for them, and re-layouts, shards(): face_material = material[:, face_nodes.T, :]  3.23 us
    dot_general x2, matrix products, surface_term(): mixing = jnp.einsum('dpfg,dfnxe->pgnxe', coupling, weighted, precision=MIX)  2.98 us
  transfers between devices with their start and end apart: 7, of which 4 were waited for; matrix products, arithmetic and copies ran while one was open for 20% of the time, Pallas kernels for 0%

profile of v10, /device:TPU:0, one launch (start us, length us, event | category | flops | bytes accessed | tf_op | source)
XLA Modules:
  0.0 81.8 jit_solution(13320909179805876077)
XLA Ops:
  0.6 1.6 %constant_dynamic-slice_fusion = (f32[5,6,35,32]{3,2,1,0:T(8,128)S(1)}, f32[5,6,35,32]{3,2,1,0:T(8,128)S(1)}) fusion(f32[5,6,35,128]{3,2,1,0:T(8,128)} %param.37, s32[]{:T(128)S(6)} %select_n.37, f32[5,6,35,128]{3,2,1,0:T(8,128)} %param.36), kind=kLoop, calls=%fused_computation.266 | loop fusion | bytes 537604 | tf_op jit(solution)/shard_map/dynamic_slice | solution.py:255
  2.3 1.1 %copy.196 = f32[5,6,35,32]{2,3,1,0:T(8,128)} copy(f32[5,6,35,32]{3,2,1,0:T(8,128)S(1)} %get-tuple-element.8) | data formatting | bytes 268800 | tf_op jit(solution)/shard_map/dynamic_slice | solution.py:255
  3.5 0.5 copy.195
  4.0 1.0 %copy.308 = f32[1,13,35,128]{3,2,0,1:T(8,128)S(1)} copy(f32[1,13,35,128]{3,0,2,1:T(1,128)} %param.26) | data formatting | bytes 465920
  4.9 1.6 %multiply_reduce_fusion.2 = f32[10,5]{1,0:T(8,128)S(1)} fusion(f32[5,6,35,32]{2,3,1,0:T(8,128)} %copy.196, f32[10,6,35,32]{2,3,1,0:T(8,128)S(1)} %copy.195), kind=kLoop, calls=%fused_computation.5 | loop fusion | flops 671950 | bytes 403400 | tf_op jit(solution)/shard_map/reduce_sum | solution.py:260
  6.7 0.6 gather_fusion.1
  7.5 0.2 reshape.362
  7.7 0.4 fusion.35
  8.0 0.7 fusion.139
  8.8 5.5 %collective-permute-start = (f32[13,15,64]{2,1,0:T(8,128)}, f32[13,15,64]{2,1,0:T(8,128)}, u32[]{:S(2)}, u32[]{:S(2)}) collective-permute-start(f32[13,15,64]{2,1,0:T(8,128)} %get-tuple-element.47), channel_id=1, source_target_pairs={{0,1},{1,2},{2,3},{3,4},{4,5},{5,6},{6,7},{8,9},{9,10},{10,11},{11... | collective-permute-start | bytes 149768 | tf_op jit(solution)/shard_map/ppermute | solution.py:21
  14.3 1.5 %collective-permute-start.1 = (f32[13,15,64]{2,1,0:T(8,128)}, f32[13,15,64]{2,1,0:T(8,128)}, u32[]{:S(2)}, u32[]{:S(2)}) collective-permute-start(f32[13,15,64]{2,1,0:T(8,128)} %get-tuple-element.46), channel_id=1, source_target_pairs={{1,0},{2,1},{3,2},{4,3},{5,4},{6,5},{7,6},{9,8},{10,9},{11,10},{12... | collective-permute-start | bytes 149768 | tf_op jit(solution)/shard_map/ppermute | solution.py:22
  15.8 0.2 iota_compare_fusion
  16.1 0.6 fusion.27
  16.7 0.5 convolution_bitcast_fusion.3
  17.4 0.4 fusion.136
  17.7 0.5 convolution_bitcast_fusion.1
  18.5 0.5 convolution_bitcast_fusion
  19.3 0.7 copy-done.11
  20.0 1.7 %fusion.5 = f32[13,35,128]{2,0,1:T(8,128)} fusion(f32[3,13,35,128,1]{3,2,0,1,4:T(8,128)S(1)} %maximum_bitcast_fusion, f32[6,35,128]{2,0,1:T(8,128)S(1)} %copy.197, f32[3,6,13,13]{3,2,1,0:T(8,128)S(1)} %copy-done.11), kind=kOutput, calls=%fused_computation.17 | convolution fusion | flops 82409600 | bytes 1051528 | tf_op jit(solution)/shard_map/dpfg,dfae->pgae/dot_general | solution.py:133
  21.7 1.0 %maximum_bitcast_fusion.2 = f32[3,13,35,128,1]{3,2,0,1,4:T(8,128)} fusion(f32[1,13,35,128]{3,2,0,1:T(8,128)S(1)} %get-tuple-element.33, f32[1,13,35,128]{3,2,0,1:T(8,128)S(1)} %get-tuple-element.32, f32[1,13,35,128]{3,2,0,1:T(8,128)S(1)} %get-tuple-element.31), kind=kLoop, calls=%fused_computation.51 | loop fusion | flops 349440 | bytes 1397760 | tf_op jit(solution)/shard_map/stack | solution.py:128
  22.7 0.3 multiply_add_fusion
  23.0 1.0 %maximum_bitcast_fusion.3 = f32[3,13,35,128,1]{3,2,0,1,4:T(8,128)} fusion(f32[1,13,35,128]{3,2,0,1:T(8,128)S(1)} %get-tuple-element.30, f32[1,13,35,128]{3,2,0,1:T(8,128)S(1)} %get-tuple-element.29, f32[1,13,35,128]{3,2,0,1:T(8,128)S(1)} %get-tuple-element.28), kind=kLoop, calls=%fused_computation.52 | loop fusion | flops 349440 | bytes 1397760 | tf_op jit(solution)/shard_map/stack | solution.py:128
  23.9 1.5 %gather_fusion = f32[60,6,128]{2,0,1:T(8,128)} fusion(f32[6,35,128]{2,1,0:T(8,128)S(1)} %copy-done, s32[1024]{0:T(1024)S(1)} %pad_clamp_fusion), kind=kCustom, calls=%fused_computation | custom fusion | bytes 368880 | tf_op jit(solution)/shard_map/gather | solution.py:232
  25.4 1.7 %copy.259 = f32[60,6,128]{2,1,0:T(8,128)} copy(f32[60,6,128]{2,0,1:T(8,128)} %gather_fusion) | data formatting | bytes 368640 | tf_op jit(solution)/shard_map/gather | solution.py:232
  27.2 1.2 %convolution_add_fusion.3 = f32[13,15,512]{2,1,0:T(8,128)S(1)} fusion(f32[13,15,512]{2,1,0:T(8,128)S(1)} %fusion.27, f32[13,15,64]{2,1,0:T(8,128)} %collective-permute-done, pred[640,512]{1,0:T(32,128)(4,1)S(1)} %iota_compare_fusion), kind=kOutput, calls=%fused_computation.35 | convolution fusion | flops 76776960 | bytes 908032 | tf_op jit(solution)/shard_map/fns,sj->fnj/dot_general | solution.py:271
  28.4 1.2 %convolution_add_fusion.2 = f32[13,15,512]{2,1,0:T(8,128)S(1)} fusion(f32[13,15,512]{2,1,0:T(8,128)S(1)} %convolution_add_fusion.3, f32[13,15,64]{2,1,0:T(8,128)} %collective-permute-done.1, pred[640,512]{1,0:T(32,128)(4,1)S(1)} %iota_compare_fusion), kind=kOutput, calls=%fused_computation.34 | convolution fusion | flops 76776960 | bytes 908032 | tf_op jit(solution)/shard_map/fns,sj->fnj/dot_general | solution.py:274
  29.7 0.6 multiply_reduce_fusion.1
  30.3 0.9 %reshape.363 = f32[13,15,4,128]{3,2,1,0:T(4,128)} reshape(f32[13,15,512]{2,1,0:T(8,128)S(1)} %multiply_reduce_fusion.1) | data formatting | bytes 798720 | tf_op jit(solution)/shard_map/reshape | solution.py:278
  31.2 1.1 %copy_subtract_fusion.1 = f32[13,15,4,128]{3,0,2,1:T(8,128)S(1)} fusion(f32[13,15,4,128]{3,0,2,1:T(8,128)S(1)} %bitcast.776, f32[13,15,4,128]{3,2,1,0:T(4,128)} %reshape.363), kind=kLoop, calls=%fused_computation.60 | loop fusion | flops 99840 | bytes 1198080 | tf_op jit(solution)/shard_map/sub | solution.py:278
  32.4 1.5 %fusion.1 = f32[13,15,4,128]{3,0,2,1:T(8,128)S(1)} fusion(f32[6,15,4,128]{3,0,2,1:T(8,128)S(1)} %bitcast.792, f32[13,15,4,128]{3,0,2,1:T(8,128)S(1)} %copy_subtract_fusion.1, f32[3,4,128]{2,0,1:T(4,128)S(1)} %copy.201, f32[3,6,13,13]{3,2,1,0:T(8,128)S(1)} %copy-done.12), kind=kOutput, calls=%fused_computation.9 | convolution fusion | flops 141573120 | bytes 1001352 | tf_op jit(solution)/shard_map/dpfg,dfnxe->pgnxe/dot_general | solution.py:145
  34.0 0.9 %copy-done.5 = f32[13,35,128]{2,0,1:T(8,128)S(1)} copy-done((f32[13,35,128]{2,0,1:T(8,128)S(1)}, f32[13,35,128]{2,0,1:T(8,128)}, u32[]{:S(2)}) %copy-start.5) | copy-done | bytes 232984
  34.8 0.6 fusion.14
  35.5 0.6 gather_fusion.2
  36.2 0.9 %copy.211 = f32[13,15,4,128]{3,2,1,0:T(4,128)} copy(f32[13,15,4,128]{3,0,2,1:T(8,128)S(1)} %bitcast.777) | data formatting | bytes 798720 | tf_op jit(solution)/shard_map/gather | solution.py:266
  37.1 1.2 %reshape.364 = f32[13,15,512]{2,1,0:T(8,128)S(1)} reshape(f32[13,15,4,128]{3,2,1,0:T(4,128)} %copy.211) | data formatting | bytes 798720 | tf_op jit(solution)/shard_map/reshape | solution.py:267
  38.3 0.6 fusion.26
  39.0 0.4 fusion.33
  39.3 0.5 convolution_bitcast_fusion.2
  39.9 4.7 %collective-permute-start.2 = (f32[13,15,64]{2,1,0:T(8,128)S(1)}, f32[13,15,64]{2,1,0:T(8,128)S(1)}, u32[]{:S(2)}, u32[]{:S(2)}) collective-permute-start(f32[13,15,64]{2,1,0:T(8,128)S(1)} %get-tuple-element.45), channel_id=1, source_target_pairs={{0,1},{1,2},{2,3},{3,4},{4,5},{5,6},{6,7},{8,9},{9,10},{10,11},{11... | collective-permute-start | bytes 149768 | tf_op jit(solution)/shard_map/ppermute | solution.py:21
  44.6 1.5 %collective-permute-start.3 = (f32[13,15,64]{2,1,0:T(8,128)S(1)}, f32[13,15,64]{2,1,0:T(8,128)S(1)}, u32[]{:S(2)}, u32[]{:S(2)}) collective-permute-start(f32[13,15,64]{2,1,0:T(8,128)S(1)} %get-tuple-element.44), channel_id=1, source_target_pairs={{1,0},{2,1},{3,2},{4,3},{5,4},{6,5},{7,6},{9,8},{10,9},{11,10},{12... | collective-permute-start | bytes 149768 | tf_op jit(solution)/shard_map/ppermute | solution.py:22
  46.4 1.8 %fusion.3 = f32[6,35,128]{2,0,1:T(8,128)} fusion(f32[3,13,35,128,1]{3,2,0,1,4:T(8,128)S(1)} %copy-done.10, f32[13,35,128]{2,0,1:T(8,128)S(1)} %copy-done.2, f32[3,6,13,13]{3,2,1,0:T(8,128)S(1)} %copy-done.13), kind=kOutput, calls=%fused_computation.13 | convolution fusion | flops 82440960 | bytes 1051528 | tf_op jit(solution)/shard_map/dpfg,dgae->pfae/dot_general | solution.py:139
  48.3 0.8 %copy-done.4 = f32[6,35,128]{2,0,1:T(8,128)S(1)} copy-done((f32[6,35,128]{2,0,1:T(8,128)S(1)}, f32[6,35,128]{2,0,1:T(8,128)}, u32[]{:S(2)}) %copy-start.4) | copy-done | bytes 107544
  49.1 1.7 %fusion.4 = f32[13,35,128]{2,0,1:T(8,128)} fusion(f32[3,13,35,128,1]{3,2,0,1,4:T(8,128)S(1)} %maximum_bitcast_fusion.1, f32[6,35,128]{2,0,1:T(8,128)S(1)} %copy-done.4, f32[3,6,13,13]{3,2,1,0:T(8,128)S(1)} %copy-done.13), kind=kOutput, calls=%fused_computation.15 | convolution fusion | flops 82409600 | bytes 1051528 | tf_op jit(solution)/shard_map/dpfg,dfae->pgae/dot_general | solution.py:133
  50.7 0.3 convolution_add_fusion.1
  51.1 0.2 collective-permute-done.3
  51.2 0.3 convolution_add_fusion
  51.6 0.6 multiply_reduce_fusion
  52.5 0.6 copy-done.14
  53.2 1.5 %fusion = f32[13,15,4,128]{3,0,2,1:T(8,128)S(1)} fusion(f32[6,15,4,128]{3,0,2,1:T(8,128)S(1)} %bitcast.793, f32[13,15,4,128]{3,0,2,1:T(8,128)S(1)} %copy_subtract_fusion, f32[3,4,128]{2,0,1:T(4,128)S(1)} %copy-done.41, f32[3,6,13,13]{3,2,1,0:T(8,128)S(1)} %copy-done.14), kind=kOutput, calls=%fused_computation.7 | convolution fusion | flops 141573120 | bytes 1001352 | tf_op jit(solution)/shard_map/dpfg,dfnxe->pgnxe/dot_general | solution.py:145
  54.8 0.9 %copy-done.6 = f32[13,35,128]{2,0,1:T(8,128)S(1)} copy-done((f32[13,35,128]{2,0,1:T(8,128)S(1)}, f32[13,35,128]{2,0,1:T(8,128)}, u32[]{:S(2)}) %copy-start.6) | copy-done | bytes 232984
  55.7 0.6 fusion.17
  56.4 0.5 copy-done.9
  56.8 1.1 %fusion.2 = f32[6,35,128]{2,0,1:T(8,128)S(1)} fusion(f32[3,13,35,128,1]{3,2,0,1,4:T(8,128)S(1)} %copy-done.9, f32[13,35,128]{2,0,1:T(8,128)S(1)} %copy.225, f32[3,6,13,13]{3,2,1,0:T(8,128)S(1)} %copy-done.14), kind=kOutput, calls=%fused_computation.11 | convolution fusion | flops 82440960 | bytes 1051528 | tf_op jit(solution)/shard_map/dpfg,dgae->pfae/dot_general | solution.py:139
  58.1 1.6 %collective-permute-start.4 = (f32[6,35,64]{2,0,1:T(8,128)S(1)}, f32[6,35,64]{2,0,1:T(8,128)S(1)}, u32[]{:S(2)}, u32[]{:S(2)}) collective-permute-start(f32[6,35,64]{2,0,1:T(8,128)S(1)} %slice_select_fusion.1), channel_id=1, source_target_pairs={{0,16},{8,24},{16,0},{24,8},{1,17},{9,25},{17,1},{25,9},{2,18},{10... | collective-permute-start | bytes 161288 | tf_op jit(solution)/shard_map/ppermute | solution.py:161
  59.7 3.6 %collective-permute-done.4 = f32[6,35,64]{2,0,1:T(8,128)S(1)} collective-permute-done((f32[6,35,64]{2,0,1:T(8,128)S(1)}, f32[6,35,64]{2,0,1:T(8,128)S(1)}, u32[]{:S(2)}, u32[]{:S(2)}) %collective-permute-start.4) | collective-permute-done | bytes 53792 | tf_op jit(solution)/shard_map/ppermute | solution.py:161
  63.6 1.3 %collective-permute-done.5 = f32[6,35,32]{2,0,1:T(8,128)S(1)} collective-permute-done((f32[6,35,32]{2,0,1:T(8,128)S(1)}, f32[6,35,32]{2,0,1:T(8,128)S(1)}, u32[]{:S(2)}, u32[]{:S(2)}) %collective-permute-start.5) | collective-permute-done | bytes 26912 | tf_op jit(solution)/shard_map/ppermute | solution.py:161
  65.0 0.3 fusion.11
  65.4 0.6 broadcast_in_dim.16
  66.0 7.1 %all-to-all-start = ((f32[32,1,60]{2,1,0:T(1,128)}), f32[32,1,60]{2,1,0:T(1,128)S(1)}, u32[]{:S(2)}, u32[]{:S(2)}) async-start(f32[32,1,60]{2,1,0:T(1,128)} %broadcast_in_dim.16), calls=%async_computation | async-start | bytes 32768 | tf_op jit(solution)/shard_map/all_to_all | solution.py:290
  73.2 0.9 %copy.229 = f32[1,13,35,128]{3,0,2,1:T(1,128)} copy(f32[1,13,35,128]{3,2,1,0:T(8,128)S(1)} %bitcast.779) | data formatting | bytes 465920
  74.1 6.1 %all-to-all-done = f32[32,1,60]{2,1,0:T(1,128)S(1)} async-done(((f32[32,1,60]{2,1,0:T(1,128)}), f32[32,1,60]{2,1,0:T(1,128)S(1)}, u32[]{:S(2)}, u32[]{:S(2)}) %all-to-all-start) | async-done | bytes 7712 | tf_op jit(solution)/shard_map/all_to_all | solution.py:290
  80.6 0.2 slice_reduce_fusion
  80.8 0.2 fusion.10
  81.1 0.8 copy.230
  (145 shorter events, 3.2 us)
Async XLA Ops:
  3.9 2.6 %copy-start.49 = (s32[60]{0:T(128)S(1)}, s32[60]{0:T(128)}, u32[]{:S(2)}) copy-start(s32[60]{0:T(128)} %constant.67) | copy-start | bytes 724
  6.6 1.0 %copy-start.45 = (s32[128]{0:T(128)S(1)}, s32[128]{0:T(128)}, u32[]{:S(2)}) copy-start(s32[128]{0:T(128)} %param.35) | copy-start | bytes 1540
  7.3 8.5 %copy-start.47 = (s32[4,128]{1,0:T(4,128)S(1)}, s32[4,128]{1,0:T(4,128)}, u32[]{:S(2)}) copy-start(s32[4,128]{1,0:T(4,128)} %param.34) | copy-start | bytes 6148
  7.3 8.5 %copy-start.44 = (s32[4,128]{1,0:T(4,128)S(1)}, s32[4,128]{1,0:T(4,128)}, u32[]{:S(2)}) copy-start(s32[4,128]{1,0:T(4,128)} %param.33) | copy-start | bytes 6148
  7.7 9.0 %copy-start.48 = (f32[4,128]{1,0:T(4,128)S(1)}, f32[4,128]{1,0:T(4,128)}, u32[]{:S(2)}) copy-start(f32[4,128]{1,0:T(4,128)} %param.32) | copy-start | bytes 6148
  7.7 9.0 %copy-start.7 = (f32[3,35,35,1]{2,1,0,3:T(8,128)S(1)}, f32[3,35,35,1]{2,1,0,3:T(8,128)}, u32[]{:S(2)}) copy-start(f32[3,35,35,1]{2,1,0,3:T(8,128)} %constant.70) | copy-start | bytes 44104
  8.8 18.4 %collective-permute-start = (f32[13,15,64]{2,1,0:T(8,128)}, f32[13,15,64]{2,1,0:T(8,128)}, u32[]{:S(2)}, u32[]{:S(2)}) collective-permute-start(f32[13,15,64]{2,1,0:T(8,128)} %get-tuple-element.47), channel_id=1, source_target_pairs={{0,1},{1,2},{2,3},{3,4},{4,5},{5,6},{6,7},{8,9},{9,10},{10,11},{11... | collective-permute-start | bytes 149768 | tf_op jit(solution)/shard_map/ppermute | solution.py:21
  14.3 14.1 %collective-permute-start.1 = (f32[13,15,64]{2,1,0:T(8,128)}, f32[13,15,64]{2,1,0:T(8,128)}, u32[]{:S(2)}, u32[]{:S(2)}) collective-permute-start(f32[13,15,64]{2,1,0:T(8,128)} %get-tuple-element.46), channel_id=1, source_target_pairs={{1,0},{2,1},{3,2},{4,3},{5,4},{6,5},{7,6},{9,8},{10,9},{11,10},{12... | collective-permute-start | bytes 149768 | tf_op jit(solution)/shard_map/ppermute | solution.py:22
  15.8 1.4 %copy-start.43 = (f32[3,3,128]{2,1,0:T(4,128)S(1)}, f32[3,3,128]{2,1,0:T(4,128)}, u32[]{:S(2)}) copy-start(f32[3,3,128]{2,1,0:T(4,128)} %param.30) | copy-start | bytes 13828
  15.8 1.4 %copy-start = (f32[6,35,128]{2,1,0:T(8,128)S(1)}, f32[6,35,128]{2,1,0:T(8,128)}, u32[]{:S(2)}) copy-start(f32[6,35,128]{2,1,0:T(8,128)} %param.28) | copy-start | bytes 322564
  16.0 1.3 %copy-start.15 = (f32[1,2,13,35,128]{4,1,3,2,0:T(2,128)S(1)}, f32[1,2,13,35,128]{4,1,3,2,0:T(2,128)}, u32[]{:S(2)}) copy-start(f32[1,2,13,35,128]{4,1,3,2,0:T(2,128)} %param.27) | copy-start | bytes 1397764
  17.2 1.8 %copy-start.20 = (f32[128]{0:T(128)}, f32[128]{0:T(128)S(1)}, u32[]{:S(2)}) copy-start(f32[128]{0:T(128)S(1)} %get-tuple-element.50) | copy-start | bytes 1540
  17.2 1.8 %copy-start.22 = (f32[128]{0:T(128)}, f32[128]{0:T(128)S(1)}, u32[]{:S(2)}) copy-start(f32[128]{0:T(128)S(1)} %get-tuple-element.51) | copy-start | bytes 1540
  17.2 1.8 %copy-start.24 = (f32[128]{0:T(128)}, f32[128]{0:T(128)S(1)}, u32[]{:S(2)}) copy-start(f32[128]{0:T(128)S(1)} %get-tuple-element.52) | copy-start | bytes 1540
  17.3 1.8 %copy-start.26 = (f32[128]{0:T(128)}, f32[128]{0:T(128)S(1)}, u32[]{:S(2)}) copy-start(f32[128]{0:T(128)S(1)} %get-tuple-element.53) | copy-start | bytes 1540
  17.3 1.8 %copy-start.28 = (f32[128]{0:T(128)}, f32[128]{0:T(128)S(1)}, u32[]{:S(2)}) copy-start(f32[128]{0:T(128)S(1)} %get-tuple-element.54) | copy-start | bytes 1540
  17.3 1.8 %copy-start.30 = (f32[128]{0:T(128)}, f32[128]{0:T(128)S(1)}, u32[]{:S(2)}) copy-start(f32[128]{0:T(128)S(1)} %get-tuple-element.55) | copy-start | bytes 1540
  17.3 1.8 %copy-start.32 = (f32[128]{0:T(128)}, f32[128]{0:T(128)S(1)}, u32[]{:S(2)}) copy-start(f32[128]{0:T(128)S(1)} %get-tuple-element.56) | copy-start | bytes 1540
  17.3 1.9 %copy-start.3 = (f32[6,35,128]{2,0,1:T(8,128)}, f32[6,35,128]{2,0,1:T(8,128)S(1)}, u32[]{:S(2)}) copy-start(f32[6,35,128]{2,0,1:T(8,128)S(1)} %copy.197) | copy-start | bytes 322564
  19.0 0.9 %copy-start.11 = (f32[3,6,13,13]{3,2,1,0:T(8,128)S(1)}, f32[3,6,13,13]{3,2,1,0:T(8,128)}, u32[]{:S(2)}) copy-start(f32[3,6,13,13]{3,2,1,0:T(8,128)} %param.29) | copy-start | bytes 36508
  20.0 2.7 %copy-start.34 = (f32[15,15]{1,0:T(8,128)S(1)}, f32[15,15]{1,0:T(8,128)}, u32[]{:S(2)}) copy-start(f32[15,15]{1,0:T(8,128)} %constant.63.clone) | copy-start | bytes 2704
  20.0 2.7 %copy-start.35 = (f32[15,15]{1,0:T(8,128)S(1)}, f32[15,15]{1,0:T(8,128)}, u32[]{:S(2)}) copy-start(f32[15,15]{1,0:T(8,128)} %constant.62.clone) | copy-start | bytes 2704
  20.0 2.7 %copy-start.36 = (f32[15,15]{1,0:T(8,128)S(1)}, f32[15,15]{1,0:T(8,128)}, u32[]{:S(2)}) copy-start(f32[15,15]{1,0:T(8,128)} %constant.61.clone) | copy-start | bytes 2704
  20.0 2.7 %copy-start.37 = (f32[15,15]{1,0:T(8,128)S(1)}, f32[15,15]{1,0:T(8,128)}, u32[]{:S(2)}) copy-start(f32[15,15]{1,0:T(8,128)} %constant.60.clone) | copy-start | bytes 2704
  20.0 2.7 %copy-start.38 = (f32[15,15]{1,0:T(8,128)S(1)}, f32[15,15]{1,0:T(8,128)}, u32[]{:S(2)}) copy-start(f32[15,15]{1,0:T(8,128)} %constant.59.clone) | copy-start | bytes 2704
  20.0 2.7 %copy-start.39 = (f32[15,15]{1,0:T(8,128)S(1)}, f32[15,15]{1,0:T(8,128)}, u32[]{:S(2)}) copy-start(f32[15,15]{1,0:T(8,128)} %constant.58.clone) | copy-start | bytes 2704
  23.9 3.2 %copy-start.42 = (f32[3,4,128]{2,1,0:T(4,128)S(1)}, f32[3,4,128]{2,1,0:T(4,128)}, u32[]{:S(2)}) copy-start(f32[3,4,128]{2,1,0:T(4,128)} %param.31) | copy-start | bytes 18436
  27.2 5.2 %copy-start.40 = (f32[3,4,128]{2,0,1:T(4,128)}, f32[3,4,128]{2,0,1:T(4,128)S(1)}, u32[]{:S(2)}) copy-start(f32[3,4,128]{2,0,1:T(4,128)S(1)} %copy.201) | copy-start | bytes 18436
  31.2 1.2 %copy-start.12 = (f32[3,6,13,13]{3,2,1,0:T(8,128)S(1)}, f32[3,6,13,13]{3,2,1,0:T(8,128)}, u32[]{:S(2)}) copy-start(f32[3,6,13,13]{3,2,1,0:T(8,128)} %param.29) | copy-start | bytes 36508
  31.2 1.2 %copy-start.16 = (f32[60,6,128]{2,1,0:T(8,128)S(1)}, f32[60,6,128]{2,1,0:T(8,128)}, u32[]{:S(2)}) copy-start(f32[60,6,128]{2,1,0:T(8,128)} %copy.259) | copy-start | bytes 552964
  33.8 1.0 %copy-start.5 = (f32[13,35,128]{2,0,1:T(8,128)S(1)}, f32[13,35,128]{2,0,1:T(8,128)}, u32[]{:S(2)}) copy-start(f32[13,35,128]{2,0,1:T(8,128)} %fusion.5) | copy-start | bytes 698884
  33.9 1.0 %copy-start.19 = (f32[4,35,15,1]{1,2,0,3:T(8,128)S(1)}, f32[4,35,15,1]{1,2,0,3:T(8,128)}, u32[]{:S(2)}) copy-start(f32[4,35,15,1]{1,2,0,3:T(8,128)} %constant.71) | copy-start | bytes 25204
  35.5 0.7 copy-start.1
  36.2 2.7 %copy-start.46 = (s32[128]{0:T(128)S(1)}, s32[128]{0:T(128)}, u32[]{:S(2)}) copy-start(s32[128]{0:T(128)} %param.35) | copy-start | bytes 1540
  37.1 2.2 %copy-start.8 = (f32[3,35,35,1]{2,1,0,3:T(8,128)S(1)}, f32[3,35,35,1]{2,1,0,3:T(8,128)}, u32[]{:S(2)}) copy-start(f32[3,35,35,1]{2,1,0,3:T(8,128)} %constant.70) | copy-start | bytes 44104
  38.9 7.3 %copy-start.21 = (f32[128]{0:T(128)S(1)}, f32[128]{0:T(128)}, u32[]{:S(2)}) copy-start(f32[128]{0:T(128)} %copy-done.20) | copy-start | bytes 1540
  38.9 7.3 %copy-start.23 = (f32[128]{0:T(128)S(1)}, f32[128]{0:T(128)}, u32[]{:S(2)}) copy-start(f32[128]{0:T(128)} %copy-done.22) | copy-start | bytes 1540
  38.9 7.3 %copy-start.25 = (f32[128]{0:T(128)S(1)}, f32[128]{0:T(128)}, u32[]{:S(2)}) copy-start(f32[128]{0:T(128)} %copy-done.24) | copy-start | bytes 1540
  38.9 7.3 %copy-start.27 = (f32[128]{0:T(128)S(1)}, f32[128]{0:T(128)}, u32[]{:S(2)}) copy-start(f32[128]{0:T(128)} %copy-done.26) | copy-start | bytes 1540
  38.9 7.3 %copy-start.29 = (f32[128]{0:T(128)S(1)}, f32[128]{0:T(128)}, u32[]{:S(2)}) copy-start(f32[128]{0:T(128)} %copy-done.28) | copy-start | bytes 1540
  38.9 7.3 %copy-start.31 = (f32[128]{0:T(128)S(1)}, f32[128]{0:T(128)}, u32[]{:S(2)}) copy-start(f32[128]{0:T(128)} %copy-done.30) | copy-start | bytes 1540
  38.9 7.3 %copy-start.33 = (f32[128]{0:T(128)S(1)}, f32[128]{0:T(128)}, u32[]{:S(2)}) copy-start(f32[128]{0:T(128)} %copy-done.32) | copy-start | bytes 1540
  39.8 6.6 %copy-start.2 = (f32[13,35,128]{2,0,1:T(8,128)S(1)}, f32[13,35,128]{2,0,1:T(8,128)}, u32[]{:S(2)}) copy-start(f32[13,35,128]{2,0,1:T(8,128)} %copy-done.1) | copy-start | bytes 698884
  39.8 6.6 %copy-start.10 = (f32[3,13,35,128,1]{3,2,0,1,4:T(8,128)S(1)}, f32[3,13,35,128,1]{3,2,0,1,4:T(8,128)}, u32[]{:S(2)}) copy-start(f32[3,13,35,128,1]{3,2,0,1,4:T(8,128)} %maximum_bitcast_fusion.2) | copy-start | bytes 2096644
  39.8 6.6 %copy-start.13 = (f32[3,6,13,13]{3,2,1,0:T(8,128)S(1)}, f32[3,6,13,13]{3,2,1,0:T(8,128)}, u32[]{:S(2)}) copy-start(f32[3,6,13,13]{3,2,1,0:T(8,128)} %param.29) | copy-start | bytes 36508
  39.9 10.8 %collective-permute-start.2 = (f32[13,15,64]{2,1,0:T(8,128)S(1)}, f32[13,15,64]{2,1,0:T(8,128)S(1)}, u32[]{:S(2)}, u32[]{:S(2)}) collective-permute-start(f32[13,15,64]{2,1,0:T(8,128)S(1)} %get-tuple-element.45), channel_id=1, source_target_pairs={{0,1},{1,2},{2,3},{3,4},{4,5},{5,6},{6,7},{8,9},{9,10},{10,11},{11... | collective-permute-start | bytes 149768 | tf_op jit(solution)/shard_map/ppermute | solution.py:21
  44.6 6.6 %collective-permute-start.3 = (f32[13,15,64]{2,1,0:T(8,128)S(1)}, f32[13,15,64]{2,1,0:T(8,128)S(1)}, u32[]{:S(2)}, u32[]{:S(2)}) collective-permute-start(f32[13,15,64]{2,1,0:T(8,128)S(1)} %get-tuple-element.44), channel_id=1, source_target_pairs={{1,0},{2,1},{3,2},{4,3},{5,4},{6,5},{7,6},{9,8},{10,9},{11,10},{12... | collective-permute-start | bytes 149768 | tf_op jit(solution)/shard_map/ppermute | solution.py:22
  48.2 0.9 %copy-start.4 = (f32[6,35,128]{2,0,1:T(8,128)S(1)}, f32[6,35,128]{2,0,1:T(8,128)}, u32[]{:S(2)}) copy-start(f32[6,35,128]{2,0,1:T(8,128)} %copy-done.3) | copy-start | bytes 322564
  52.2 0.9 %copy-start.14 = (f32[3,6,13,13]{3,2,1,0:T(8,128)S(1)}, f32[3,6,13,13]{3,2,1,0:T(8,128)}, u32[]{:S(2)}) copy-start(f32[3,6,13,13]{3,2,1,0:T(8,128)} %param.29) | copy-start | bytes 36508
  52.2 1.0 %copy-start.17 = (f32[60,6,128]{2,1,0:T(8,128)S(1)}, f32[60,6,128]{2,1,0:T(8,128)}, u32[]{:S(2)}) copy-start(f32[60,6,128]{2,1,0:T(8,128)} %copy.259) | copy-start | bytes 552964
  52.2 1.0 %copy-start.41 = (f32[3,4,128]{2,0,1:T(4,128)S(1)}, f32[3,4,128]{2,0,1:T(4,128)}, u32[]{:S(2)}) copy-start(f32[3,4,128]{2,0,1:T(4,128)} %copy-done.40) | copy-start | bytes 18436
  54.7 1.0 %copy-start.6 = (f32[13,35,128]{2,0,1:T(8,128)S(1)}, f32[13,35,128]{2,0,1:T(8,128)}, u32[]{:S(2)}) copy-start(f32[13,35,128]{2,0,1:T(8,128)} %fusion.4) | copy-start | bytes 698884
  55.7 1.1 %copy-start.9 = (f32[3,13,35,128,1]{3,2,0,1,4:T(8,128)S(1)}, f32[3,13,35,128,1]{3,2,0,1,4:T(8,128)}, u32[]{:S(2)}) copy-start(f32[3,13,35,128,1]{3,2,0,1,4:T(8,128)} %maximum_bitcast_fusion.3) | copy-start | bytes 2096644
  56.3 1.6 %copy-start.18 = (f32[6,35,128]{2,0,1:T(8,128)S(1)}, f32[6,35,128]{2,0,1:T(8,128)}, u32[]{:S(2)}) copy-start(f32[6,35,128]{2,0,1:T(8,128)} %fusion.3) | copy-start | bytes 322564
  58.1 5.2 %collective-permute-start.4 = (f32[6,35,64]{2,0,1:T(8,128)S(1)}, f32[6,35,64]{2,0,1:T(8,128)S(1)}, u32[]{:S(2)}, u32[]{:S(2)}) collective-permute-start(f32[6,35,64]{2,0,1:T(8,128)S(1)} %slice_select_fusion.1), channel_id=1, source_target_pairs={{0,16},{8,24},{16,0},{24,8},{1,17},{9,25},{17,1},{25,9},{2,18},{10... | collective-permute-start | bytes 161288 | tf_op jit(solution)/shard_map/ppermute | solution.py:161
  63.5 1.4 %collective-permute-start.5 = (f32[6,35,32]{2,0,1:T(8,128)S(1)}, f32[6,35,32]{2,0,1:T(8,128)S(1)}, u32[]{:S(2)}, u32[]{:S(2)}) collective-permute-start(f32[6,35,32]{2,0,1:T(8,128)S(1)} %slice_select_fusion), channel_id=1, source_target_pairs={{0,8},{8,0},{16,24},{24,16},{1,9},{9,1},{17,25},{25,17},{2,10},{10... | collective-permute-start | bytes 80648 | tf_op jit(solution)/shard_map/ppermute | solution.py:161
  66.0 14.2 %all-to-all-start = ((f32[32,1,60]{2,1,0:T(1,128)}), f32[32,1,60]{2,1,0:T(1,128)S(1)}, u32[]{:S(2)}, u32[]{:S(2)}) async-start(f32[32,1,60]{2,1,0:T(1,128)} %broadcast_in_dim.16), calls=%async_computation | async-start | bytes 32768 | tf_op jit(solution)/shard_map/all_to_all | solution.py:290

commit v11 on v10

--- a/solution.py
+++ b/solution.py
@@ -229,7 +229,10 @@
     border = send_faces.shape[0] // 2
     slot_count = 4 * elements + 2 * border
     adjoint = adjoint_state[0]
-    face_material = material[:, face_nodes.T, :]
+    node_select = jnp.asarray(np.eye(node_count, dtype=np.float32)[face_nodes.T.reshape(-1)])
+    face_material = jnp.einsum(
+        "ma,pae->pme", node_select, material, precision=HIGH
+    ).reshape(params, face_width, 4, elements)
     neighbours = face_neighbours.reshape(-1)
     orient = face_orientation.reshape(-1)
     face_total = 4 * elements
@@ -263,7 +266,9 @@
     )
     gradient = jnp.zeros((params, node_count, elements), jnp.float32)
     for step_index in range(forward_states.shape[1]):
-        inner_trace = adjoint[:, face_nodes.T, :]
+        inner_trace = jnp.einsum(
+            "ma,fae->fme", node_select, adjoint, precision=HIGH
+        ).reshape(fields, face_width, 4, elements)
         flat_trace = inner_trace.reshape(fields, face_width, 4 * elements)
         sent_traces = jnp.einsum("fns,sj->fnj", flat_trace, send_pick, precision=HIGH)
         extended = padded(sent_traces, (("mesh", 2),), border)

time: 82.4 us -> 85.4 us (1.036)
  waiting for transfers between devices: 11.1 us -> 15.9 us
  local copies, waits for them, and re-layouts: 20.8 us -> 16.4 us
  matrix products: 17.3 us -> 20.6 us
  starting transfers between devices: 21.9 us -> 20.8 us
    gather x6 -> x0, local copies, waits for them, and re-layouts: 5.54 us -> none  [the longest x2 3.23 us: shards(): face_material = material[:, face_nodes.T, :]]
    ppermute x2, waiting for transfers between devices: 0.16 us -> 4.95 us  [padded(): after = lax.ppermute(first, axis, down)]
    dot_general x0 -> x3, matrix products: none -> 1.46 us  [the longest x2 1.09 us: shards(): jnp.einsum('ma,fae->fme', node_select, adjoint, precision=HIGH)]
    reshape x2, local copies, waits for them, and re-layouts: 1.03 us -> 2.06 us  [shards(): jump_trace = turned.reshape(fields, face_width, 4, elements) - inner_trace]
    all_to_all x1, starting transfers between devices: 7.1 us -> 6.08 us  [combine_sums(): lax.all_to_all(spread, ('shot', 'mesh'), 0, 0, tiled=False)]
    dot_general x4, matrix products: 1.93 us -> 2.83 us  [spatial_of(): reference_grads = jnp.einsum('rab,fbe->rfae', derivs, field, precision=MIX)]
    unnamed x105 -> x71, local copies, waits for them, and re-layouts: 7.38 us -> 6.65 us
where the time goes in v11:
time: 85.4 us; the launch traced here: 84.8 us
  starting transfers between devices  20.8 us (24%)
  matrix products  20.6 us (24%)
  local copies, waits for them, and re-layouts  16.4 us (19%)
  waiting for transfers between devices  15.9 us (19%)
  other arithmetic  9.68 us (11%)
  between operations  1.5 us (2%)
    ppermute x2, starting transfers between devices, padded(): before = lax.ppermute(last, axis, up)  10.3 us
    unnamed x71, local copies, waits for them, and re-layouts  6.65 us
    all_to_all x1, waiting for transfers between devices, combine_sums(): lax.all_to_all(spread, ('shot', 'mesh'), 0, 0, tiled=False)  6.1 us
    all_to_all x1, starting transfers between devices, combine_sums(): lax.all_to_all(spread, ('shot', 'mesh'), 0, 0, tiled=False)  6.08 us
    ppermute x2, waiting for transfers between devices, padded(): after = lax.ppermute(first, axis, down)  4.95 us
    ppermute x2, waiting for transfers between devices, halving_sum(): lax.ppermute(jnp.where(upper, low, high), axis, [(i, i ^ bit) for i in ra...  4.84 us
    dot_general x2, matrix products, volume_term(): mixing = jnp.einsum('dpfg,dfae->pgae', coupling, spatial, precision=MIX)  3.29 us
    dot_general x2, matrix products, surface_term(): mixing = jnp.einsum('dpfg,dfnxe->pgnxe', coupling, weighted, precision=MIX)  2.93 us
  transfers between devices with their start and end apart: 7, of which 4 were waited for; matrix products, arithmetic and copies ran while one was open for 20% of the time, Pallas kernels for 0%

profile of v11, /device:TPU:0, one launch (start us, length us, event | category | flops | bytes accessed | tf_op | source)
XLA Modules:
  0.0 84.8 jit_solution(6690240962669439948)
XLA Ops:
  0.6 1.6 %constant_dynamic-slice_fusion = (f32[5,6,35,32]{3,2,1,0:T(8,128)S(1)}, f32[5,6,35,32]{3,2,1,0:T(8,128)S(1)}) fusion(f32[5,6,35,128]{3,2,1,0:T(8,128)} %param.32, s32[]{:T(128)S(6)} %select_n.28, f32[5,6,35,128]{3,2,1,0:T(8,128)} %param.31), kind=kLoop, calls=%fused_computation.265 | loop fusion | bytes 537604 | tf_op jit(solution)/shard_map/dynamic_slice | solution.py:258
  2.3 1.1 %copy.179 = f32[5,6,35,32]{2,3,1,0:T(8,128)} copy(f32[5,6,35,32]{3,2,1,0:T(8,128)S(1)} %get-tuple-element.8) | data formatting | bytes 268800 | tf_op jit(solution)/shard_map/dynamic_slice | solution.py:258
  3.5 0.5 copy.178
  3.9 1.0 %copy.291 = f32[1,13,35,128]{3,2,0,1:T(8,128)S(1)} copy(f32[1,13,35,128]{3,0,2,1:T(1,128)} %param.21) | data formatting | bytes 465920
  4.9 1.6 %multiply_reduce_fusion.2 = f32[10,5]{1,0:T(8,128)S(1)} fusion(f32[5,6,35,32]{2,3,1,0:T(8,128)} %copy.179, f32[10,6,35,32]{2,3,1,0:T(8,128)S(1)} %copy.178), kind=kLoop, calls=%fused_computation.2 | loop fusion | flops 671950 | bytes 403400 | tf_op jit(solution)/shard_map/reduce_sum | solution.py:263
  6.6 0.5 convolution_bitcast_fusion.5
  7.3 0.4 fusion.35
  7.6 0.7 fusion.139
  8.4 5.5 %collective-permute-start = (f32[13,15,64]{2,1,0:T(8,128)}, f32[13,15,64]{2,1,0:T(8,128)}, u32[]{:S(2)}, u32[]{:S(2)}) collective-permute-start(f32[13,15,64]{2,1,0:T(8,128)} %get-tuple-element.47), channel_id=1, source_target_pairs={{0,1},{1,2},{2,3},{3,4},{4,5},{5,6},{6,7},{8,9},{9,10},{10,11},{11... | collective-permute-start | bytes 149768 | tf_op jit(solution)/shard_map/ppermute | solution.py:21
  13.9 1.5 %collective-permute-start.1 = (f32[13,15,64]{2,1,0:T(8,128)}, f32[13,15,64]{2,1,0:T(8,128)}, u32[]{:S(2)}, u32[]{:S(2)}) collective-permute-start(f32[13,15,64]{2,1,0:T(8,128)} %get-tuple-element.46), channel_id=1, source_target_pairs={{1,0},{2,1},{3,2},{4,3},{5,4},{6,5},{7,6},{9,8},{10,9},{11,10},{12... | collective-permute-start | bytes 149768 | tf_op jit(solution)/shard_map/ppermute | solution.py:22
  15.4 0.4 convolution_bitcast_fusion.8
  15.8 0.5 convolution_bitcast_fusion.3
  16.3 0.2 iota_compare_fusion
  16.6 1.4 %fusion.27 = f32[13,15,512]{2,1,0:T(8,128)} fusion(f32[13,15,512]{2,1,0:T(8,128)S(1)} %reshape_reshape.6, pred[640,512]{1,0:T(32,128)(4,1)S(1)} %iota_compare_fusion), kind=kOutput, calls=%fused_computation.58 | convolution fusion | flops 613416960 | bytes 1087488 | tf_op jit(solution)/shard_map/fns,sj->fnj/dot_general | solution.py:275
  18.0 0.4 fusion.136
  18.3 0.5 convolution_bitcast_fusion
  19.1 0.5 convolution_bitcast_fusion.1
  19.8 0.7 copy-done.8
  20.5 1.6 %fusion.5 = f32[13,35,128]{2,0,1:T(8,128)} fusion(f32[3,13,35,128,1]{3,2,0,1,4:T(8,128)S(1)} %maximum_bitcast_fusion, f32[6,35,128]{2,0,1:T(8,128)S(1)} %copy.180, f32[3,6,13,13]{3,2,1,0:T(8,128)S(1)} %copy-done.8), kind=kOutput, calls=%fused_computation.14 | convolution fusion | flops 82409600 | bytes 1051528 | tf_op jit(solution)/shard_map/dpfg,dfae->pgae/dot_general | solution.py:133
  22.2 1.0 %maximum_bitcast_fusion.3 = f32[3,13,35,128,1]{3,2,0,1,4:T(8,128)} fusion(f32[1,13,35,128]{3,2,0,1:T(8,128)S(1)} %get-tuple-element.30, f32[1,13,35,128]{3,2,0,1:T(8,128)S(1)} %get-tuple-element.29, f32[1,13,35,128]{3,2,0,1:T(8,128)S(1)} %get-tuple-element.28), kind=kLoop, calls=%fused_computation.52 | loop fusion | flops 349440 | bytes 1397760 | tf_op jit(solution)/shard_map/stack | solution.py:128
  23.2 0.3 multiply_add_fusion
  23.5 1.0 %maximum_bitcast_fusion.2 = f32[3,13,35,128,1]{3,2,0,1,4:T(8,128)} fusion(f32[1,13,35,128]{3,2,0,1:T(8,128)S(1)} %get-tuple-element.33, f32[1,13,35,128]{3,2,0,1:T(8,128)S(1)} %get-tuple-element.32, f32[1,13,35,128]{3,2,0,1:T(8,128)S(1)} %get-tuple-element.31), kind=kLoop, calls=%fused_computation.51 | loop fusion | flops 349440 | bytes 1397760 | tf_op jit(solution)/shard_map/stack | solution.py:128
  24.5 1.0 %copy.241 = f32[13,60,128]{2,0,1:T(8,128)} copy(f32[13,60,128]{2,1,0:T(8,128)S(1)} %convolution_bitcast_fusion.5) | data formatting | bytes 798720 | tf_op jit(solution)/shard_map/reshape | solution.py:271
  25.7 1.4 %convolution_add_fusion.3 = f32[13,15,512]{2,1,0:T(8,128)S(1)} fusion(f32[13,15,512]{2,1,0:T(8,128)} %fusion.27, f32[13,15,64]{2,1,0:T(8,128)} %collective-permute-done, pred[640,512]{1,0:T(32,128)(4,1)S(1)} %iota_compare_fusion), kind=kOutput, calls=%fused_computation.33 | convolution fusion | flops 76776960 | bytes 881408 | tf_op jit(solution)/shard_map/fns,sj->fnj/dot_general | solution.py:276
  27.2 1.2 %convolution_add_fusion.2 = f32[13,15,512]{2,1,0:T(8,128)S(1)} fusion(f32[13,15,512]{2,1,0:T(8,128)S(1)} %convolution_add_fusion.3, f32[13,15,64]{2,1,0:T(8,128)} %collective-permute-done.1, pred[640,512]{1,0:T(32,128)(4,1)S(1)} %iota_compare_fusion), kind=kOutput, calls=%fused_computation.32 | convolution fusion | flops 76776960 | bytes 908032 | tf_op jit(solution)/shard_map/fns,sj->fnj/dot_general | solution.py:279
  28.4 1.4 %multiply_reduce_fusion.1 = f32[13,15,512]{2,1,0:T(8,128)} fusion(f32[15,15,512]{2,1,0:T(8,128)S(1)} %multiply_add_fusion, f32[13,15,512]{2,1,0:T(8,128)S(1)} %convolution_add_fusion.2), kind=kLoop, calls=%fused_computation.1 | loop fusion | flops 2895360 | bytes 1259520 | tf_op jit(solution)/shard_map/reduce_sum | solution.py:282
  29.8 1.9 %reshape.366 = f32[13,15,4,128]{3,2,1,0:T(4,128)} reshape(f32[13,15,512]{2,1,0:T(8,128)} %multiply_reduce_fusion.1) | data formatting | bytes 798720 | tf_op jit(solution)/shard_map/reshape | solution.py:283
  31.7 1.1 %copy_subtract_fusion.1 = f32[13,15,4,128]{3,0,2,1:T(8,128)S(1)} fusion(f32[13,15,4,128]{3,0,2,1:T(8,128)S(1)} %bitcast.783, f32[13,15,4,128]{3,2,1,0:T(4,128)} %reshape.366), kind=kLoop, calls=%fused_computation.60 | loop fusion | flops 99840 | bytes 1198080 | tf_op jit(solution)/shard_map/sub | solution.py:283
  32.8 1.4 %fusion.1 = f32[13,15,4,128]{3,0,2,1:T(8,128)S(1)} fusion(f32[6,15,4,128]{3,0,2,1:T(8,128)S(1)} %bitcast.797, f32[13,15,4,128]{3,0,2,1:T(8,128)S(1)} %copy_subtract_fusion.1, f32[3,4,128]{2,0,1:T(4,128)S(1)} %copy.184, f32[3,6,13,13]{3,2,1,0:T(8,128)S(1)} %copy-done.8), kind=kOutput, calls=%fused_computation.6 | convolution fusion | flops 141573120 | bytes 1001352 | tf_op jit(solution)/shard_map/dpfg,dfnxe->pgnxe/dot_general | solution.py:145
  34.4 0.9 %copy-done.3 = f32[13,35,128]{2,0,1:T(8,128)S(1)} copy-done((f32[13,35,128]{2,0,1:T(8,128)S(1)}, f32[13,35,128]{2,0,1:T(8,128)}, u32[]{:S(2)}) %copy-start.3) | copy-done | bytes 232984
  35.2 0.6 fusion.14
  35.8 1.4 %convolution_bitcast_fusion.2 = f32[3,13,35,128]{3,2,0,1:T(8,128)} fusion(f32[3,35,35,1]{2,1,0,3:T(8,128)S(1)} %copy-done.5, f32[13,35,128]{2,1,0:T(8,128)S(1)} %fusion.14), kind=kOutput, calls=%fused_computation.24 | convolution fusion | flops 36691200 | bytes 946540 | tf_op jit(solution)/shard_map/rab,fbe->rfae/dot_general | solution.py:121
  37.2 0.5 convolution_bitcast_fusion.4
  37.9 0.6 fusion.26
  38.5 0.4 fusion.33
  39.2 4.8 %collective-permute-start.2 = (f32[13,15,64]{2,1,0:T(8,128)S(1)}, f32[13,15,64]{2,1,0:T(8,128)S(1)}, u32[]{:S(2)}, u32[]{:S(2)}) collective-permute-start(f32[13,15,64]{2,1,0:T(8,128)S(1)} %get-tuple-element.45), channel_id=1, source_target_pairs={{0,1},{1,2},{2,3},{3,4},{4,5},{5,6},{6,7},{8,9},{9,10},{10,11},{11... | collective-permute-start | bytes 149768 | tf_op jit(solution)/shard_map/ppermute | solution.py:21
  44.0 1.8 %fusion.3 = f32[6,35,128]{2,0,1:T(8,128)} fusion(f32[3,13,35,128,1]{3,2,0,1,4:T(8,128)S(1)} %copy-done.7, f32[13,35,128]{2,0,1:T(8,128)S(1)} %copy.201, f32[3,6,13,13]{3,2,1,0:T(8,128)S(1)} %copy-done.8), kind=kOutput, calls=%fused_computation.10 | convolution fusion | flops 82440960 | bytes 1051528 | tf_op jit(solution)/shard_map/dpfg,dgae->pfae/dot_general | solution.py:139
  45.9 1.6 %fusion.4 = f32[13,35,128]{2,0,1:T(8,128)} fusion(f32[3,13,35,128,1]{3,2,0,1,4:T(8,128)S(1)} %maximum_bitcast_fusion.1, f32[6,35,128]{2,0,1:T(8,128)S(1)} %copy.180, f32[3,6,13,13]{3,2,1,0:T(8,128)S(1)} %copy-done.8), kind=kOutput, calls=%fused_computation.12 | convolution fusion | flops 82409600 | bytes 1051528 | tf_op jit(solution)/shard_map/dpfg,dfae->pgae/dot_general | solution.py:133
  47.5 1.0 %copy.248 = f32[13,60,128]{2,0,1:T(8,128)} copy(f32[13,60,128]{2,1,0:T(8,128)S(1)} %convolution_bitcast_fusion.4) | data formatting | bytes 798720 | tf_op jit(solution)/shard_map/reshape | solution.py:271
  48.5 1.3 %collective-permute-start.3 = (f32[13,15,64]{2,1,0:T(8,128)S(1)}, f32[13,15,64]{2,1,0:T(8,128)S(1)}, u32[]{:S(2)}, u32[]{:S(2)}) collective-permute-start(f32[13,15,64]{2,1,0:T(8,128)S(1)} %get-tuple-element.44), channel_id=1, source_target_pairs={{1,0},{2,1},{3,2},{4,3},{5,4},{6,5},{7,6},{9,8},{10,9},{11,10},{12... | collective-permute-start | bytes 149768 | tf_op jit(solution)/shard_map/ppermute | solution.py:22
  49.8 0.3 convolution_add_fusion.1
  50.2 4.9 %collective-permute-done.3 = f32[13,15,64]{2,1,0:T(8,128)S(1)} collective-permute-done((f32[13,15,64]{2,1,0:T(8,128)S(1)}, f32[13,15,64]{2,1,0:T(8,128)S(1)}, u32[]{:S(2)}, u32[]{:S(2)}) %collective-permute-start.3) | collective-permute-done | bytes 49952 | tf_op jit(solution)/shard_map/ppermute | solution.py:22
  55.1 0.3 convolution_add_fusion
  55.5 0.6 multiply_reduce_fusion
  56.1 0.1 reshape.368
  56.3 0.2 copy-done.2
  56.6 0.3 copy-done.25
  56.8 0.4 copy-done.12
  57.2 1.5 %fusion = f32[13,15,4,128]{3,0,2,1:T(8,128)S(1)} fusion(f32[6,15,4,128]{3,0,2,1:T(8,128)S(1)} %bitcast.798, f32[13,15,4,128]{3,0,2,1:T(8,128)S(1)} %copy_subtract_fusion, f32[3,4,128]{2,0,1:T(4,128)S(1)} %copy-done.25, f32[3,6,13,13]{3,2,1,0:T(8,128)S(1)} %copy-done.8), kind=kOutput, calls=%fused_computation.4 | convolution fusion | flops 141573120 | bytes 1001352 | tf_op jit(solution)/shard_map/dpfg,dfnxe->pgnxe/dot_general | solution.py:145
  58.8 0.9 %copy-done.4 = f32[13,35,128]{2,0,1:T(8,128)S(1)} copy-done((f32[13,35,128]{2,0,1:T(8,128)S(1)}, f32[13,35,128]{2,0,1:T(8,128)}, u32[]{:S(2)}) %copy-start.4) | copy-done | bytes 232984
  59.7 0.6 fusion.17
  60.4 0.5 copy-done.6
  60.8 1.1 %fusion.2 = f32[6,35,128]{2,0,1:T(8,128)S(1)} fusion(f32[3,13,35,128,1]{3,2,0,1,4:T(8,128)S(1)} %copy-done.6, f32[13,35,128]{2,0,1:T(8,128)S(1)} %copy.206, f32[3,6,13,13]{3,2,1,0:T(8,128)S(1)} %copy-done.8), kind=kOutput, calls=%fused_computation.8 | convolution fusion | flops 82440960 | bytes 1051528 | tf_op jit(solution)/shard_map/dpfg,dgae->pfae/dot_general | solution.py:139
  62.1 1.6 %collective-permute-start.4 = (f32[6,35,64]{2,0,1:T(8,128)S(1)}, f32[6,35,64]{2,0,1:T(8,128)S(1)}, u32[]{:S(2)}, u32[]{:S(2)}) collective-permute-start(f32[6,35,64]{2,0,1:T(8,128)S(1)} %slice_select_fusion.1), channel_id=1, source_target_pairs={{0,16},{8,24},{16,0},{24,8},{1,17},{9,25},{17,1},{25,9},{2,18},{10... | collective-permute-start | bytes 161288 | tf_op jit(solution)/shard_map/ppermute | solution.py:161
  63.7 3.6 %collective-permute-done.4 = f32[6,35,64]{2,0,1:T(8,128)S(1)} collective-permute-done((f32[6,35,64]{2,0,1:T(8,128)S(1)}, f32[6,35,64]{2,0,1:T(8,128)S(1)}, u32[]{:S(2)}, u32[]{:S(2)}) %collective-permute-start.4) | collective-permute-done | bytes 53792 | tf_op jit(solution)/shard_map/ppermute | solution.py:161
  67.7 1.3 %collective-permute-done.5 = f32[6,35,32]{2,0,1:T(8,128)S(1)} collective-permute-done((f32[6,35,32]{2,0,1:T(8,128)S(1)}, f32[6,35,32]{2,0,1:T(8,128)S(1)}, u32[]{:S(2)}, u32[]{:S(2)}) %collective-permute-start.5) | collective-permute-done | bytes 26912 | tf_op jit(solution)/shard_map/ppermute | solution.py:161
  69.1 0.3 fusion.11
  69.4 0.6 broadcast_in_dim.7
  70.1 6.1 %all-to-all-start = ((f32[32,1,60]{2,1,0:T(1,128)}), f32[32,1,60]{2,1,0:T(1,128)S(1)}, u32[]{:S(2)}, u32[]{:S(2)}) async-start(f32[32,1,60]{2,1,0:T(1,128)} %broadcast_in_dim.7), calls=%async_computation | async-start | bytes 32768 | tf_op jit(solution)/shard_map/all_to_all | solution.py:295
  76.2 0.9 %copy.210 = f32[1,13,35,128]{3,0,2,1:T(1,128)} copy(f32[1,13,35,128]{3,2,1,0:T(8,128)S(1)} %bitcast.782) | data formatting | bytes 465920
  77.1 6.1 %all-to-all-done = f32[32,1,60]{2,1,0:T(1,128)S(1)} async-done(((f32[32,1,60]{2,1,0:T(1,128)}), f32[32,1,60]{2,1,0:T(1,128)S(1)}, u32[]{:S(2)}, u32[]{:S(2)}) %all-to-all-start) | async-done | bytes 7712 | tf_op jit(solution)/shard_map/all_to_all | solution.py:295
  83.6 0.2 slice_reduce_fusion
  83.8 0.2 fusion.10
  84.1 0.8 copy.211
  (109 shorter events, 2.9 us)
Async XLA Ops:
  3.9 2.6 %copy-start.13 = (f32[60,35,1]{0,1,2:T(8,128)S(1)}, f32[60,35,1]{0,1,2:T(8,128)}, u32[]{:S(2)}) copy-start(f32[60,35,1]{0,1,2:T(8,128)} %constant.62) | copy-start | bytes 25204
  4.9 2.3 %copy-start.29 = (s32[128]{0:T(128)S(1)}, s32[128]{0:T(128)}, u32[]{:S(2)}) copy-start(s32[128]{0:T(128)} %param.30) | copy-start | bytes 1540
  6.6 8.7 %copy-start.9 = (f32[6,35,128]{2,1,0:T(8,128)S(1)}, f32[6,35,128]{2,1,0:T(8,128)}, u32[]{:S(2)}) copy-start(f32[6,35,128]{2,1,0:T(8,128)} %param.23) | copy-start | bytes 322564
  7.1 8.6 %copy-start.5 = (f32[3,35,35,1]{2,1,0,3:T(8,128)S(1)}, f32[3,35,35,1]{2,1,0,3:T(8,128)}, u32[]{:S(2)}) copy-start(f32[3,35,35,1]{2,1,0,3:T(8,128)} %constant.61) | copy-start | bytes 44104
  7.2 9.1 %copy-start.27 = (f32[3,3,128]{2,1,0:T(4,128)S(1)}, f32[3,3,128]{2,1,0:T(4,128)}, u32[]{:S(2)}) copy-start(f32[3,3,128]{2,1,0:T(4,128)} %param.25) | copy-start | bytes 13828
  7.2 9.1 %copy-start.28 = (s32[4,128]{1,0:T(4,128)S(1)}, s32[4,128]{1,0:T(4,128)}, u32[]{:S(2)}) copy-start(s32[4,128]{1,0:T(4,128)} %param.28) | copy-start | bytes 6148
  8.4 17.3 %collective-permute-start = (f32[13,15,64]{2,1,0:T(8,128)}, f32[13,15,64]{2,1,0:T(8,128)}, u32[]{:S(2)}, u32[]{:S(2)}) collective-permute-start(f32[13,15,64]{2,1,0:T(8,128)} %get-tuple-element.47), channel_id=1, source_target_pairs={{0,1},{1,2},{2,3},{3,4},{4,5},{5,6},{6,7},{8,9},{9,10},{10,11},{11... | collective-permute-start | bytes 149768 | tf_op jit(solution)/shard_map/ppermute | solution.py:21
  13.9 13.3 %collective-permute-start.1 = (f32[13,15,64]{2,1,0:T(8,128)}, f32[13,15,64]{2,1,0:T(8,128)}, u32[]{:S(2)}, u32[]{:S(2)}) collective-permute-start(f32[13,15,64]{2,1,0:T(8,128)} %get-tuple-element.46), channel_id=1, source_target_pairs={{1,0},{2,1},{3,2},{4,3},{5,4},{6,5},{7,6},{9,8},{10,9},{11,10},{12... | collective-permute-start | bytes 149768 | tf_op jit(solution)/shard_map/ppermute | solution.py:22
  15.8 2.2 %copy-start.31 = (s32[4,128]{1,0:T(4,128)S(1)}, s32[4,128]{1,0:T(4,128)}, u32[]{:S(2)}) copy-start(s32[4,128]{1,0:T(4,128)} %param.29) | copy-start | bytes 6148
  15.8 2.2 %copy-start.32 = (f32[4,128]{1,0:T(4,128)S(1)}, f32[4,128]{1,0:T(4,128)}, u32[]{:S(2)}) copy-start(f32[4,128]{1,0:T(4,128)} %param.27) | copy-start | bytes 6148
  15.8 2.2 %copy-start.10 = (f32[1,2,13,35,128]{4,1,3,2,0:T(2,128)S(1)}, f32[1,2,13,35,128]{4,1,3,2,0:T(2,128)}, u32[]{:S(2)}) copy-start(f32[1,2,13,35,128]{4,1,3,2,0:T(2,128)} %param.22) | copy-start | bytes 1397764
  16.3 3.3 %copy-start.16 = (f32[128]{0:T(128)}, f32[128]{0:T(128)S(1)}, u32[]{:S(2)}) copy-start(f32[128]{0:T(128)S(1)} %get-tuple-element.56) | copy-start | bytes 1540
  19.6 0.9 %copy-start.8 = (f32[3,6,13,13]{3,2,1,0:T(8,128)S(1)}, f32[3,6,13,13]{3,2,1,0:T(8,128)}, u32[]{:S(2)}) copy-start(f32[3,6,13,13]{3,2,1,0:T(8,128)} %param.24) | copy-start | bytes 36508
  20.5 2.7 %copy-start.18 = (f32[15,15]{1,0:T(8,128)S(1)}, f32[15,15]{1,0:T(8,128)}, u32[]{:S(2)}) copy-start(f32[15,15]{1,0:T(8,128)} %constant.20.clone) | copy-start | bytes 2704
  20.5 2.7 %copy-start.19 = (f32[15,15]{1,0:T(8,128)S(1)}, f32[15,15]{1,0:T(8,128)}, u32[]{:S(2)}) copy-start(f32[15,15]{1,0:T(8,128)} %constant.54.clone) | copy-start | bytes 2704
  20.5 2.7 %copy-start.20 = (f32[15,15]{1,0:T(8,128)S(1)}, f32[15,15]{1,0:T(8,128)}, u32[]{:S(2)}) copy-start(f32[15,15]{1,0:T(8,128)} %constant.55.clone) | copy-start | bytes 2704
  20.5 2.7 %copy-start.21 = (f32[15,15]{1,0:T(8,128)S(1)}, f32[15,15]{1,0:T(8,128)}, u32[]{:S(2)}) copy-start(f32[15,15]{1,0:T(8,128)} %constant.56.clone) | copy-start | bytes 2704
  20.5 2.7 %copy-start.22 = (f32[15,15]{1,0:T(8,128)S(1)}, f32[15,15]{1,0:T(8,128)}, u32[]{:S(2)}) copy-start(f32[15,15]{1,0:T(8,128)} %constant.57.clone) | copy-start | bytes 2704
  20.5 2.7 %copy-start.23 = (f32[15,15]{1,0:T(8,128)S(1)}, f32[15,15]{1,0:T(8,128)}, u32[]{:S(2)}) copy-start(f32[15,15]{1,0:T(8,128)} %constant.58.clone) | copy-start | bytes 2704
  23.5 2.2 %copy-start.26 = (f32[3,4,128]{2,1,0:T(4,128)S(1)}, f32[3,4,128]{2,1,0:T(4,128)}, u32[]{:S(2)}) copy-start(f32[3,4,128]{2,1,0:T(4,128)} %param.26) | copy-start | bytes 18436
  25.6 7.2 %copy-start.11 = (f32[6,60,128]{2,0,1:T(8,128)}, f32[6,60,128]{2,0,1:T(8,128)S(1)}, u32[]{:S(2)}) copy-start(f32[6,60,128]{2,0,1:T(8,128)S(1)} %copy.240) | copy-start | bytes 552964
  25.7 7.1 %copy-start.24 = (f32[3,4,128]{2,0,1:T(4,128)}, f32[3,4,128]{2,0,1:T(4,128)S(1)}, u32[]{:S(2)}) copy-start(f32[3,4,128]{2,0,1:T(4,128)S(1)} %copy.184) | copy-start | bytes 18436
  28.4 3.3 %copy-start.1 = (f32[13,60,128]{2,0,1:T(8,128)S(1)}, f32[13,60,128]{2,0,1:T(8,128)}, u32[]{:S(2)}) copy-start(f32[13,60,128]{2,0,1:T(8,128)} %copy.241) | copy-start | bytes 1198084
  34.3 1.0 %copy-start.3 = (f32[13,35,128]{2,0,1:T(8,128)S(1)}, f32[13,35,128]{2,0,1:T(8,128)}, u32[]{:S(2)}) copy-start(f32[13,35,128]{2,0,1:T(8,128)} %fusion.5) | copy-start | bytes 698884
  34.3 1.0 %copy-start.15 = (f32[4,35,15,1]{1,2,0,3:T(8,128)S(1)}, f32[4,35,15,1]{1,2,0,3:T(8,128)}, u32[]{:S(2)}) copy-start(f32[4,35,15,1]{1,2,0,3:T(8,128)} %constant.63) | copy-start | bytes 25204
  37.8 0.7 copy-start.30
  37.9 1.1 %copy-start = (f32[3,13,35,128]{3,2,0,1:T(8,128)S(1)}, f32[3,13,35,128]{3,2,0,1:T(8,128)}, u32[]{:S(2)}) copy-start(f32[3,13,35,128]{3,2,0,1:T(8,128)} %convolution_bitcast_fusion.2) | copy-start | bytes 2096644
  37.9 1.1 %copy-start.17 = (f32[128]{0:T(128)S(1)}, f32[128]{0:T(128)}, u32[]{:S(2)}) copy-start(f32[128]{0:T(128)} %copy-done.16) | copy-start | bytes 1540
  38.9 5.2 %copy-start.7 = (f32[3,13,35,128,1]{3,2,0,1,4:T(8,128)S(1)}, f32[3,13,35,128,1]{3,2,0,1,4:T(8,128)}, u32[]{:S(2)}) copy-start(f32[3,13,35,128,1]{3,2,0,1,4:T(8,128)} %maximum_bitcast_fusion.2) | copy-start | bytes 2096644
  39.2 10.6 %collective-permute-start.2 = (f32[13,15,64]{2,1,0:T(8,128)S(1)}, f32[13,15,64]{2,1,0:T(8,128)S(1)}, u32[]{:S(2)}, u32[]{:S(2)}) collective-permute-start(f32[13,15,64]{2,1,0:T(8,128)S(1)} %get-tuple-element.45), channel_id=1, source_target_pairs={{0,1},{1,2},{2,3},{3,4},{4,5},{5,6},{6,7},{8,9},{9,10},{10,11},{11... | collective-permute-start | bytes 149768 | tf_op jit(solution)/shard_map/ppermute | solution.py:21
  48.5 6.6 %collective-permute-start.3 = (f32[13,15,64]{2,1,0:T(8,128)S(1)}, f32[13,15,64]{2,1,0:T(8,128)S(1)}, u32[]{:S(2)}, u32[]{:S(2)}) collective-permute-start(f32[13,15,64]{2,1,0:T(8,128)S(1)} %get-tuple-element.44), channel_id=1, source_target_pairs={{1,0},{2,1},{3,2},{4,3},{5,4},{6,5},{7,6},{9,8},{10,9},{11,10},{12... | collective-permute-start | bytes 149768 | tf_op jit(solution)/shard_map/ppermute | solution.py:22
  55.5 1.0 %copy-start.2 = (f32[13,60,128]{2,0,1:T(8,128)S(1)}, f32[13,60,128]{2,0,1:T(8,128)}, u32[]{:S(2)}) copy-start(f32[13,60,128]{2,0,1:T(8,128)} %copy.248) | copy-start | bytes 1198084
  56.1 0.7 copy-start.25
  56.3 1.0 %copy-start.12 = (f32[6,60,128]{2,0,1:T(8,128)S(1)}, f32[6,60,128]{2,0,1:T(8,128)}, u32[]{:S(2)}) copy-start(f32[6,60,128]{2,0,1:T(8,128)} %copy-done.11) | copy-start | bytes 552964
  58.7 1.0 %copy-start.4 = (f32[13,35,128]{2,0,1:T(8,128)S(1)}, f32[13,35,128]{2,0,1:T(8,128)}, u32[]{:S(2)}) copy-start(f32[13,35,128]{2,0,1:T(8,128)} %fusion.4) | copy-start | bytes 698884
  59.7 1.1 %copy-start.6 = (f32[3,13,35,128,1]{3,2,0,1,4:T(8,128)S(1)}, f32[3,13,35,128,1]{3,2,0,1,4:T(8,128)}, u32[]{:S(2)}) copy-start(f32[3,13,35,128,1]{3,2,0,1,4:T(8,128)} %maximum_bitcast_fusion.3) | copy-start | bytes 2096644
  60.3 1.7 %copy-start.14 = (f32[6,35,128]{2,0,1:T(8,128)S(1)}, f32[6,35,128]{2,0,1:T(8,128)}, u32[]{:S(2)}) copy-start(f32[6,35,128]{2,0,1:T(8,128)} %fusion.3) | copy-start | bytes 322564
  62.1 5.2 %collective-permute-start.4 = (f32[6,35,64]{2,0,1:T(8,128)S(1)}, f32[6,35,64]{2,0,1:T(8,128)S(1)}, u32[]{:S(2)}, u32[]{:S(2)}) collective-permute-start(f32[6,35,64]{2,0,1:T(8,128)S(1)} %slice_select_fusion.1), channel_id=1, source_target_pairs={{0,16},{8,24},{16,0},{24,8},{1,17},{9,25},{17,1},{25,9},{2,18},{10... | collective-permute-start | bytes 161288 | tf_op jit(solution)/shard_map/ppermute | solution.py:161
  67.5 1.4 %collective-permute-start.5 = (f32[6,35,32]{2,0,1:T(8,128)S(1)}, f32[6,35,32]{2,0,1:T(8,128)S(1)}, u32[]{:S(2)}, u32[]{:S(2)}) collective-permute-start(f32[6,35,32]{2,0,1:T(8,128)S(1)} %slice_select_fusion), channel_id=1, source_target_pairs={{0,8},{8,0},{16,24},{24,16},{1,9},{9,1},{17,25},{25,17},{2,10},{10... | collective-permute-start | bytes 80648 | tf_op jit(solution)/shard_map/ppermute | solution.py:161
  70.1 13.2 %all-to-all-start = ((f32[32,1,60]{2,1,0:T(1,128)}), f32[32,1,60]{2,1,0:T(1,128)S(1)}, u32[]{:S(2)}, u32[]{:S(2)}) async-start(f32[32,1,60]{2,1,0:T(1,128)} %broadcast_in_dim.7), calls=%async_computation | async-start | bytes 32768 | tf_op jit(solution)/shard_map/all_to_all | solution.py:295

commit v12 on v10

--- a/solution.py
+++ b/solution.py
@@ -265,14 +265,14 @@
     for step_index in range(forward_states.shape[1]):
         inner_trace = adjoint[:, face_nodes.T, :]
         flat_trace = inner_trace.reshape(fields, face_width, 4 * elements)
-        sent_traces = jnp.einsum("fns,sj->fnj", flat_trace, send_pick, precision=HIGH)
+        sent_traces = jnp.einsum("fns,sj->fnj", flat_trace, send_pick, precision=MIX)
         extended = padded(sent_traces, (("mesh", 2),), border)
-        gathered = jnp.einsum("fns,sj->fnj", flat_trace, local_pick, precision=HIGH)
+        gathered = jnp.einsum("fns,sj->fnj", flat_trace, local_pick, precision=MIX)
         gathered = gathered + jnp.einsum(
-            "fns,sj->fnj", extended[:, :, :border], below_pick, precision=HIGH
+            "fns,sj->fnj", extended[:, :, :border], below_pick, precision=MIX
         )
         gathered = gathered + jnp.einsum(
-            "fns,sj->fnj", extended[:, :, 3 * border :], above_pick, precision=HIGH
+            "fns,sj->fnj", extended[:, :, 3 * border :], above_pick, precision=MIX
         )
         turned = jnp.sum(gathered[:, :, None, :] * node_turn[None], axis=1)
         jump_trace = turned.reshape(fields, face_width, 4, elements) - inner_trace

time: 82.4 us -> 81.8 us (level)
  no operation moved by 1% of the time
where the time goes in v12:
time: 81.8 us; the launch traced here: 81.2 us
  starting transfers between devices  21.9 us (27%)
  local copies, waits for them, and re-layouts  20.8 us (25%)
  matrix products  16.7 us (20%)
  waiting for transfers between devices  11.2 us (14%)
  other arithmetic  8.98 us (11%)
  between operations  1.76 us (2%)
    ppermute x2, starting transfers between devices, padded(): before = lax.ppermute(last, axis, up)  10.2 us
    unnamed x105, local copies, waits for them, and re-layouts  7.38 us
    all_to_all x1, starting transfers between devices, combine_sums(): lax.all_to_all(spread, ('shot', 'mesh'), 0, 0, tiled=False)  7.05 us
    all_to_all x1, waiting for transfers between devices, combine_sums(): lax.all_to_all(spread, ('shot', 'mesh'), 0, 0, tiled=False)  6.1 us
    ppermute x2, waiting for transfers between devices, halving_sum(): lax.ppermute(jnp.where(upper, low, high), axis, [(i, i ^ bit) for i in ra...  4.84 us
    dot_general x2, matrix products, volume_term(): mixing = jnp.einsum('dpfg,dfae->pgae', coupling, spatial, precision=MIX)  3.32 us
    gather x2, local copies, waits for them, and re-layouts, shards(): face_material = material[:, face_nodes.T, :]  3.23 us
    dot_general x2, matrix products, surface_term(): mixing = jnp.einsum('dpfg,dfnxe->pgnxe', coupling, weighted, precision=MIX)  2.98 us
  transfers between devices with their start and end apart: 7, of which 4 were waited for; matrix products, arithmetic and copies ran while one was open for 20% of the time, Pallas kernels for 0%

profile of v12, /device:TPU:0, one launch (start us, length us, event | category | flops | bytes accessed | tf_op | source)
XLA Modules:
  0.0 81.2 jit_solution(13590638097792883403)
XLA Ops:
  0.6 1.6 %constant_dynamic-slice_fusion = (f32[5,6,35,32]{3,2,1,0:T(8,128)S(1)}, f32[5,6,35,32]{3,2,1,0:T(8,128)S(1)}) fusion(f32[5,6,35,128]{3,2,1,0:T(8,128)} %param.37, s32[]{:T(128)S(6)} %select_n.37, f32[5,6,35,128]{3,2,1,0:T(8,128)} %param.36), kind=kLoop, calls=%fused_computation.266 | loop fusion | bytes 537604 | tf_op jit(solution)/shard_map/dynamic_slice | solution.py:255
  2.3 1.1 %copy.196 = f32[5,6,35,32]{2,3,1,0:T(8,128)} copy(f32[5,6,35,32]{3,2,1,0:T(8,128)S(1)} %get-tuple-element.8) | data formatting | bytes 268800 | tf_op jit(solution)/shard_map/dynamic_slice | solution.py:255
  3.5 0.5 copy.195
  4.0 1.0 %copy.308 = f32[1,13,35,128]{3,2,0,1:T(8,128)S(1)} copy(f32[1,13,35,128]{3,0,2,1:T(1,128)} %param.26) | data formatting | bytes 465920
  4.9 1.6 %multiply_reduce_fusion.2 = f32[10,5]{1,0:T(8,128)S(1)} fusion(f32[5,6,35,32]{2,3,1,0:T(8,128)} %copy.196, f32[10,6,35,32]{2,3,1,0:T(8,128)S(1)} %copy.195), kind=kLoop, calls=%fused_computation.5 | loop fusion | flops 671950 | bytes 403400 | tf_op jit(solution)/shard_map/reduce_sum | solution.py:260
  6.7 0.6 gather_fusion.1
  7.5 0.2 reshape.362
  7.7 0.3 fusion.35
  8.0 0.7 fusion.139
  8.7 5.5 %collective-permute-start = (f32[13,15,64]{2,1,0:T(8,128)}, f32[13,15,64]{2,1,0:T(8,128)}, u32[]{:S(2)}, u32[]{:S(2)}) collective-permute-start(f32[13,15,64]{2,1,0:T(8,128)} %get-tuple-element.47), channel_id=1, source_target_pairs={{0,1},{1,2},{2,3},{3,4},{4,5},{5,6},{6,7},{8,9},{9,10},{10,11},{11... | collective-permute-start | bytes 149768 | tf_op jit(solution)/shard_map/ppermute | solution.py:21
  14.2 1.5 %collective-permute-start.1 = (f32[13,15,64]{2,1,0:T(8,128)}, f32[13,15,64]{2,1,0:T(8,128)}, u32[]{:S(2)}, u32[]{:S(2)}) collective-permute-start(f32[13,15,64]{2,1,0:T(8,128)} %get-tuple-element.46), channel_id=1, source_target_pairs={{1,0},{2,1},{3,2},{4,3},{5,4},{6,5},{7,6},{9,8},{10,9},{11,10},{12... | collective-permute-start | bytes 149768 | tf_op jit(solution)/shard_map/ppermute | solution.py:22
  15.8 0.2 iota_compare_fusion
  16.0 0.5 fusion.27
  16.5 0.5 convolution_bitcast_fusion.3
  17.2 0.4 fusion.136
  17.5 0.5 convolution_bitcast_fusion.1
  18.3 0.5 convolution_bitcast_fusion
  19.1 0.7 copy-done.11
  19.8 1.7 %fusion.5 = f32[13,35,128]{2,0,1:T(8,128)} fusion(f32[3,13,35,128,1]{3,2,0,1,4:T(8,128)S(1)} %maximum_bitcast_fusion, f32[6,35,128]{2,0,1:T(8,128)S(1)} %copy.197, f32[3,6,13,13]{3,2,1,0:T(8,128)S(1)} %copy-done.11), kind=kOutput, calls=%fused_computation.17 | convolution fusion | flops 82409600 | bytes 1051528 | tf_op jit(solution)/shard_map/dpfg,dfae->pgae/dot_general | solution.py:133
  21.5 1.0 %maximum_bitcast_fusion.2 = f32[3,13,35,128,1]{3,2,0,1,4:T(8,128)} fusion(f32[1,13,35,128]{3,2,0,1:T(8,128)S(1)} %get-tuple-element.33, f32[1,13,35,128]{3,2,0,1:T(8,128)S(1)} %get-tuple-element.32, f32[1,13,35,128]{3,2,0,1:T(8,128)S(1)} %get-tuple-element.31), kind=kLoop, calls=%fused_computation.51 | loop fusion | flops 349440 | bytes 1397760 | tf_op jit(solution)/shard_map/stack | solution.py:128
  22.5 0.3 multiply_add_fusion
  22.8 1.0 %maximum_bitcast_fusion.3 = f32[3,13,35,128,1]{3,2,0,1,4:T(8,128)} fusion(f32[1,13,35,128]{3,2,0,1:T(8,128)S(1)} %get-tuple-element.30, f32[1,13,35,128]{3,2,0,1:T(8,128)S(1)} %get-tuple-element.29, f32[1,13,35,128]{3,2,0,1:T(8,128)S(1)} %get-tuple-element.28), kind=kLoop, calls=%fused_computation.52 | loop fusion | flops 349440 | bytes 1397760 | tf_op jit(solution)/shard_map/stack | solution.py:128
  23.7 1.5 %gather_fusion = f32[60,6,128]{2,0,1:T(8,128)} fusion(f32[6,35,128]{2,1,0:T(8,128)S(1)} %copy-done, s32[1024]{0:T(1024)S(1)} %pad_clamp_fusion), kind=kCustom, calls=%fused_computation | custom fusion | bytes 368880 | tf_op jit(solution)/shard_map/gather | solution.py:232
  25.2 1.7 %copy.259 = f32[60,6,128]{2,1,0:T(8,128)} copy(f32[60,6,128]{2,0,1:T(8,128)} %gather_fusion) | data formatting | bytes 368640 | tf_op jit(solution)/shard_map/gather | solution.py:232
  27.0 1.2 %convolution_add_fusion.3 = f32[13,15,512]{2,1,0:T(8,128)S(1)} fusion(f32[13,15,512]{2,1,0:T(8,128)S(1)} %fusion.27, f32[13,15,64]{2,1,0:T(8,128)} %collective-permute-done, pred[640,512]{1,0:T(32,128)(4,1)S(1)} %iota_compare_fusion), kind=kOutput, calls=%fused_computation.35 | convolution fusion | flops 38438400 | bytes 908032 | tf_op jit(solution)/shard_map/fns,sj->fnj/dot_general | solution.py:271
  28.2 1.2 %convolution_add_fusion.2 = f32[13,15,512]{2,1,0:T(8,128)S(1)} fusion(f32[13,15,512]{2,1,0:T(8,128)S(1)} %convolution_add_fusion.3, f32[13,15,64]{2,1,0:T(8,128)} %collective-permute-done.1, pred[640,512]{1,0:T(32,128)(4,1)S(1)} %iota_compare_fusion), kind=kOutput, calls=%fused_computation.34 | convolution fusion | flops 38438400 | bytes 908032 | tf_op jit(solution)/shard_map/fns,sj->fnj/dot_general | solution.py:274
  29.4 0.6 multiply_reduce_fusion.1
  30.0 0.9 %reshape.363 = f32[13,15,4,128]{3,2,1,0:T(4,128)} reshape(f32[13,15,512]{2,1,0:T(8,128)S(1)} %multiply_reduce_fusion.1) | data formatting | bytes 798720 | tf_op jit(solution)/shard_map/reshape | solution.py:278
  30.9 1.1 %copy_subtract_fusion.1 = f32[13,15,4,128]{3,0,2,1:T(8,128)S(1)} fusion(f32[13,15,4,128]{3,0,2,1:T(8,128)S(1)} %bitcast.776, f32[13,15,4,128]{3,2,1,0:T(4,128)} %reshape.363), kind=kLoop, calls=%fused_computation.60 | loop fusion | flops 99840 | bytes 1198080 | tf_op jit(solution)/shard_map/sub | solution.py:278
  32.0 1.5 %fusion.1 = f32[13,15,4,128]{3,0,2,1:T(8,128)S(1)} fusion(f32[6,15,4,128]{3,0,2,1:T(8,128)S(1)} %bitcast.792, f32[13,15,4,128]{3,0,2,1:T(8,128)S(1)} %copy_subtract_fusion.1, f32[3,4,128]{2,0,1:T(4,128)S(1)} %copy.201, f32[3,6,13,13]{3,2,1,0:T(8,128)S(1)} %copy-done.12), kind=kOutput, calls=%fused_computation.9 | convolution fusion | flops 141573120 | bytes 1001352 | tf_op jit(solution)/shard_map/dpfg,dfnxe->pgnxe/dot_general | solution.py:145
  33.6 0.9 %copy-done.5 = f32[13,35,128]{2,0,1:T(8,128)S(1)} copy-done((f32[13,35,128]{2,0,1:T(8,128)S(1)}, f32[13,35,128]{2,0,1:T(8,128)}, u32[]{:S(2)}) %copy-start.5) | copy-done | bytes 232984
  34.5 0.6 fusion.14
  35.2 0.6 gather_fusion.2
  35.9 0.9 %copy.211 = f32[13,15,4,128]{3,2,1,0:T(4,128)} copy(f32[13,15,4,128]{3,0,2,1:T(8,128)S(1)} %bitcast.777) | data formatting | bytes 798720 | tf_op jit(solution)/shard_map/gather | solution.py:266
  36.8 1.2 %reshape.364 = f32[13,15,512]{2,1,0:T(8,128)S(1)} reshape(f32[13,15,4,128]{3,2,1,0:T(4,128)} %copy.211) | data formatting | bytes 798720 | tf_op jit(solution)/shard_map/reshape | solution.py:267
  38.0 0.5 fusion.26
  38.5 0.3 fusion.33
  38.8 0.5 convolution_bitcast_fusion.2
  39.4 4.7 %collective-permute-start.2 = (f32[13,15,64]{2,1,0:T(8,128)S(1)}, f32[13,15,64]{2,1,0:T(8,128)S(1)}, u32[]{:S(2)}, u32[]{:S(2)}) collective-permute-start(f32[13,15,64]{2,1,0:T(8,128)S(1)} %get-tuple-element.45), channel_id=1, source_target_pairs={{0,1},{1,2},{2,3},{3,4},{4,5},{5,6},{6,7},{8,9},{9,10},{10,11},{11... | collective-permute-start | bytes 149768 | tf_op jit(solution)/shard_map/ppermute | solution.py:21
  44.1 1.5 %collective-permute-start.3 = (f32[13,15,64]{2,1,0:T(8,128)S(1)}, f32[13,15,64]{2,1,0:T(8,128)S(1)}, u32[]{:S(2)}, u32[]{:S(2)}) collective-permute-start(f32[13,15,64]{2,1,0:T(8,128)S(1)} %get-tuple-element.44), channel_id=1, source_target_pairs={{1,0},{2,1},{3,2},{4,3},{5,4},{6,5},{7,6},{9,8},{10,9},{11,10},{12... | collective-permute-start | bytes 149768 | tf_op jit(solution)/shard_map/ppermute | solution.py:22
  45.9 1.8 %fusion.3 = f32[6,35,128]{2,0,1:T(8,128)} fusion(f32[3,13,35,128,1]{3,2,0,1,4:T(8,128)S(1)} %copy-done.10, f32[13,35,128]{2,0,1:T(8,128)S(1)} %copy-done.2, f32[3,6,13,13]{3,2,1,0:T(8,128)S(1)} %copy-done.13), kind=kOutput, calls=%fused_computation.13 | convolution fusion | flops 82440960 | bytes 1051528 | tf_op jit(solution)/shard_map/dpfg,dgae->pfae/dot_general | solution.py:139
  47.8 0.8 %copy-done.4 = f32[6,35,128]{2,0,1:T(8,128)S(1)} copy-done((f32[6,35,128]{2,0,1:T(8,128)S(1)}, f32[6,35,128]{2,0,1:T(8,128)}, u32[]{:S(2)}) %copy-start.4) | copy-done | bytes 107544
  48.6 1.7 %fusion.4 = f32[13,35,128]{2,0,1:T(8,128)} fusion(f32[3,13,35,128,1]{3,2,0,1,4:T(8,128)S(1)} %maximum_bitcast_fusion.1, f32[6,35,128]{2,0,1:T(8,128)S(1)} %copy-done.4, f32[3,6,13,13]{3,2,1,0:T(8,128)S(1)} %copy-done.13), kind=kOutput, calls=%fused_computation.15 | convolution fusion | flops 82409600 | bytes 1051528 | tf_op jit(solution)/shard_map/dpfg,dfae->pgae/dot_general | solution.py:133
  50.2 0.3 convolution_add_fusion.1
  50.5 0.2 collective-permute-done.3
  50.7 0.3 convolution_add_fusion
  51.0 0.6 multiply_reduce_fusion
  51.9 0.6 copy-done.14
  52.7 1.5 %fusion = f32[13,15,4,128]{3,0,2,1:T(8,128)S(1)} fusion(f32[6,15,4,128]{3,0,2,1:T(8,128)S(1)} %bitcast.793, f32[13,15,4,128]{3,0,2,1:T(8,128)S(1)} %copy_subtract_fusion, f32[3,4,128]{2,0,1:T(4,128)S(1)} %copy-done.41, f32[3,6,13,13]{3,2,1,0:T(8,128)S(1)} %copy-done.14), kind=kOutput, calls=%fused_computation.7 | convolution fusion | flops 141573120 | bytes 1001352 | tf_op jit(solution)/shard_map/dpfg,dfnxe->pgnxe/dot_general | solution.py:145
  54.3 0.9 %copy-done.6 = f32[13,35,128]{2,0,1:T(8,128)S(1)} copy-done((f32[13,35,128]{2,0,1:T(8,128)S(1)}, f32[13,35,128]{2,0,1:T(8,128)}, u32[]{:S(2)}) %copy-start.6) | copy-done | bytes 232984
  55.1 0.6 fusion.17
  55.8 0.5 copy-done.9
  56.3 1.1 %fusion.2 = f32[6,35,128]{2,0,1:T(8,128)S(1)} fusion(f32[3,13,35,128,1]{3,2,0,1,4:T(8,128)S(1)} %copy-done.9, f32[13,35,128]{2,0,1:T(8,128)S(1)} %copy.225, f32[3,6,13,13]{3,2,1,0:T(8,128)S(1)} %copy-done.14), kind=kOutput, calls=%fused_computation.11 | convolution fusion | flops 82440960 | bytes 1051528 | tf_op jit(solution)/shard_map/dpfg,dgae->pfae/dot_general | solution.py:139
  57.5 1.6 %collective-permute-start.4 = (f32[6,35,64]{2,0,1:T(8,128)S(1)}, f32[6,35,64]{2,0,1:T(8,128)S(1)}, u32[]{:S(2)}, u32[]{:S(2)}) collective-permute-start(f32[6,35,64]{2,0,1:T(8,128)S(1)} %slice_select_fusion.1), channel_id=1, source_target_pairs={{0,16},{8,24},{16,0},{24,8},{1,17},{9,25},{17,1},{25,9},{2,18},{10... | collective-permute-start | bytes 161288 | tf_op jit(solution)/shard_map/ppermute | solution.py:161
  59.1 3.6 %collective-permute-done.4 = f32[6,35,64]{2,0,1:T(8,128)S(1)} collective-permute-done((f32[6,35,64]{2,0,1:T(8,128)S(1)}, f32[6,35,64]{2,0,1:T(8,128)S(1)}, u32[]{:S(2)}, u32[]{:S(2)}) %collective-permute-start.4) | collective-permute-done | bytes 53792 | tf_op jit(solution)/shard_map/ppermute | solution.py:161
  63.1 1.3 %collective-permute-done.5 = f32[6,35,32]{2,0,1:T(8,128)S(1)} collective-permute-done((f32[6,35,32]{2,0,1:T(8,128)S(1)}, f32[6,35,32]{2,0,1:T(8,128)S(1)}, u32[]{:S(2)}, u32[]{:S(2)}) %collective-permute-start.5) | collective-permute-done | bytes 26912 | tf_op jit(solution)/shard_map/ppermute | solution.py:161
  64.5 0.3 fusion.11
  64.9 0.6 broadcast_in_dim.16
  65.5 7.0 %all-to-all-start = ((f32[32,1,60]{2,1,0:T(1,128)}), f32[32,1,60]{2,1,0:T(1,128)S(1)}, u32[]{:S(2)}, u32[]{:S(2)}) async-start(f32[32,1,60]{2,1,0:T(1,128)} %broadcast_in_dim.16), calls=%async_computation | async-start | bytes 32768 | tf_op jit(solution)/shard_map/all_to_all | solution.py:290
  72.6 0.9 %copy.229 = f32[1,13,35,128]{3,0,2,1:T(1,128)} copy(f32[1,13,35,128]{3,2,1,0:T(8,128)S(1)} %bitcast.779) | data formatting | bytes 465920
  73.5 6.1 %all-to-all-done = f32[32,1,60]{2,1,0:T(1,128)S(1)} async-done(((f32[32,1,60]{2,1,0:T(1,128)}), f32[32,1,60]{2,1,0:T(1,128)S(1)}, u32[]{:S(2)}, u32[]{:S(2)}) %all-to-all-start) | async-done | bytes 7712 | tf_op jit(solution)/shard_map/all_to_all | solution.py:290
  80.0 0.2 slice_reduce_fusion
  80.2 0.2 fusion.10
  80.5 0.8 copy.230
  (145 shorter events, 3.2 us)
Async XLA Ops:
  3.9 2.6 %copy-start.49 = (s32[60]{0:T(128)S(1)}, s32[60]{0:T(128)}, u32[]{:S(2)}) copy-start(s32[60]{0:T(128)} %constant.67) | copy-start | bytes 724
  6.6 1.0 %copy-start.45 = (s32[128]{0:T(128)S(1)}, s32[128]{0:T(128)}, u32[]{:S(2)}) copy-start(s32[128]{0:T(128)} %param.35) | copy-start | bytes 1540
  7.3 8.4 %copy-start.47 = (s32[4,128]{1,0:T(4,128)S(1)}, s32[4,128]{1,0:T(4,128)}, u32[]{:S(2)}) copy-start(s32[4,128]{1,0:T(4,128)} %param.34) | copy-start | bytes 6148
  7.3 8.4 %copy-start.44 = (s32[4,128]{1,0:T(4,128)S(1)}, s32[4,128]{1,0:T(4,128)}, u32[]{:S(2)}) copy-start(s32[4,128]{1,0:T(4,128)} %param.33) | copy-start | bytes 6148
  7.7 8.8 %copy-start.48 = (f32[4,128]{1,0:T(4,128)S(1)}, f32[4,128]{1,0:T(4,128)}, u32[]{:S(2)}) copy-start(f32[4,128]{1,0:T(4,128)} %param.32) | copy-start | bytes 6148
  7.7 8.8 %copy-start.7 = (f32[3,35,35,1]{2,1,0,3:T(8,128)S(1)}, f32[3,35,35,1]{2,1,0,3:T(8,128)}, u32[]{:S(2)}) copy-start(f32[3,35,35,1]{2,1,0,3:T(8,128)} %constant.70) | copy-start | bytes 44104
  8.7 18.3 %collective-permute-start = (f32[13,15,64]{2,1,0:T(8,128)}, f32[13,15,64]{2,1,0:T(8,128)}, u32[]{:S(2)}, u32[]{:S(2)}) collective-permute-start(f32[13,15,64]{2,1,0:T(8,128)} %get-tuple-element.47), channel_id=1, source_target_pairs={{0,1},{1,2},{2,3},{3,4},{4,5},{5,6},{6,7},{8,9},{9,10},{10,11},{11... | collective-permute-start | bytes 149768 | tf_op jit(solution)/shard_map/ppermute | solution.py:21
  14.2 13.9 %collective-permute-start.1 = (f32[13,15,64]{2,1,0:T(8,128)}, f32[13,15,64]{2,1,0:T(8,128)}, u32[]{:S(2)}, u32[]{:S(2)}) collective-permute-start(f32[13,15,64]{2,1,0:T(8,128)} %get-tuple-element.46), channel_id=1, source_target_pairs={{1,0},{2,1},{3,2},{4,3},{5,4},{6,5},{7,6},{9,8},{10,9},{11,10},{12... | collective-permute-start | bytes 149768 | tf_op jit(solution)/shard_map/ppermute | solution.py:22
  15.7 1.3 %copy-start.43 = (f32[3,3,128]{2,1,0:T(4,128)S(1)}, f32[3,3,128]{2,1,0:T(4,128)}, u32[]{:S(2)}) copy-start(f32[3,3,128]{2,1,0:T(4,128)} %param.30) | copy-start | bytes 13828
  15.8 1.3 %copy-start = (f32[6,35,128]{2,1,0:T(8,128)S(1)}, f32[6,35,128]{2,1,0:T(8,128)}, u32[]{:S(2)}) copy-start(f32[6,35,128]{2,1,0:T(8,128)} %param.28) | copy-start | bytes 322564
  16.0 1.2 %copy-start.15 = (f32[1,2,13,35,128]{4,1,3,2,0:T(2,128)S(1)}, f32[1,2,13,35,128]{4,1,3,2,0:T(2,128)}, u32[]{:S(2)}) copy-start(f32[1,2,13,35,128]{4,1,3,2,0:T(2,128)} %param.27) | copy-start | bytes 1397764
  17.0 1.7 %copy-start.20 = (f32[128]{0:T(128)}, f32[128]{0:T(128)S(1)}, u32[]{:S(2)}) copy-start(f32[128]{0:T(128)S(1)} %get-tuple-element.50) | copy-start | bytes 1540
  17.0 1.7 %copy-start.22 = (f32[128]{0:T(128)}, f32[128]{0:T(128)S(1)}, u32[]{:S(2)}) copy-start(f32[128]{0:T(128)S(1)} %get-tuple-element.51) | copy-start | bytes 1540
  17.1 1.7 %copy-start.24 = (f32[128]{0:T(128)}, f32[128]{0:T(128)S(1)}, u32[]{:S(2)}) copy-start(f32[128]{0:T(128)S(1)} %get-tuple-element.52) | copy-start | bytes 1540
  17.1 1.7 %copy-start.26 = (f32[128]{0:T(128)}, f32[128]{0:T(128)S(1)}, u32[]{:S(2)}) copy-start(f32[128]{0:T(128)S(1)} %get-tuple-element.53) | copy-start | bytes 1540
  17.1 1.7 %copy-start.28 = (f32[128]{0:T(128)}, f32[128]{0:T(128)S(1)}, u32[]{:S(2)}) copy-start(f32[128]{0:T(128)S(1)} %get-tuple-element.54) | copy-start | bytes 1540
  17.1 1.7 %copy-start.30 = (f32[128]{0:T(128)}, f32[128]{0:T(128)S(1)}, u32[]{:S(2)}) copy-start(f32[128]{0:T(128)S(1)} %get-tuple-element.55) | copy-start | bytes 1540
  17.1 1.7 %copy-start.32 = (f32[128]{0:T(128)}, f32[128]{0:T(128)S(1)}, u32[]{:S(2)}) copy-start(f32[128]{0:T(128)S(1)} %get-tuple-element.56) | copy-start | bytes 1540
  17.1 1.9 %copy-start.3 = (f32[6,35,128]{2,0,1:T(8,128)}, f32[6,35,128]{2,0,1:T(8,128)S(1)}, u32[]{:S(2)}) copy-start(f32[6,35,128]{2,0,1:T(8,128)S(1)} %copy.197) | copy-start | bytes 322564
  18.8 0.9 %copy-start.11 = (f32[3,6,13,13]{3,2,1,0:T(8,128)S(1)}, f32[3,6,13,13]{3,2,1,0:T(8,128)}, u32[]{:S(2)}) copy-start(f32[3,6,13,13]{3,2,1,0:T(8,128)} %param.29) | copy-start | bytes 36508
  19.8 2.7 %copy-start.34 = (f32[15,15]{1,0:T(8,128)S(1)}, f32[15,15]{1,0:T(8,128)}, u32[]{:S(2)}) copy-start(f32[15,15]{1,0:T(8,128)} %constant.63.clone) | copy-start | bytes 2704
  19.8 2.7 %copy-start.35 = (f32[15,15]{1,0:T(8,128)S(1)}, f32[15,15]{1,0:T(8,128)}, u32[]{:S(2)}) copy-start(f32[15,15]{1,0:T(8,128)} %constant.62.clone) | copy-start | bytes 2704
  19.8 2.7 %copy-start.36 = (f32[15,15]{1,0:T(8,128)S(1)}, f32[15,15]{1,0:T(8,128)}, u32[]{:S(2)}) copy-start(f32[15,15]{1,0:T(8,128)} %constant.61.clone) | copy-start | bytes 2704
  19.8 2.7 %copy-start.37 = (f32[15,15]{1,0:T(8,128)S(1)}, f32[15,15]{1,0:T(8,128)}, u32[]{:S(2)}) copy-start(f32[15,15]{1,0:T(8,128)} %constant.60.clone) | copy-start | bytes 2704
  19.8 2.7 %copy-start.38 = (f32[15,15]{1,0:T(8,128)S(1)}, f32[15,15]{1,0:T(8,128)}, u32[]{:S(2)}) copy-start(f32[15,15]{1,0:T(8,128)} %constant.59.clone) | copy-start | bytes 2704
  19.8 2.7 %copy-start.39 = (f32[15,15]{1,0:T(8,128)S(1)}, f32[15,15]{1,0:T(8,128)}, u32[]{:S(2)}) copy-start(f32[15,15]{1,0:T(8,128)} %constant.58.clone) | copy-start | bytes 2704
  23.7 3.2 %copy-start.42 = (f32[3,4,128]{2,1,0:T(4,128)S(1)}, f32[3,4,128]{2,1,0:T(4,128)}, u32[]{:S(2)}) copy-start(f32[3,4,128]{2,1,0:T(4,128)} %param.31) | copy-start | bytes 18436
  27.0 5.0 %copy-start.40 = (f32[3,4,128]{2,0,1:T(4,128)}, f32[3,4,128]{2,0,1:T(4,128)S(1)}, u32[]{:S(2)}) copy-start(f32[3,4,128]{2,0,1:T(4,128)S(1)} %copy.201) | copy-start | bytes 18436
  30.9 1.2 %copy-start.12 = (f32[3,6,13,13]{3,2,1,0:T(8,128)S(1)}, f32[3,6,13,13]{3,2,1,0:T(8,128)}, u32[]{:S(2)}) copy-start(f32[3,6,13,13]{3,2,1,0:T(8,128)} %param.29) | copy-start | bytes 36508
  30.9 1.2 %copy-start.16 = (f32[60,6,128]{2,1,0:T(8,128)S(1)}, f32[60,6,128]{2,1,0:T(8,128)}, u32[]{:S(2)}) copy-start(f32[60,6,128]{2,1,0:T(8,128)} %copy.259) | copy-start | bytes 552964
  33.5 1.0 %copy-start.5 = (f32[13,35,128]{2,0,1:T(8,128)S(1)}, f32[13,35,128]{2,0,1:T(8,128)}, u32[]{:S(2)}) copy-start(f32[13,35,128]{2,0,1:T(8,128)} %fusion.5) | copy-start | bytes 698884
  33.5 1.0 %copy-start.19 = (f32[4,35,15,1]{1,2,0,3:T(8,128)S(1)}, f32[4,35,15,1]{1,2,0,3:T(8,128)}, u32[]{:S(2)}) copy-start(f32[4,35,15,1]{1,2,0,3:T(8,128)} %constant.71) | copy-start | bytes 25204
  35.2 0.7 copy-start.1
  35.9 2.6 %copy-start.46 = (s32[128]{0:T(128)S(1)}, s32[128]{0:T(128)}, u32[]{:S(2)}) copy-start(s32[128]{0:T(128)} %param.35) | copy-start | bytes 1540
  36.8 2.0 %copy-start.8 = (f32[3,35,35,1]{2,1,0,3:T(8,128)S(1)}, f32[3,35,35,1]{2,1,0,3:T(8,128)}, u32[]{:S(2)}) copy-start(f32[3,35,35,1]{2,1,0,3:T(8,128)} %constant.70) | copy-start | bytes 44104
  38.4 7.2 %copy-start.21 = (f32[128]{0:T(128)S(1)}, f32[128]{0:T(128)}, u32[]{:S(2)}) copy-start(f32[128]{0:T(128)} %copy-done.20) | copy-start | bytes 1540
  38.4 7.2 %copy-start.23 = (f32[128]{0:T(128)S(1)}, f32[128]{0:T(128)}, u32[]{:S(2)}) copy-start(f32[128]{0:T(128)} %copy-done.22) | copy-start | bytes 1540
  38.5 7.2 %copy-start.25 = (f32[128]{0:T(128)S(1)}, f32[128]{0:T(128)}, u32[]{:S(2)}) copy-start(f32[128]{0:T(128)} %copy-done.24) | copy-start | bytes 1540
  38.5 7.2 %copy-start.27 = (f32[128]{0:T(128)S(1)}, f32[128]{0:T(128)}, u32[]{:S(2)}) copy-start(f32[128]{0:T(128)} %copy-done.26) | copy-start | bytes 1540
  38.5 7.2 %copy-start.29 = (f32[128]{0:T(128)S(1)}, f32[128]{0:T(128)}, u32[]{:S(2)}) copy-start(f32[128]{0:T(128)} %copy-done.28) | copy-start | bytes 1540
  38.5 7.2 %copy-start.31 = (f32[128]{0:T(128)S(1)}, f32[128]{0:T(128)}, u32[]{:S(2)}) copy-start(f32[128]{0:T(128)} %copy-done.30) | copy-start | bytes 1540
  38.5 7.2 %copy-start.33 = (f32[128]{0:T(128)S(1)}, f32[128]{0:T(128)}, u32[]{:S(2)}) copy-start(f32[128]{0:T(128)} %copy-done.32) | copy-start | bytes 1540
  39.3 6.6 %copy-start.2 = (f32[13,35,128]{2,0,1:T(8,128)S(1)}, f32[13,35,128]{2,0,1:T(8,128)}, u32[]{:S(2)}) copy-start(f32[13,35,128]{2,0,1:T(8,128)} %copy-done.1) | copy-start | bytes 698884
  39.3 6.6 %copy-start.10 = (f32[3,13,35,128,1]{3,2,0,1,4:T(8,128)S(1)}, f32[3,13,35,128,1]{3,2,0,1,4:T(8,128)}, u32[]{:S(2)}) copy-start(f32[3,13,35,128,1]{3,2,0,1,4:T(8,128)} %maximum_bitcast_fusion.2) | copy-start | bytes 2096644
  39.3 6.6 %copy-start.13 = (f32[3,6,13,13]{3,2,1,0:T(8,128)S(1)}, f32[3,6,13,13]{3,2,1,0:T(8,128)}, u32[]{:S(2)}) copy-start(f32[3,6,13,13]{3,2,1,0:T(8,128)} %param.29) | copy-start | bytes 36508
  39.4 10.8 %collective-permute-start.2 = (f32[13,15,64]{2,1,0:T(8,128)S(1)}, f32[13,15,64]{2,1,0:T(8,128)S(1)}, u32[]{:S(2)}, u32[]{:S(2)}) collective-permute-start(f32[13,15,64]{2,1,0:T(8,128)S(1)} %get-tuple-element.45), channel_id=1, source_target_pairs={{0,1},{1,2},{2,3},{3,4},{4,5},{5,6},{6,7},{8,9},{9,10},{10,11},{11... | collective-permute-start | bytes 149768 | tf_op jit(solution)/shard_map/ppermute | solution.py:21
  44.1 6.6 %collective-permute-start.3 = (f32[13,15,64]{2,1,0:T(8,128)S(1)}, f32[13,15,64]{2,1,0:T(8,128)S(1)}, u32[]{:S(2)}, u32[]{:S(2)}) collective-permute-start(f32[13,15,64]{2,1,0:T(8,128)S(1)} %get-tuple-element.44), channel_id=1, source_target_pairs={{1,0},{2,1},{3,2},{4,3},{5,4},{6,5},{7,6},{9,8},{10,9},{11,10},{12... | collective-permute-start | bytes 149768 | tf_op jit(solution)/shard_map/ppermute | solution.py:22
  47.7 0.9 %copy-start.4 = (f32[6,35,128]{2,0,1:T(8,128)S(1)}, f32[6,35,128]{2,0,1:T(8,128)}, u32[]{:S(2)}) copy-start(f32[6,35,128]{2,0,1:T(8,128)} %copy-done.3) | copy-start | bytes 322564
  51.6 0.9 %copy-start.14 = (f32[3,6,13,13]{3,2,1,0:T(8,128)S(1)}, f32[3,6,13,13]{3,2,1,0:T(8,128)}, u32[]{:S(2)}) copy-start(f32[3,6,13,13]{3,2,1,0:T(8,128)} %param.29) | copy-start | bytes 36508
  51.7 1.0 %copy-start.17 = (f32[60,6,128]{2,1,0:T(8,128)S(1)}, f32[60,6,128]{2,1,0:T(8,128)}, u32[]{:S(2)}) copy-start(f32[60,6,128]{2,1,0:T(8,128)} %copy.259) | copy-start | bytes 552964
  51.7 1.0 %copy-start.41 = (f32[3,4,128]{2,0,1:T(4,128)S(1)}, f32[3,4,128]{2,0,1:T(4,128)}, u32[]{:S(2)}) copy-start(f32[3,4,128]{2,0,1:T(4,128)} %copy-done.40) | copy-start | bytes 18436
  54.2 1.0 %copy-start.6 = (f32[13,35,128]{2,0,1:T(8,128)S(1)}, f32[13,35,128]{2,0,1:T(8,128)}, u32[]{:S(2)}) copy-start(f32[13,35,128]{2,0,1:T(8,128)} %fusion.4) | copy-start | bytes 698884
  55.1 1.1 %copy-start.9 = (f32[3,13,35,128,1]{3,2,0,1,4:T(8,128)S(1)}, f32[3,13,35,128,1]{3,2,0,1,4:T(8,128)}, u32[]{:S(2)}) copy-start(f32[3,13,35,128,1]{3,2,0,1,4:T(8,128)} %maximum_bitcast_fusion.3) | copy-start | bytes 2096644
  55.7 1.6 %copy-start.18 = (f32[6,35,128]{2,0,1:T(8,128)S(1)}, f32[6,35,128]{2,0,1:T(8,128)}, u32[]{:S(2)}) copy-start(f32[6,35,128]{2,0,1:T(8,128)} %fusion.3) | copy-start | bytes 322564
  57.5 5.2 %collective-permute-start.4 = (f32[6,35,64]{2,0,1:T(8,128)S(1)}, f32[6,35,64]{2,0,1:T(8,128)S(1)}, u32[]{:S(2)}, u32[]{:S(2)}) collective-permute-start(f32[6,35,64]{2,0,1:T(8,128)S(1)} %slice_select_fusion.1), channel_id=1, source_target_pairs={{0,16},{8,24},{16,0},{24,8},{1,17},{9,25},{17,1},{25,9},{2,18},{10... | collective-permute-start | bytes 161288 | tf_op jit(solution)/shard_map/ppermute | solution.py:161
  62.9 1.4 %collective-permute-start.5 = (f32[6,35,32]{2,0,1:T(8,128)S(1)}, f32[6,35,32]{2,0,1:T(8,128)S(1)}, u32[]{:S(2)}, u32[]{:S(2)}) collective-permute-start(f32[6,35,32]{2,0,1:T(8,128)S(1)} %slice_select_fusion), channel_id=1, source_target_pairs={{0,8},{8,0},{16,24},{24,16},{1,9},{9,1},{17,25},{25,17},{2,10},{10... | collective-permute-start | bytes 80648 | tf_op jit(solution)/shard_map/ppermute | solution.py:161
  65.5 14.1 %all-to-all-start = ((f32[32,1,60]{2,1,0:T(1,128)}), f32[32,1,60]{2,1,0:T(1,128)S(1)}, u32[]{:S(2)}, u32[]{:S(2)}) async-start(f32[32,1,60]{2,1,0:T(1,128)} %broadcast_in_dim.16), calls=%async_computation | async-start | bytes 32768 | tf_op jit(solution)/shard_map/all_to_all | solution.py:290

commit v13 on v12

--- a/solution.py
+++ b/solution.py
@@ -254,10 +254,21 @@
     def own_share(rows):
         return lax.dynamic_slice_in_dim(rows, share_start, share_width, rows.ndim - 1)
 
-    step_share = own_share(history_steps)
-    change_share = own_share(history_changes)
-    both_share = jnp.concatenate([step_share, change_share], axis=0)
-    gram = jnp.sum(both_share[:, None] * change_share[None, :], axis=(2, 3, 4))
+    lane_pick = (
+        jnp.arange(elements, dtype=jnp.int32)[:, None]
+        == share_start + jnp.arange(share_width, dtype=jnp.int32)[None, :]
+    ).astype(jnp.float32)
+    both_share = jnp.einsum(
+        "ipae,ej->ipaj",
+        jnp.concatenate([history_steps, history_changes], axis=0),
+        lane_pick,
+        precision=HIGH,
+    )
+    pairs = history_steps.shape[0]
+    step_share = both_share[:pairs]
+    change_share = both_share[pairs:]
+    both_flat = both_share.reshape(2 * pairs, -1)
+    gram = jnp.dot(both_flat, both_flat[pairs:].T, precision=HIGH)
     step_share, change_share, gram, adjoint = lax.optimization_barrier(
         (step_share, change_share, gram, adjoint)
     )

time: 81.8 us -> 79 us (0.966)
  local copies, waits for them, and re-layouts: 20.8 us -> 14.4 us
  matrix products: 16.7 us -> 22.2 us
  other arithmetic: 8.98 us -> 7.68 us
    dot_general x0 -> x2, matrix products: none -> 6.24 us  [the longest x1 3.73 us: shards(): jnp.einsum('ipae,ej->ipaj', jnp.concatenate([history_steps, history_chang...]
    dynamic_slice x2 -> x0, local copies, waits for them, and re-layouts: 2.72 us -> none  [own_share(): lax.dynamic_slice_in_dim(rows, share_start, share_width, rows.ndim - 1)]
    unnamed x105 -> x96, local copies, waits for them, and re-layouts: 7.38 us -> 5.36 us
    reduce_sum x1 -> x0, other arithmetic: 1.65 us -> none  [shards(): gram = jnp.sum(both_share[:, None] * change_share[None, :], axis=(2, 3, 4))]
    gather x2, local copies, waits for them, and re-layouts: 3.23 us -> 1.65 us  [shards(): face_material = material[:, face_nodes.T, :]]
  transfers between devices with their start and end apart: 7 -> 7, of which waited for: 4 -> 4; matrix products, arithmetic and copies ran while one was open for 20% -> 18% of each run, Pallas kernels for 0% -> 0%
where the time goes in v13:
time: 79 us; the launch traced here: 78.5 us
  matrix products  22.2 us (28%)
  starting transfers between devices  21.1 us (27%)
  local copies, waits for them, and re-layouts  14.4 us (18%)
  waiting for transfers between devices  11.4 us (14%)
  other arithmetic  7.68 us (10%)
  between operations  1.73 us (2%)
    ppermute x2, starting transfers between devices, padded(): before = lax.ppermute(last, axis, up)  10.2 us
    all_to_all x1, starting transfers between devices, combine_sums(): lax.all_to_all(spread, ('shot', 'mesh'), 0, 0, tiled=False)  6.34 us
    all_to_all x1, waiting for transfers between devices, combine_sums(): lax.all_to_all(spread, ('shot', 'mesh'), 0, 0, tiled=False)  5.95 us
    unnamed x96, local copies, waits for them, and re-layouts  5.36 us
    ppermute x2, waiting for transfers between devices, halving_sum(): lax.ppermute(jnp.where(upper, low, high), axis, [(i, i ^ bit) for i in ra...  4.51 us
    dot_general x1, matrix products, shards(): jnp.einsum('ipae,ej->ipaj', jnp.concatenate([history_steps, history_chang...  3.73 us
    dot_general x2, matrix products, surface_term(): mixing = jnp.einsum('dpfg,dfnxe->pgnxe', coupling, weighted, precision=MIX)  2.98 us
    ppermute x2, starting transfers between devices, padded(): after = lax.ppermute(first, axis, down)  2.97 us
  transfers between devices with their start and end apart: 7, of which 4 were waited for; matrix products, arithmetic and copies ran while one was open for 18% of the time, Pallas kernels for 0%

profile of v13, /device:TPU:0, one launch (start us, length us, event | category | flops | bytes accessed | tf_op | source)
XLA Modules:
  0.0 78.5 jit_solution(3196763843694844447)
XLA Ops:
  0.6 3.7 %fusion.12 = f32[10,6,35,32]{2,3,1,0:T(8,128)S(1)} fusion(f32[5,6,35,128]{3,2,1,0:T(8,128)} %param.37, f32[5,6,35,128]{3,2,1,0:T(8,128)} %param.36, s32[32]{0:T(128)S(1)} %iota_add_fusion), kind=kOutput, calls=%fused_computation.28 | convolution fusion | flops 103492096 | bytes 1344128 | tf_op jit(solution)/shard_map/ipae,ej->ipaj/dot_general | solution.py:261
  4.5 2.5 %fusion.22 = f32[10,5]{0,1:T(8,128)S(1)} fusion(f32[10,6,35,32]{2,3,1,0:T(8,128)S(1)} %fusion.12, f32[5,6,35,32]{2,3,1,0:T(8,128)S(1)} %get-tuple-element.8), kind=kOutput, calls=%fused_computation.44 | convolution fusion | flops 4032000 | bytes 403400 | tf_op jit(solution)/shard_map/dot_general | solution.py:271
  7.1 0.6 gather_fusion.1
  7.8 0.2 copy.256
  8.0 0.2 reshape.367
  8.1 0.3 copy-done.41
  8.4 0.3 fusion.45
  8.7 0.7 fusion.155
  9.5 5.5 %collective-permute-start = (f32[13,15,64]{2,1,0:T(8,128)}, f32[13,15,64]{2,1,0:T(8,128)}, u32[]{:S(2)}, u32[]{:S(2)}) collective-permute-start(f32[13,15,64]{2,1,0:T(8,128)} %get-tuple-element.51), channel_id=1, source_target_pairs={{0,1},{1,2},{2,3},{3,4},{4,5},{5,6},{6,7},{8,9},{9,10},{10,11},{11... | collective-permute-start | bytes 149768 | tf_op jit(solution)/shard_map/ppermute | solution.py:21
  15.0 1.5 %collective-permute-start.1 = (f32[13,15,64]{2,1,0:T(8,128)}, f32[13,15,64]{2,1,0:T(8,128)}, u32[]{:S(2)}, u32[]{:S(2)}) collective-permute-start(f32[13,15,64]{2,1,0:T(8,128)} %get-tuple-element.50), channel_id=1, source_target_pairs={{1,0},{2,1},{3,2},{4,3},{5,4},{6,5},{7,6},{9,8},{10,9},{11,10},{12... | collective-permute-start | bytes 149768 | tf_op jit(solution)/shard_map/ppermute | solution.py:22
  16.5 0.2 iota_compare_fusion
  16.7 0.5 fusion.37
  17.2 0.5 convolution_bitcast_fusion.3
  17.9 0.4 fusion.152
  18.3 0.5 convolution_bitcast_fusion
  18.7 0.1 multiply_add_fusion.12
  19.0 0.5 convolution_bitcast_fusion.1
  19.8 0.8 %copy-done.8 = f32[3,6,13,13]{3,2,1,0:T(8,128)S(1)} copy-done((f32[3,6,13,13]{3,2,1,0:T(8,128)S(1)}, f32[3,6,13,13]{3,2,1,0:T(8,128)}, u32[]{:S(2)}) %copy-start.8) | copy-done | bytes 12192
  20.6 1.6 %fusion.5 = f32[13,35,128]{2,0,1:T(8,128)} fusion(f32[3,13,35,128,1]{3,2,0,1,4:T(8,128)S(1)} %maximum_bitcast_fusion, f32[6,35,128]{2,0,1:T(8,128)S(1)} %copy.250, f32[3,6,13,13]{3,2,1,0:T(8,128)S(1)} %copy-done.8), kind=kOutput, calls=%fused_computation.16 | convolution fusion | flops 82409600 | bytes 1051528 | tf_op jit(solution)/shard_map/dpfg,dfae->pgae/dot_general | solution.py:133
  22.3 1.0 %maximum_bitcast_fusion.3 = f32[3,13,35,128,1]{3,2,0,1,4:T(8,128)} fusion(f32[1,13,35,128]{3,2,0,1:T(8,128)S(1)} %get-tuple-element.37, f32[1,13,35,128]{3,2,0,1:T(8,128)S(1)} %get-tuple-element.36, f32[1,13,35,128]{3,2,0,1:T(8,128)S(1)} %get-tuple-element.35), kind=kLoop, calls=%fused_computation.57 | loop fusion | flops 349440 | bytes 1397760 | tf_op jit(solution)/shard_map/stack | solution.py:128
  23.3 0.3 multiply_add_fusion
  23.6 1.0 %maximum_bitcast_fusion.2 = f32[3,13,35,128,1]{3,2,0,1,4:T(8,128)} fusion(f32[1,13,35,128]{3,2,0,1:T(8,128)S(1)} %get-tuple-element.34, f32[1,13,35,128]{3,2,0,1:T(8,128)S(1)} %get-tuple-element.33, f32[1,13,35,128]{3,2,0,1:T(8,128)S(1)} %get-tuple-element.32), kind=kLoop, calls=%fused_computation.56 | loop fusion | flops 349440 | bytes 1397760 | tf_op jit(solution)/shard_map/stack | solution.py:128
  24.6 0.8 %gather_fusion = f32[60,6,128]{2,0,1:T(8,128)S(1)} fusion(f32[6,35,128]{2,1,0:T(8,128)S(1)} %copy-done, s32[1024]{0:T(1024)S(1)} %pad_clamp_fusion), kind=kCustom, calls=%fused_computation | custom fusion | bytes 368880 | tf_op jit(solution)/shard_map/gather | solution.py:232
  25.4 0.8 %copy.317 = f32[60,6,128]{2,1,0:T(8,128)} copy(f32[60,6,128]{2,0,1:T(8,128)S(1)} %gather_fusion) | data formatting | bytes 368640 | tf_op jit(solution)/shard_map/gather | solution.py:232
  26.3 1.2 %convolution_add_fusion.3 = f32[13,15,512]{2,1,0:T(8,128)S(1)} fusion(f32[13,15,512]{2,1,0:T(8,128)S(1)} %fusion.37, f32[13,15,64]{2,1,0:T(8,128)} %collective-permute-done, pred[640,512]{1,0:T(32,128)(4,1)S(1)} %iota_compare_fusion), kind=kOutput, calls=%fused_computation.35 | convolution fusion | flops 38438400 | bytes 908032 | tf_op jit(solution)/shard_map/fns,sj->fnj/dot_general | solution.py:282
  27.5 1.2 %convolution_add_fusion.2 = f32[13,15,512]{2,1,0:T(8,128)S(1)} fusion(f32[13,15,512]{2,1,0:T(8,128)S(1)} %convolution_add_fusion.3, f32[13,15,64]{2,1,0:T(8,128)} %collective-permute-done.1, pred[640,512]{1,0:T(32,128)(4,1)S(1)} %iota_compare_fusion), kind=kOutput, calls=%fused_computation.34 | convolution fusion | flops 38438400 | bytes 908032 | tf_op jit(solution)/shard_map/fns,sj->fnj/dot_general | solution.py:285
  28.6 0.6 multiply_reduce_fusion.1
  29.3 0.9 %reshape.368 = f32[13,15,4,128]{3,2,1,0:T(4,128)} reshape(f32[13,15,512]{2,1,0:T(8,128)S(1)} %multiply_reduce_fusion.1) | data formatting | bytes 798720 | tf_op jit(solution)/shard_map/reshape | solution.py:289
  30.2 1.1 %copy_subtract_fusion.1 = f32[13,15,4,128]{3,0,2,1:T(8,128)S(1)} fusion(f32[13,15,4,128]{3,0,2,1:T(8,128)S(1)} %bitcast.785, f32[13,15,4,128]{3,2,1,0:T(4,128)} %reshape.368), kind=kLoop, calls=%fused_computation.66 | loop fusion | flops 99840 | bytes 1198080 | tf_op jit(solution)/shard_map/sub | solution.py:289
  31.3 1.5 %fusion.1 = f32[13,15,4,128]{3,0,2,1:T(8,128)S(1)} fusion(f32[6,15,4,128]{3,0,2,1:T(8,128)S(1)} %bitcast.801, f32[13,15,4,128]{3,0,2,1:T(8,128)S(1)} %copy_subtract_fusion.1, f32[3,4,128]{2,0,1:T(4,128)S(1)} %copy.254, f32[3,6,13,13]{3,2,1,0:T(8,128)S(1)} %copy-done.9), kind=kOutput, calls=%fused_computation.8 | convolution fusion | flops 141573120 | bytes 1001352 | tf_op jit(solution)/shard_map/dpfg,dfnxe->pgnxe/dot_general | solution.py:145
  32.9 0.9 %copy-done.3 = f32[13,35,128]{2,0,1:T(8,128)S(1)} copy-done((f32[13,35,128]{2,0,1:T(8,128)S(1)}, f32[13,35,128]{2,0,1:T(8,128)}, u32[]{:S(2)}) %copy-start.3) | copy-done | bytes 232984
  33.7 0.6 fusion.18
  34.4 0.6 gather_fusion.2
  35.0 0.9 %copy.264 = f32[13,15,4,128]{3,2,1,0:T(4,128)} copy(f32[13,15,4,128]{3,0,2,1:T(8,128)S(1)} %bitcast.786) | data formatting | bytes 798720 | tf_op jit(solution)/shard_map/gather | solution.py:277
  35.9 1.2 %reshape.369 = f32[13,15,512]{2,1,0:T(8,128)S(1)} reshape(f32[13,15,4,128]{3,2,1,0:T(4,128)} %copy.264) | data formatting | bytes 798720 | tf_op jit(solution)/shard_map/reshape | solution.py:278
  37.1 0.5 fusion.36
  37.7 0.3 fusion.43
  38.0 0.5 convolution_bitcast_fusion.2
  38.6 4.7 %collective-permute-start.2 = (f32[13,15,64]{2,1,0:T(8,128)S(1)}, f32[13,15,64]{2,1,0:T(8,128)S(1)}, u32[]{:S(2)}, u32[]{:S(2)}) collective-permute-start(f32[13,15,64]{2,1,0:T(8,128)S(1)} %get-tuple-element.49), channel_id=1, source_target_pairs={{0,1},{1,2},{2,3},{3,4},{4,5},{5,6},{6,7},{8,9},{9,10},{10,11},{11... | collective-permute-start | bytes 149768 | tf_op jit(solution)/shard_map/ppermute | solution.py:21
  43.3 1.5 %collective-permute-start.3 = (f32[13,15,64]{2,1,0:T(8,128)S(1)}, f32[13,15,64]{2,1,0:T(8,128)S(1)}, u32[]{:S(2)}, u32[]{:S(2)}) collective-permute-start(f32[13,15,64]{2,1,0:T(8,128)S(1)} %get-tuple-element.48), channel_id=1, source_target_pairs={{1,0},{2,1},{3,2},{4,3},{5,4},{6,5},{7,6},{9,8},{10,9},{11,10},{12... | collective-permute-start | bytes 149768 | tf_op jit(solution)/shard_map/ppermute | solution.py:22
  45.0 1.8 %fusion.3 = f32[6,35,128]{2,0,1:T(8,128)} fusion(f32[3,13,35,128,1]{3,2,0,1,4:T(8,128)S(1)} %copy-done.7, f32[13,35,128]{2,0,1:T(8,128)S(1)} %copy.263, f32[3,6,13,13]{3,2,1,0:T(8,128)S(1)} %copy-done.10), kind=kOutput, calls=%fused_computation.12 | convolution fusion | flops 82440960 | bytes 1051528 | tf_op jit(solution)/shard_map/dpfg,dgae->pfae/dot_general | solution.py:139
  46.9 0.8 %copy-done.2 = f32[6,35,128]{2,0,1:T(8,128)S(1)} copy-done((f32[6,35,128]{2,0,1:T(8,128)S(1)}, f32[6,35,128]{2,0,1:T(8,128)}, u32[]{:S(2)}) %copy-start.2) | copy-done | bytes 107544
  47.7 0.9 %fusion.4 = f32[13,35,128]{2,0,1:T(8,128)S(1)} fusion(f32[3,13,35,128,1]{3,2,0,1,4:T(8,128)S(1)} %maximum_bitcast_fusion.1, f32[6,35,128]{2,0,1:T(8,128)S(1)} %copy-done.2, f32[3,6,13,13]{3,2,1,0:T(8,128)S(1)} %copy-done.10), kind=kOutput, calls=%fused_computation.14 | convolution fusion | flops 82409600 | bytes 1051528 | tf_op jit(solution)/shard_map/dpfg,dfae->pgae/dot_general | solution.py:133
  48.6 0.3 convolution_add_fusion.1
  48.9 0.9 %collective-permute-done.3 = f32[13,15,64]{2,1,0:T(8,128)S(1)} collective-permute-done((f32[13,15,64]{2,1,0:T(8,128)S(1)}, f32[13,15,64]{2,1,0:T(8,128)S(1)}, u32[]{:S(2)}, u32[]{:S(2)}) %collective-permute-start.3) | collective-permute-done | bytes 49952 | tf_op jit(solution)/shard_map/ppermute | solution.py:22
  49.9 0.3 convolution_add_fusion
  50.1 0.6 multiply_reduce_fusion
  50.8 0.1 reshape.370
  51.0 0.8 %copy-done.11 = f32[3,6,13,13]{3,2,1,0:T(8,128)S(1)} copy-done((f32[3,6,13,13]{3,2,1,0:T(8,128)S(1)}, f32[3,6,13,13]{3,2,1,0:T(8,128)}, u32[]{:S(2)}) %copy-start.11) | copy-done | bytes 12192
  51.9 1.5 %fusion = f32[13,15,4,128]{3,0,2,1:T(8,128)S(1)} fusion(f32[6,15,4,128]{3,0,2,1:T(8,128)S(1)} %bitcast.802, f32[13,15,4,128]{3,0,2,1:T(8,128)S(1)} %copy_subtract_fusion, f32[3,4,128]{2,0,1:T(4,128)S(1)} %copy.254, f32[3,6,13,13]{3,2,1,0:T(8,128)S(1)} %copy-done.11), kind=kOutput, calls=%fused_computation.6 | convolution fusion | flops 141573120 | bytes 1001352 | tf_op jit(solution)/shard_map/dpfg,dfnxe->pgnxe/dot_general | solution.py:145
  53.5 0.6 fusion.21
  54.2 0.5 copy-done.6
  54.7 1.1 %fusion.2 = f32[6,35,128]{2,0,1:T(8,128)S(1)} fusion(f32[3,13,35,128,1]{3,2,0,1,4:T(8,128)S(1)} %copy-done.6, f32[13,35,128]{2,0,1:T(8,128)S(1)} %copy.278, f32[3,6,13,13]{3,2,1,0:T(8,128)S(1)} %copy-done.11), kind=kOutput, calls=%fused_computation.10 | convolution fusion | flops 82440960 | bytes 1051528 | tf_op jit(solution)/shard_map/dpfg,dgae->pfae/dot_general | solution.py:139
  55.9 1.6 %collective-permute-start.4 = (f32[6,35,64]{2,1,0:T(8,128)S(1)}, f32[6,35,64]{2,1,0:T(8,128)S(1)}, u32[]{:S(2)}, u32[]{:S(2)}) collective-permute-start(f32[6,35,64]{2,1,0:T(8,128)S(1)} %slice_select_fusion.1), channel_id=1, source_target_pairs={{0,16},{8,24},{16,0},{24,8},{1,17},{9,25},{17,1},{25,9},{2,18},{10... | collective-permute-start | bytes 161288 | tf_op jit(solution)/shard_map/ppermute | solution.py:161
  57.5 3.4 %collective-permute-done.4 = f32[6,35,64]{2,1,0:T(8,128)S(1)} collective-permute-done((f32[6,35,64]{2,1,0:T(8,128)S(1)}, f32[6,35,64]{2,1,0:T(8,128)S(1)}, u32[]{:S(2)}, u32[]{:S(2)}) %collective-permute-start.4) | collective-permute-done | bytes 53792 | tf_op jit(solution)/shard_map/ppermute | solution.py:161
  61.4 1.1 %collective-permute-done.5 = f32[6,35,32]{2,1,0:T(8,128)S(1)} collective-permute-done((f32[6,35,32]{2,1,0:T(8,128)S(1)}, f32[6,35,32]{2,1,0:T(8,128)S(1)}, u32[]{:S(2)}, u32[]{:S(2)}) %collective-permute-start.5) | collective-permute-done | bytes 26912 | tf_op jit(solution)/shard_map/ppermute | solution.py:161
  62.7 0.2 fusion.26
  63.0 0.6 broadcast_in_dim.16
  63.7 6.3 %all-to-all-start = ((f32[32,1,60]{2,1,0:T(1,128)}), f32[32,1,60]{2,1,0:T(1,128)S(1)}, u32[]{:S(2)}, u32[]{:S(2)}) async-start(f32[32,1,60]{2,1,0:T(1,128)} %broadcast_in_dim.16), calls=%async_computation | async-start | bytes 32768 | tf_op jit(solution)/shard_map/all_to_all | solution.py:301
  70.1 0.9 %copy.286 = f32[1,13,35,128]{3,0,2,1:T(1,128)} copy(f32[1,13,35,128]{3,2,1,0:T(8,128)S(1)} %bitcast.788) | data formatting | bytes 465920
  71.1 5.9 %all-to-all-done = f32[32,1,60]{2,1,0:T(1,128)S(1)} async-done(((f32[32,1,60]{2,1,0:T(1,128)}), f32[32,1,60]{2,1,0:T(1,128)S(1)}, u32[]{:S(2)}, u32[]{:S(2)}) %all-to-all-start) | async-done | bytes 7712 | tf_op jit(solution)/shard_map/all_to_all | solution.py:301
  77.5 0.2 slice_reduce_fusion
  77.7 0.2 fusion.25
  77.9 0.6 neg.22
  (137 shorter events, 3.0 us)
Async XLA Ops:
  4.5 2.5 %copy-start.15 = (f32[1,13,35,128]{3,0,2,1:T(1,128)S(1)}, f32[1,13,35,128]{3,0,2,1:T(1,128)}, u32[]{:S(2)}) copy-start(f32[1,13,35,128]{3,0,2,1:T(1,128)} %param.26) | copy-start | bytes 698884
  4.5 2.6 %copy-start.45 = (s32[60]{0:T(128)S(1)}, s32[60]{0:T(128)}, u32[]{:S(2)}) copy-start(s32[60]{0:T(128)} %constant.65) | copy-start | bytes 724
  7.8 0.7 copy-start.41
  7.9 8.5 %copy-start.43 = (s32[4,128]{1,0:T(4,128)S(1)}, s32[4,128]{1,0:T(4,128)}, u32[]{:S(2)}) copy-start(s32[4,128]{1,0:T(4,128)} %param.34) | copy-start | bytes 6148
  7.9 8.5 %copy-start.40 = (s32[4,128]{1,0:T(4,128)S(1)}, s32[4,128]{1,0:T(4,128)}, u32[]{:S(2)}) copy-start(s32[4,128]{1,0:T(4,128)} %param.33) | copy-start | bytes 6148
  8.7 8.5 %copy-start.44 = (f32[4,128]{1,0:T(4,128)S(1)}, f32[4,128]{1,0:T(4,128)}, u32[]{:S(2)}) copy-start(f32[4,128]{1,0:T(4,128)} %param.32) | copy-start | bytes 6148
  8.7 8.5 %copy-start.4 = (f32[3,35,35,1]{2,1,0,3:T(8,128)S(1)}, f32[3,35,35,1]{2,1,0,3:T(8,128)}, u32[]{:S(2)}) copy-start(f32[3,35,35,1]{2,1,0,3:T(8,128)} %constant.68) | copy-start | bytes 44104
  9.5 16.8 %collective-permute-start = (f32[13,15,64]{2,1,0:T(8,128)}, f32[13,15,64]{2,1,0:T(8,128)}, u32[]{:S(2)}, u32[]{:S(2)}) collective-permute-start(f32[13,15,64]{2,1,0:T(8,128)} %get-tuple-element.51), channel_id=1, source_target_pairs={{0,1},{1,2},{2,3},{3,4},{4,5},{5,6},{6,7},{8,9},{9,10},{10,11},{11... | collective-permute-start | bytes 149768 | tf_op jit(solution)/shard_map/ppermute | solution.py:21
  15.0 12.5 %collective-permute-start.1 = (f32[13,15,64]{2,1,0:T(8,128)}, f32[13,15,64]{2,1,0:T(8,128)}, u32[]{:S(2)}, u32[]{:S(2)}) collective-permute-start(f32[13,15,64]{2,1,0:T(8,128)} %get-tuple-element.50), channel_id=1, source_target_pairs={{1,0},{2,1},{3,2},{4,3},{5,4},{6,5},{7,6},{9,8},{10,9},{11,10},{12... | collective-permute-start | bytes 149768 | tf_op jit(solution)/shard_map/ppermute | solution.py:22
  16.7 1.0 %copy-start.39 = (f32[3,3,128]{2,1,0:T(4,128)S(1)}, f32[3,3,128]{2,1,0:T(4,128)}, u32[]{:S(2)}) copy-start(f32[3,3,128]{2,1,0:T(4,128)} %param.30) | copy-start | bytes 13828
  16.7 1.1 %copy-start = (f32[6,35,128]{2,1,0:T(8,128)S(1)}, f32[6,35,128]{2,1,0:T(8,128)}, u32[]{:S(2)}) copy-start(f32[6,35,128]{2,1,0:T(8,128)} %param.28) | copy-start | bytes 322564
  16.7 1.2 %copy-start.12 = (f32[1,2,13,35,128]{4,1,3,2,0:T(2,128)S(1)}, f32[1,2,13,35,128]{4,1,3,2,0:T(2,128)}, u32[]{:S(2)}) copy-start(f32[1,2,13,35,128]{4,1,3,2,0:T(2,128)} %param.27) | copy-start | bytes 1397764
  17.8 1.8 %copy-start.18 = (f32[128]{0:T(128)}, f32[128]{0:T(128)S(1)}, u32[]{:S(2)}) copy-start(f32[128]{0:T(128)S(1)} %get-tuple-element.54) | copy-start | bytes 1540
  17.8 1.8 %copy-start.20 = (f32[128]{0:T(128)}, f32[128]{0:T(128)S(1)}, u32[]{:S(2)}) copy-start(f32[128]{0:T(128)S(1)} %get-tuple-element.55) | copy-start | bytes 1540
  17.8 1.8 %copy-start.22 = (f32[128]{0:T(128)}, f32[128]{0:T(128)S(1)}, u32[]{:S(2)}) copy-start(f32[128]{0:T(128)S(1)} %get-tuple-element.56) | copy-start | bytes 1540
  17.8 1.8 %copy-start.24 = (f32[128]{0:T(128)}, f32[128]{0:T(128)S(1)}, u32[]{:S(2)}) copy-start(f32[128]{0:T(128)S(1)} %get-tuple-element.57) | copy-start | bytes 1540
  17.8 1.8 %copy-start.26 = (f32[128]{0:T(128)}, f32[128]{0:T(128)S(1)}, u32[]{:S(2)}) copy-start(f32[128]{0:T(128)S(1)} %get-tuple-element.58) | copy-start | bytes 1540
  17.8 1.8 %copy-start.28 = (f32[128]{0:T(128)}, f32[128]{0:T(128)S(1)}, u32[]{:S(2)}) copy-start(f32[128]{0:T(128)S(1)} %get-tuple-element.59) | copy-start | bytes 1540
  17.8 1.8 %copy-start.30 = (f32[128]{0:T(128)}, f32[128]{0:T(128)S(1)}, u32[]{:S(2)}) copy-start(f32[128]{0:T(128)S(1)} %get-tuple-element.60) | copy-start | bytes 1540
  17.9 1.9 %copy-start.1 = (f32[6,35,128]{2,0,1:T(8,128)}, f32[6,35,128]{2,0,1:T(8,128)S(1)}, u32[]{:S(2)}) copy-start(f32[6,35,128]{2,0,1:T(8,128)S(1)} %copy.250) | copy-start | bytes 322564
  19.7 0.9 %copy-start.8 = (f32[3,6,13,13]{3,2,1,0:T(8,128)S(1)}, f32[3,6,13,13]{3,2,1,0:T(8,128)}, u32[]{:S(2)}) copy-start(f32[3,6,13,13]{3,2,1,0:T(8,128)} %param.29) | copy-start | bytes 36508
  22.3 1.0 %copy-start.32 = (f32[15,15]{1,0:T(8,128)S(1)}, f32[15,15]{1,0:T(8,128)}, u32[]{:S(2)}) copy-start(f32[15,15]{1,0:T(8,128)} %constant.61.clone) | copy-start | bytes 2704
  22.3 1.0 %copy-start.33 = (f32[15,15]{1,0:T(8,128)S(1)}, f32[15,15]{1,0:T(8,128)}, u32[]{:S(2)}) copy-start(f32[15,15]{1,0:T(8,128)} %constant.60.clone) | copy-start | bytes 2704
  22.3 1.0 %copy-start.34 = (f32[15,15]{1,0:T(8,128)S(1)}, f32[15,15]{1,0:T(8,128)}, u32[]{:S(2)}) copy-start(f32[15,15]{1,0:T(8,128)} %constant.59.clone) | copy-start | bytes 2704
  22.3 1.0 %copy-start.35 = (f32[15,15]{1,0:T(8,128)S(1)}, f32[15,15]{1,0:T(8,128)}, u32[]{:S(2)}) copy-start(f32[15,15]{1,0:T(8,128)} %constant.58.clone) | copy-start | bytes 2704
  22.3 1.0 %copy-start.36 = (f32[15,15]{1,0:T(8,128)S(1)}, f32[15,15]{1,0:T(8,128)}, u32[]{:S(2)}) copy-start(f32[15,15]{1,0:T(8,128)} %constant.57.clone) | copy-start | bytes 2704
  22.3 1.0 %copy-start.37 = (f32[15,15]{1,0:T(8,128)S(1)}, f32[15,15]{1,0:T(8,128)}, u32[]{:S(2)}) copy-start(f32[15,15]{1,0:T(8,128)} %constant.56.clone) | copy-start | bytes 2704
  24.6 1.7 %copy-start.38 = (f32[3,4,128]{2,1,0:T(4,128)S(1)}, f32[3,4,128]{2,1,0:T(4,128)}, u32[]{:S(2)}) copy-start(f32[3,4,128]{2,1,0:T(4,128)} %param.31) | copy-start | bytes 18436
  29.3 2.0 %copy-start.9 = (f32[3,6,13,13]{3,2,1,0:T(8,128)S(1)}, f32[3,6,13,13]{3,2,1,0:T(8,128)}, u32[]{:S(2)}) copy-start(f32[3,6,13,13]{3,2,1,0:T(8,128)} %param.29) | copy-start | bytes 36508
  29.3 2.0 %copy-start.13 = (f32[60,6,128]{2,1,0:T(8,128)S(1)}, f32[60,6,128]{2,1,0:T(8,128)}, u32[]{:S(2)}) copy-start(f32[60,6,128]{2,1,0:T(8,128)} %copy.317) | copy-start | bytes 552964
  32.8 1.0 %copy-start.3 = (f32[13,35,128]{2,0,1:T(8,128)S(1)}, f32[13,35,128]{2,0,1:T(8,128)}, u32[]{:S(2)}) copy-start(f32[13,35,128]{2,0,1:T(8,128)} %fusion.5) | copy-start | bytes 698884
  32.8 1.0 %copy-start.17 = (f32[4,35,15,1]{1,2,0,3:T(8,128)S(1)}, f32[4,35,15,1]{1,2,0,3:T(8,128)}, u32[]{:S(2)}) copy-start(f32[4,35,15,1]{1,2,0,3:T(8,128)} %constant.69) | copy-start | bytes 25204
  35.9 1.7 %copy-start.42 = (s32[128]{0:T(128)S(1)}, s32[128]{0:T(128)}, u32[]{:S(2)}) copy-start(s32[128]{0:T(128)} %param.35) | copy-start | bytes 1540
  37.1 0.9 %copy-start.5 = (f32[3,35,35,1]{2,1,0,3:T(8,128)S(1)}, f32[3,35,35,1]{2,1,0,3:T(8,128)}, u32[]{:S(2)}) copy-start(f32[3,35,35,1]{2,1,0,3:T(8,128)} %constant.68) | copy-start | bytes 44104
  37.6 7.2 %copy-start.19 = (f32[128]{0:T(128)S(1)}, f32[128]{0:T(128)}, u32[]{:S(2)}) copy-start(f32[128]{0:T(128)} %copy-done.18) | copy-start | bytes 1540
  37.6 7.2 %copy-start.21 = (f32[128]{0:T(128)S(1)}, f32[128]{0:T(128)}, u32[]{:S(2)}) copy-start(f32[128]{0:T(128)} %copy-done.20) | copy-start | bytes 1540
  37.6 7.2 %copy-start.23 = (f32[128]{0:T(128)S(1)}, f32[128]{0:T(128)}, u32[]{:S(2)}) copy-start(f32[128]{0:T(128)} %copy-done.22) | copy-start | bytes 1540
  37.6 7.2 %copy-start.25 = (f32[128]{0:T(128)S(1)}, f32[128]{0:T(128)}, u32[]{:S(2)}) copy-start(f32[128]{0:T(128)} %copy-done.24) | copy-start | bytes 1540
  37.6 7.2 %copy-start.27 = (f32[128]{0:T(128)S(1)}, f32[128]{0:T(128)}, u32[]{:S(2)}) copy-start(f32[128]{0:T(128)} %copy-done.26) | copy-start | bytes 1540
  37.6 7.2 %copy-start.29 = (f32[128]{0:T(128)S(1)}, f32[128]{0:T(128)}, u32[]{:S(2)}) copy-start(f32[128]{0:T(128)} %copy-done.28) | copy-start | bytes 1540
  37.6 7.2 %copy-start.31 = (f32[128]{0:T(128)S(1)}, f32[128]{0:T(128)}, u32[]{:S(2)}) copy-start(f32[128]{0:T(128)} %copy-done.30) | copy-start | bytes 1540
  38.5 6.5 %copy-start.7 = (f32[3,13,35,128,1]{3,2,0,1,4:T(8,128)S(1)}, f32[3,13,35,128,1]{3,2,0,1,4:T(8,128)}, u32[]{:S(2)}) copy-start(f32[3,13,35,128,1]{3,2,0,1,4:T(8,128)} %maximum_bitcast_fusion.2) | copy-start | bytes 2096644
  38.5 6.5 %copy-start.10 = (f32[3,6,13,13]{3,2,1,0:T(8,128)S(1)}, f32[3,6,13,13]{3,2,1,0:T(8,128)}, u32[]{:S(2)}) copy-start(f32[3,6,13,13]{3,2,1,0:T(8,128)} %param.29) | copy-start | bytes 36508
  38.6 10.0 %collective-permute-start.2 = (f32[13,15,64]{2,1,0:T(8,128)S(1)}, f32[13,15,64]{2,1,0:T(8,128)S(1)}, u32[]{:S(2)}, u32[]{:S(2)}) collective-permute-start(f32[13,15,64]{2,1,0:T(8,128)S(1)} %get-tuple-element.49), channel_id=1, source_target_pairs={{0,1},{1,2},{2,3},{3,4},{4,5},{5,6},{6,7},{8,9},{9,10},{10,11},{11... | collective-permute-start | bytes 149768 | tf_op jit(solution)/shard_map/ppermute | solution.py:21
  43.3 6.6 %collective-permute-start.3 = (f32[13,15,64]{2,1,0:T(8,128)S(1)}, f32[13,15,64]{2,1,0:T(8,128)S(1)}, u32[]{:S(2)}, u32[]{:S(2)}) collective-permute-start(f32[13,15,64]{2,1,0:T(8,128)S(1)} %get-tuple-element.48), channel_id=1, source_target_pairs={{1,0},{2,1},{3,2},{4,3},{5,4},{6,5},{7,6},{9,8},{10,9},{11,10},{12... | collective-permute-start | bytes 149768 | tf_op jit(solution)/shard_map/ppermute | solution.py:22
  46.8 0.9 %copy-start.2 = (f32[6,35,128]{2,0,1:T(8,128)S(1)}, f32[6,35,128]{2,0,1:T(8,128)}, u32[]{:S(2)}) copy-start(f32[6,35,128]{2,0,1:T(8,128)} %copy-done.1) | copy-start | bytes 322564
  50.9 0.9 %copy-start.11 = (f32[3,6,13,13]{3,2,1,0:T(8,128)S(1)}, f32[3,6,13,13]{3,2,1,0:T(8,128)}, u32[]{:S(2)}) copy-start(f32[3,6,13,13]{3,2,1,0:T(8,128)} %param.29) | copy-start | bytes 36508
  50.9 1.0 %copy-start.14 = (f32[60,6,128]{2,1,0:T(8,128)S(1)}, f32[60,6,128]{2,1,0:T(8,128)}, u32[]{:S(2)}) copy-start(f32[60,6,128]{2,1,0:T(8,128)} %copy.317) | copy-start | bytes 552964
  53.5 1.1 %copy-start.6 = (f32[3,13,35,128,1]{3,2,0,1,4:T(8,128)S(1)}, f32[3,13,35,128,1]{3,2,0,1,4:T(8,128)}, u32[]{:S(2)}) copy-start(f32[3,13,35,128,1]{3,2,0,1,4:T(8,128)} %maximum_bitcast_fusion.3) | copy-start | bytes 2096644
  54.7 1.1 %copy-start.16 = (f32[6,35,128]{2,0,1:T(8,128)S(1)}, f32[6,35,128]{2,0,1:T(8,128)}, u32[]{:S(2)}) copy-start(f32[6,35,128]{2,0,1:T(8,128)} %fusion.3) | copy-start | bytes 322564
  55.9 4.9 %collective-permute-start.4 = (f32[6,35,64]{2,1,0:T(8,128)S(1)}, f32[6,35,64]{2,1,0:T(8,128)S(1)}, u32[]{:S(2)}, u32[]{:S(2)}) collective-permute-start(f32[6,35,64]{2,1,0:T(8,128)S(1)} %slice_select_fusion.1), channel_id=1, source_target_pairs={{0,16},{8,24},{16,0},{24,8},{1,17},{9,25},{17,1},{25,9},{2,18},{10... | collective-permute-start | bytes 161288 | tf_op jit(solution)/shard_map/ppermute | solution.py:161
  61.1 1.4 %collective-permute-start.5 = (f32[6,35,32]{2,1,0:T(8,128)S(1)}, f32[6,35,32]{2,1,0:T(8,128)S(1)}, u32[]{:S(2)}, u32[]{:S(2)}) collective-permute-start(f32[6,35,32]{2,1,0:T(8,128)S(1)} %slice_select_fusion), channel_id=1, source_target_pairs={{0,8},{8,0},{16,24},{24,16},{1,9},{9,1},{17,25},{25,17},{2,10},{10... | collective-permute-start | bytes 80648 | tf_op jit(solution)/shard_map/ppermute | solution.py:161
  63.7 13.4 %all-to-all-start = ((f32[32,1,60]{2,1,0:T(1,128)}), f32[32,1,60]{2,1,0:T(1,128)S(1)}, u32[]{:S(2)}, u32[]{:S(2)}) async-start(f32[32,1,60]{2,1,0:T(1,128)} %broadcast_in_dim.16), calls=%async_computation | async-start | bytes 32768 | tf_op jit(solution)/shard_map/all_to_all | solution.py:301

commit v14 on v13

--- a/solution.py
+++ b/solution.py
@@ -262,13 +262,12 @@
         "ipae,ej->ipaj",
         jnp.concatenate([history_steps, history_changes], axis=0),
         lane_pick,
-        precision=HIGH,
+        precision=MIX,
     )
     pairs = history_steps.shape[0]
     step_share = both_share[:pairs]
     change_share = both_share[pairs:]
-    both_flat = both_share.reshape(2 * pairs, -1)
-    gram = jnp.dot(both_flat, both_flat[pairs:].T, precision=HIGH)
+    gram = jnp.sum(both_share[:, None] * change_share[None, :], axis=(2, 3, 4))
     step_share, change_share, gram, adjoint = lax.optimization_barrier(
         (step_share, change_share, gram, adjoint)
     )

time: 79 us -> 76.7 us (0.971)
  matrix products: 22.2 us -> 18.9 us
    dot_general x1 -> x0, matrix products: 2.51 us -> none  [shards(): gram = jnp.dot(both_flat, both_flat[pairs:].T, precision=HIGH)]
    dot_general x1, matrix products: 3.73 us -> 2.93 us  [shards(): jnp.einsum('ipae,ej->ipaj', jnp.concatenate([history_steps, history_chang...]
    unnamed x96 -> x100, local copies, waits for them, and re-layouts: 5.36 us -> 5.67 us
  transfers between devices with their start and end apart: 7 -> 7, of which waited for: 4 -> 4; matrix products, arithmetic and copies ran while one was open for 18% -> 19% of each run, Pallas kernels for 0% -> 0%
where the time goes in v14:
time: 76.7 us; the launch traced here: 76.2 us
  starting transfers between devices  21.1 us (28%)
  matrix products  18.9 us (25%)
  local copies, waits for them, and re-layouts  14.6 us (19%)
  waiting for transfers between devices  11.5 us (15%)
  other arithmetic  8.29 us (11%)
  between operations  1.76 us (2%)
    ppermute x2, starting transfers between devices, padded(): before = lax.ppermute(last, axis, up)  10.2 us
    all_to_all x1, starting transfers between devices, combine_sums(): lax.all_to_all(spread, ('shot', 'mesh'), 0, 0, tiled=False)  6.33 us
    all_to_all x1, waiting for transfers between devices, combine_sums(): lax.all_to_all(spread, ('shot', 'mesh'), 0, 0, tiled=False)  5.95 us
    unnamed x100, local copies, waits for them, and re-layouts  5.67 us
    ppermute x2, waiting for transfers between devices, halving_sum(): lax.ppermute(jnp.where(upper, low, high), axis, [(i, i ^ bit) for i in ra...  4.6 us
    dot_general x2, matrix products, surface_term(): mixing = jnp.einsum('dpfg,dfnxe->pgnxe', coupling, weighted, precision=MIX)  2.98 us
    ppermute x2, starting transfers between devices, padded(): after = lax.ppermute(first, axis, down)  2.97 us
    dot_general x1, matrix products, shards(): jnp.einsum('ipae,ej->ipaj', jnp.concatenate([history_steps, history_chang...  2.93 us
  transfers between devices with their start and end apart: 7, of which 4 were waited for; matrix products, arithmetic and copies ran while one was open for 19% of the time, Pallas kernels for 0%

profile of v14, /device:TPU:0, one launch (start us, length us, event | category | flops | bytes accessed | tf_op | source)
XLA Modules:
  0.0 76.2 jit_solution(6061686045184057268)
XLA Ops:
  0.6 2.9 %fusion.10 = f32[10,6,35,32]{2,3,1,0:T(8,128)S(1)} fusion(f32[5,6,35,128]{3,2,1,0:T(8,128)} %param.37, f32[5,6,35,128]{3,2,1,0:T(8,128)} %param.36, s32[32]{0:T(128)S(1)} %iota_add_fusion), kind=kOutput, calls=%fused_computation.27 | convolution fusion | flops 51882496 | bytes 1344128 | tf_op jit(solution)/shard_map/ipae,ej->ipaj/dot_general | solution.py:261
  3.7 0.6 multiply_reduce_fusion.2
  4.3 0.3 copy-done.15
  4.7 0.6 gather_fusion.1
  5.4 0.2 copy.244
  5.6 0.2 reshape.367
  5.7 0.3 copy-done.43
  6.0 0.3 fusion.39
  6.4 0.7 fusion.149
  7.1 5.5 %collective-permute-start = (f32[13,15,64]{2,1,0:T(8,128)}, f32[13,15,64]{2,1,0:T(8,128)}, u32[]{:S(2)}, u32[]{:S(2)}) collective-permute-start(f32[13,15,64]{2,1,0:T(8,128)} %get-tuple-element.51), channel_id=1, source_target_pairs={{0,1},{1,2},{2,3},{3,4},{4,5},{5,6},{6,7},{8,9},{9,10},{10,11},{11... | collective-permute-start | bytes 149768 | tf_op jit(solution)/shard_map/ppermute | solution.py:21
  12.6 1.5 %collective-permute-start.1 = (f32[13,15,64]{2,1,0:T(8,128)}, f32[13,15,64]{2,1,0:T(8,128)}, u32[]{:S(2)}, u32[]{:S(2)}) collective-permute-start(f32[13,15,64]{2,1,0:T(8,128)} %get-tuple-element.50), channel_id=1, source_target_pairs={{1,0},{2,1},{3,2},{4,3},{5,4},{6,5},{7,6},{9,8},{10,9},{11,10},{12... | collective-permute-start | bytes 149768 | tf_op jit(solution)/shard_map/ppermute | solution.py:22
  14.1 0.2 iota_compare_fusion
  14.3 0.5 fusion.31
  14.8 0.5 convolution_bitcast_fusion.3
  15.5 0.4 fusion.146
  15.9 0.5 convolution_bitcast_fusion
  16.7 0.5 convolution_bitcast_fusion.1
  17.5 0.8 %copy-done.8 = f32[3,6,13,13]{3,2,1,0:T(8,128)S(1)} copy-done((f32[3,6,13,13]{3,2,1,0:T(8,128)S(1)}, f32[3,6,13,13]{3,2,1,0:T(8,128)}, u32[]{:S(2)}) %copy-start.8) | copy-done | bytes 12192
  18.3 1.6 %fusion.5 = f32[13,35,128]{2,0,1:T(8,128)} fusion(f32[3,13,35,128,1]{3,2,0,1,4:T(8,128)S(1)} %maximum_bitcast_fusion, f32[6,35,128]{2,0,1:T(8,128)S(1)} %copy.238, f32[3,6,13,13]{3,2,1,0:T(8,128)S(1)} %copy-done.8), kind=kOutput, calls=%fused_computation.17 | convolution fusion | flops 82409600 | bytes 1051528 | tf_op jit(solution)/shard_map/dpfg,dfae->pgae/dot_general | solution.py:133
  19.9 1.0 %maximum_bitcast_fusion.3 = f32[3,13,35,128,1]{3,2,0,1,4:T(8,128)} fusion(f32[1,13,35,128]{3,2,0,1:T(8,128)S(1)} %get-tuple-element.37, f32[1,13,35,128]{3,2,0,1:T(8,128)S(1)} %get-tuple-element.36, f32[1,13,35,128]{3,2,0,1:T(8,128)S(1)} %get-tuple-element.35), kind=kLoop, calls=%fused_computation.55 | loop fusion | flops 349440 | bytes 1397760 | tf_op jit(solution)/shard_map/stack | solution.py:128
  21.0 0.3 multiply_add_fusion
  21.2 1.0 %maximum_bitcast_fusion.2 = f32[3,13,35,128,1]{3,2,0,1,4:T(8,128)} fusion(f32[1,13,35,128]{3,2,0,1:T(8,128)S(1)} %get-tuple-element.34, f32[1,13,35,128]{3,2,0,1:T(8,128)S(1)} %get-tuple-element.33, f32[1,13,35,128]{3,2,0,1:T(8,128)S(1)} %get-tuple-element.32), kind=kLoop, calls=%fused_computation.54 | loop fusion | flops 349440 | bytes 1397760 | tf_op jit(solution)/shard_map/stack | solution.py:128
  22.2 0.8 %gather_fusion = f32[60,6,128]{2,0,1:T(8,128)S(1)} fusion(f32[6,35,128]{2,1,0:T(8,128)S(1)} %copy-done, s32[1024]{0:T(1024)S(1)} %pad_clamp_fusion), kind=kCustom, calls=%fused_computation | custom fusion | bytes 368880 | tf_op jit(solution)/shard_map/gather | solution.py:232
  23.1 0.8 %copy.303 = f32[60,6,128]{2,1,0:T(8,128)} copy(f32[60,6,128]{2,0,1:T(8,128)S(1)} %gather_fusion) | data formatting | bytes 368640 | tf_op jit(solution)/shard_map/gather | solution.py:232
  23.9 1.2 %convolution_add_fusion.3 = f32[13,15,512]{2,1,0:T(8,128)S(1)} fusion(f32[13,15,512]{2,1,0:T(8,128)S(1)} %fusion.31, f32[13,15,64]{2,1,0:T(8,128)} %collective-permute-done, pred[640,512]{1,0:T(32,128)(4,1)S(1)} %iota_compare_fusion), kind=kOutput, calls=%fused_computation.34 | convolution fusion | flops 38438400 | bytes 908032 | tf_op jit(solution)/shard_map/fns,sj->fnj/dot_general | solution.py:281
  25.1 1.2 %convolution_add_fusion.2 = f32[13,15,512]{2,1,0:T(8,128)S(1)} fusion(f32[13,15,512]{2,1,0:T(8,128)S(1)} %convolution_add_fusion.3, f32[13,15,64]{2,1,0:T(8,128)} %collective-permute-done.1, pred[640,512]{1,0:T(32,128)(4,1)S(1)} %iota_compare_fusion), kind=kOutput, calls=%fused_computation.33 | convolution fusion | flops 38438400 | bytes 908032 | tf_op jit(solution)/shard_map/fns,sj->fnj/dot_general | solution.py:284
  26.3 0.6 multiply_reduce_fusion.1
  26.9 0.9 %reshape.368 = f32[13,15,4,128]{3,2,1,0:T(4,128)} reshape(f32[13,15,512]{2,1,0:T(8,128)S(1)} %multiply_reduce_fusion.1) | data formatting | bytes 798720 | tf_op jit(solution)/shard_map/reshape | solution.py:288
  27.8 1.1 %copy_subtract_fusion.1 = f32[13,15,4,128]{3,0,2,1:T(8,128)S(1)} fusion(f32[13,15,4,128]{3,0,2,1:T(8,128)S(1)} %bitcast.781, f32[13,15,4,128]{3,2,1,0:T(4,128)} %reshape.368), kind=kLoop, calls=%fused_computation.63 | loop fusion | flops 99840 | bytes 1198080 | tf_op jit(solution)/shard_map/sub | solution.py:288
  28.9 1.5 %fusion.1 = f32[13,15,4,128]{3,0,2,1:T(8,128)S(1)} fusion(f32[6,15,4,128]{3,0,2,1:T(8,128)S(1)} %bitcast.797, f32[13,15,4,128]{3,0,2,1:T(8,128)S(1)} %copy_subtract_fusion.1, f32[3,4,128]{2,0,1:T(4,128)S(1)} %copy.242, f32[3,6,13,13]{3,2,1,0:T(8,128)S(1)} %copy-done.9), kind=kOutput, calls=%fused_computation.9 | convolution fusion | flops 141573120 | bytes 1001352 | tf_op jit(solution)/shard_map/dpfg,dfnxe->pgnxe/dot_general | solution.py:145
  30.5 0.9 %copy-done.3 = f32[13,35,128]{2,0,1:T(8,128)S(1)} copy-done((f32[13,35,128]{2,0,1:T(8,128)S(1)}, f32[13,35,128]{2,0,1:T(8,128)}, u32[]{:S(2)}) %copy-start.3) | copy-done | bytes 232984
  31.4 0.6 fusion.16
  32.0 0.6 gather_fusion.2
  32.7 0.9 %copy.252 = f32[13,15,4,128]{3,2,1,0:T(4,128)} copy(f32[13,15,4,128]{3,0,2,1:T(8,128)S(1)} %bitcast.782) | data formatting | bytes 798720 | tf_op jit(solution)/shard_map/gather | solution.py:276
  33.6 1.2 %reshape.369 = f32[13,15,512]{2,1,0:T(8,128)S(1)} reshape(f32[13,15,4,128]{3,2,1,0:T(4,128)} %copy.252) | data formatting | bytes 798720 | tf_op jit(solution)/shard_map/reshape | solution.py:277
  34.7 0.5 fusion.30
  35.3 0.3 fusion.37
  35.6 0.5 convolution_bitcast_fusion.2
  36.2 4.7 %collective-permute-start.2 = (f32[13,15,64]{2,1,0:T(8,128)S(1)}, f32[13,15,64]{2,1,0:T(8,128)S(1)}, u32[]{:S(2)}, u32[]{:S(2)}) collective-permute-start(f32[13,15,64]{2,1,0:T(8,128)S(1)} %get-tuple-element.49), channel_id=1, source_target_pairs={{0,1},{1,2},{2,3},{3,4},{4,5},{5,6},{6,7},{8,9},{9,10},{10,11},{11... | collective-permute-start | bytes 149768 | tf_op jit(solution)/shard_map/ppermute | solution.py:21
  40.9 1.5 %collective-permute-start.3 = (f32[13,15,64]{2,1,0:T(8,128)S(1)}, f32[13,15,64]{2,1,0:T(8,128)S(1)}, u32[]{:S(2)}, u32[]{:S(2)}) collective-permute-start(f32[13,15,64]{2,1,0:T(8,128)S(1)} %get-tuple-element.48), channel_id=1, source_target_pairs={{1,0},{2,1},{3,2},{4,3},{5,4},{6,5},{7,6},{9,8},{10,9},{11,10},{12... | collective-permute-start | bytes 149768 | tf_op jit(solution)/shard_map/ppermute | solution.py:22
  42.7 1.8 %fusion.3 = f32[6,35,128]{2,0,1:T(8,128)} fusion(f32[3,13,35,128,1]{3,2,0,1,4:T(8,128)S(1)} %copy-done.7, f32[13,35,128]{2,0,1:T(8,128)S(1)} %copy.251, f32[3,6,13,13]{3,2,1,0:T(8,128)S(1)} %copy-done.10), kind=kOutput, calls=%fused_computation.13 | convolution fusion | flops 82440960 | bytes 1051528 | tf_op jit(solution)/shard_map/dpfg,dgae->pfae/dot_general | solution.py:139
  44.5 0.8 %copy-done.2 = f32[6,35,128]{2,0,1:T(8,128)S(1)} copy-done((f32[6,35,128]{2,0,1:T(8,128)S(1)}, f32[6,35,128]{2,0,1:T(8,128)}, u32[]{:S(2)}) %copy-start.2) | copy-done | bytes 107544
  45.4 0.9 %fusion.4 = f32[13,35,128]{2,0,1:T(8,128)S(1)} fusion(f32[3,13,35,128,1]{3,2,0,1,4:T(8,128)S(1)} %maximum_bitcast_fusion.1, f32[6,35,128]{2,0,1:T(8,128)S(1)} %copy-done.2, f32[3,6,13,13]{3,2,1,0:T(8,128)S(1)} %copy-done.10), kind=kOutput, calls=%fused_computation.15 | convolution fusion | flops 82409600 | bytes 1051528 | tf_op jit(solution)/shard_map/dpfg,dfae->pgae/dot_general | solution.py:133
  46.3 0.3 convolution_add_fusion.1
  46.6 0.9 %collective-permute-done.3 = f32[13,15,64]{2,1,0:T(8,128)S(1)} collective-permute-done((f32[13,15,64]{2,1,0:T(8,128)S(1)}, f32[13,15,64]{2,1,0:T(8,128)S(1)}, u32[]{:S(2)}, u32[]{:S(2)}) %collective-permute-start.3) | collective-permute-done | bytes 49952 | tf_op jit(solution)/shard_map/ppermute | solution.py:22
  47.5 0.3 convolution_add_fusion
  47.8 0.6 multiply_reduce_fusion
  48.4 0.1 reshape.370
  48.7 0.8 %copy-done.11 = f32[3,6,13,13]{3,2,1,0:T(8,128)S(1)} copy-done((f32[3,6,13,13]{3,2,1,0:T(8,128)S(1)}, f32[3,6,13,13]{3,2,1,0:T(8,128)}, u32[]{:S(2)}) %copy-start.11) | copy-done | bytes 12192
  49.6 1.5 %fusion = f32[13,15,4,128]{3,0,2,1:T(8,128)S(1)} fusion(f32[6,15,4,128]{3,0,2,1:T(8,128)S(1)} %bitcast.798, f32[13,15,4,128]{3,0,2,1:T(8,128)S(1)} %copy_subtract_fusion, f32[3,4,128]{2,0,1:T(4,128)S(1)} %copy.242, f32[3,6,13,13]{3,2,1,0:T(8,128)S(1)} %copy-done.11), kind=kOutput, calls=%fused_computation.7 | convolution fusion | flops 141573120 | bytes 1001352 | tf_op jit(solution)/shard_map/dpfg,dfnxe->pgnxe/dot_general | solution.py:145
  51.2 0.6 fusion.19
  51.9 0.5 copy-done.6
  52.3 1.1 %fusion.2 = f32[6,35,128]{2,0,1:T(8,128)S(1)} fusion(f32[3,13,35,128,1]{3,2,0,1,4:T(8,128)S(1)} %copy-done.6, f32[13,35,128]{2,0,1:T(8,128)S(1)} %copy.266, f32[3,6,13,13]{3,2,1,0:T(8,128)S(1)} %copy-done.11), kind=kOutput, calls=%fused_computation.11 | convolution fusion | flops 82440960 | bytes 1051528 | tf_op jit(solution)/shard_map/dpfg,dgae->pfae/dot_general | solution.py:139
  53.6 1.6 %collective-permute-start.4 = (f32[6,35,64]{2,1,0:T(8,128)S(1)}, f32[6,35,64]{2,1,0:T(8,128)S(1)}, u32[]{:S(2)}, u32[]{:S(2)}) collective-permute-start(f32[6,35,64]{2,1,0:T(8,128)S(1)} %slice_select_fusion.1), channel_id=1, source_target_pairs={{0,16},{8,24},{16,0},{24,8},{1,17},{9,25},{17,1},{25,9},{2,18},{10... | collective-permute-start | bytes 161288 | tf_op jit(solution)/shard_map/ppermute | solution.py:161
  55.2 3.4 %collective-permute-done.4 = f32[6,35,64]{2,1,0:T(8,128)S(1)} collective-permute-done((f32[6,35,64]{2,1,0:T(8,128)S(1)}, f32[6,35,64]{2,1,0:T(8,128)S(1)}, u32[]{:S(2)}, u32[]{:S(2)}) %collective-permute-start.4) | collective-permute-done | bytes 53792 | tf_op jit(solution)/shard_map/ppermute | solution.py:161
  58.9 1.2 %collective-permute-done.5 = f32[6,35,32]{2,1,0:T(8,128)S(1)} collective-permute-done((f32[6,35,32]{2,1,0:T(8,128)S(1)}, f32[6,35,32]{2,1,0:T(8,128)S(1)}, u32[]{:S(2)}, u32[]{:S(2)}) %collective-permute-start.5) | collective-permute-done | bytes 26912 | tf_op jit(solution)/shard_map/ppermute | solution.py:161
  60.4 0.2 fusion.21
  60.7 0.6 broadcast_in_dim.16
  61.3 6.3 %all-to-all-start = ((f32[32,1,60]{2,1,0:T(1,128)}), f32[32,1,60]{2,1,0:T(1,128)S(1)}, u32[]{:S(2)}, u32[]{:S(2)}) async-start(f32[32,1,60]{2,1,0:T(1,128)} %broadcast_in_dim.16), calls=%async_computation | async-start | bytes 32768 | tf_op jit(solution)/shard_map/all_to_all | solution.py:300
  67.7 0.9 %copy.273 = f32[1,13,35,128]{3,0,2,1:T(1,128)} copy(f32[1,13,35,128]{3,2,1,0:T(8,128)S(1)} %bitcast.784) | data formatting | bytes 465920
  68.8 5.9 %all-to-all-done = f32[32,1,60]{2,1,0:T(1,128)S(1)} async-done(((f32[32,1,60]{2,1,0:T(1,128)}), f32[32,1,60]{2,1,0:T(1,128)S(1)}, u32[]{:S(2)}, u32[]{:S(2)}) %all-to-all-start) | async-done | bytes 7712 | tf_op jit(solution)/shard_map/all_to_all | solution.py:300
  75.2 0.2 slice_reduce_fusion
  75.3 0.2 fusion.20
  75.5 0.6 neg.22
  (140 shorter events, 3.0 us)
Async XLA Ops:
  3.7 0.9 %copy-start.15 = (f32[1,13,35,128]{3,0,2,1:T(1,128)S(1)}, f32[1,13,35,128]{3,0,2,1:T(1,128)}, u32[]{:S(2)}) copy-start(f32[1,13,35,128]{3,0,2,1:T(1,128)} %param.26) | copy-start | bytes 698884
  3.7 1.0 %copy-start.47 = (s32[60]{0:T(128)S(1)}, s32[60]{0:T(128)}, u32[]{:S(2)}) copy-start(s32[60]{0:T(128)} %constant.65) | copy-start | bytes 724
  5.4 0.7 copy-start.43
  5.5 8.5 %copy-start.45 = (s32[4,128]{1,0:T(4,128)S(1)}, s32[4,128]{1,0:T(4,128)}, u32[]{:S(2)}) copy-start(s32[4,128]{1,0:T(4,128)} %param.34) | copy-start | bytes 6148
  5.6 8.5 %copy-start.42 = (s32[4,128]{1,0:T(4,128)S(1)}, s32[4,128]{1,0:T(4,128)}, u32[]{:S(2)}) copy-start(s32[4,128]{1,0:T(4,128)} %param.33) | copy-start | bytes 6148
  6.3 8.5 %copy-start.46 = (f32[4,128]{1,0:T(4,128)S(1)}, f32[4,128]{1,0:T(4,128)}, u32[]{:S(2)}) copy-start(f32[4,128]{1,0:T(4,128)} %param.32) | copy-start | bytes 6148
  6.3 8.5 %copy-start.4 = (f32[3,35,35,1]{2,1,0,3:T(8,128)S(1)}, f32[3,35,35,1]{2,1,0,3:T(8,128)}, u32[]{:S(2)}) copy-start(f32[3,35,35,1]{2,1,0,3:T(8,128)} %constant.68) | copy-start | bytes 44104
  7.1 16.8 %collective-permute-start = (f32[13,15,64]{2,1,0:T(8,128)}, f32[13,15,64]{2,1,0:T(8,128)}, u32[]{:S(2)}, u32[]{:S(2)}) collective-permute-start(f32[13,15,64]{2,1,0:T(8,128)} %get-tuple-element.51), channel_id=1, source_target_pairs={{0,1},{1,2},{2,3},{3,4},{4,5},{5,6},{6,7},{8,9},{9,10},{10,11},{11... | collective-permute-start | bytes 149768 | tf_op jit(solution)/shard_map/ppermute | solution.py:21
  12.6 12.5 %collective-permute-start.1 = (f32[13,15,64]{2,1,0:T(8,128)}, f32[13,15,64]{2,1,0:T(8,128)}, u32[]{:S(2)}, u32[]{:S(2)}) collective-permute-start(f32[13,15,64]{2,1,0:T(8,128)} %get-tuple-element.50), channel_id=1, source_target_pairs={{1,0},{2,1},{3,2},{4,3},{5,4},{6,5},{7,6},{9,8},{10,9},{11,10},{12... | collective-permute-start | bytes 149768 | tf_op jit(solution)/shard_map/ppermute | solution.py:22
  14.3 1.0 %copy-start.41 = (f32[3,3,128]{2,1,0:T(4,128)S(1)}, f32[3,3,128]{2,1,0:T(4,128)}, u32[]{:S(2)}) copy-start(f32[3,3,128]{2,1,0:T(4,128)} %param.30) | copy-start | bytes 13828
  14.3 1.0 %copy-start = (f32[6,35,128]{2,1,0:T(8,128)S(1)}, f32[6,35,128]{2,1,0:T(8,128)}, u32[]{:S(2)}) copy-start(f32[6,35,128]{2,1,0:T(8,128)} %param.28) | copy-start | bytes 322564
  14.3 1.2 %copy-start.12 = (f32[1,2,13,35,128]{4,1,3,2,0:T(2,128)S(1)}, f32[1,2,13,35,128]{4,1,3,2,0:T(2,128)}, u32[]{:S(2)}) copy-start(f32[1,2,13,35,128]{4,1,3,2,0:T(2,128)} %param.27) | copy-start | bytes 1397764
  15.4 1.8 %copy-start.18 = (f32[128]{0:T(128)}, f32[128]{0:T(128)S(1)}, u32[]{:S(2)}) copy-start(f32[128]{0:T(128)S(1)} %get-tuple-element.53) | copy-start | bytes 1540
  15.4 1.8 %copy-start.20 = (f32[128]{0:T(128)}, f32[128]{0:T(128)S(1)}, u32[]{:S(2)}) copy-start(f32[128]{0:T(128)S(1)} %get-tuple-element.54) | copy-start | bytes 1540
  15.4 1.8 %copy-start.22 = (f32[128]{0:T(128)}, f32[128]{0:T(128)S(1)}, u32[]{:S(2)}) copy-start(f32[128]{0:T(128)S(1)} %get-tuple-element.55) | copy-start | bytes 1540
  15.4 1.8 %copy-start.24 = (f32[128]{0:T(128)}, f32[128]{0:T(128)S(1)}, u32[]{:S(2)}) copy-start(f32[128]{0:T(128)S(1)} %get-tuple-element.56) | copy-start | bytes 1540
  15.4 1.8 %copy-start.26 = (f32[128]{0:T(128)}, f32[128]{0:T(128)S(1)}, u32[]{:S(2)}) copy-start(f32[128]{0:T(128)S(1)} %get-tuple-element.57) | copy-start | bytes 1540
  15.4 1.8 %copy-start.28 = (f32[128]{0:T(128)}, f32[128]{0:T(128)S(1)}, u32[]{:S(2)}) copy-start(f32[128]{0:T(128)S(1)} %get-tuple-element.58) | copy-start | bytes 1540
  15.4 1.8 %copy-start.30 = (f32[128]{0:T(128)}, f32[128]{0:T(128)S(1)}, u32[]{:S(2)}) copy-start(f32[128]{0:T(128)S(1)} %get-tuple-element.59) | copy-start | bytes 1540
  15.4 1.8 %copy-start.32 = (f32[128]{0:T(128)}, f32[128]{0:T(128)S(1)}, u32[]{:S(2)}) copy-start(f32[128]{0:T(128)S(1)} %get-tuple-element.60) | copy-start | bytes 1540
  15.5 2.0 %copy-start.1 = (f32[6,35,128]{2,0,1:T(8,128)}, f32[6,35,128]{2,0,1:T(8,128)S(1)}, u32[]{:S(2)}) copy-start(f32[6,35,128]{2,0,1:T(8,128)S(1)} %copy.238) | copy-start | bytes 322564
  17.4 0.9 %copy-start.8 = (f32[3,6,13,13]{3,2,1,0:T(8,128)S(1)}, f32[3,6,13,13]{3,2,1,0:T(8,128)}, u32[]{:S(2)}) copy-start(f32[3,6,13,13]{3,2,1,0:T(8,128)} %param.29) | copy-start | bytes 36508
  19.9 1.0 %copy-start.34 = (f32[15,15]{1,0:T(8,128)S(1)}, f32[15,15]{1,0:T(8,128)}, u32[]{:S(2)}) copy-start(f32[15,15]{1,0:T(8,128)} %constant.61.clone) | copy-start | bytes 2704
  19.9 1.0 %copy-start.35 = (f32[15,15]{1,0:T(8,128)S(1)}, f32[15,15]{1,0:T(8,128)}, u32[]{:S(2)}) copy-start(f32[15,15]{1,0:T(8,128)} %constant.60.clone) | copy-start | bytes 2704
  19.9 1.0 %copy-start.36 = (f32[15,15]{1,0:T(8,128)S(1)}, f32[15,15]{1,0:T(8,128)}, u32[]{:S(2)}) copy-start(f32[15,15]{1,0:T(8,128)} %constant.59.clone) | copy-start | bytes 2704
  19.9 1.0 %copy-start.37 = (f32[15,15]{1,0:T(8,128)S(1)}, f32[15,15]{1,0:T(8,128)}, u32[]{:S(2)}) copy-start(f32[15,15]{1,0:T(8,128)} %constant.58.clone) | copy-start | bytes 2704
  19.9 1.0 %copy-start.38 = (f32[15,15]{1,0:T(8,128)S(1)}, f32[15,15]{1,0:T(8,128)}, u32[]{:S(2)}) copy-start(f32[15,15]{1,0:T(8,128)} %constant.57.clone) | copy-start | bytes 2704
  19.9 1.0 %copy-start.39 = (f32[15,15]{1,0:T(8,128)S(1)}, f32[15,15]{1,0:T(8,128)}, u32[]{:S(2)}) copy-start(f32[15,15]{1,0:T(8,128)} %constant.56.clone) | copy-start | bytes 2704
  22.2 1.7 %copy-start.40 = (f32[3,4,128]{2,1,0:T(4,128)S(1)}, f32[3,4,128]{2,1,0:T(4,128)}, u32[]{:S(2)}) copy-start(f32[3,4,128]{2,1,0:T(4,128)} %param.31) | copy-start | bytes 18436
  26.9 2.0 %copy-start.9 = (f32[3,6,13,13]{3,2,1,0:T(8,128)S(1)}, f32[3,6,13,13]{3,2,1,0:T(8,128)}, u32[]{:S(2)}) copy-start(f32[3,6,13,13]{3,2,1,0:T(8,128)} %param.29) | copy-start | bytes 36508
  26.9 2.0 %copy-start.13 = (f32[60,6,128]{2,1,0:T(8,128)S(1)}, f32[60,6,128]{2,1,0:T(8,128)}, u32[]{:S(2)}) copy-start(f32[60,6,128]{2,1,0:T(8,128)} %copy.303) | copy-start | bytes 552964
  30.4 1.0 %copy-start.3 = (f32[13,35,128]{2,0,1:T(8,128)S(1)}, f32[13,35,128]{2,0,1:T(8,128)}, u32[]{:S(2)}) copy-start(f32[13,35,128]{2,0,1:T(8,128)} %fusion.5) | copy-start | bytes 698884
  30.4 1.0 %copy-start.17 = (f32[4,35,15,1]{1,2,0,3:T(8,128)S(1)}, f32[4,35,15,1]{1,2,0,3:T(8,128)}, u32[]{:S(2)}) copy-start(f32[4,35,15,1]{1,2,0,3:T(8,128)} %constant.69) | copy-start | bytes 25204
  33.6 1.7 %copy-start.44 = (s32[128]{0:T(128)S(1)}, s32[128]{0:T(128)}, u32[]{:S(2)}) copy-start(s32[128]{0:T(128)} %param.35) | copy-start | bytes 1540
  34.7 0.9 %copy-start.5 = (f32[3,35,35,1]{2,1,0,3:T(8,128)S(1)}, f32[3,35,35,1]{2,1,0,3:T(8,128)}, u32[]{:S(2)}) copy-start(f32[3,35,35,1]{2,1,0,3:T(8,128)} %constant.68) | copy-start | bytes 44104
  35.2 7.2 %copy-start.19 = (f32[128]{0:T(128)S(1)}, f32[128]{0:T(128)}, u32[]{:S(2)}) copy-start(f32[128]{0:T(128)} %copy-done.18) | copy-start | bytes 1540
  35.2 7.2 %copy-start.21 = (f32[128]{0:T(128)S(1)}, f32[128]{0:T(128)}, u32[]{:S(2)}) copy-start(f32[128]{0:T(128)} %copy-done.20) | copy-start | bytes 1540
  35.2 7.2 %copy-start.23 = (f32[128]{0:T(128)S(1)}, f32[128]{0:T(128)}, u32[]{:S(2)}) copy-start(f32[128]{0:T(128)} %copy-done.22) | copy-start | bytes 1540
  35.3 7.2 %copy-start.25 = (f32[128]{0:T(128)S(1)}, f32[128]{0:T(128)}, u32[]{:S(2)}) copy-start(f32[128]{0:T(128)} %copy-done.24) | copy-start | bytes 1540
  35.3 7.2 %copy-start.27 = (f32[128]{0:T(128)S(1)}, f32[128]{0:T(128)}, u32[]{:S(2)}) copy-start(f32[128]{0:T(128)} %copy-done.26) | copy-start | bytes 1540
  35.3 7.2 %copy-start.29 = (f32[128]{0:T(128)S(1)}, f32[128]{0:T(128)}, u32[]{:S(2)}) copy-start(f32[128]{0:T(128)} %copy-done.28) | copy-start | bytes 1540
  35.3 7.2 %copy-start.31 = (f32[128]{0:T(128)S(1)}, f32[128]{0:T(128)}, u32[]{:S(2)}) copy-start(f32[128]{0:T(128)} %copy-done.30) | copy-start | bytes 1540
  35.3 7.2 %copy-start.33 = (f32[128]{0:T(128)S(1)}, f32[128]{0:T(128)}, u32[]{:S(2)}) copy-start(f32[128]{0:T(128)} %copy-done.32) | copy-start | bytes 1540
  36.1 6.6 %copy-start.7 = (f32[3,13,35,128,1]{3,2,0,1,4:T(8,128)S(1)}, f32[3,13,35,128,1]{3,2,0,1,4:T(8,128)}, u32[]{:S(2)}) copy-start(f32[3,13,35,128,1]{3,2,0,1,4:T(8,128)} %maximum_bitcast_fusion.2) | copy-start | bytes 2096644
  36.1 6.6 %copy-start.10 = (f32[3,6,13,13]{3,2,1,0:T(8,128)S(1)}, f32[3,6,13,13]{3,2,1,0:T(8,128)}, u32[]{:S(2)}) copy-start(f32[3,6,13,13]{3,2,1,0:T(8,128)} %param.29) | copy-start | bytes 36508
  36.2 10.1 %collective-permute-start.2 = (f32[13,15,64]{2,1,0:T(8,128)S(1)}, f32[13,15,64]{2,1,0:T(8,128)S(1)}, u32[]{:S(2)}, u32[]{:S(2)}) collective-permute-start(f32[13,15,64]{2,1,0:T(8,128)S(1)} %get-tuple-element.49), channel_id=1, source_target_pairs={{0,1},{1,2},{2,3},{3,4},{4,5},{5,6},{6,7},{8,9},{9,10},{10,11},{11... | collective-permute-start | bytes 149768 | tf_op jit(solution)/shard_map/ppermute | solution.py:21
  40.9 6.6 %collective-permute-start.3 = (f32[13,15,64]{2,1,0:T(8,128)S(1)}, f32[13,15,64]{2,1,0:T(8,128)S(1)}, u32[]{:S(2)}, u32[]{:S(2)}) collective-permute-start(f32[13,15,64]{2,1,0:T(8,128)S(1)} %get-tuple-element.48), channel_id=1, source_target_pairs={{1,0},{2,1},{3,2},{4,3},{5,4},{6,5},{7,6},{9,8},{10,9},{11,10},{12... | collective-permute-start | bytes 149768 | tf_op jit(solution)/shard_map/ppermute | solution.py:22
  44.5 0.9 %copy-start.2 = (f32[6,35,128]{2,0,1:T(8,128)S(1)}, f32[6,35,128]{2,0,1:T(8,128)}, u32[]{:S(2)}) copy-start(f32[6,35,128]{2,0,1:T(8,128)} %copy-done.1) | copy-start | bytes 322564
  48.6 0.9 %copy-start.11 = (f32[3,6,13,13]{3,2,1,0:T(8,128)S(1)}, f32[3,6,13,13]{3,2,1,0:T(8,128)}, u32[]{:S(2)}) copy-start(f32[3,6,13,13]{3,2,1,0:T(8,128)} %param.29) | copy-start | bytes 36508
  48.6 1.0 %copy-start.14 = (f32[60,6,128]{2,1,0:T(8,128)S(1)}, f32[60,6,128]{2,1,0:T(8,128)}, u32[]{:S(2)}) copy-start(f32[60,6,128]{2,1,0:T(8,128)} %copy.303) | copy-start | bytes 552964
  51.2 1.1 %copy-start.6 = (f32[3,13,35,128,1]{3,2,0,1,4:T(8,128)S(1)}, f32[3,13,35,128,1]{3,2,0,1,4:T(8,128)}, u32[]{:S(2)}) copy-start(f32[3,13,35,128,1]{3,2,0,1,4:T(8,128)} %maximum_bitcast_fusion.3) | copy-start | bytes 2096644
  52.3 1.1 %copy-start.16 = (f32[6,35,128]{2,0,1:T(8,128)S(1)}, f32[6,35,128]{2,0,1:T(8,128)}, u32[]{:S(2)}) copy-start(f32[6,35,128]{2,0,1:T(8,128)} %fusion.3) | copy-start | bytes 322564
  53.6 4.9 %collective-permute-start.4 = (f32[6,35,64]{2,1,0:T(8,128)S(1)}, f32[6,35,64]{2,1,0:T(8,128)S(1)}, u32[]{:S(2)}, u32[]{:S(2)}) collective-permute-start(f32[6,35,64]{2,1,0:T(8,128)S(1)} %slice_select_fusion.1), channel_id=1, source_target_pairs={{0,16},{8,24},{16,0},{24,8},{1,17},{9,25},{17,1},{25,9},{2,18},{10... | collective-permute-start | bytes 161288 | tf_op jit(solution)/shard_map/ppermute | solution.py:161
  58.8 1.4 %collective-permute-start.5 = (f32[6,35,32]{2,1,0:T(8,128)S(1)}, f32[6,35,32]{2,1,0:T(8,128)S(1)}, u32[]{:S(2)}, u32[]{:S(2)}) collective-permute-start(f32[6,35,32]{2,1,0:T(8,128)S(1)} %slice_select_fusion), channel_id=1, source_target_pairs={{0,8},{8,0},{16,24},{24,16},{1,9},{9,1},{17,25},{25,17},{2,10},{10... | collective-permute-start | bytes 80648 | tf_op jit(solution)/shard_map/ppermute | solution.py:161
  61.3 13.4 %all-to-all-start = ((f32[32,1,60]{2,1,0:T(1,128)}), f32[32,1,60]{2,1,0:T(1,128)S(1)}, u32[]{:S(2)}, u32[]{:S(2)}) async-start(f32[32,1,60]{2,1,0:T(1,128)} %broadcast_in_dim.16), calls=%async_computation | async-start | bytes 32768 | tf_op jit(solution)/shard_map/all_to_all | solution.py:300

commit v15 on v14

--- a/solution.py
+++ b/solution.py
@@ -272,7 +272,14 @@
         (step_share, change_share, gram, adjoint)
     )
     gradient = jnp.zeros((params, node_count, elements), jnp.float32)
-    for step_index in range(forward_states.shape[1]):
+    steps = forward_states.shape[1]
+    forward_spatial = spatial_of(
+        forward_states[0].reshape(steps * fields, node_count, elements), metric, derivs
+    ).reshape(3, steps, fields, node_count, elements)
+    forward_mixing = jnp.einsum(
+        "dpfg,dtgae->tpfae", coupling, forward_spatial, precision=MIX
+    )
+    for step_index in range(steps):
         inner_trace = adjoint[:, face_nodes.T, :]
         flat_trace = inner_trace.reshape(fields, face_width, 4 * elements)
         sent_traces = jnp.einsum("fns,sj->fnj", flat_trace, send_pick, precision=MIX)
@@ -290,8 +297,8 @@
             jump_trace, face_material, face_normals, face_scale, coupling, lift_tables
         )
         adjoint = adjoint + STEP_SIZE * change
-        gradient = gradient + STEP_SIZE * kernel_term(
-            adjoint, forward_states[0, step_index], coupling, metric, derivs
+        gradient = gradient + STEP_SIZE * jnp.sum(
+            forward_mixing[step_index] * adjoint[None], axis=1
         )
     device_count = shot_count * lax.axis_size("mesh")
 

time: 76.7 us -> 77.5 us (1.010)
  local copies, waits for them, and re-layouts: 14.6 us -> 11.2 us
  matrix products: 18.9 us -> 21.4 us
  waiting for transfers between devices: 11.5 us -> 13.4 us
    unnamed x100 -> x101, local copies, waits for them, and re-layouts: 5.67 us -> 1.52 us
    another operation x4 -> x2, other arithmetic: 2.16 us -> 0.17 us  [spatial_of(): return jnp.stack(rows)]
    ppermute x2, waiting for transfers between devices: 0.93 us -> 2.84 us  [padded(): after = lax.ppermute(first, axis, down)]
    reduce_sum x0 -> x1, other arithmetic: none -> 1.1 us  [shards(): jnp.sum(forward_mixing[step_index] * adjoint[None], axis=1)]
    sub x2, other arithmetic: 1.14 us -> 2.16 us  [shards(): jump_trace = turned.reshape(fields, face_width, 4, elements) - inner_trace]
    reshape x2, local copies, waits for them, and re-layouts: 1.03 us -> 1.81 us  [shards(): jump_trace = turned.reshape(fields, face_width, 4, elements) - inner_trace]
    dot_general x4 -> x3, matrix products: 1.92 us -> 2.56 us  [spatial_of(): reference_grads = jnp.einsum('rab,fbe->rfae', derivs, field, precision=MIX)]
    dot_general x2 -> x1, matrix products: 2.88 us -> 3.29 us  [shards(): jnp.einsum('dpfg,dtgae->tpfae', coupling, forward_spatial, precision=MIX)]
  transfers between devices with their start and end apart: 7 -> 7, of which waited for: 4 -> 4; matrix products, arithmetic and copies ran while one was open for 19% -> 18% of each run, Pallas kernels for 0% -> 0%
where the time goes in v15:
time: 77.5 us; the launch traced here: 77 us
  matrix products  21.4 us (28%)
  starting transfers between devices  20.8 us (27%)
  waiting for transfers between devices  13.4 us (17%)
  local copies, waits for them, and re-layouts  11.2 us (14%)
  other arithmetic  8.43 us (11%)
  between operations  1.84 us (2%)
    ppermute x2, starting transfers between devices, padded(): before = lax.ppermute(last, axis, up)  10.1 us
    all_to_all x1, starting transfers between devices, combine_sums(): lax.all_to_all(spread, ('shot', 'mesh'), 0, 0, tiled=False)  6.06 us
    all_to_all x1, waiting for transfers between devices, combine_sums(): lax.all_to_all(spread, ('shot', 'mesh'), 0, 0, tiled=False)  5.95 us
    ppermute x2, waiting for transfers between devices, halving_sum(): lax.ppermute(jnp.where(upper, low, high), axis, [(i, i ^ bit) for i in ra...  4.6 us
    dot_general x2, matrix products, volume_term(): mixing = jnp.einsum('dpfg,dfae->pgae', coupling, spatial, precision=MIX)  3.29 us
    dot_general x1, matrix products, shards(): jnp.einsum('dpfg,dtgae->tpfae', coupling, forward_spatial, precision=MIX)  3.29 us
    dot_general x2, matrix products, surface_term(): mixing = jnp.einsum('dpfg,dfnxe->pgnxe', coupling, weighted, precision=MIX)  2.98 us
    dot_general x1, matrix products, shards(): jnp.einsum('ipae,ej->ipaj', jnp.concatenate([history_steps, history_chang...  2.97 us
  transfers between devices with their start and end apart: 7, of which 4 were waited for; matrix products, arithmetic and copies ran while one was open for 18% of the time, Pallas kernels for 0%

profile of v15, /device:TPU:0, one launch (start us, length us, event | category | flops | bytes accessed | tf_op | source)
XLA Modules:
  0.0 77.0 jit_solution(8086831181885338965)
XLA Ops:
  0.7 3.0 %fusion.18 = f32[10,6,35,32]{2,3,1,0:T(8,128)S(1)} fusion(f32[5,6,35,128]{3,2,1,0:T(8,128)} %param.37, f32[5,6,35,128]{3,2,1,0:T(8,128)} %param.36, s32[32]{0:T(128)S(1)} %iota_add_fusion), kind=kOutput, calls=%fused_computation.35 | convolution fusion | flops 51882496 | bytes 1344128 | tf_op jit(solution)/shard_map/ipae,ej->ipaj/dot_general | solution.py:261
  3.7 0.6 multiply_reduce_fusion.2
  4.4 0.2 copy-done.11
  4.7 0.6 gather_fusion.1
  5.4 0.2 copy.225
  5.5 0.2 reshape.371
  5.7 0.3 fusion.45
  6.1 0.7 fusion.152
  6.8 5.5 %collective-permute-start = (f32[13,15,64]{2,1,0:T(8,128)}, f32[13,15,64]{2,1,0:T(8,128)}, u32[]{:S(2)}, u32[]{:S(2)}) collective-permute-start(f32[13,15,64]{2,1,0:T(8,128)} %get-tuple-element.48), channel_id=1, source_target_pairs={{0,1},{1,2},{2,3},{3,4},{4,5},{5,6},{6,7},{8,9},{9,10},{10,11},{11... | collective-permute-start | bytes 149768 | tf_op jit(solution)/shard_map/ppermute | solution.py:21
  12.3 1.5 %collective-permute-start.1 = (f32[13,15,64]{2,1,0:T(8,128)}, f32[13,15,64]{2,1,0:T(8,128)}, u32[]{:S(2)}, u32[]{:S(2)}) collective-permute-start(f32[13,15,64]{2,1,0:T(8,128)} %get-tuple-element.47), channel_id=1, source_target_pairs={{1,0},{2,1},{3,2},{4,3},{5,4},{6,5},{7,6},{9,8},{10,9},{11,10},{12... | collective-permute-start | bytes 149768 | tf_op jit(solution)/shard_map/ppermute | solution.py:22
  13.8 0.2 iota_compare_fusion
  14.0 0.5 fusion.37
  14.6 0.5 convolution_bitcast_fusion.3
  15.3 0.8 convolution_bitcast_fusion.1
  16.1 0.1 multiply_add_fusion.9
  16.3 0.3 multiply_add_fusion.2
  16.6 0.1 copy.241
  16.7 0.1 copy.240
  16.8 0.1 copy.239
  17.1 3.3 %convolution_bitcast_fusion = f32[2,6,13,35,128]{4,2,1,3,0:T(8,128)} fusion(f32[1,2,13,35,128]{4,2,0,3,1:T(8,128)S(1)} %copy.241, f32[1,2,13,35,128]{4,2,0,3,1:T(8,128)S(1)} %copy.240, f32[1,2,13,35,128]{4,2,0,3,1:T(8,128)S(1)} %copy.239, f32[3,6,13,13]{3,2,1,0:T(8,128)S(1)} %copy-done), kind=kOutput, calls=%fused_computation.10 | convolution fusion | flops 164236800 | bytes 4205448 | tf_op jit(solution)/shard_map/dpfg,dtgae->tpfae/dot_general | solution.py:279
  20.4 0.3 multiply_add_fusion.3
  20.7 1.7 %fusion.13 = f32[13,35,128]{2,0,1:T(8,128)} fusion(f32[3,13,35,128,1]{3,2,0,1,4:T(8,128)S(1)} %maximum_bitcast_fusion, f32[6,35,128]{2,0,1:T(8,128)S(1)} %copy.219, f32[3,6,13,13]{3,2,1,0:T(8,128)S(1)} %copy-done), kind=kOutput, calls=%fused_computation.26 | convolution fusion | flops 82409600 | bytes 1051528 | tf_op jit(solution)/shard_map/dpfg,dfae->pgae/dot_general | solution.py:133
  22.4 0.8 %gather_fusion = f32[60,6,128]{2,0,1:T(8,128)S(1)} fusion(f32[6,35,128]{2,1,0:T(8,128)S(1)} %copy-done.1, s32[1024]{0:T(1024)S(1)} %pad_clamp_fusion), kind=kCustom, calls=%fused_computation | custom fusion | bytes 368880 | tf_op jit(solution)/shard_map/gather | solution.py:232
  23.2 0.8 %copy.277 = f32[60,6,128]{2,1,0:T(8,128)} copy(f32[60,6,128]{2,0,1:T(8,128)S(1)} %gather_fusion) | data formatting | bytes 368640 | tf_op jit(solution)/shard_map/gather | solution.py:232
  24.1 1.2 %convolution_add_fusion.3 = f32[13,15,512]{2,1,0:T(8,128)S(1)} fusion(f32[13,15,512]{2,1,0:T(8,128)S(1)} %fusion.37, f32[13,15,64]{2,1,0:T(8,128)} %collective-permute-done, pred[640,512]{1,0:T(32,128)(4,1)S(1)} %iota_compare_fusion), kind=kOutput, calls=%fused_computation.42 | convolution fusion | flops 38438400 | bytes 908032 | tf_op jit(solution)/shard_map/fns,sj->fnj/dot_general | solution.py:288
  25.3 1.2 %convolution_add_fusion.2 = f32[13,15,512]{2,1,0:T(8,128)S(1)} fusion(f32[13,15,512]{2,1,0:T(8,128)S(1)} %convolution_add_fusion.3, f32[13,15,64]{2,1,0:T(8,128)} %collective-permute-done.1, pred[640,512]{1,0:T(32,128)(4,1)S(1)} %iota_compare_fusion), kind=kOutput, calls=%fused_computation.41 | convolution fusion | flops 38438400 | bytes 908032 | tf_op jit(solution)/shard_map/fns,sj->fnj/dot_general | solution.py:291
  26.5 0.6 multiply_reduce_fusion.1
  27.1 0.9 %reshape.372 = f32[13,15,4,128]{3,2,1,0:T(4,128)} reshape(f32[13,15,512]{2,1,0:T(8,128)S(1)} %multiply_reduce_fusion.1) | data formatting | bytes 798720 | tf_op jit(solution)/shard_map/reshape | solution.py:295
  28.0 1.1 %copy_subtract_fusion.1 = f32[13,15,4,128]{3,0,2,1:T(8,128)S(1)} fusion(f32[13,15,4,128]{3,0,2,1:T(8,128)S(1)} %bitcast.778, f32[13,15,4,128]{3,2,1,0:T(4,128)} %reshape.372), kind=kLoop, calls=%fused_computation.70 | loop fusion | flops 99840 | bytes 1198080 | tf_op jit(solution)/shard_map/sub | solution.py:295
  29.1 1.5 %fusion.1 = f32[13,15,4,128]{3,0,2,1:T(8,128)S(1)} fusion(f32[6,15,4,128]{3,0,2,1:T(8,128)S(1)} %bitcast.798, f32[13,15,4,128]{3,0,2,1:T(8,128)S(1)} %copy_subtract_fusion.1, f32[3,4,128]{2,0,1:T(4,128)S(1)} %copy.223, f32[3,6,13,13]{3,2,1,0:T(8,128)S(1)} %copy-done), kind=kOutput, calls=%fused_computation.9 | convolution fusion | flops 141573120 | bytes 1001352 | tf_op jit(solution)/shard_map/dpfg,dfnxe->pgnxe/dot_general | solution.py:145
  30.7 0.6 fusion.24
  31.4 0.6 gather_fusion.2
  32.0 0.9 %copy.233 = f32[13,15,4,128]{3,2,1,0:T(4,128)} copy(f32[13,15,4,128]{3,0,2,1:T(8,128)S(1)} %bitcast.779) | data formatting | bytes 798720 | tf_op jit(solution)/shard_map/gather | solution.py:283
  32.9 1.2 %reshape.373 = f32[13,15,512]{2,1,0:T(8,128)S(1)} reshape(f32[13,15,4,128]{3,2,1,0:T(4,128)} %copy.233) | data formatting | bytes 798720 | tf_op jit(solution)/shard_map/reshape | solution.py:284
  34.2 0.5 fusion.36
  34.6 0.9 %fusion.43 = f32[13,15,128]{2,1,0:T(8,128)S(1)} fusion(f32[13,15,512]{2,1,0:T(8,128)S(1)} %reshape.373, s32[128]{0:T(128)} %param.35), kind=kOutput, calls=%fused_computation.87 | convolution fusion | flops 76742656 | bytes 499712 | tf_op jit(solution)/shard_map/fns,sj->fnj/dot_general | solution.py:285
  35.6 1.3 %convolution_bitcast_fusion.2 = f32[3,13,35,128]{3,2,0,1:T(8,128)S(1)} fusion(f32[3,35,35,1]{2,1,0,3:T(8,128)} %constant.68, f32[13,35,128]{2,1,0:T(8,128)S(1)} %fusion.24), kind=kOutput, calls=%fused_computation.33 | convolution fusion | flops 36691200 | bytes 946540 | tf_op jit(solution)/shard_map/rab,fbe->rfae/dot_general | solution.py:121
  37.0 4.6 %collective-permute-start.2 = (f32[13,15,64]{2,1,0:T(8,128)S(1)}, f32[13,15,64]{2,1,0:T(8,128)S(1)}, u32[]{:S(2)}, u32[]{:S(2)}) collective-permute-start(f32[13,15,64]{2,1,0:T(8,128)S(1)} %get-tuple-element.46), channel_id=1, source_target_pairs={{0,1},{1,2},{2,3},{3,4},{4,5},{5,6},{6,7},{8,9},{9,10},{10,11},{11... | collective-permute-start | bytes 149768 | tf_op jit(solution)/shard_map/ppermute | solution.py:21
  41.6 1.5 %collective-permute-start.3 = (f32[13,15,64]{2,1,0:T(8,128)S(1)}, f32[13,15,64]{2,1,0:T(8,128)S(1)}, u32[]{:S(2)}, u32[]{:S(2)}) collective-permute-start(f32[13,15,64]{2,1,0:T(8,128)S(1)} %get-tuple-element.45), channel_id=1, source_target_pairs={{1,0},{2,1},{3,2},{4,3},{5,4},{6,5},{7,6},{9,8},{10,9},{11,10},{12... | collective-permute-start | bytes 149768 | tf_op jit(solution)/shard_map/ppermute | solution.py:22
  43.2 0.1 multiply_add_fusion.6
  43.4 1.6 %fusion.12 = f32[13,35,128]{2,0,1:T(8,128)} fusion(f32[3,13,35,128,1]{3,2,0,1,4:T(8,128)S(1)} %maximum_bitcast_fusion.1, f32[6,35,128]{2,0,1:T(8,128)S(1)} %copy-done.4, f32[3,6,13,13]{3,2,1,0:T(8,128)S(1)} %copy-done), kind=kOutput, calls=%fused_computation.24 | convolution fusion | flops 82409600 | bytes 1051528 | tf_op jit(solution)/shard_map/dpfg,dfae->pgae/dot_general | solution.py:133
  45.0 0.3 convolution_add_fusion.1
  45.3 2.8 %collective-permute-done.3 = f32[13,15,64]{2,1,0:T(8,128)S(1)} collective-permute-done((f32[13,15,64]{2,1,0:T(8,128)S(1)}, f32[13,15,64]{2,1,0:T(8,128)S(1)}, u32[]{:S(2)}, u32[]{:S(2)}) %collective-permute-start.3) | collective-permute-done | bytes 49952 | tf_op jit(solution)/shard_map/ppermute | solution.py:22
  48.2 0.3 convolution_add_fusion
  48.5 0.6 multiply_reduce_fusion
  49.1 0.9 %reshape.374 = f32[13,15,4,128]{3,2,1,0:T(4,128)} reshape(f32[13,15,512]{2,1,0:T(8,128)S(1)} %multiply_reduce_fusion) | data formatting | bytes 798720 | tf_op jit(solution)/shard_map/reshape | solution.py:295
  50.0 1.1 %copy_subtract_fusion = f32[13,15,4,128]{3,0,2,1:T(8,128)S(1)} fusion(f32[13,15,4,128]{3,0,2,1:T(8,128)S(1)} %bitcast.780, f32[13,15,4,128]{3,2,1,0:T(4,128)} %reshape.374), kind=kLoop, calls=%fused_computation.69 | loop fusion | flops 99840 | bytes 1198080 | tf_op jit(solution)/shard_map/sub | solution.py:295
  51.2 1.5 %fusion = f32[13,15,4,128]{3,0,2,1:T(8,128)S(1)} fusion(f32[6,15,4,128]{3,0,2,1:T(8,128)S(1)} %bitcast.799, f32[13,15,4,128]{3,0,2,1:T(8,128)S(1)} %copy_subtract_fusion, f32[3,4,128]{2,0,1:T(4,128)S(1)} %copy.223, f32[3,6,13,13]{3,2,1,0:T(8,128)S(1)} %copy-done), kind=kOutput, calls=%fused_computation.7 | convolution fusion | flops 141573120 | bytes 1001352 | tf_op jit(solution)/shard_map/dpfg,dfnxe->pgnxe/dot_general | solution.py:145
  52.8 0.6 fusion.27
  53.4 1.1 %fusion.5 = (f32[6,35,128]{2,0,1:T(8,128)S(1)}, f32[6,35,128]{2,0,1:T(8,128)S(1)}) fusion(f32[2,6,13,35,128]{4,2,1,3,0:T(8,128)S(1)} %copy-done.2, f32[13,35,128]{2,0,1:T(8,128)S(1)} %copy.232, f32[13,35,128]{2,0,1:T(8,128)S(1)} %copy.244), kind=kLoop, calls=%fused_computation.16 | loop fusion | flops 1344000 | bytes 3476480 | tf_op jit(solution)/shard_map/reduce_sum | solution.py:300
  54.7 1.6 %collective-permute-start.4 = (f32[6,35,64]{2,1,0:T(8,128)S(1)}, f32[6,35,64]{2,1,0:T(8,128)S(1)}, u32[]{:S(2)}, u32[]{:S(2)}) collective-permute-start(f32[6,35,64]{2,1,0:T(8,128)S(1)} %slice_select_fusion.1), channel_id=1, source_target_pairs={{0,16},{8,24},{16,0},{24,8},{1,17},{9,25},{17,1},{25,9},{2,18},{10... | collective-permute-start | bytes 161288 | tf_op jit(solution)/shard_map/ppermute | solution.py:161
  56.3 3.4 %collective-permute-done.4 = f32[6,35,64]{2,1,0:T(8,128)S(1)} collective-permute-done((f32[6,35,64]{2,1,0:T(8,128)S(1)}, f32[6,35,64]{2,1,0:T(8,128)S(1)}, u32[]{:S(2)}, u32[]{:S(2)}) %collective-permute-start.4) | collective-permute-done | bytes 53792 | tf_op jit(solution)/shard_map/ppermute | solution.py:161
  60.0 1.2 %collective-permute-done.5 = f32[6,35,32]{2,1,0:T(8,128)S(1)} collective-permute-done((f32[6,35,32]{2,1,0:T(8,128)S(1)}, f32[6,35,32]{2,1,0:T(8,128)S(1)}, u32[]{:S(2)}, u32[]{:S(2)}) %collective-permute-start.5) | collective-permute-done | bytes 26912 | tf_op jit(solution)/shard_map/ppermute | solution.py:161
  61.4 0.1 copy.247
  61.5 0.2 fusion.29
  61.8 0.6 broadcast_in_dim.16
  62.4 6.1 %all-to-all-start = ((f32[32,1,60]{2,1,0:T(1,128)}), f32[32,1,60]{2,1,0:T(1,128)S(1)}, u32[]{:S(2)}, u32[]{:S(2)}) async-start(f32[32,1,60]{2,1,0:T(1,128)} %broadcast_in_dim.16), calls=%async_computation | async-start | bytes 32768 | tf_op jit(solution)/shard_map/all_to_all | solution.py:307
  68.6 0.9 %copy.251 = f32[1,13,35,128]{3,0,2,1:T(1,128)} copy(f32[1,13,35,128]{3,2,1,0:T(8,128)S(1)} %bitcast.781) | data formatting | bytes 465920
  69.5 0.1 copy.250
  69.6 5.9 %all-to-all-done = f32[32,1,60]{2,1,0:T(1,128)S(1)} async-done(((f32[32,1,60]{2,1,0:T(1,128)}), f32[32,1,60]{2,1,0:T(1,128)S(1)}, u32[]{:S(2)}, u32[]{:S(2)}) %all-to-all-start) | async-done | bytes 7712 | tf_op jit(solution)/shard_map/all_to_all | solution.py:307
  75.6 0.1 broadcast_add_fusion
  76.0 0.2 slice_reduce_fusion
  76.1 0.2 fusion.28
  76.3 0.6 neg.22
  (139 shorter events, 2.0 us)
Async XLA Ops:
  0.6 16.4 %copy-start = (f32[3,6,13,13]{3,2,1,0:T(8,128)S(1)}, f32[3,6,13,13]{3,2,1,0:T(8,128)}, u32[]{:S(2)}) copy-start(f32[3,6,13,13]{3,2,1,0:T(8,128)} %param.29) | copy-start | bytes 36508
  3.6 0.9 %copy-start.11 = (f32[1,13,35,128]{3,0,2,1:T(1,128)S(1)}, f32[1,13,35,128]{3,0,2,1:T(1,128)}, u32[]{:S(2)}) copy-start(f32[1,13,35,128]{3,0,2,1:T(1,128)} %param.26) | copy-start | bytes 698884
  3.7 1.0 %copy-start.47 = (s32[60]{0:T(128)S(1)}, s32[60]{0:T(128)}, u32[]{:S(2)}) copy-start(s32[60]{0:T(128)} %constant.65) | copy-start | bytes 724
  4.6 1.1 %copy-start.44 = (s32[128]{0:T(128)S(1)}, s32[128]{0:T(128)}, u32[]{:S(2)}) copy-start(s32[128]{0:T(128)} %param.35) | copy-start | bytes 1540
  4.7 9.1 %copy-start.45 = (s32[4,128]{1,0:T(4,128)S(1)}, s32[4,128]{1,0:T(4,128)}, u32[]{:S(2)}) copy-start(s32[4,128]{1,0:T(4,128)} %param.34) | copy-start | bytes 6148
  4.7 9.1 %copy-start.43 = (s32[4,128]{1,0:T(4,128)S(1)}, s32[4,128]{1,0:T(4,128)}, u32[]{:S(2)}) copy-start(s32[4,128]{1,0:T(4,128)} %param.33) | copy-start | bytes 6148
  5.5 9.0 %copy-start.46 = (f32[4,128]{1,0:T(4,128)S(1)}, f32[4,128]{1,0:T(4,128)}, u32[]{:S(2)}) copy-start(f32[4,128]{1,0:T(4,128)} %param.32) | copy-start | bytes 6148
  5.5 9.0 %copy-start.10 = (f32[3,35,35,1]{2,1,0,3:T(8,128)S(1)}, f32[3,35,35,1]{2,1,0,3:T(8,128)}, u32[]{:S(2)}) copy-start(f32[3,35,35,1]{2,1,0,3:T(8,128)} %constant.68) | copy-start | bytes 44104
  5.7 9.3 %copy-start.42 = (f32[3,3,128]{2,1,0:T(4,128)S(1)}, f32[3,3,128]{2,1,0:T(4,128)}, u32[]{:S(2)}) copy-start(f32[3,3,128]{2,1,0:T(4,128)} %param.30) | copy-start | bytes 13828
  5.7 9.4 %copy-start.1 = (f32[6,35,128]{2,1,0:T(8,128)S(1)}, f32[6,35,128]{2,1,0:T(8,128)}, u32[]{:S(2)}) copy-start(f32[6,35,128]{2,1,0:T(8,128)} %param.28) | copy-start | bytes 322564
  6.0 9.2 %copy-start.7 = (f32[1,2,13,35,128]{4,1,3,2,0:T(2,128)S(1)}, f32[1,2,13,35,128]{4,1,3,2,0:T(2,128)}, u32[]{:S(2)}) copy-start(f32[1,2,13,35,128]{4,1,3,2,0:T(2,128)} %param.27) | copy-start | bytes 1397764
  6.8 17.3 %collective-permute-start = (f32[13,15,64]{2,1,0:T(8,128)}, f32[13,15,64]{2,1,0:T(8,128)}, u32[]{:S(2)}, u32[]{:S(2)}) collective-permute-start(f32[13,15,64]{2,1,0:T(8,128)} %get-tuple-element.48), channel_id=1, source_target_pairs={{0,1},{1,2},{2,3},{3,4},{4,5},{5,6},{6,7},{8,9},{9,10},{10,11},{11... | collective-permute-start | bytes 149768 | tf_op jit(solution)/shard_map/ppermute | solution.py:21
  12.3 13.0 %collective-permute-start.1 = (f32[13,15,64]{2,1,0:T(8,128)}, f32[13,15,64]{2,1,0:T(8,128)}, u32[]{:S(2)}, u32[]{:S(2)}) collective-permute-start(f32[13,15,64]{2,1,0:T(8,128)} %get-tuple-element.47), channel_id=1, source_target_pairs={{1,0},{2,1},{3,2},{4,3},{5,4},{6,5},{7,6},{9,8},{10,9},{11,10},{12... | collective-permute-start | bytes 149768 | tf_op jit(solution)/shard_map/ppermute | solution.py:22
  14.0 1.3 %copy-start.14 = (f32[3,35,35,1]{2,1,3,0:T(8,128)S(1)}, f32[3,35,35,1]{2,1,3,0:T(8,128)}, u32[]{:S(2)}) copy-start(f32[3,35,35,1]{2,1,3,0:T(8,128)} %constant.70) | copy-start | bytes 44104
  14.5 16.0 %copy-start.15 = (f32[4,128]{1,0:T(4,128)}, f32[4,128]{1,0:T(4,128)S(1)}, u32[]{:S(2)}) copy-start(f32[4,128]{1,0:T(4,128)S(1)} %broadcast_multiply_fusion) | copy-start | bytes 6148
  15.1 1.1 %copy-start.23 = (f32[128]{0:T(128)}, f32[128]{0:T(128)S(1)}, u32[]{:S(2)}) copy-start(f32[128]{0:T(128)S(1)} %get-tuple-element.49) | copy-start | bytes 1540
  15.1 1.1 %copy-start.25 = (f32[128]{0:T(128)}, f32[128]{0:T(128)S(1)}, u32[]{:S(2)}) copy-start(f32[128]{0:T(128)S(1)} %get-tuple-element.50) | copy-start | bytes 1540
  15.1 1.1 %copy-start.27 = (f32[128]{0:T(128)}, f32[128]{0:T(128)S(1)}, u32[]{:S(2)}) copy-start(f32[128]{0:T(128)S(1)} %get-tuple-element.51) | copy-start | bytes 1540
  15.1 1.1 %copy-start.29 = (f32[128]{0:T(128)}, f32[128]{0:T(128)S(1)}, u32[]{:S(2)}) copy-start(f32[128]{0:T(128)S(1)} %get-tuple-element.52) | copy-start | bytes 1540
  15.1 1.1 %copy-start.31 = (f32[128]{0:T(128)}, f32[128]{0:T(128)S(1)}, u32[]{:S(2)}) copy-start(f32[128]{0:T(128)S(1)} %get-tuple-element.53) | copy-start | bytes 1540
  15.1 1.1 %copy-start.33 = (f32[128]{0:T(128)}, f32[128]{0:T(128)S(1)}, u32[]{:S(2)}) copy-start(f32[128]{0:T(128)S(1)} %get-tuple-element.54) | copy-start | bytes 1540
  15.2 1.1 %copy-start.35 = (f32[128]{0:T(128)}, f32[128]{0:T(128)S(1)}, u32[]{:S(2)}) copy-start(f32[128]{0:T(128)S(1)} %get-tuple-element.55) | copy-start | bytes 1540
  15.2 1.1 %copy-start.37 = (f32[128]{0:T(128)}, f32[128]{0:T(128)S(1)}, u32[]{:S(2)}) copy-start(f32[128]{0:T(128)S(1)} %get-tuple-element.56) | copy-start | bytes 1540
  15.2 1.1 %copy-start.39 = (f32[128]{0:T(128)}, f32[128]{0:T(128)S(1)}, u32[]{:S(2)}) copy-start(f32[128]{0:T(128)S(1)} %get-tuple-element.57) | copy-start | bytes 1540
  15.2 5.5 %copy-start.3 = (f32[6,35,128]{2,0,1:T(8,128)}, f32[6,35,128]{2,0,1:T(8,128)S(1)}, u32[]{:S(2)}) copy-start(f32[6,35,128]{2,0,1:T(8,128)S(1)} %copy.219) | copy-start | bytes 322564
  17.0 3.4 %copy-start.17 = (f32[15,15]{1,0:T(8,128)S(1)}, f32[15,15]{1,0:T(8,128)}, u32[]{:S(2)}) copy-start(f32[15,15]{1,0:T(8,128)} %constant.61.clone) | copy-start | bytes 2704
  17.1 3.4 %copy-start.18 = (f32[15,15]{1,0:T(8,128)S(1)}, f32[15,15]{1,0:T(8,128)}, u32[]{:S(2)}) copy-start(f32[15,15]{1,0:T(8,128)} %constant.60.clone) | copy-start | bytes 2704
  17.1 3.3 %copy-start.19 = (f32[15,15]{1,0:T(8,128)S(1)}, f32[15,15]{1,0:T(8,128)}, u32[]{:S(2)}) copy-start(f32[15,15]{1,0:T(8,128)} %constant.59.clone) | copy-start | bytes 2704
  17.1 3.3 %copy-start.20 = (f32[15,15]{1,0:T(8,128)S(1)}, f32[15,15]{1,0:T(8,128)}, u32[]{:S(2)}) copy-start(f32[15,15]{1,0:T(8,128)} %constant.58.clone) | copy-start | bytes 2704
  17.1 3.3 %copy-start.21 = (f32[15,15]{1,0:T(8,128)S(1)}, f32[15,15]{1,0:T(8,128)}, u32[]{:S(2)}) copy-start(f32[15,15]{1,0:T(8,128)} %constant.57.clone) | copy-start | bytes 2704
  17.1 3.3 %copy-start.22 = (f32[15,15]{1,0:T(8,128)S(1)}, f32[15,15]{1,0:T(8,128)}, u32[]{:S(2)}) copy-start(f32[15,15]{1,0:T(8,128)} %constant.56.clone) | copy-start | bytes 2704
  20.7 3.4 %copy-start.41 = (f32[3,4,128]{2,1,0:T(4,128)S(1)}, f32[3,4,128]{2,1,0:T(4,128)}, u32[]{:S(2)}) copy-start(f32[3,4,128]{2,1,0:T(4,128)} %param.31) | copy-start | bytes 18436
  26.4 2.6 %copy-start.8 = (f32[60,6,128]{2,1,0:T(8,128)S(1)}, f32[60,6,128]{2,1,0:T(8,128)}, u32[]{:S(2)}) copy-start(f32[60,6,128]{2,1,0:T(8,128)} %copy.277) | copy-start | bytes 552964
  29.1 1.6 %copy-start.5 = (f32[13,35,128]{2,0,1:T(8,128)S(1)}, f32[13,35,128]{2,0,1:T(8,128)}, u32[]{:S(2)}) copy-start(f32[13,35,128]{2,0,1:T(8,128)} %fusion.13) | copy-start | bytes 698884
  29.1 1.6 %copy-start.12 = (f32[4,35,15,1]{1,2,0,3:T(8,128)S(1)}, f32[4,35,15,1]{1,2,0,3:T(8,128)}, u32[]{:S(2)}) copy-start(f32[4,35,15,1]{1,2,0,3:T(8,128)} %constant.69) | copy-start | bytes 25204
  34.1 9.0 %copy-start.24 = (f32[128]{0:T(128)S(1)}, f32[128]{0:T(128)}, u32[]{:S(2)}) copy-start(f32[128]{0:T(128)} %copy-done.23) | copy-start | bytes 1540
  34.1 9.0 %copy-start.26 = (f32[128]{0:T(128)S(1)}, f32[128]{0:T(128)}, u32[]{:S(2)}) copy-start(f32[128]{0:T(128)} %copy-done.25) | copy-start | bytes 1540
  34.1 9.0 %copy-start.28 = (f32[128]{0:T(128)S(1)}, f32[128]{0:T(128)}, u32[]{:S(2)}) copy-start(f32[128]{0:T(128)} %copy-done.27) | copy-start | bytes 1540
  34.1 9.0 %copy-start.30 = (f32[128]{0:T(128)S(1)}, f32[128]{0:T(128)}, u32[]{:S(2)}) copy-start(f32[128]{0:T(128)} %copy-done.29) | copy-start | bytes 1540
  34.1 9.0 %copy-start.32 = (f32[128]{0:T(128)S(1)}, f32[128]{0:T(128)}, u32[]{:S(2)}) copy-start(f32[128]{0:T(128)} %copy-done.31) | copy-start | bytes 1540
  34.1 9.0 %copy-start.34 = (f32[128]{0:T(128)S(1)}, f32[128]{0:T(128)}, u32[]{:S(2)}) copy-start(f32[128]{0:T(128)} %copy-done.33) | copy-start | bytes 1540
  34.1 9.0 %copy-start.36 = (f32[128]{0:T(128)S(1)}, f32[128]{0:T(128)}, u32[]{:S(2)}) copy-start(f32[128]{0:T(128)} %copy-done.35) | copy-start | bytes 1540
  34.1 9.0 %copy-start.38 = (f32[128]{0:T(128)S(1)}, f32[128]{0:T(128)}, u32[]{:S(2)}) copy-start(f32[128]{0:T(128)} %copy-done.37) | copy-start | bytes 1540
  34.1 9.0 %copy-start.40 = (f32[128]{0:T(128)S(1)}, f32[128]{0:T(128)}, u32[]{:S(2)}) copy-start(f32[128]{0:T(128)} %copy-done.39) | copy-start | bytes 1540
  36.9 6.5 %copy-start.4 = (f32[6,35,128]{2,0,1:T(8,128)S(1)}, f32[6,35,128]{2,0,1:T(8,128)}, u32[]{:S(2)}) copy-start(f32[6,35,128]{2,0,1:T(8,128)} %copy-done.3) | copy-start | bytes 322564
  37.0 8.0 %collective-permute-start.2 = (f32[13,15,64]{2,1,0:T(8,128)S(1)}, f32[13,15,64]{2,1,0:T(8,128)S(1)}, u32[]{:S(2)}, u32[]{:S(2)}) collective-permute-start(f32[13,15,64]{2,1,0:T(8,128)S(1)} %get-tuple-element.46), channel_id=1, source_target_pairs={{0,1},{1,2},{2,3},{3,4},{4,5},{5,6},{6,7},{8,9},{9,10},{10,11},{11... | collective-permute-start | bytes 149768 | tf_op jit(solution)/shard_map/ppermute | solution.py:21
  41.6 6.6 %collective-permute-start.3 = (f32[13,15,64]{2,1,0:T(8,128)S(1)}, f32[13,15,64]{2,1,0:T(8,128)S(1)}, u32[]{:S(2)}, u32[]{:S(2)}) collective-permute-start(f32[13,15,64]{2,1,0:T(8,128)S(1)} %get-tuple-element.45), channel_id=1, source_target_pairs={{1,0},{2,1},{3,2},{4,3},{5,4},{6,5},{7,6},{9,8},{10,9},{11,10},{12... | collective-permute-start | bytes 149768 | tf_op jit(solution)/shard_map/ppermute | solution.py:22
  48.5 2.6 %copy-start.9 = (f32[60,6,128]{2,1,0:T(8,128)S(1)}, f32[60,6,128]{2,1,0:T(8,128)}, u32[]{:S(2)}) copy-start(f32[60,6,128]{2,1,0:T(8,128)} %copy.277) | copy-start | bytes 552964
  50.0 2.6 %copy-start.16 = (f32[4,128]{1,0:T(4,128)S(1)}, f32[4,128]{1,0:T(4,128)}, u32[]{:S(2)}) copy-start(f32[4,128]{1,0:T(4,128)} %copy-done.15) | copy-start | bytes 6148
  51.1 1.6 %copy-start.6 = (f32[13,35,128]{2,0,1:T(8,128)S(1)}, f32[13,35,128]{2,0,1:T(8,128)}, u32[]{:S(2)}) copy-start(f32[13,35,128]{2,0,1:T(8,128)} %fusion.12) | copy-start | bytes 698884
  51.1 1.6 %copy-start.13 = (f32[4,35,15,1]{1,2,0,3:T(8,128)S(1)}, f32[4,35,15,1]{1,2,0,3:T(8,128)}, u32[]{:S(2)}) copy-start(f32[4,35,15,1]{1,2,0,3:T(8,128)} %constant.69) | copy-start | bytes 25204
  51.1 2.3 %copy-start.2 = (f32[2,6,13,35,128]{4,2,1,3,0:T(8,128)S(1)}, f32[2,6,13,35,128]{4,2,1,3,0:T(8,128)}, u32[]{:S(2)}) copy-start(f32[2,6,13,35,128]{4,2,1,3,0:T(8,128)} %convolution_bitcast_fusion) | copy-start | bytes 8386564
  54.7 4.9 %collective-permute-start.4 = (f32[6,35,64]{2,1,0:T(8,128)S(1)}, f32[6,35,64]{2,1,0:T(8,128)S(1)}, u32[]{:S(2)}, u32[]{:S(2)}) collective-permute-start(f32[6,35,64]{2,1,0:T(8,128)S(1)} %slice_select_fusion.1), channel_id=1, source_target_pairs={{0,16},{8,24},{16,0},{24,8},{1,17},{9,25},{17,1},{25,9},{2,18},{10... | collective-permute-start | bytes 161288 | tf_op jit(solution)/shard_map/ppermute | solution.py:161
  59.9 1.4 %collective-permute-start.5 = (f32[6,35,32]{2,1,0:T(8,128)S(1)}, f32[6,35,32]{2,1,0:T(8,128)S(1)}, u32[]{:S(2)}, u32[]{:S(2)}) collective-permute-start(f32[6,35,32]{2,1,0:T(8,128)S(1)} %slice_select_fusion), channel_id=1, source_target_pairs={{0,8},{8,0},{16,24},{24,16},{1,9},{9,1},{17,25},{25,17},{2,10},{10... | collective-permute-start | bytes 80648 | tf_op jit(solution)/shard_map/ppermute | solution.py:161
  62.4 13.1 %all-to-all-start = ((f32[32,1,60]{2,1,0:T(1,128)}), f32[32,1,60]{2,1,0:T(1,128)S(1)}, u32[]{:S(2)}, u32[]{:S(2)}) async-start(f32[32,1,60]{2,1,0:T(1,128)} %broadcast_in_dim.16), calls=%async_computation | async-start | bytes 32768 | tf_op jit(solution)/shard_map/all_to_all | solution.py:307

commit v16 on v14

--- a/solution.py
+++ b/solution.py
@@ -268,15 +268,16 @@
     step_share = both_share[:pairs]
     change_share = both_share[pairs:]
     gram = jnp.sum(both_share[:, None] * change_share[None, :], axis=(2, 3, 4))
-    step_share, change_share, gram, adjoint = lax.optimization_barrier(
-        (step_share, change_share, gram, adjoint)
-    )
     gradient = jnp.zeros((params, node_count, elements), jnp.float32)
     for step_index in range(forward_states.shape[1]):
         inner_trace = adjoint[:, face_nodes.T, :]
         flat_trace = inner_trace.reshape(fields, face_width, 4 * elements)
         sent_traces = jnp.einsum("fns,sj->fnj", flat_trace, send_pick, precision=MIX)
         extended = padded(sent_traces, (("mesh", 2),), border)
+        if step_index == 0:
+            step_share, change_share, gram, extended = lax.optimization_barrier(
+                (step_share, change_share, gram, extended)
+            )
         gathered = jnp.einsum("fns,sj->fnj", flat_trace, local_pick, precision=MIX)
         gathered = gathered + jnp.einsum(
             "fns,sj->fnj", extended[:, :, :border], below_pick, precision=MIX

time: 76.7 us -> 76.2 us (level)
  matrix products: 18.9 us -> 17 us
  local copies, waits for them, and re-layouts: 14.6 us -> 15.8 us
  other arithmetic: 8.29 us -> 9.07 us
    unnamed x100 -> x96, local copies, waits for them, and re-layouts: 5.67 us -> 7.64 us
    concatenate x0 -> x1, other arithmetic: none -> 1.09 us  [padded(): x = jnp.concatenate([before, x, after], axis=dim)]
    sub x2, other arithmetic: 1.14 us -> 0.16 us  [shards(): jump_trace = turned.reshape(fields, face_width, 4, elements) - inner_trace]
    dot_general x2, matrix products: 1.45 us -> 0.55 us  [shards(): jnp.einsum('fns,sj->fnj', extended[:, :, :border], below_pick, precision=...]
    dot_general x2, matrix products: 1.46 us -> 0.61 us  [shards(): jnp.einsum('fns,sj->fnj', extended[:, :, 3 * border:], above_pick, precis...]
  transfers between devices with their start and end apart: 7 -> 7, of which waited for: 4 -> 4; matrix products, arithmetic and copies ran while one was open for 19% -> 22% of each run, Pallas kernels for 0% -> 0%
where the time goes in v16:
time: 76.2 us; the launch traced here: 75.6 us
  starting transfers between devices  20.6 us (27%)
  matrix products  17 us (22%)
  local copies, waits for them, and re-layouts  15.8 us (21%)
  waiting for transfers between devices  11.5 us (15%)
  other arithmetic  9.07 us (12%)
  between operations  1.65 us (2%)
    ppermute x2, starting transfers between devices, padded(): before = lax.ppermute(last, axis, up)  10.5 us
    unnamed x96, local copies, waits for them, and re-layouts  7.64 us
    all_to_all x1, waiting for transfers between devices, combine_sums(): lax.all_to_all(spread, ('shot', 'mesh'), 0, 0, tiled=False)  5.95 us
    all_to_all x1, starting transfers between devices, combine_sums(): lax.all_to_all(spread, ('shot', 'mesh'), 0, 0, tiled=False)  5.72 us
    ppermute x2, waiting for transfers between devices, halving_sum(): lax.ppermute(jnp.where(upper, low, high), axis, [(i, i ^ bit) for i in ra...  4.6 us
    dot_general x2, matrix products, surface_term(): mixing = jnp.einsum('dpfg,dfnxe->pgnxe', coupling, weighted, precision=MIX)  2.97 us
    dot_general x2, matrix products, kernel_term(): mixing = jnp.einsum('dpfg,dgae->pfae', coupling, spatial, precision=MIX)  2.87 us
    ppermute x2, starting transfers between devices, padded(): after = lax.ppermute(first, axis, down)  2.75 us
  transfers between devices with their start and end apart: 7, of which 4 were waited for; matrix products, arithmetic and copies ran while one was open for 22% of the time, Pallas kernels for 0%

profile of v16, /device:TPU:0, one launch (start us, length us, event | category | flops | bytes accessed | tf_op | source)
XLA Modules:
  0.0 75.6 jit_solution(10889633383068618927)
XLA Ops:
  0.6 0.7 pad_clamp_fusion
  1.3 1.0 %copy.352 = f32[1,13,35,128]{3,1,2,0:T(8,128)S(1)} copy(f32[1,13,35,128]{3,0,2,1:T(1,128)} %param.26) | data formatting | bytes 465920
  2.3 0.6 gather_fusion.1
  3.3 0.3 copy-done.42
  3.6 0.3 fusion.38
  3.9 0.7 fusion.150
  4.6 1.3 %collective-permute-start.1 = (f32[13,15,64]{2,1,0:T(8,128)}, f32[13,15,64]{2,1,0:T(8,128)}, u32[]{:S(2)}, u32[]{:S(2)}) collective-permute-start(f32[13,15,64]{2,1,0:T(8,128)} %get-tuple-element.51), channel_id=1, source_target_pairs={{1,0},{2,1},{3,2},{4,3},{5,4},{6,5},{7,6},{9,8},{10,9},{11,10},{12... | collective-permute-start | bytes 149768 | tf_op jit(solution)/shard_map/ppermute | solution.py:22
  5.9 6.1 %collective-permute-start = (f32[13,15,64]{2,1,0:T(8,128)}, f32[13,15,64]{2,1,0:T(8,128)}, u32[]{:S(2)}, u32[]{:S(2)}) collective-permute-start(f32[13,15,64]{2,1,0:T(8,128)} %get-tuple-element.50), channel_id=1, source_target_pairs={{0,1},{1,2},{2,3},{3,4},{4,5},{5,6},{6,7},{8,9},{9,10},{10,11},{11... | collective-permute-start | bytes 149768 | tf_op jit(solution)/shard_map/ppermute | solution.py:21
  12.0 0.2 iota_compare_fusion
  12.3 0.5 fusion.31
  12.8 2.8 %fusion.10 = f32[10,6,35,32]{2,3,1,0:T(8,128)S(1)} fusion(f32[5,6,35,128]{3,2,1,0:T(8,128)S(1)} %copy-done.9, f32[5,6,35,128]{3,2,1,0:T(8,128)} %param.36, s32[32]{0:T(128)S(1)} %iota_add_fusion), kind=kOutput, calls=%fused_computation.27 | convolution fusion | flops 51882496 | bytes 1344128 | tf_op jit(solution)/shard_map/ipae,ej->ipaj/dot_general | solution.py:261
  15.7 0.6 multiply_reduce_fusion.2
  16.3 0.3 copy-done.1
  16.6 0.5 convolution_bitcast_fusion.3
  17.2 0.2 copy-done.14
  17.4 0.4 fusion.147
  17.7 0.5 convolution_bitcast_fusion
  18.5 0.5 convolution_bitcast_fusion.1
  19.3 0.8 %copy-done.10 = f32[3,6,13,13]{3,2,1,0:T(8,128)S(1)} copy-done((f32[3,6,13,13]{3,2,1,0:T(8,128)S(1)}, f32[3,6,13,13]{3,2,1,0:T(8,128)}, u32[]{:S(2)}) %copy-start.10) | copy-done | bytes 12192
  20.1 1.7 %fusion.5 = f32[13,35,128]{2,0,1:T(8,128)} fusion(f32[3,13,35,128,1]{3,2,1,0,4:T(8,128)S(1)} %maximum_bitcast_fusion, f32[6,35,128]{2,0,1:T(8,128)S(1)} %copy.232, f32[3,6,13,13]{3,2,1,0:T(8,128)S(1)} %copy-done.10), kind=kOutput, calls=%fused_computation.17 | convolution fusion | flops 82409600 | bytes 1051528 | tf_op jit(solution)/shard_map/dpfg,dfae->pgae/dot_general | solution.py:133
  21.8 1.0 %maximum_bitcast_fusion.3 = f32[3,13,35,128,1]{3,2,1,0,4:T(8,128)} fusion(f32[1,13,35,128]{3,2,1,0:T(8,128)S(1)} %get-tuple-element.37, f32[1,13,35,128]{3,2,1,0:T(8,128)S(1)} %get-tuple-element.36, f32[1,13,35,128]{3,2,1,0:T(8,128)S(1)} %get-tuple-element.35), kind=kLoop, calls=%fused_computation.55 | loop fusion | flops 349440 | bytes 1397760 | tf_op jit(solution)/shard_map/stack | solution.py:128
  22.8 0.3 multiply_add_fusion
  23.1 1.0 %maximum_bitcast_fusion.2 = f32[3,13,35,128,1]{3,2,1,0,4:T(8,128)} fusion(f32[1,13,35,128]{3,2,1,0:T(8,128)S(1)} %get-tuple-element.34, f32[1,13,35,128]{3,2,1,0:T(8,128)S(1)} %get-tuple-element.33, f32[1,13,35,128]{3,2,1,0:T(8,128)S(1)} %get-tuple-element.32), kind=kLoop, calls=%fused_computation.54 | loop fusion | flops 349440 | bytes 1397760 | tf_op jit(solution)/shard_map/stack | solution.py:128
  24.1 0.8 %gather_fusion = f32[60,6,128]{2,0,1:T(8,128)S(1)} fusion(f32[6,35,128]{2,1,0:T(8,128)S(1)} %copy-done, s32[1024]{0:T(1024)S(1)} %pad_clamp_fusion), kind=kCustom, calls=%fused_computation | custom fusion | bytes 368880 | tf_op jit(solution)/shard_map/gather | solution.py:232
  25.0 0.8 %copy.292 = f32[60,6,128]{2,1,0:T(8,128)} copy(f32[60,6,128]{2,0,1:T(8,128)S(1)} %gather_fusion) | data formatting | bytes 368640 | tf_op jit(solution)/shard_map/gather | solution.py:232
  25.8 1.1 %pad_maximum_fusion = f32[13,15,256]{2,1,0:T(8,128)S(1)} fusion(f32[13,15,64]{2,1,0:T(8,128)} %collective-permute-done.1, f32[13,15,128]{2,1,0:T(8,128)S(1)} %fusion.38, f32[13,15,64]{2,1,0:T(8,128)} %collective-permute-done), kind=kLoop, calls=%fused_computation.91 | loop fusion | flops 99840 | bytes 399360 | tf_op jit(solution)/shard_map/concatenate | solution.py:23
  26.9 0.3 convolution_add_fusion.3
  27.2 0.3 convolution_add_fusion.2
  27.5 0.6 multiply_reduce_fusion.1
  28.4 0.8 %copy-done.11 = f32[3,6,13,13]{3,2,1,0:T(8,128)S(1)} copy-done((f32[3,6,13,13]{3,2,1,0:T(8,128)S(1)}, f32[3,6,13,13]{3,2,1,0:T(8,128)}, u32[]{:S(2)}) %copy-start.11) | copy-done | bytes 12192
  29.3 1.5 %fusion.1 = f32[13,15,4,128]{3,0,2,1:T(8,128)S(1)} fusion(f32[6,15,4,128]{3,0,2,1:T(8,128)S(1)} %bitcast.791, f32[13,15,4,128]{3,0,2,1:T(8,128)S(1)} %copy_subtract_fusion.1, f32[3,4,128]{2,0,1:T(4,128)S(1)} %copy.236, f32[3,6,13,13]{3,2,1,0:T(8,128)S(1)} %copy-done.11), kind=kOutput, calls=%fused_computation.9 | convolution fusion | flops 141573120 | bytes 1001352 | tf_op jit(solution)/shard_map/dpfg,dfnxe->pgnxe/dot_general | solution.py:145
  30.9 0.9 %copy-done.4 = f32[13,35,128]{2,0,1:T(8,128)S(1)} copy-done((f32[13,35,128]{2,0,1:T(8,128)S(1)}, f32[13,35,128]{2,0,1:T(8,128)}, u32[]{:S(2)}) %copy-start.4) | copy-done | bytes 232984
  31.7 0.6 fusion.16
  32.4 0.6 gather_fusion.2
  33.0 0.9 %copy.247 = f32[13,15,4,128]{3,2,1,0:T(4,128)} copy(f32[13,15,4,128]{3,0,2,1:T(8,128)S(1)} %bitcast.775) | data formatting | bytes 798720 | tf_op jit(solution)/shard_map/gather | solution.py:273
  34.0 1.2 %reshape.369 = f32[13,15,512]{2,1,0:T(8,128)S(1)} reshape(f32[13,15,4,128]{3,2,1,0:T(4,128)} %copy.247) | data formatting | bytes 798720 | tf_op jit(solution)/shard_map/reshape | solution.py:274
  35.2 0.5 fusion.30
  35.7 0.3 fusion.36
  36.0 0.5 convolution_bitcast_fusion.2
  36.6 4.3 %collective-permute-start.2 = (f32[13,15,64]{2,1,0:T(8,128)S(1)}, f32[13,15,64]{2,1,0:T(8,128)S(1)}, u32[]{:S(2)}, u32[]{:S(2)}) collective-permute-start(f32[13,15,64]{2,1,0:T(8,128)S(1)} %get-tuple-element.49), channel_id=1, source_target_pairs={{0,1},{1,2},{2,3},{3,4},{4,5},{5,6},{6,7},{8,9},{9,10},{10,11},{11... | collective-permute-start | bytes 149768 | tf_op jit(solution)/shard_map/ppermute | solution.py:21
  41.0 1.5 %collective-permute-start.3 = (f32[13,15,64]{2,1,0:T(8,128)S(1)}, f32[13,15,64]{2,1,0:T(8,128)S(1)}, u32[]{:S(2)}, u32[]{:S(2)}) collective-permute-start(f32[13,15,64]{2,1,0:T(8,128)S(1)} %get-tuple-element.48), channel_id=1, source_target_pairs={{1,0},{2,1},{3,2},{4,3},{5,4},{6,5},{7,6},{9,8},{10,9},{11,10},{12... | collective-permute-start | bytes 149768 | tf_op jit(solution)/shard_map/ppermute | solution.py:22
  42.7 1.8 %fusion.3 = f32[6,35,128]{2,0,1:T(8,128)} fusion(f32[3,13,35,128,1]{3,2,1,0,4:T(8,128)S(1)} %copy-done.8, f32[13,35,128]{2,0,1:T(8,128)S(1)} %copy.246, f32[3,6,13,13]{3,2,1,0:T(8,128)S(1)} %copy-done.12), kind=kOutput, calls=%fused_computation.13 | convolution fusion | flops 82440960 | bytes 1051528 | tf_op jit(solution)/shard_map/dpfg,dgae->pfae/dot_general | solution.py:139
  44.6 0.8 %copy-done.3 = f32[6,35,128]{2,0,1:T(8,128)S(1)} copy-done((f32[6,35,128]{2,0,1:T(8,128)S(1)}, f32[6,35,128]{2,0,1:T(8,128)}, u32[]{:S(2)}) %copy-start.3) | copy-done | bytes 107544
  45.4 0.9 %fusion.4 = f32[13,35,128]{2,0,1:T(8,128)S(1)} fusion(f32[3,13,35,128,1]{3,2,1,0,4:T(8,128)S(1)} %maximum_bitcast_fusion.1, f32[6,35,128]{2,0,1:T(8,128)S(1)} %copy-done.3, f32[3,6,13,13]{3,2,1,0:T(8,128)S(1)} %copy-done.12), kind=kOutput, calls=%fused_computation.15 | convolution fusion | flops 82409600 | bytes 1051528 | tf_op jit(solution)/shard_map/dpfg,dfae->pgae/dot_general | solution.py:133
  46.3 0.3 convolution_add_fusion.1
  46.6 1.0 %collective-permute-done.3 = f32[13,15,64]{2,1,0:T(8,128)S(1)} collective-permute-done((f32[13,15,64]{2,1,0:T(8,128)S(1)}, f32[13,15,64]{2,1,0:T(8,128)S(1)}, u32[]{:S(2)}, u32[]{:S(2)}) %collective-permute-start.3) | collective-permute-done | bytes 49952 | tf_op jit(solution)/shard_map/ppermute | solution.py:22
  47.6 0.3 convolution_add_fusion
  47.9 0.6 multiply_reduce_fusion
  48.8 0.8 %copy-done.13 = f32[3,6,13,13]{3,2,1,0:T(8,128)S(1)} copy-done((f32[3,6,13,13]{3,2,1,0:T(8,128)S(1)}, f32[3,6,13,13]{3,2,1,0:T(8,128)}, u32[]{:S(2)}) %copy-start.13) | copy-done | bytes 12192
  49.7 1.5 %fusion = f32[13,15,4,128]{3,0,2,1:T(8,128)S(1)} fusion(f32[6,15,4,128]{3,0,2,1:T(8,128)S(1)} %bitcast.792, f32[13,15,4,128]{3,0,2,1:T(8,128)S(1)} %copy_subtract_fusion, f32[3,4,128]{2,0,1:T(4,128)S(1)} %copy.236, f32[3,6,13,13]{3,2,1,0:T(8,128)S(1)} %copy-done.13), kind=kOutput, calls=%fused_computation.7 | convolution fusion | flops 141573120 | bytes 1001352 | tf_op jit(solution)/shard_map/dpfg,dfnxe->pgnxe/dot_general | solution.py:145
  51.3 0.6 fusion.19
  51.9 0.5 copy-done.7
  52.4 1.1 %fusion.2 = f32[6,35,128]{2,0,1:T(8,128)S(1)} fusion(f32[3,13,35,128,1]{3,2,1,0,4:T(8,128)S(1)} %copy-done.7, f32[13,35,128]{2,0,1:T(8,128)S(1)} %copy.259, f32[3,6,13,13]{3,2,1,0:T(8,128)S(1)} %copy-done.13), kind=kOutput, calls=%fused_computation.11 | convolution fusion | flops 82440960 | bytes 1051528 | tf_op jit(solution)/shard_map/dpfg,dgae->pfae/dot_general | solution.py:139
  53.7 1.6 %collective-permute-start.4 = (f32[6,35,64]{2,1,0:T(8,128)S(1)}, f32[6,35,64]{2,1,0:T(8,128)S(1)}, u32[]{:S(2)}, u32[]{:S(2)}) collective-permute-start(f32[6,35,64]{2,1,0:T(8,128)S(1)} %slice_select_fusion.1), channel_id=1, source_target_pairs={{0,16},{8,24},{16,0},{24,8},{1,17},{9,25},{17,1},{25,9},{2,18},{10... | collective-permute-start | bytes 161288 | tf_op jit(solution)/shard_map/ppermute | solution.py:161
  55.3 3.4 %collective-permute-done.4 = f32[6,35,64]{2,1,0:T(8,128)S(1)} collective-permute-done((f32[6,35,64]{2,1,0:T(8,128)S(1)}, f32[6,35,64]{2,1,0:T(8,128)S(1)}, u32[]{:S(2)}, u32[]{:S(2)}) %collective-permute-start.4) | collective-permute-done | bytes 53792 | tf_op jit(solution)/shard_map/ppermute | solution.py:161
  59.0 1.2 %collective-permute-done.5 = f32[6,35,32]{2,1,0:T(8,128)S(1)} collective-permute-done((f32[6,35,32]{2,1,0:T(8,128)S(1)}, f32[6,35,32]{2,1,0:T(8,128)S(1)}, u32[]{:S(2)}, u32[]{:S(2)}) %collective-permute-start.5) | collective-permute-done | bytes 26912 | tf_op jit(solution)/shard_map/ppermute | solution.py:161
  60.5 0.2 fusion.21
  60.8 0.6 broadcast_in_dim.16
  61.4 5.7 %all-to-all-start = ((f32[32,1,60]{2,1,0:T(1,128)}), f32[32,1,60]{2,1,0:T(1,128)S(1)}, u32[]{:S(2)}, u32[]{:S(2)}) async-start(f32[32,1,60]{2,1,0:T(1,128)} %broadcast_in_dim.16), calls=%async_computation | async-start | bytes 32768 | tf_op jit(solution)/shard_map/all_to_all | solution.py:301
  67.2 0.9 %copy.266 = f32[1,13,35,128]{3,0,2,1:T(1,128)} copy(f32[1,13,35,128]{3,2,1,0:T(8,128)S(1)} %bitcast.777) | data formatting | bytes 465920
  68.3 5.9 %all-to-all-done = f32[32,1,60]{2,1,0:T(1,128)S(1)} async-done(((f32[32,1,60]{2,1,0:T(1,128)}), f32[32,1,60]{2,1,0:T(1,128)S(1)}, u32[]{:S(2)}, u32[]{:S(2)}) %all-to-all-start) | async-done | bytes 7712 | tf_op jit(solution)/shard_map/all_to_all | solution.py:301
  74.6 0.2 slice_reduce_fusion
  74.8 0.2 fusion.20
  75.0 0.6 neg.22
  (136 shorter events, 3.7 us)
Async XLA Ops:
  2.9 0.7 copy-start.42
  3.1 9.0 %copy-start.44 = (s32[4,128]{1,0:T(4,128)S(1)}, s32[4,128]{1,0:T(4,128)}, u32[]{:S(2)}) copy-start(s32[4,128]{1,0:T(4,128)} %param.34) | copy-start | bytes 6148
  3.1 9.0 %copy-start.41 = (s32[4,128]{1,0:T(4,128)S(1)}, s32[4,128]{1,0:T(4,128)}, u32[]{:S(2)}) copy-start(s32[4,128]{1,0:T(4,128)} %param.33) | copy-start | bytes 6148
  3.9 8.9 %copy-start.9 = (f32[5,6,35,128]{3,2,1,0:T(8,128)S(1)}, f32[5,6,35,128]{3,2,1,0:T(8,128)}, u32[]{:S(2)}) copy-start(f32[5,6,35,128]{3,2,1,0:T(8,128)} %param.37) | copy-start | bytes 1612804
  4.6 21.2 %collective-permute-start.1 = (f32[13,15,64]{2,1,0:T(8,128)}, f32[13,15,64]{2,1,0:T(8,128)}, u32[]{:S(2)}, u32[]{:S(2)}) collective-permute-start(f32[13,15,64]{2,1,0:T(8,128)} %get-tuple-element.51), channel_id=1, source_target_pairs={{1,0},{2,1},{3,2},{4,3},{5,4},{6,5},{7,6},{9,8},{10,9},{11,10},{12... | collective-permute-start | bytes 149768 | tf_op jit(solution)/shard_map/ppermute | solution.py:22
  5.9 19.9 %collective-permute-start = (f32[13,15,64]{2,1,0:T(8,128)}, f32[13,15,64]{2,1,0:T(8,128)}, u32[]{:S(2)}, u32[]{:S(2)}) collective-permute-start(f32[13,15,64]{2,1,0:T(8,128)} %get-tuple-element.50), channel_id=1, source_target_pairs={{0,1},{1,2},{2,3},{3,4},{4,5},{5,6},{6,7},{8,9},{9,10},{10,11},{11... | collective-permute-start | bytes 149768 | tf_op jit(solution)/shard_map/ppermute | solution.py:21
  15.6 0.7 copy-start.45
  15.6 0.9 %copy-start.1 = (f32[1,13,35,128]{3,0,2,1:T(1,128)S(1)}, f32[1,13,35,128]{3,0,2,1:T(1,128)}, u32[]{:S(2)}) copy-start(f32[1,13,35,128]{3,0,2,1:T(1,128)} %param.26) | copy-start | bytes 698884
  15.6 0.9 %copy-start.5 = (f32[3,35,35,1]{2,1,3,0:T(8,128)S(1)}, f32[3,35,35,1]{2,1,3,0:T(8,128)}, u32[]{:S(2)}) copy-start(f32[3,35,35,1]{2,1,3,0:T(8,128)} %constant.68) | copy-start | bytes 44104
  15.7 1.4 %copy-start.40 = (f32[3,3,128]{2,1,0:T(4,128)S(1)}, f32[3,3,128]{2,1,0:T(4,128)}, u32[]{:S(2)}) copy-start(f32[3,3,128]{2,1,0:T(4,128)} %param.30) | copy-start | bytes 13828
  15.7 1.4 %copy-start = (f32[6,35,128]{2,1,0:T(8,128)S(1)}, f32[6,35,128]{2,1,0:T(8,128)}, u32[]{:S(2)}) copy-start(f32[6,35,128]{2,1,0:T(8,128)} %param.28) | copy-start | bytes 322564
  16.3 1.1 %copy-start.14 = (f32[1,2,13,35,128]{4,1,3,2,0:T(2,128)S(1)}, f32[1,2,13,35,128]{4,1,3,2,0:T(2,128)}, u32[]{:S(2)}) copy-start(f32[1,2,13,35,128]{4,1,3,2,0:T(2,128)} %param.27) | copy-start | bytes 1397764
  17.1 1.9 %copy-start.19 = (f32[128]{0:T(128)}, f32[128]{0:T(128)S(1)}, u32[]{:S(2)}) copy-start(f32[128]{0:T(128)S(1)} %get-tuple-element.54) | copy-start | bytes 1540
  17.1 1.9 %copy-start.21 = (f32[128]{0:T(128)}, f32[128]{0:T(128)S(1)}, u32[]{:S(2)}) copy-start(f32[128]{0:T(128)S(1)} %get-tuple-element.55) | copy-start | bytes 1540
  17.1 1.9 %copy-start.23 = (f32[128]{0:T(128)}, f32[128]{0:T(128)S(1)}, u32[]{:S(2)}) copy-start(f32[128]{0:T(128)S(1)} %get-tuple-element.56) | copy-start | bytes 1540
  17.1 1.9 %copy-start.25 = (f32[128]{0:T(128)}, f32[128]{0:T(128)S(1)}, u32[]{:S(2)}) copy-start(f32[128]{0:T(128)S(1)} %get-tuple-element.57) | copy-start | bytes 1540
  17.1 1.9 %copy-start.27 = (f32[128]{0:T(128)}, f32[128]{0:T(128)S(1)}, u32[]{:S(2)}) copy-start(f32[128]{0:T(128)S(1)} %get-tuple-element.58) | copy-start | bytes 1540
  17.2 1.9 %copy-start.29 = (f32[128]{0:T(128)}, f32[128]{0:T(128)S(1)}, u32[]{:S(2)}) copy-start(f32[128]{0:T(128)S(1)} %get-tuple-element.59) | copy-start | bytes 1540
  17.2 1.9 %copy-start.31 = (f32[128]{0:T(128)}, f32[128]{0:T(128)S(1)}, u32[]{:S(2)}) copy-start(f32[128]{0:T(128)S(1)} %get-tuple-element.60) | copy-start | bytes 1540
  17.4 1.9 %copy-start.2 = (f32[6,35,128]{2,0,1:T(8,128)}, f32[6,35,128]{2,0,1:T(8,128)S(1)}, u32[]{:S(2)}) copy-start(f32[6,35,128]{2,0,1:T(8,128)S(1)} %copy.232) | copy-start | bytes 322564
  19.2 0.9 %copy-start.10 = (f32[3,6,13,13]{3,2,1,0:T(8,128)S(1)}, f32[3,6,13,13]{3,2,1,0:T(8,128)}, u32[]{:S(2)}) copy-start(f32[3,6,13,13]{3,2,1,0:T(8,128)} %param.29) | copy-start | bytes 36508
  21.8 1.0 %copy-start.33 = (f32[15,15]{1,0:T(8,128)S(1)}, f32[15,15]{1,0:T(8,128)}, u32[]{:S(2)}) copy-start(f32[15,15]{1,0:T(8,128)} %constant.61.clone) | copy-start | bytes 2704
  21.8 1.0 %copy-start.34 = (f32[15,15]{1,0:T(8,128)S(1)}, f32[15,15]{1,0:T(8,128)}, u32[]{:S(2)}) copy-start(f32[15,15]{1,0:T(8,128)} %constant.60.clone) | copy-start | bytes 2704
  21.8 1.0 %copy-start.35 = (f32[15,15]{1,0:T(8,128)S(1)}, f32[15,15]{1,0:T(8,128)}, u32[]{:S(2)}) copy-start(f32[15,15]{1,0:T(8,128)} %constant.59.clone) | copy-start | bytes 2704
  21.8 1.0 %copy-start.36 = (f32[15,15]{1,0:T(8,128)S(1)}, f32[15,15]{1,0:T(8,128)}, u32[]{:S(2)}) copy-start(f32[15,15]{1,0:T(8,128)} %constant.58.clone) | copy-start | bytes 2704
  21.8 1.0 %copy-start.37 = (f32[15,15]{1,0:T(8,128)S(1)}, f32[15,15]{1,0:T(8,128)}, u32[]{:S(2)}) copy-start(f32[15,15]{1,0:T(8,128)} %constant.57.clone) | copy-start | bytes 2704
  21.8 1.0 %copy-start.38 = (f32[15,15]{1,0:T(8,128)S(1)}, f32[15,15]{1,0:T(8,128)}, u32[]{:S(2)}) copy-start(f32[15,15]{1,0:T(8,128)} %constant.56.clone) | copy-start | bytes 2704
  24.1 1.7 %copy-start.39 = (f32[3,4,128]{2,1,0:T(4,128)S(1)}, f32[3,4,128]{2,1,0:T(4,128)}, u32[]{:S(2)}) copy-start(f32[3,4,128]{2,1,0:T(4,128)} %param.31) | copy-start | bytes 18436
  28.3 0.9 %copy-start.11 = (f32[3,6,13,13]{3,2,1,0:T(8,128)S(1)}, f32[3,6,13,13]{3,2,1,0:T(8,128)}, u32[]{:S(2)}) copy-start(f32[3,6,13,13]{3,2,1,0:T(8,128)} %param.29) | copy-start | bytes 36508
  28.3 1.0 %copy-start.15 = (f32[60,6,128]{2,1,0:T(8,128)S(1)}, f32[60,6,128]{2,1,0:T(8,128)}, u32[]{:S(2)}) copy-start(f32[60,6,128]{2,1,0:T(8,128)} %copy.292) | copy-start | bytes 552964
  30.8 1.0 %copy-start.4 = (f32[13,35,128]{2,0,1:T(8,128)S(1)}, f32[13,35,128]{2,0,1:T(8,128)}, u32[]{:S(2)}) copy-start(f32[13,35,128]{2,0,1:T(8,128)} %fusion.5) | copy-start | bytes 698884
  30.8 1.0 %copy-start.18 = (f32[4,35,15,1]{1,2,0,3:T(8,128)S(1)}, f32[4,35,15,1]{1,2,0,3:T(8,128)}, u32[]{:S(2)}) copy-start(f32[4,35,15,1]{1,2,0,3:T(8,128)} %constant.69) | copy-start | bytes 25204
  34.0 1.7 %copy-start.43 = (s32[128]{0:T(128)S(1)}, s32[128]{0:T(128)}, u32[]{:S(2)}) copy-start(s32[128]{0:T(128)} %param.35) | copy-start | bytes 1540
  35.2 0.9 %copy-start.6 = (f32[3,35,35,1]{2,1,3,0:T(8,128)S(1)}, f32[3,35,35,1]{2,1,3,0:T(8,128)}, u32[]{:S(2)}) copy-start(f32[3,35,35,1]{2,1,3,0:T(8,128)} %constant.68) | copy-start | bytes 44104
  35.7 6.8 %copy-start.20 = (f32[128]{0:T(128)S(1)}, f32[128]{0:T(128)}, u32[]{:S(2)}) copy-start(f32[128]{0:T(128)} %copy-done.19) | copy-start | bytes 1540
  35.7 6.8 %copy-start.22 = (f32[128]{0:T(128)S(1)}, f32[128]{0:T(128)}, u32[]{:S(2)}) copy-start(f32[128]{0:T(128)} %copy-done.21) | copy-start | bytes 1540
  35.7 6.8 %copy-start.24 = (f32[128]{0:T(128)S(1)}, f32[128]{0:T(128)}, u32[]{:S(2)}) copy-start(f32[128]{0:T(128)} %copy-done.23) | copy-start | bytes 1540
  35.7 6.8 %copy-start.26 = (f32[128]{0:T(128)S(1)}, f32[128]{0:T(128)}, u32[]{:S(2)}) copy-start(f32[128]{0:T(128)} %copy-done.25) | copy-start | bytes 1540
  35.7 6.8 %copy-start.28 = (f32[128]{0:T(128)S(1)}, f32[128]{0:T(128)}, u32[]{:S(2)}) copy-start(f32[128]{0:T(128)} %copy-done.27) | copy-start | bytes 1540
  35.7 6.8 %copy-start.30 = (f32[128]{0:T(128)S(1)}, f32[128]{0:T(128)}, u32[]{:S(2)}) copy-start(f32[128]{0:T(128)} %copy-done.29) | copy-start | bytes 1540
  35.7 6.8 %copy-start.32 = (f32[128]{0:T(128)S(1)}, f32[128]{0:T(128)}, u32[]{:S(2)}) copy-start(f32[128]{0:T(128)} %copy-done.31) | copy-start | bytes 1540
  36.5 6.2 %copy-start.8 = (f32[3,13,35,128,1]{3,2,1,0,4:T(8,128)S(1)}, f32[3,13,35,128,1]{3,2,1,0,4:T(8,128)}, u32[]{:S(2)}) copy-start(f32[3,13,35,128,1]{3,2,1,0,4:T(8,128)} %maximum_bitcast_fusion.2) | copy-start | bytes 2096644
  36.5 6.2 %copy-start.12 = (f32[3,6,13,13]{3,2,1,0:T(8,128)S(1)}, f32[3,6,13,13]{3,2,1,0:T(8,128)}, u32[]{:S(2)}) copy-start(f32[3,6,13,13]{3,2,1,0:T(8,128)} %param.29) | copy-start | bytes 36508
  36.6 9.7 %collective-permute-start.2 = (f32[13,15,64]{2,1,0:T(8,128)S(1)}, f32[13,15,64]{2,1,0:T(8,128)S(1)}, u32[]{:S(2)}, u32[]{:S(2)}) collective-permute-start(f32[13,15,64]{2,1,0:T(8,128)S(1)} %get-tuple-element.49), channel_id=1, source_target_pairs={{0,1},{1,2},{2,3},{3,4},{4,5},{5,6},{6,7},{8,9},{9,10},{10,11},{11... | collective-permute-start | bytes 149768 | tf_op jit(solution)/shard_map/ppermute | solution.py:21
  41.0 6.6 %collective-permute-start.3 = (f32[13,15,64]{2,1,0:T(8,128)S(1)}, f32[13,15,64]{2,1,0:T(8,128)S(1)}, u32[]{:S(2)}, u32[]{:S(2)}) collective-permute-start(f32[13,15,64]{2,1,0:T(8,128)S(1)} %get-tuple-element.48), channel_id=1, source_target_pairs={{1,0},{2,1},{3,2},{4,3},{5,4},{6,5},{7,6},{9,8},{10,9},{11,10},{12... | collective-permute-start | bytes 149768 | tf_op jit(solution)/shard_map/ppermute | solution.py:22
  44.5 0.9 %copy-start.3 = (f32[6,35,128]{2,0,1:T(8,128)S(1)}, f32[6,35,128]{2,0,1:T(8,128)}, u32[]{:S(2)}) copy-start(f32[6,35,128]{2,0,1:T(8,128)} %copy-done.2) | copy-start | bytes 322564
  48.7 0.9 %copy-start.13 = (f32[3,6,13,13]{3,2,1,0:T(8,128)S(1)}, f32[3,6,13,13]{3,2,1,0:T(8,128)}, u32[]{:S(2)}) copy-start(f32[3,6,13,13]{3,2,1,0:T(8,128)} %param.29) | copy-start | bytes 36508
  48.7 1.0 %copy-start.16 = (f32[60,6,128]{2,1,0:T(8,128)S(1)}, f32[60,6,128]{2,1,0:T(8,128)}, u32[]{:S(2)}) copy-start(f32[60,6,128]{2,1,0:T(8,128)} %copy.292) | copy-start | bytes 552964
  51.3 1.1 %copy-start.7 = (f32[3,13,35,128,1]{3,2,1,0,4:T(8,128)S(1)}, f32[3,13,35,128,1]{3,2,1,0,4:T(8,128)}, u32[]{:S(2)}) copy-start(f32[3,13,35,128,1]{3,2,1,0,4:T(8,128)} %maximum_bitcast_fusion.3) | copy-start | bytes 2096644
  52.4 1.1 %copy-start.17 = (f32[6,35,128]{2,0,1:T(8,128)S(1)}, f32[6,35,128]{2,0,1:T(8,128)}, u32[]{:S(2)}) copy-start(f32[6,35,128]{2,0,1:T(8,128)} %fusion.3) | copy-start | bytes 322564
  53.7 4.9 %collective-permute-start.4 = (f32[6,35,64]{2,1,0:T(8,128)S(1)}, f32[6,35,64]{2,1,0:T(8,128)S(1)}, u32[]{:S(2)}, u32[]{:S(2)}) collective-permute-start(f32[6,35,64]{2,1,0:T(8,128)S(1)} %slice_select_fusion.1), channel_id=1, source_target_pairs={{0,16},{8,24},{16,0},{24,8},{1,17},{9,25},{17,1},{25,9},{2,18},{10... | collective-permute-start | bytes 161288 | tf_op jit(solution)/shard_map/ppermute | solution.py:161
  58.9 1.4 %collective-permute-start.5 = (f32[6,35,32]{2,1,0:T(8,128)S(1)}, f32[6,35,32]{2,1,0:T(8,128)S(1)}, u32[]{:S(2)}, u32[]{:S(2)}) collective-permute-start(f32[6,35,32]{2,1,0:T(8,128)S(1)} %slice_select_fusion), channel_id=1, source_target_pairs={{0,8},{8,0},{16,24},{24,16},{1,9},{9,1},{17,25},{25,17},{2,10},{10... | collective-permute-start | bytes 80648 | tf_op jit(solution)/shard_map/ppermute | solution.py:161
  61.4 12.8 %all-to-all-start = ((f32[32,1,60]{2,1,0:T(1,128)}), f32[32,1,60]{2,1,0:T(1,128)S(1)}, u32[]{:S(2)}, u32[]{:S(2)}) async-start(f32[32,1,60]{2,1,0:T(1,128)} %broadcast_in_dim.16), calls=%async_computation | async-start | bytes 32768 | tf_op jit(solution)/shard_map/all_to_all | solution.py:301

commit v17 on v16

--- a/solution.py
+++ b/solution.py
@@ -151,9 +151,13 @@
 
 def halving_sum(values, axis, count):
     position = lax.axis_index(axis)
-    work = values
-    bit = count // 2
-    while bit >= 1:
+    bits = count.bit_length() - 1
+    order = [int(format(chunk, "0%db" % bits)[::-1] or "0", 2) for chunk in range(count)]
+    width = values.shape[-1] // count
+    work = values.reshape(values.shape[:-1] + (count, width))[..., order, :]
+    work = work.reshape(values.shape)
+    bit = 1
+    while bit < count:
         width = work.shape[-1] // 2
         upper = (position & bit) != 0
         low = work[..., :width]
@@ -162,7 +166,7 @@
             jnp.where(upper, low, high), axis, [(i, i ^ bit) for i in range(count)]
         )
         work = jnp.where(upper, high, low) + sent
-        bit //= 2
+        bit *= 2
     return work
 
 

time: 76.2 us -> 77.5 us (1.017)
  transfers between devices with their start and end apart: 7 -> 7, of which waited for: 4 -> 4; matrix products, arithmetic and copies ran while one was open for 22% -> 21% of each run, Pallas kernels for 0% -> 0%
where the time goes in v17:
time: 77.5 us; the launch traced here: 76.9 us
  starting transfers between devices  20.6 us (27%)
  matrix products  17 us (22%)
  local copies, waits for them, and re-layouts  16.5 us (21%)
  waiting for transfers between devices  11.7 us (15%)
  other arithmetic  9.41 us (12%)
  between operations  1.66 us (2%)
    ppermute x2, starting transfers between devices, padded(): before = lax.ppermute(last, axis, up)  10.5 us
    unnamed x96, local copies, waits for them, and re-layouts  7.65 us
    all_to_all x1, waiting for transfers between devices, combine_sums(): lax.all_to_all(spread, ('shot', 'mesh'), 0, 0, tiled=False)  6.06 us
    all_to_all x1, starting transfers between devices, combine_sums(): lax.all_to_all(spread, ('shot', 'mesh'), 0, 0, tiled=False)  5.74 us
    ppermute x2, waiting for transfers between devices, halving_sum(): lax.ppermute(jnp.where(upper, low, high), axis, [(i, i ^ bit) for i in ra...  4.66 us
    dot_general x2, matrix products, surface_term(): mixing = jnp.einsum('dpfg,dfnxe->pgnxe', coupling, weighted, precision=MIX)  2.97 us
    dot_general x2, matrix products, kernel_term(): mixing = jnp.einsum('dpfg,dgae->pfae', coupling, spatial, precision=MIX)  2.87 us
    dot_general x1, matrix products, shards(): jnp.einsum('ipae,ej->ipaj', jnp.concatenate([history_steps, history_chang...  2.75 us
  transfers between devices with their start and end apart: 7, of which 4 were waited for; matrix products, arithmetic and copies ran while one was open for 21% of the time, Pallas kernels for 0%

profile of v17, /device:TPU:0, one launch (start us, length us, event | category | flops | bytes accessed | tf_op | source)
XLA Modules:
  0.0 76.9 jit_solution(13373590220951754177)
XLA Ops:
  0.6 1.0 %copy.324 = f32[1,13,35,128]{3,1,2,0:T(8,128)S(1)} copy(f32[1,13,35,128]{3,0,2,1:T(1,128)} %param.27) | data formatting | bytes 465920
  1.6 1.3 %pad_clamp_fusion = (s32[1024]{0:T(1024)}, s32[1024]{0:T(1024)S(1)}) fusion(s32[4]{0:T(128)} %constant.77, s32[60]{0:T(128)} %constant.74), kind=kLoop, calls=%fused_computation.258 | loop fusion | flops 2048 | bytes 8448 | tf_op jit(solution)/shard_map/gather | solution.py:157
  2.9 0.6 gather_fusion.1
  3.9 0.3 copy-done.42
  4.2 0.3 fusion.38
  4.5 0.7 fusion.149
  5.2 1.3 %collective-permute-start.1 = (f32[13,15,64]{2,1,0:T(8,128)}, f32[13,15,64]{2,1,0:T(8,128)}, u32[]{:S(2)}, u32[]{:S(2)}) collective-permute-start(f32[13,15,64]{2,1,0:T(8,128)} %get-tuple-element.49), channel_id=1, source_target_pairs={{1,0},{2,1},{3,2},{4,3},{5,4},{6,5},{7,6},{9,8},{10,9},{11,10},{12... | collective-permute-start | bytes 149768 | tf_op jit(solution)/shard_map/ppermute | solution.py:22
  6.5 6.2 %collective-permute-start = (f32[13,15,64]{2,1,0:T(8,128)}, f32[13,15,64]{2,1,0:T(8,128)}, u32[]{:S(2)}, u32[]{:S(2)}) collective-permute-start(f32[13,15,64]{2,1,0:T(8,128)} %get-tuple-element.48), channel_id=1, source_target_pairs={{0,1},{1,2},{2,3},{3,4},{4,5},{5,6},{6,7},{8,9},{9,10},{10,11},{11... | collective-permute-start | bytes 149768 | tf_op jit(solution)/shard_map/ppermute | solution.py:21
  12.7 0.2 iota_compare_fusion
  12.9 0.5 fusion.31
  13.4 2.8 %fusion.10 = f32[10,6,35,32]{2,3,1,0:T(8,128)S(1)} fusion(f32[5,6,35,128]{3,2,1,0:T(8,128)S(1)} %copy-done.9, f32[5,6,35,128]{3,2,1,0:T(8,128)} %param.37, s32[32]{0:T(128)S(1)} %iota_add_fusion), kind=kOutput, calls=%fused_computation.28 | convolution fusion | flops 51882496 | bytes 1344128 | tf_op jit(solution)/shard_map/ipae,ej->ipaj/dot_general | solution.py:265
  16.3 0.6 multiply_reduce_fusion.2
  16.9 0.3 copy-done.1
  17.2 0.5 convolution_bitcast_fusion.3
  18.0 0.4 fusion.146
  18.4 0.5 convolution_bitcast_fusion.1
  19.1 0.5 convolution_bitcast_fusion
  19.9 0.8 %copy-done.10 = f32[3,6,13,13]{3,2,1,0:T(8,128)S(1)} copy-done((f32[3,6,13,13]{3,2,1,0:T(8,128)S(1)}, f32[3,6,13,13]{3,2,1,0:T(8,128)}, u32[]{:S(2)}) %copy-start.10) | copy-done | bytes 12192
  20.8 1.7 %fusion.5 = f32[13,35,128]{2,0,1:T(8,128)} fusion(f32[3,13,35,128,1]{3,2,1,0,4:T(8,128)S(1)} %maximum_bitcast_fusion, f32[6,35,128]{2,0,1:T(8,128)S(1)} %copy.206, f32[3,6,13,13]{3,2,1,0:T(8,128)S(1)} %copy-done.10), kind=kOutput, calls=%fused_computation.18 | convolution fusion | flops 82409600 | bytes 1051528 | tf_op jit(solution)/shard_map/dpfg,dfae->pgae/dot_general | solution.py:133
  22.5 1.0 %maximum_bitcast_fusion.2 = f32[3,13,35,128,1]{3,2,1,0,4:T(8,128)} fusion(f32[1,13,35,128]{3,2,1,0:T(8,128)S(1)} %get-tuple-element.35, f32[1,13,35,128]{3,2,1,0:T(8,128)S(1)} %get-tuple-element.34, f32[1,13,35,128]{3,2,1,0:T(8,128)S(1)} %get-tuple-element.33), kind=kLoop, calls=%fused_computation.55 | loop fusion | flops 349440 | bytes 1397760 | tf_op jit(solution)/shard_map/stack | solution.py:128
  23.5 0.3 multiply_add_fusion
  23.8 1.0 %maximum_bitcast_fusion.3 = f32[3,13,35,128,1]{3,2,1,0,4:T(8,128)} fusion(f32[1,13,35,128]{3,2,1,0:T(8,128)S(1)} %get-tuple-element.32, f32[1,13,35,128]{3,2,1,0:T(8,128)S(1)} %get-tuple-element.31, f32[1,13,35,128]{3,2,1,0:T(8,128)S(1)} %get-tuple-element.30), kind=kLoop, calls=%fused_computation.56 | loop fusion | flops 349440 | bytes 1397760 | tf_op jit(solution)/shard_map/stack | solution.py:128
  24.8 0.8 %gather_fusion = f32[60,6,128]{2,0,1:T(8,128)S(1)} fusion(f32[6,35,128]{2,1,0:T(8,128)S(1)} %copy-done, s32[1024]{0:T(1024)S(1)} %get-tuple-element.66), kind=kCustom, calls=%fused_computation | custom fusion | bytes 368880 | tf_op jit(solution)/shard_map/gather | solution.py:236
  25.6 0.8 %copy.265 = f32[60,6,128]{2,1,0:T(8,128)} copy(f32[60,6,128]{2,0,1:T(8,128)S(1)} %gather_fusion) | data formatting | bytes 368640 | tf_op jit(solution)/shard_map/gather | solution.py:236
  26.5 1.1 %pad_maximum_fusion = f32[13,15,256]{2,1,0:T(8,128)S(1)} fusion(f32[13,15,64]{2,1,0:T(8,128)} %collective-permute-done.1, f32[13,15,128]{2,1,0:T(8,128)S(1)} %fusion.38, f32[13,15,64]{2,1,0:T(8,128)} %collective-permute-done), kind=kLoop, calls=%fused_computation.92 | loop fusion | flops 99840 | bytes 399360 | tf_op jit(solution)/shard_map/concatenate | solution.py:23
  27.6 0.3 convolution_add_fusion.3
  27.9 0.3 convolution_add_fusion.2
  28.2 0.6 multiply_reduce_fusion.1
  29.1 0.8 %copy-done.11 = f32[3,6,13,13]{3,2,1,0:T(8,128)S(1)} copy-done((f32[3,6,13,13]{3,2,1,0:T(8,128)S(1)}, f32[3,6,13,13]{3,2,1,0:T(8,128)}, u32[]{:S(2)}) %copy-start.11) | copy-done | bytes 12192
  30.0 1.5 %fusion.1 = f32[13,15,4,128]{3,0,2,1:T(8,128)S(1)} fusion(f32[6,15,4,128]{3,0,2,1:T(8,128)S(1)} %bitcast.798, f32[13,15,4,128]{3,0,2,1:T(8,128)S(1)} %copy_subtract_fusion.1, f32[3,4,128]{2,0,1:T(4,128)S(1)} %copy.210, f32[3,6,13,13]{3,2,1,0:T(8,128)S(1)} %copy-done.11), kind=kOutput, calls=%fused_computation.10 | convolution fusion | flops 141573120 | bytes 1001352 | tf_op jit(solution)/shard_map/dpfg,dfnxe->pgnxe/dot_general | solution.py:145
  31.6 0.9 %copy-done.4 = f32[13,35,128]{2,0,1:T(8,128)S(1)} copy-done((f32[13,35,128]{2,0,1:T(8,128)S(1)}, f32[13,35,128]{2,0,1:T(8,128)}, u32[]{:S(2)}) %copy-start.4) | copy-done | bytes 232984
  32.4 0.6 fusion.16
  33.1 0.6 gather_fusion.2
  33.7 0.9 %copy.221 = f32[13,15,4,128]{3,2,1,0:T(4,128)} copy(f32[13,15,4,128]{3,0,2,1:T(8,128)S(1)} %bitcast.778) | data formatting | bytes 798720 | tf_op jit(solution)/shard_map/gather | solution.py:277
  34.7 1.2 %reshape.380 = f32[13,15,512]{2,1,0:T(8,128)S(1)} reshape(f32[13,15,4,128]{3,2,1,0:T(4,128)} %copy.221) | data formatting | bytes 798720 | tf_op jit(solution)/shard_map/reshape | solution.py:278
  35.9 0.5 fusion.30
  36.4 0.3 fusion.36
  36.7 0.5 convolution_bitcast_fusion.2
  37.3 4.3 %collective-permute-start.2 = (f32[13,15,64]{2,1,0:T(8,128)S(1)}, f32[13,15,64]{2,1,0:T(8,128)S(1)}, u32[]{:S(2)}, u32[]{:S(2)}) collective-permute-start(f32[13,15,64]{2,1,0:T(8,128)S(1)} %get-tuple-element.47), channel_id=1, source_target_pairs={{0,1},{1,2},{2,3},{3,4},{4,5},{5,6},{6,7},{8,9},{9,10},{10,11},{11... | collective-permute-start | bytes 149768 | tf_op jit(solution)/shard_map/ppermute | solution.py:21
  41.7 1.5 %collective-permute-start.3 = (f32[13,15,64]{2,1,0:T(8,128)S(1)}, f32[13,15,64]{2,1,0:T(8,128)S(1)}, u32[]{:S(2)}, u32[]{:S(2)}) collective-permute-start(f32[13,15,64]{2,1,0:T(8,128)S(1)} %get-tuple-element.46), channel_id=1, source_target_pairs={{1,0},{2,1},{3,2},{4,3},{5,4},{6,5},{7,6},{9,8},{10,9},{11,10},{12... | collective-permute-start | bytes 149768 | tf_op jit(solution)/shard_map/ppermute | solution.py:22
  43.4 1.8 %fusion.3 = f32[6,35,128]{2,0,1:T(8,128)} fusion(f32[3,13,35,128,1]{3,2,1,0,4:T(8,128)S(1)} %copy-done.8, f32[13,35,128]{2,0,1:T(8,128)S(1)} %copy.220, f32[3,6,13,13]{3,2,1,0:T(8,128)S(1)} %copy-done.12), kind=kOutput, calls=%fused_computation.14 | convolution fusion | flops 82440960 | bytes 1051528 | tf_op jit(solution)/shard_map/dpfg,dgae->pfae/dot_general | solution.py:139
  45.2 0.8 %copy-done.3 = f32[6,35,128]{2,0,1:T(8,128)S(1)} copy-done((f32[6,35,128]{2,0,1:T(8,128)S(1)}, f32[6,35,128]{2,0,1:T(8,128)}, u32[]{:S(2)}) %copy-start.3) | copy-done | bytes 107544
  46.1 0.9 %fusion.4 = f32[13,35,128]{2,0,1:T(8,128)S(1)} fusion(f32[3,13,35,128,1]{3,2,1,0,4:T(8,128)S(1)} %maximum_bitcast_fusion.1, f32[6,35,128]{2,0,1:T(8,128)S(1)} %copy-done.3, f32[3,6,13,13]{3,2,1,0:T(8,128)S(1)} %copy-done.12), kind=kOutput, calls=%fused_computation.16 | convolution fusion | flops 82409600 | bytes 1051528 | tf_op jit(solution)/shard_map/dpfg,dfae->pgae/dot_general | solution.py:133
  47.0 0.3 convolution_add_fusion.1
  47.3 1.0 %collective-permute-done.3 = f32[13,15,64]{2,1,0:T(8,128)S(1)} collective-permute-done((f32[13,15,64]{2,1,0:T(8,128)S(1)}, f32[13,15,64]{2,1,0:T(8,128)S(1)}, u32[]{:S(2)}, u32[]{:S(2)}) %collective-permute-start.3) | collective-permute-done | bytes 49952 | tf_op jit(solution)/shard_map/ppermute | solution.py:22
  48.3 0.3 convolution_add_fusion
  48.6 0.6 multiply_reduce_fusion
  49.4 0.8 %copy-done.13 = f32[3,6,13,13]{3,2,1,0:T(8,128)S(1)} copy-done((f32[3,6,13,13]{3,2,1,0:T(8,128)S(1)}, f32[3,6,13,13]{3,2,1,0:T(8,128)}, u32[]{:S(2)}) %copy-start.13) | copy-done | bytes 12192
  50.4 1.5 %fusion = f32[13,15,4,128]{3,0,2,1:T(8,128)S(1)} fusion(f32[6,15,4,128]{3,0,2,1:T(8,128)S(1)} %bitcast.799, f32[13,15,4,128]{3,0,2,1:T(8,128)S(1)} %copy_subtract_fusion, f32[3,4,128]{2,0,1:T(4,128)S(1)} %copy.210, f32[3,6,13,13]{3,2,1,0:T(8,128)S(1)} %copy-done.13), kind=kOutput, calls=%fused_computation.8 | convolution fusion | flops 141573120 | bytes 1001352 | tf_op jit(solution)/shard_map/dpfg,dfnxe->pgnxe/dot_general | solution.py:145
  51.9 0.6 fusion.19
  52.6 0.5 copy-done.7
  53.1 1.1 %fusion.2 = f32[6,35,128]{2,0,1:T(8,128)S(1)} fusion(f32[3,13,35,128,1]{3,2,1,0,4:T(8,128)S(1)} %copy-done.7, f32[13,35,128]{2,0,1:T(8,128)S(1)} %copy.233, f32[3,6,13,13]{3,2,1,0:T(8,128)S(1)} %copy-done.13), kind=kOutput, calls=%fused_computation.12 | convolution fusion | flops 82440960 | bytes 1051528 | tf_op jit(solution)/shard_map/dpfg,dgae->pfae/dot_general | solution.py:139
  54.2 0.2 copy.280
  54.4 0.7 gather_fusion.3
  55.3 1.4 %collective-permute-done.4 = f32[6,35,64]{1,2,0:T(8,128)S(1)} collective-permute-done((f32[6,35,64]{1,2,0:T(8,128)S(1)}, f32[6,35,64]{1,2,0:T(8,128)S(1)}, u32[]{:S(2)}, u32[]{:S(2)}) %collective-permute-start.4) | collective-permute-done | bytes 53792 | tf_op jit(solution)/shard_map/ppermute | solution.py:165
  56.8 1.6 %collective-permute-start.5 = (f32[6,35,32]{1,2,0:T(8,128)S(1)}, f32[6,35,32]{1,2,0:T(8,128)S(1)}, u32[]{:S(2)}, u32[]{:S(2)}) collective-permute-start(f32[6,35,32]{1,2,0:T(8,128)S(1)} %slice_select_fusion.1), channel_id=1, source_target_pairs={{0,16},{8,24},{16,0},{24,8},{1,17},{9,25},{17,1},{25,9},{2,18},{10... | collective-permute-start | bytes 80648 | tf_op jit(solution)/shard_map/ppermute | solution.py:165
  58.4 3.2 %collective-permute-done.5 = f32[6,35,32]{1,2,0:T(8,128)S(1)} collective-permute-done((f32[6,35,32]{1,2,0:T(8,128)S(1)}, f32[6,35,32]{1,2,0:T(8,128)S(1)}, u32[]{:S(2)}, u32[]{:S(2)}) %collective-permute-start.5) | collective-permute-done | bytes 26912 | tf_op jit(solution)/shard_map/ppermute | solution.py:165
  61.7 0.2 fusion.21
  62.0 0.6 broadcast_in_dim.19
  62.6 5.7 %all-to-all-start = ((f32[32,1,60]{2,1,0:T(1,128)}), f32[32,1,60]{2,1,0:T(1,128)S(1)}, u32[]{:S(2)}, u32[]{:S(2)}) async-start(f32[32,1,60]{2,1,0:T(1,128)} %broadcast_in_dim.19), calls=%async_computation | async-start | bytes 32768 | tf_op jit(solution)/shard_map/all_to_all | solution.py:305
  68.5 0.9 %copy.239 = f32[1,13,35,128]{3,0,2,1:T(1,128)} copy(f32[1,13,35,128]{3,2,1,0:T(8,128)S(1)} %bitcast.782) | data formatting | bytes 465920
  69.4 6.1 %all-to-all-done = f32[32,1,60]{2,1,0:T(1,128)S(1)} async-done(((f32[32,1,60]{2,1,0:T(1,128)}), f32[32,1,60]{2,1,0:T(1,128)S(1)}, u32[]{:S(2)}, u32[]{:S(2)}) %all-to-all-start) | async-done | bytes 7712 | tf_op jit(solution)/shard_map/all_to_all | solution.py:305
  76.1 0.2 fusion.20
  76.3 0.6 neg.22
  (137 shorter events, 3.6 us)
Async XLA Ops:
  3.5 0.7 copy-start.42
  3.7 9.0 %copy-start.44 = (s32[4,128]{1,0:T(4,128)S(1)}, s32[4,128]{1,0:T(4,128)}, u32[]{:S(2)}) copy-start(s32[4,128]{1,0:T(4,128)} %param.35) | copy-start | bytes 6148
  3.7 9.0 %copy-start.41 = (s32[4,128]{1,0:T(4,128)S(1)}, s32[4,128]{1,0:T(4,128)}, u32[]{:S(2)}) copy-start(s32[4,128]{1,0:T(4,128)} %param.34) | copy-start | bytes 6148
  4.5 8.9 %copy-start.9 = (f32[5,6,35,128]{3,2,1,0:T(8,128)S(1)}, f32[5,6,35,128]{3,2,1,0:T(8,128)}, u32[]{:S(2)}) copy-start(f32[5,6,35,128]{3,2,1,0:T(8,128)} %param.38) | copy-start | bytes 1612804
  5.2 21.3 %collective-permute-start.1 = (f32[13,15,64]{2,1,0:T(8,128)}, f32[13,15,64]{2,1,0:T(8,128)}, u32[]{:S(2)}, u32[]{:S(2)}) collective-permute-start(f32[13,15,64]{2,1,0:T(8,128)} %get-tuple-element.49), channel_id=1, source_target_pairs={{1,0},{2,1},{3,2},{4,3},{5,4},{6,5},{7,6},{9,8},{10,9},{11,10},{12... | collective-permute-start | bytes 149768 | tf_op jit(solution)/shard_map/ppermute | solution.py:22
  6.5 20.0 %collective-permute-start = (f32[13,15,64]{2,1,0:T(8,128)}, f32[13,15,64]{2,1,0:T(8,128)}, u32[]{:S(2)}, u32[]{:S(2)}) collective-permute-start(f32[13,15,64]{2,1,0:T(8,128)} %get-tuple-element.48), channel_id=1, source_target_pairs={{0,1},{1,2},{2,3},{3,4},{4,5},{5,6},{6,7},{8,9},{9,10},{10,11},{11... | collective-permute-start | bytes 149768 | tf_op jit(solution)/shard_map/ppermute | solution.py:21
  16.2 0.7 copy-start.45
  16.3 0.9 %copy-start.1 = (f32[1,13,35,128]{3,0,2,1:T(1,128)S(1)}, f32[1,13,35,128]{3,0,2,1:T(1,128)}, u32[]{:S(2)}) copy-start(f32[1,13,35,128]{3,0,2,1:T(1,128)} %param.27) | copy-start | bytes 698884
  16.3 0.9 %copy-start.5 = (f32[3,35,35,1]{2,1,3,0:T(8,128)S(1)}, f32[3,35,35,1]{2,1,3,0:T(8,128)}, u32[]{:S(2)}) copy-start(f32[3,35,35,1]{2,1,3,0:T(8,128)} %constant.78) | copy-start | bytes 44104
  16.3 1.4 %copy-start.40 = (f32[3,3,128]{2,1,0:T(4,128)S(1)}, f32[3,3,128]{2,1,0:T(4,128)}, u32[]{:S(2)}) copy-start(f32[3,3,128]{2,1,0:T(4,128)} %param.31) | copy-start | bytes 13828
  16.3 1.4 %copy-start = (f32[6,35,128]{2,1,0:T(8,128)S(1)}, f32[6,35,128]{2,1,0:T(8,128)}, u32[]{:S(2)}) copy-start(f32[6,35,128]{2,1,0:T(8,128)} %param.29) | copy-start | bytes 322564
  16.9 1.1 %copy-start.14 = (f32[1,2,13,35,128]{4,1,3,2,0:T(2,128)S(1)}, f32[1,2,13,35,128]{4,1,3,2,0:T(2,128)}, u32[]{:S(2)}) copy-start(f32[1,2,13,35,128]{4,1,3,2,0:T(2,128)} %param.28) | copy-start | bytes 1397764
  17.7 1.9 %copy-start.19 = (f32[128]{0:T(128)}, f32[128]{0:T(128)S(1)}, u32[]{:S(2)}) copy-start(f32[128]{0:T(128)S(1)} %get-tuple-element.52) | copy-start | bytes 1540
  17.7 1.9 %copy-start.21 = (f32[128]{0:T(128)}, f32[128]{0:T(128)S(1)}, u32[]{:S(2)}) copy-start(f32[128]{0:T(128)S(1)} %get-tuple-element.53) | copy-start | bytes 1540
  17.7 1.9 %copy-start.23 = (f32[128]{0:T(128)}, f32[128]{0:T(128)S(1)}, u32[]{:S(2)}) copy-start(f32[128]{0:T(128)S(1)} %get-tuple-element.54) | copy-start | bytes 1540
  17.8 1.9 %copy-start.25 = (f32[128]{0:T(128)}, f32[128]{0:T(128)S(1)}, u32[]{:S(2)}) copy-start(f32[128]{0:T(128)S(1)} %get-tuple-element.55) | copy-start | bytes 1540
  17.8 1.9 %copy-start.27 = (f32[128]{0:T(128)}, f32[128]{0:T(128)S(1)}, u32[]{:S(2)}) copy-start(f32[128]{0:T(128)S(1)} %get-tuple-element.56) | copy-start | bytes 1540
  17.8 1.9 %copy-start.29 = (f32[128]{0:T(128)}, f32[128]{0:T(128)S(1)}, u32[]{:S(2)}) copy-start(f32[128]{0:T(128)S(1)} %get-tuple-element.57) | copy-start | bytes 1540
  17.8 1.9 %copy-start.31 = (f32[128]{0:T(128)}, f32[128]{0:T(128)S(1)}, u32[]{:S(2)}) copy-start(f32[128]{0:T(128)S(1)} %get-tuple-element.58) | copy-start | bytes 1540
  18.0 1.9 %copy-start.2 = (f32[6,35,128]{2,0,1:T(8,128)}, f32[6,35,128]{2,0,1:T(8,128)S(1)}, u32[]{:S(2)}) copy-start(f32[6,35,128]{2,0,1:T(8,128)S(1)} %copy.206) | copy-start | bytes 322564
  19.8 0.9 %copy-start.10 = (f32[3,6,13,13]{3,2,1,0:T(8,128)S(1)}, f32[3,6,13,13]{3,2,1,0:T(8,128)}, u32[]{:S(2)}) copy-start(f32[3,6,13,13]{3,2,1,0:T(8,128)} %param.30) | copy-start | bytes 36508
  22.4 1.1 %copy-start.33 = (f32[15,15]{1,0:T(8,128)S(1)}, f32[15,15]{1,0:T(8,128)}, u32[]{:S(2)}) copy-start(f32[15,15]{1,0:T(8,128)} %constant.65.clone) | copy-start | bytes 2704
  22.4 1.1 %copy-start.34 = (f32[15,15]{1,0:T(8,128)S(1)}, f32[15,15]{1,0:T(8,128)}, u32[]{:S(2)}) copy-start(f32[15,15]{1,0:T(8,128)} %constant.64.clone) | copy-start | bytes 2704
  22.4 1.1 %copy-start.35 = (f32[15,15]{1,0:T(8,128)S(1)}, f32[15,15]{1,0:T(8,128)}, u32[]{:S(2)}) copy-start(f32[15,15]{1,0:T(8,128)} %constant.63.clone) | copy-start | bytes 2704
  22.4 1.1 %copy-start.36 = (f32[15,15]{1,0:T(8,128)S(1)}, f32[15,15]{1,0:T(8,128)}, u32[]{:S(2)}) copy-start(f32[15,15]{1,0:T(8,128)} %constant.62.clone) | copy-start | bytes 2704
  22.5 1.1 %copy-start.37 = (f32[15,15]{1,0:T(8,128)S(1)}, f32[15,15]{1,0:T(8,128)}, u32[]{:S(2)}) copy-start(f32[15,15]{1,0:T(8,128)} %constant.22.clone) | copy-start | bytes 2704
  22.5 1.1 %copy-start.38 = (f32[15,15]{1,0:T(8,128)S(1)}, f32[15,15]{1,0:T(8,128)}, u32[]{:S(2)}) copy-start(f32[15,15]{1,0:T(8,128)} %constant.21.clone) | copy-start | bytes 2704
  24.8 1.7 %copy-start.39 = (f32[3,4,128]{2,1,0:T(4,128)S(1)}, f32[3,4,128]{2,1,0:T(4,128)}, u32[]{:S(2)}) copy-start(f32[3,4,128]{2,1,0:T(4,128)} %param.32) | copy-start | bytes 18436
  29.0 0.9 %copy-start.11 = (f32[3,6,13,13]{3,2,1,0:T(8,128)S(1)}, f32[3,6,13,13]{3,2,1,0:T(8,128)}, u32[]{:S(2)}) copy-start(f32[3,6,13,13]{3,2,1,0:T(8,128)} %param.30) | copy-start | bytes 36508
  29.0 1.0 %copy-start.15 = (f32[60,6,128]{2,1,0:T(8,128)S(1)}, f32[60,6,128]{2,1,0:T(8,128)}, u32[]{:S(2)}) copy-start(f32[60,6,128]{2,1,0:T(8,128)} %copy.265) | copy-start | bytes 552964
  31.5 1.0 %copy-start.4 = (f32[13,35,128]{2,0,1:T(8,128)S(1)}, f32[13,35,128]{2,0,1:T(8,128)}, u32[]{:S(2)}) copy-start(f32[13,35,128]{2,0,1:T(8,128)} %fusion.5) | copy-start | bytes 698884
  31.5 1.0 %copy-start.18 = (f32[4,35,15,1]{1,2,0,3:T(8,128)S(1)}, f32[4,35,15,1]{1,2,0,3:T(8,128)}, u32[]{:S(2)}) copy-start(f32[4,35,15,1]{1,2,0,3:T(8,128)} %constant.79) | copy-start | bytes 25204
  34.7 1.7 %copy-start.43 = (s32[128]{0:T(128)S(1)}, s32[128]{0:T(128)}, u32[]{:S(2)}) copy-start(s32[128]{0:T(128)} %param.36) | copy-start | bytes 1540
  35.8 0.9 %copy-start.6 = (f32[3,35,35,1]{2,1,3,0:T(8,128)S(1)}, f32[3,35,35,1]{2,1,3,0:T(8,128)}, u32[]{:S(2)}) copy-start(f32[3,35,35,1]{2,1,3,0:T(8,128)} %constant.78) | copy-start | bytes 44104
  36.3 6.8 %copy-start.20 = (f32[128]{0:T(128)S(1)}, f32[128]{0:T(128)}, u32[]{:S(2)}) copy-start(f32[128]{0:T(128)} %copy-done.19) | copy-start | bytes 1540
  36.4 6.8 %copy-start.22 = (f32[128]{0:T(128)S(1)}, f32[128]{0:T(128)}, u32[]{:S(2)}) copy-start(f32[128]{0:T(128)} %copy-done.21) | copy-start | bytes 1540
  36.4 6.8 %copy-start.24 = (f32[128]{0:T(128)S(1)}, f32[128]{0:T(128)}, u32[]{:S(2)}) copy-start(f32[128]{0:T(128)} %copy-done.23) | copy-start | bytes 1540
  36.4 6.8 %copy-start.26 = (f32[128]{0:T(128)S(1)}, f32[128]{0:T(128)}, u32[]{:S(2)}) copy-start(f32[128]{0:T(128)} %copy-done.25) | copy-start | bytes 1540
  36.4 6.8 %copy-start.28 = (f32[128]{0:T(128)S(1)}, f32[128]{0:T(128)}, u32[]{:S(2)}) copy-start(f32[128]{0:T(128)} %copy-done.27) | copy-start | bytes 1540
  36.4 6.8 %copy-start.30 = (f32[128]{0:T(128)S(1)}, f32[128]{0:T(128)}, u32[]{:S(2)}) copy-start(f32[128]{0:T(128)} %copy-done.29) | copy-start | bytes 1540
  36.4 6.8 %copy-start.32 = (f32[128]{0:T(128)S(1)}, f32[128]{0:T(128)}, u32[]{:S(2)}) copy-start(f32[128]{0:T(128)} %copy-done.31) | copy-start | bytes 1540
  37.2 6.2 %copy-start.8 = (f32[3,13,35,128,1]{3,2,1,0,4:T(8,128)S(1)}, f32[3,13,35,128,1]{3,2,1,0,4:T(8,128)}, u32[]{:S(2)}) copy-start(f32[3,13,35,128,1]{3,2,1,0,4:T(8,128)} %maximum_bitcast_fusion.2) | copy-start | bytes 2096644
  37.2 6.2 %copy-start.12 = (f32[3,6,13,13]{3,2,1,0:T(8,128)S(1)}, f32[3,6,13,13]{3,2,1,0:T(8,128)}, u32[]{:S(2)}) copy-start(f32[3,6,13,13]{3,2,1,0:T(8,128)} %param.30) | copy-start | bytes 36508
  37.3 9.7 %collective-permute-start.2 = (f32[13,15,64]{2,1,0:T(8,128)S(1)}, f32[13,15,64]{2,1,0:T(8,128)S(1)}, u32[]{:S(2)}, u32[]{:S(2)}) collective-permute-start(f32[13,15,64]{2,1,0:T(8,128)S(1)} %get-tuple-element.47), channel_id=1, source_target_pairs={{0,1},{1,2},{2,3},{3,4},{4,5},{5,6},{6,7},{8,9},{9,10},{10,11},{11... | collective-permute-start | bytes 149768 | tf_op jit(solution)/shard_map/ppermute | solution.py:21
  41.7 6.6 %collective-permute-start.3 = (f32[13,15,64]{2,1,0:T(8,128)S(1)}, f32[13,15,64]{2,1,0:T(8,128)S(1)}, u32[]{:S(2)}, u32[]{:S(2)}) collective-permute-start(f32[13,15,64]{2,1,0:T(8,128)S(1)} %get-tuple-element.46), channel_id=1, source_target_pairs={{1,0},{2,1},{3,2},{4,3},{5,4},{6,5},{7,6},{9,8},{10,9},{11,10},{12... | collective-permute-start | bytes 149768 | tf_op jit(solution)/shard_map/ppermute | solution.py:22
  45.2 0.9 %copy-start.3 = (f32[6,35,128]{2,0,1:T(8,128)S(1)}, f32[6,35,128]{2,0,1:T(8,128)}, u32[]{:S(2)}) copy-start(f32[6,35,128]{2,0,1:T(8,128)} %copy-done.2) | copy-start | bytes 322564
  49.3 0.9 %copy-start.13 = (f32[3,6,13,13]{3,2,1,0:T(8,128)S(1)}, f32[3,6,13,13]{3,2,1,0:T(8,128)}, u32[]{:S(2)}) copy-start(f32[3,6,13,13]{3,2,1,0:T(8,128)} %param.30) | copy-start | bytes 36508
  49.4 1.0 %copy-start.16 = (f32[60,6,128]{2,1,0:T(8,128)S(1)}, f32[60,6,128]{2,1,0:T(8,128)}, u32[]{:S(2)}) copy-start(f32[60,6,128]{2,1,0:T(8,128)} %copy.265) | copy-start | bytes 552964
  51.9 1.1 %copy-start.7 = (f32[3,13,35,128,1]{3,2,1,0,4:T(8,128)S(1)}, f32[3,13,35,128,1]{3,2,1,0,4:T(8,128)}, u32[]{:S(2)}) copy-start(f32[3,13,35,128,1]{3,2,1,0,4:T(8,128)} %maximum_bitcast_fusion.3) | copy-start | bytes 2096644
  53.1 1.1 %copy-start.17 = (f32[6,35,128]{2,0,1:T(8,128)S(1)}, f32[6,35,128]{2,0,1:T(8,128)}, u32[]{:S(2)}) copy-start(f32[6,35,128]{2,0,1:T(8,128)} %fusion.3) | copy-start | bytes 322564
  55.2 1.5 %collective-permute-start.4 = (f32[6,35,64]{1,2,0:T(8,128)S(1)}, f32[6,35,64]{1,2,0:T(8,128)S(1)}, u32[]{:S(2)}, u32[]{:S(2)}) collective-permute-start(f32[6,35,64]{1,2,0:T(8,128)S(1)} %slice_select_fusion), channel_id=1, source_target_pairs={{0,8},{8,0},{16,24},{24,16},{1,9},{9,1},{17,25},{25,17},{2,10},{10... | collective-permute-start | bytes 161288 | tf_op jit(solution)/shard_map/ppermute | solution.py:165
  56.8 4.9 %collective-permute-start.5 = (f32[6,35,32]{1,2,0:T(8,128)S(1)}, f32[6,35,32]{1,2,0:T(8,128)S(1)}, u32[]{:S(2)}, u32[]{:S(2)}) collective-permute-start(f32[6,35,32]{1,2,0:T(8,128)S(1)} %slice_select_fusion.1), channel_id=1, source_target_pairs={{0,16},{8,24},{16,0},{24,8},{1,17},{9,25},{17,1},{25,9},{2,18},{10... | collective-permute-start | bytes 80648 | tf_op jit(solution)/shard_map/ppermute | solution.py:165
  62.6 12.8 %all-to-all-start = ((f32[32,1,60]{2,1,0:T(1,128)}), f32[32,1,60]{2,1,0:T(1,128)S(1)}, u32[]{:S(2)}, u32[]{:S(2)}) async-start(f32[32,1,60]{2,1,0:T(1,128)} %broadcast_in_dim.19), calls=%async_computation | async-start | bytes 32768 | tf_op jit(solution)/shard_map/all_to_all | solution.py:305

commit v18 on v16

--- a/solution.py
+++ b/solution.py
@@ -119,13 +119,8 @@
 
 def spatial_of(field, metric, derivs):
     reference_grads = jnp.einsum("rab,fbe->rfae", derivs, field, precision=MIX)
-    rows = []
-    for direction_axis in range(3):
-        total = metric[0, direction_axis] * reference_grads[0]
-        total = total + metric[1, direction_axis] * reference_grads[1]
-        total = total + metric[2, direction_axis] * reference_grads[2]
-        rows.append(total)
-    return jnp.stack(rows)
+    weighted = metric[:, :, None, None, :] * reference_grads[:, None]
+    return weighted[0] + weighted[1] + weighted[2]
 
 
 def volume_term(adjoint, material, coupling, metric, derivs):

time: 76.2 us -> 81.5 us (1.070)
  matrix products: 17 us -> 20.8 us
  other arithmetic: 9.07 us -> 11.1 us
  waiting for transfers between devices: 11.5 us -> 10.5 us
    unnamed x96 -> x82, local copies, waits for them, and re-layouts: 7.64 us -> 2.92 us
    mul x0 -> x2, other arithmetic: none -> 2.52 us  [spatial_of(): weighted = metric[:, :, None, None, :] * reference_grads[:, None]]
    transpose x0 -> x4, local copies, waits for them, and re-layouts: none -> 2.49 us  [spatial_of(): reference_grads = jnp.einsum('rab,fbe->rfae', derivs, field, precision=MIX)]
    another operation x4 -> x0, other arithmetic: 2.17 us -> none  [spatial_of(): return jnp.stack(rows)]
    gather x2, local copies, waits for them, and re-layouts: 1.64 us -> 3.37 us  [shards(): face_material = material[:, face_nodes.T, :]]
    dot_general x1, matrix products: 2.75 us -> 1.66 us  [shards(): jnp.einsum('ipae,ej->ipaj', jnp.concatenate([history_steps, history_chang...]
    dot_general x2, matrix products: 2.97 us -> 4.04 us  [surface_term(): mixing = jnp.einsum('dpfg,dfnxe->pgnxe', coupling, weighted, precision=MIX)]
    dot_general x2, matrix products: 0.55 us -> 1.63 us  [shards(): jnp.einsum('fns,sj->fnj', extended[:, :, :border], below_pick, precision=...]
  transfers between devices with their start and end apart: 7 -> 7, of which waited for: 4 -> 3; matrix products, arithmetic and copies ran while one was open for 22% -> 28% of each run, Pallas kernels for 0% -> 0%
where the time goes in v18:
time: 81.5 us; the launch traced here: 81 us
  matrix products  20.8 us (26%)
  starting transfers between devices  20.8 us (26%)
  local copies, waits for them, and re-layouts  16 us (20%)
  other arithmetic  11.1 us (14%)
  waiting for transfers between devices  10.5 us (13%)
  between operations  1.65 us (2%)
    ppermute x2, starting transfers between devices, padded(): before = lax.ppermute(last, axis, up)  10.9 us
    all_to_all x1, waiting for transfers between devices, combine_sums(): lax.all_to_all(spread, ('shot', 'mesh'), 0, 0, tiled=False)  5.95 us
    all_to_all x1, starting transfers between devices, combine_sums(): lax.all_to_all(spread, ('shot', 'mesh'), 0, 0, tiled=False)  5.73 us
    ppermute x2, waiting for transfers between devices, halving_sum(): lax.ppermute(jnp.where(upper, low, high), axis, [(i, i ^ bit) for i in ra...  4.59 us
    dot_general x2, matrix products, surface_term(): mixing = jnp.einsum('dpfg,dfnxe->pgnxe', coupling, weighted, precision=MIX)  4.04 us
    dot_general x2, matrix products, kernel_term(): mixing = jnp.einsum('dpfg,dgae->pfae', coupling, spatial, precision=MIX)  3.92 us
    gather x2, local copies, waits for them, and re-layouts, shards(): face_material = material[:, face_nodes.T, :]  3.37 us
    unnamed x82, local copies, waits for them, and re-layouts  2.92 us
  transfers between devices with their start and end apart: 7, of which 3 were waited for; matrix products, arithmetic and copies ran while one was open for 28% of the time, Pallas kernels for 0%

profile of v18, /device:TPU:0, one launch (start us, length us, event | category | flops | bytes accessed | tf_op | source)
XLA Modules:
  0.0 81.0 jit_solution(514923833354753500)
XLA Ops:
  0.7 0.7 pad_clamp_fusion
  1.4 1.0 %copy.325 = f32[1,13,35,128]{3,1,2,0:T(8,128)S(1)} copy(f32[1,13,35,128]{3,0,2,1:T(1,128)} %param.26) | data formatting | bytes 465920
  2.4 0.6 gather_fusion.1
  3.0 0.2 copy.232
  3.2 0.2 reshape.380
  3.4 0.3 fusion.46
  3.7 0.7 fusion.158
  4.4 5.5 %collective-permute-start = (f32[13,15,64]{2,1,0:T(8,128)}, f32[13,15,64]{2,1,0:T(8,128)}, u32[]{:S(2)}, u32[]{:S(2)}) collective-permute-start(f32[13,15,64]{2,1,0:T(8,128)} %get-tuple-element.38), channel_id=1, source_target_pairs={{0,1},{1,2},{2,3},{3,4},{4,5},{5,6},{6,7},{8,9},{9,10},{10,11},{11... | collective-permute-start | bytes 149768 | tf_op jit(solution)/shard_map/ppermute | solution.py:21
  9.9 1.3 %collective-permute-start.1 = (f32[13,15,64]{2,1,0:T(8,128)}, f32[13,15,64]{2,1,0:T(8,128)}, u32[]{:S(2)}, u32[]{:S(2)}) collective-permute-start(f32[13,15,64]{2,1,0:T(8,128)} %get-tuple-element.39), channel_id=1, source_target_pairs={{1,0},{2,1},{3,2},{4,3},{5,4},{6,5},{7,6},{9,8},{10,9},{11,10},{12... | collective-permute-start | bytes 149768 | tf_op jit(solution)/shard_map/ppermute | solution.py:22
  11.2 0.6 broadcast_multiply_fusion.4
  11.9 0.2 iota_compare_fusion
  12.1 1.3 %fusion.39 = f32[13,15,512]{2,1,0:T(8,128)} fusion(f32[13,15,512]{2,1,0:T(8,128)S(1)} %reshape.380, pred[640,512]{1,0:T(32,128)(4,1)S(1)} %iota_compare_fusion), kind=kOutput, calls=%fused_computation.73 | convolution fusion | flops 306708480 | bytes 1087488 | tf_op jit(solution)/shard_map/fns,sj->fnj/dot_general | solution.py:276
  13.4 0.4 fusion.155
  13.8 0.5 convolution_bitcast_fusion.3
  14.3 0.5 convolution_bitcast_fusion.1
  14.8 1.4 %convolution_bitcast_fusion = f32[3,13,35,128]{3,2,1,0:T(8,128)} fusion(f32[3,35,35,1]{2,1,3,0:T(8,128)S(1)} %copy-done.7, f32[1,1,13,35,128]{4,1,3,2,0:T(1,128)S(1)} %get-tuple-element.33), kind=kOutput, calls=%fused_computation.23 | convolution fusion | flops 36691200 | bytes 946540 | tf_op jit(solution)/shard_map/rab,fbe->rfae/dot_general | solution.py:121
  16.1 0.2 copy.227
  16.3 1.7 %fusion.10 = f32[10,6,35,32]{2,3,1,0:T(8,128)S(1)} fusion(f32[5,6,35,128]{3,2,1,0:T(8,128)S(1)} %copy-done.5, f32[5,6,35,128]{3,2,1,0:T(8,128)S(1)} %copy-done.6, s32[32]{0:T(128)S(1)} %iota_add_fusion), kind=kOutput, calls=%fused_computation.31 | convolution fusion | flops 51882496 | bytes 1344128 | tf_op jit(solution)/shard_map/ipae,ej->ipaj/dot_general | solution.py:256
  18.2 1.2 %multiply_reduce_fusion.2 = f32[10,5]{1,0:T(8,128)} fusion(f32[5,6,35,32]{2,3,1,0:T(8,128)S(1)} %get-tuple-element.8, f32[10,6,35,32]{2,3,1,0:T(8,128)S(1)} %fusion.10), kind=kLoop, calls=%fused_computation.5 | loop fusion | flops 671950 | bytes 403400 | tf_op jit(solution)/shard_map/reduce_sum | solution.py:265
  19.4 0.2 broadcast_multiply_fusion.3
  19.6 0.3 multiply_add_fusion
  19.9 1.7 %fusion.3 = f32[13,35,128]{2,0,1:T(8,128)} fusion(f32[3,3,13,35,128]{4,2,1,3,0:T(8,128)S(1)} %broadcast_multiply_fusion.3, f32[6,35,128]{2,0,1:T(8,128)S(1)} %copy.226, f32[3,6,13,13]{3,2,1,0:T(8,128)S(1)} %copy-done.35), kind=kOutput, calls=%fused_computation.13 | convolution fusion | flops 82759040 | bytes 2449288 | tf_op jit(solution)/shard_map/dpfg,dfae->pgae/dot_general | solution.py:128
  21.6 1.6 %gather_fusion = f32[60,6,128]{2,0,1:T(8,128)} fusion(f32[6,35,128]{2,1,0:T(8,128)S(1)} %copy-done, s32[1024]{0:T(1024)} %copy-done.11), kind=kCustom, calls=%fused_computation | custom fusion | bytes 368880 | tf_op jit(solution)/shard_map/gather | solution.py:227
  23.2 0.8 copy.230
  24.0 1.7 %copy.283 = f32[60,6,128]{2,1,0:T(8,128)} copy(f32[60,6,128]{2,0,1:T(8,128)} %gather_fusion) | data formatting | bytes 368640 | tf_op jit(solution)/shard_map/gather | solution.py:227
  25.7 1.1 %copy.246 = f32[3,13,35,128]{3,1,2,0:T(8,128)} copy(f32[3,13,35,128]{3,2,1,0:T(8,128)S(1)} %convolution_bitcast_fusion.1) | data formatting | bytes 1397760 | tf_op jit(solution)/shard_map/rab,fbe->rfae/transpose | solution.py:121
  26.8 1.1 %copy.250 = f32[3,13,35,128]{3,1,2,0:T(8,128)} copy(f32[3,13,35,128]{3,2,1,0:T(8,128)S(1)} %copy-done.3) | data formatting | bytes 1397760 | tf_op jit(solution)/shard_map/rab,fbe->rfae/transpose | solution.py:121
  27.9 1.1 %pad_maximum_fusion = f32[13,15,256]{2,1,0:T(8,128)S(1)} fusion(f32[13,15,64]{2,1,0:T(8,128)} %collective-permute-done.1, f32[13,15,128]{2,1,0:T(8,128)S(1)} %fusion.46, f32[13,15,64]{2,1,0:T(8,128)} %collective-permute-done), kind=kLoop, calls=%fused_computation.91 | loop fusion | flops 99840 | bytes 399360 | tf_op jit(solution)/shard_map/concatenate | solution.py:23
  29.0 1.3 %convolution_add_fusion.3 = f32[13,15,512]{2,1,0:T(8,128)S(1)} fusion(f32[13,15,512]{2,1,0:T(8,128)} %fusion.39, f32[13,15,256]{2,1,0:T(8,128)S(1)} %pad_maximum_fusion, pred[640,512]{1,0:T(32,128)(4,1)S(1)} %iota_compare_fusion), kind=kOutput, calls=%fused_computation.38 | convolution fusion | flops 38438400 | bytes 937984 | tf_op jit(solution)/shard_map/fns,sj->fnj/dot_general | solution.py:277
  30.4 0.3 convolution_add_fusion.2
  30.7 0.6 multiply_reduce_fusion.1
  31.4 0.9 %reshape.381 = f32[13,15,4,128]{3,2,1,0:T(4,128)} reshape(f32[13,15,512]{2,1,0:T(8,128)S(1)} %multiply_reduce_fusion.1) | data formatting | bytes 798720 | tf_op jit(solution)/shard_map/reshape | solution.py:284
  32.3 1.1 %copy_subtract_fusion.1 = f32[13,15,4,128]{3,0,2,1:T(8,128)S(1)} fusion(f32[13,15,4,128]{3,0,2,1:T(8,128)S(1)} %bitcast.780, f32[13,15,4,128]{3,2,1,0:T(4,128)} %reshape.381), kind=kLoop, calls=%fused_computation.75 | loop fusion | flops 99840 | bytes 1198080 | tf_op jit(solution)/shard_map/sub | solution.py:284
  33.4 1.5 %fusion.1 = f32[13,15,4,128]{3,0,2,1:T(8,128)S(1)} fusion(f32[6,15,4,128]{3,0,2,1:T(8,128)S(1)} %bitcast.798, f32[13,15,4,128]{3,0,2,1:T(8,128)S(1)} %copy_subtract_fusion.1, f32[3,4,128]{2,0,1:T(4,128)S(1)} %copy.230, f32[3,6,13,13]{3,2,1,0:T(8,128)S(1)} %copy-done.36), kind=kOutput, calls=%fused_computation.9 | convolution fusion | flops 141573120 | bytes 1001352 | tf_op jit(solution)/shard_map/dpfg,dfnxe->pgnxe/dot_general | solution.py:140
  35.1 0.6 fusion.16
  35.8 0.6 gather_fusion.2
  36.4 0.9 %copy.240 = f32[13,15,4,128]{3,2,1,0:T(4,128)} copy(f32[13,15,4,128]{3,0,2,1:T(8,128)S(1)} %bitcast.781) | data formatting | bytes 798720 | tf_op jit(solution)/shard_map/gather | solution.py:268
  37.3 1.2 %reshape.382 = f32[13,15,512]{2,1,0:T(8,128)S(1)} reshape(f32[13,15,4,128]{3,2,1,0:T(4,128)} %copy.240) | data formatting | bytes 798720 | tf_op jit(solution)/shard_map/reshape | solution.py:269
  38.5 0.3 fusion.44
  38.8 0.5 fusion.38
  39.4 1.3 %collective-permute-start.3 = (f32[13,15,64]{2,1,0:T(8,128)S(1)}, f32[13,15,64]{2,1,0:T(8,128)S(1)}, u32[]{:S(2)}, u32[]{:S(2)}) collective-permute-start(f32[13,15,64]{2,1,0:T(8,128)S(1)} %get-tuple-element.36), channel_id=1, source_target_pairs={{1,0},{2,1},{3,2},{4,3},{5,4},{6,5},{7,6},{9,8},{10,9},{11,10},{12... | collective-permute-start | bytes 149768 | tf_op jit(solution)/shard_map/ppermute | solution.py:22
  40.7 5.4 %collective-permute-start.2 = (f32[13,15,64]{2,1,0:T(8,128)S(1)}, f32[13,15,64]{2,1,0:T(8,128)S(1)}, u32[]{:S(2)}, u32[]{:S(2)}) collective-permute-start(f32[13,15,64]{2,1,0:T(8,128)S(1)} %get-tuple-element.37), channel_id=1, source_target_pairs={{0,1},{1,2},{2,3},{3,4},{4,5},{5,6},{6,7},{8,9},{9,10},{10,11},{11... | collective-permute-start | bytes 149768 | tf_op jit(solution)/shard_map/ppermute | solution.py:21
  46.1 0.5 convolution_bitcast_fusion.2
  46.5 0.2 copy.237
  46.8 2.3 %broadcast_multiply_fusion.1 = (f32[3,3,13,35,128]{4,2,1,3,0:T(8,128)S(1)}, f32[3,3,13,35,128]{4,2,1,3,0:T(8,128)S(1)}, f32[3,3,13,35,128]{4,2,1,3,0:T(8,128)}) fusion(f32[3,13,35,128]{3,1,2,0:T(8,128)S(1)} %copy-done.1, f32[3,3,128]{2,1,0:T(4,128)S(1)} %copy-done.20, f32[3,13,35,128]{3,1,2,0:T(8,128)S(1)} %copy.237, f32[3,13,35,128]{3,1,2,0:T(8,128)S(1)} %copy-done.2), kind=kLoop, calls=%fused_computation.28 | loop fusion | flops 1572480 | bytes 8391168 | tf_op jit(solution)/shard_map/mul | solution.py:122
  49.1 1.1 %fusion.5 = f32[6,35,128]{2,0,1:T(8,128)S(1)} fusion(f32[3,3,13,35,128]{4,2,1,3,0:T(8,128)S(1)} %get-tuple-element.40, f32[13,35,128]{2,0,1:T(8,128)S(1)} %copy.239, f32[3,6,13,13]{3,2,1,0:T(8,128)S(1)} %copy-done.37), kind=kOutput, calls=%fused_computation.17 | convolution fusion | flops 82790400 | bytes 2449288 | tf_op jit(solution)/shard_map/dpfg,dgae->pfae/dot_general | solution.py:134
  50.2 1.0 %fusion.2 = f32[13,35,128]{2,0,1:T(8,128)S(1)} fusion(f32[3,3,13,35,128]{4,2,1,3,0:T(8,128)S(1)} %get-tuple-element.41, f32[6,35,128]{2,0,1:T(8,128)S(1)} %copy-done.14, f32[3,6,13,13]{3,2,1,0:T(8,128)S(1)} %copy-done.37), kind=kOutput, calls=%fused_computation.11 | convolution fusion | flops 82759040 | bytes 2449288 | tf_op jit(solution)/shard_map/dpfg,dfae->pgae/dot_general | solution.py:128
  51.2 0.3 convolution_add_fusion.1
  51.5 0.3 convolution_add_fusion
  51.8 0.6 multiply_reduce_fusion
  52.7 2.6 %fusion = f32[13,15,4,128]{3,0,2,1:T(8,128)S(1)} fusion(f32[6,15,4,128]{3,0,2,1:T(8,128)} %bitcast.797, f32[13,15,4,128]{3,0,2,1:T(8,128)S(1)} %copy_subtract_fusion, f32[3,4,128]{2,0,1:T(4,128)S(1)} %copy-done.29, f32[3,6,13,13]{3,2,1,0:T(8,128)} %param.29), kind=kOutput, calls=%fused_computation.7 | convolution fusion | flops 141573120 | bytes 1001352 | tf_op jit(solution)/shard_map/dpfg,dfnxe->pgnxe/dot_general | solution.py:140
  55.4 0.6 fusion.19
  56.0 2.8 %fusion.4 = f32[6,35,128]{2,0,1:T(8,128)S(1)} fusion(f32[3,3,13,35,128]{4,2,1,3,0:T(8,128)} %get-tuple-element.42, f32[13,35,128]{2,0,1:T(8,128)S(1)} %copy.252, f32[3,6,13,13]{3,2,1,0:T(8,128)S(1)} %copy-done.38), kind=kOutput, calls=%fused_computation.15 | convolution fusion | flops 82790400 | bytes 2449288 | tf_op jit(solution)/shard_map/dpfg,dgae->pfae/dot_general | solution.py:134
  59.0 1.6 %collective-permute-start.4 = (f32[6,35,64]{2,1,0:T(8,128)S(1)}, f32[6,35,64]{2,1,0:T(8,128)S(1)}, u32[]{:S(2)}, u32[]{:S(2)}) collective-permute-start(f32[6,35,64]{2,1,0:T(8,128)S(1)} %slice_select_fusion.1), channel_id=1, source_target_pairs={{0,16},{8,24},{16,0},{24,8},{1,17},{9,25},{17,1},{25,9},{2,18},{10... | collective-permute-start | bytes 161288 | tf_op jit(solution)/shard_map/ppermute | solution.py:156
  60.6 3.4 %collective-permute-done.4 = f32[6,35,64]{2,1,0:T(8,128)S(1)} collective-permute-done((f32[6,35,64]{2,1,0:T(8,128)S(1)}, f32[6,35,64]{2,1,0:T(8,128)S(1)}, u32[]{:S(2)}, u32[]{:S(2)}) %collective-permute-start.4) | collective-permute-done | bytes 53792 | tf_op jit(solution)/shard_map/ppermute | solution.py:156
  64.3 1.2 %collective-permute-done.5 = f32[6,35,32]{2,1,0:T(8,128)S(1)} collective-permute-done((f32[6,35,32]{2,1,0:T(8,128)S(1)}, f32[6,35,32]{2,1,0:T(8,128)S(1)}, u32[]{:S(2)}, u32[]{:S(2)}) %collective-permute-start.5) | collective-permute-done | bytes 26912 | tf_op jit(solution)/shard_map/ppermute | solution.py:156
  65.8 0.2 fusion.21
  66.1 0.6 broadcast_in_dim.16
  66.7 5.7 %all-to-all-start = ((f32[32,1,60]{2,1,0:T(1,128)}), f32[32,1,60]{2,1,0:T(1,128)S(1)}, u32[]{:S(2)}, u32[]{:S(2)}) async-start(f32[32,1,60]{2,1,0:T(1,128)} %broadcast_in_dim.16), calls=%async_computation | async-start | bytes 32768 | tf_op jit(solution)/shard_map/all_to_all | solution.py:296
  72.5 0.9 %copy.259 = f32[1,13,35,128]{3,0,2,1:T(1,128)} copy(f32[1,13,35,128]{3,2,1,0:T(8,128)S(1)} %bitcast.783) | data formatting | bytes 465920
  73.6 5.9 %all-to-all-done = f32[32,1,60]{2,1,0:T(1,128)S(1)} async-done(((f32[32,1,60]{2,1,0:T(1,128)}), f32[32,1,60]{2,1,0:T(1,128)S(1)}, u32[]{:S(2)}, u32[]{:S(2)}) %all-to-all-start) | async-done | bytes 7712 | tf_op jit(solution)/shard_map/all_to_all | solution.py:296
  80.0 0.2 slice_reduce_fusion
  80.1 0.2 fusion.20
  80.3 0.6 neg.22
  (119 shorter events, 2.3 us)
Async XLA Ops:
  0.6 2.7 %copy-start.31 = (s32[128]{0:T(128)S(1)}, s32[128]{0:T(128)}, u32[]{:S(2)}) copy-start(s32[128]{0:T(128)} %param.35) | copy-start | bytes 1540
  0.6 10.6 %copy-start.34 = (f32[4,128]{1,0:T(4,128)S(1)}, f32[4,128]{1,0:T(4,128)}, u32[]{:S(2)}) copy-start(f32[4,128]{1,0:T(4,128)} %param.32) | copy-start | bytes 6148
  0.7 11.2 %copy-start.33 = (s32[4,128]{1,0:T(4,128)S(1)}, s32[4,128]{1,0:T(4,128)}, u32[]{:S(2)}) copy-start(s32[4,128]{1,0:T(4,128)} %param.34) | copy-start | bytes 6148
  0.7 11.2 %copy-start = (f32[6,35,128]{2,1,0:T(8,128)S(1)}, f32[6,35,128]{2,1,0:T(8,128)}, u32[]{:S(2)}) copy-start(f32[6,35,128]{2,1,0:T(8,128)} %param.28) | copy-start | bytes 322564
  0.7 11.2 %copy-start.30 = (s32[4,128]{1,0:T(4,128)S(1)}, s32[4,128]{1,0:T(4,128)}, u32[]{:S(2)}) copy-start(s32[4,128]{1,0:T(4,128)} %param.33) | copy-start | bytes 6148
  1.4 10.5 %copy-start.11 = (s32[1024]{0:T(1024)}, s32[1024]{0:T(1024)S(1)}, u32[]{:S(2)}) copy-start(s32[1024]{0:T(1024)S(1)} %pad_clamp_fusion) | copy-start | bytes 12292
  2.4 11.0 %copy-start.8 = (f32[1,2,13,35,128]{4,1,3,2,0:T(2,128)S(1)}, f32[1,2,13,35,128]{4,1,3,2,0:T(2,128)}, u32[]{:S(2)}) copy-start(f32[1,2,13,35,128]{4,1,3,2,0:T(2,128)} %param.27) | copy-start | bytes 1397764
  3.0 10.7 %copy-start.4 = (f32[1,13,35,128]{3,0,2,1:T(1,128)S(1)}, f32[1,13,35,128]{3,0,2,1:T(1,128)}, u32[]{:S(2)}) copy-start(f32[1,13,35,128]{3,0,2,1:T(1,128)} %param.26) | copy-start | bytes 698884
  3.0 10.7 %copy-start.7 = (f32[3,35,35,1]{2,1,3,0:T(8,128)S(1)}, f32[3,35,35,1]{2,1,3,0:T(8,128)}, u32[]{:S(2)}) copy-start(f32[3,35,35,1]{2,1,3,0:T(8,128)} %constant.68) | copy-start | bytes 44104
  4.4 23.5 %collective-permute-start = (f32[13,15,64]{2,1,0:T(8,128)}, f32[13,15,64]{2,1,0:T(8,128)}, u32[]{:S(2)}, u32[]{:S(2)}) collective-permute-start(f32[13,15,64]{2,1,0:T(8,128)} %get-tuple-element.38), channel_id=1, source_target_pairs={{0,1},{1,2},{2,3},{3,4},{4,5},{5,6},{6,7},{8,9},{9,10},{10,11},{11... | collective-permute-start | bytes 149768 | tf_op jit(solution)/shard_map/ppermute | solution.py:21
  9.9 18.0 %collective-permute-start.1 = (f32[13,15,64]{2,1,0:T(8,128)}, f32[13,15,64]{2,1,0:T(8,128)}, u32[]{:S(2)}, u32[]{:S(2)}) collective-permute-start(f32[13,15,64]{2,1,0:T(8,128)} %get-tuple-element.39), channel_id=1, source_target_pairs={{1,0},{2,1},{3,2},{4,3},{5,4},{6,5},{7,6},{9,8},{10,9},{11,10},{12... | collective-permute-start | bytes 149768 | tf_op jit(solution)/shard_map/ppermute | solution.py:22
  11.9 8.0 %copy-start.13 = (f32[6,35,128]{2,0,1:T(8,128)}, f32[6,35,128]{2,0,1:T(8,128)S(1)}, u32[]{:S(2)}) copy-start(f32[6,35,128]{2,0,1:T(8,128)S(1)} %copy.226) | copy-start | bytes 322564
  13.8 2.5 %copy-start.5 = (f32[5,6,35,128]{3,2,1,0:T(8,128)S(1)}, f32[5,6,35,128]{3,2,1,0:T(8,128)}, u32[]{:S(2)}) copy-start(f32[5,6,35,128]{3,2,1,0:T(8,128)} %param.37) | copy-start | bytes 1612804
  13.8 2.5 %copy-start.6 = (f32[5,6,35,128]{3,2,1,0:T(8,128)S(1)}, f32[5,6,35,128]{3,2,1,0:T(8,128)}, u32[]{:S(2)}) copy-start(f32[5,6,35,128]{3,2,1,0:T(8,128)} %param.36) | copy-start | bytes 1612804
  16.3 3.0 %copy-start.19 = (f32[3,3,128]{2,1,0:T(4,128)S(1)}, f32[3,3,128]{2,1,0:T(4,128)}, u32[]{:S(2)}) copy-start(f32[3,3,128]{2,1,0:T(4,128)} %param.30) | copy-start | bytes 13828
  18.1 1.5 %copy-start.22 = (f32[15,15]{1,0:T(8,128)S(1)}, f32[15,15]{1,0:T(8,128)}, u32[]{:S(2)}) copy-start(f32[15,15]{1,0:T(8,128)} %constant.61.clone) | copy-start | bytes 2704
  18.1 1.5 %copy-start.23 = (f32[15,15]{1,0:T(8,128)S(1)}, f32[15,15]{1,0:T(8,128)}, u32[]{:S(2)}) copy-start(f32[15,15]{1,0:T(8,128)} %constant.60.clone) | copy-start | bytes 2704
  18.1 1.5 %copy-start.24 = (f32[15,15]{1,0:T(8,128)S(1)}, f32[15,15]{1,0:T(8,128)}, u32[]{:S(2)}) copy-start(f32[15,15]{1,0:T(8,128)} %constant.59.clone) | copy-start | bytes 2704
  18.1 1.5 %copy-start.25 = (f32[15,15]{1,0:T(8,128)S(1)}, f32[15,15]{1,0:T(8,128)}, u32[]{:S(2)}) copy-start(f32[15,15]{1,0:T(8,128)} %constant.58.clone) | copy-start | bytes 2704
  18.1 1.5 %copy-start.26 = (f32[15,15]{1,0:T(8,128)S(1)}, f32[15,15]{1,0:T(8,128)}, u32[]{:S(2)}) copy-start(f32[15,15]{1,0:T(8,128)} %constant.57.clone) | copy-start | bytes 2704
  18.1 1.5 %copy-start.27 = (f32[15,15]{1,0:T(8,128)S(1)}, f32[15,15]{1,0:T(8,128)}, u32[]{:S(2)}) copy-start(f32[15,15]{1,0:T(8,128)} %constant.56.clone) | copy-start | bytes 2704
  18.1 1.8 %copy-start.35 = (f32[3,6,13,13]{3,2,1,0:T(8,128)S(1)}, f32[3,6,13,13]{3,2,1,0:T(8,128)}, u32[]{:S(2)}) copy-start(f32[3,6,13,13]{3,2,1,0:T(8,128)} %param.29) | copy-start | bytes 36508
  23.2 3.6 %copy-start.3 = (f32[3,13,35,128]{3,2,1,0:T(8,128)S(1)}, f32[3,13,35,128]{3,2,1,0:T(8,128)}, u32[]{:S(2)}) copy-start(f32[3,13,35,128]{3,2,1,0:T(8,128)} %convolution_bitcast_fusion) | copy-start | bytes 2096644
  24.0 9.4 %copy-start.28 = (f32[3,4,128]{2,0,1:T(4,128)}, f32[3,4,128]{2,0,1:T(4,128)S(1)}, u32[]{:S(2)}) copy-start(f32[3,4,128]{2,0,1:T(4,128)S(1)} %copy.230) | copy-start | bytes 18436
  29.0 4.4 %copy-start.10 = (f32[60,6,128]{2,1,0:T(8,128)S(1)}, f32[60,6,128]{2,1,0:T(8,128)}, u32[]{:S(2)}) copy-start(f32[60,6,128]{2,1,0:T(8,128)} %copy.283) | copy-start | bytes 552964
  29.0 4.4 %copy-start.36 = (f32[3,6,13,13]{3,2,1,0:T(8,128)S(1)}, f32[3,6,13,13]{3,2,1,0:T(8,128)}, u32[]{:S(2)}) copy-start(f32[3,6,13,13]{3,2,1,0:T(8,128)} %param.29) | copy-start | bytes 36508
  31.3 3.6 %copy-start.21 = (f32[4,128]{1,0:T(4,128)S(1)}, f32[4,128]{1,0:T(4,128)}, u32[]{:S(2)}) copy-start(f32[4,128]{1,0:T(4,128)} %broadcast_multiply_fusion.4) | copy-start | bytes 6148
  33.4 1.7 %copy-start.9 = (f32[13,35,128]{2,0,1:T(8,128)S(1)}, f32[13,35,128]{2,0,1:T(8,128)}, u32[]{:S(2)}) copy-start(f32[13,35,128]{2,0,1:T(8,128)} %fusion.3) | copy-start | bytes 698884
  33.4 1.7 %copy-start.15 = (f32[4,35,15,1]{1,2,0,3:T(8,128)S(1)}, f32[4,35,15,1]{1,2,0,3:T(8,128)}, u32[]{:S(2)}) copy-start(f32[4,35,15,1]{1,2,0,3:T(8,128)} %constant.69) | copy-start | bytes 25204
  33.4 2.3 %copy-start.12 = (s32[1024]{0:T(1024)S(1)}, s32[1024]{0:T(1024)}, u32[]{:S(2)}) copy-start(s32[1024]{0:T(1024)} %copy-done.11) | copy-start | bytes 12292
  34.9 3.6 %copy-start.32 = (s32[128]{0:T(128)S(1)}, s32[128]{0:T(128)}, u32[]{:S(2)}) copy-start(s32[128]{0:T(128)} %param.35) | copy-start | bytes 1540
  35.7 10.4 %copy-start.17 = (f32[3,35,35,1]{2,1,0,3:T(8,128)S(1)}, f32[3,35,35,1]{2,1,0,3:T(8,128)}, u32[]{:S(2)}) copy-start(f32[3,35,35,1]{2,1,0,3:T(8,128)} %constant.70) | copy-start | bytes 44104
  38.5 8.2 %copy-start.1 = (f32[3,13,35,128]{3,1,2,0:T(8,128)S(1)}, f32[3,13,35,128]{3,1,2,0:T(8,128)}, u32[]{:S(2)}) copy-start(f32[3,13,35,128]{3,1,2,0:T(8,128)} %copy.246) | copy-start | bytes 2096644
  38.5 8.2 %copy-start.2 = (f32[3,13,35,128]{3,1,2,0:T(8,128)S(1)}, f32[3,13,35,128]{3,1,2,0:T(8,128)}, u32[]{:S(2)}) copy-start(f32[3,13,35,128]{3,1,2,0:T(8,128)} %copy.250) | copy-start | bytes 2096644
  38.5 8.2 %copy-start.20 = (f32[3,3,128]{2,1,0:T(4,128)S(1)}, f32[3,3,128]{2,1,0:T(4,128)}, u32[]{:S(2)}) copy-start(f32[3,3,128]{2,1,0:T(4,128)} %param.30) | copy-start | bytes 13828
  39.4 12.1 %collective-permute-start.3 = (f32[13,15,64]{2,1,0:T(8,128)S(1)}, f32[13,15,64]{2,1,0:T(8,128)S(1)}, u32[]{:S(2)}, u32[]{:S(2)}) collective-permute-start(f32[13,15,64]{2,1,0:T(8,128)S(1)} %get-tuple-element.36), channel_id=1, source_target_pairs={{1,0},{2,1},{3,2},{4,3},{5,4},{6,5},{7,6},{9,8},{10,9},{11,10},{12... | collective-permute-start | bytes 149768 | tf_op jit(solution)/shard_map/ppermute | solution.py:22
  40.7 10.5 %collective-permute-start.2 = (f32[13,15,64]{2,1,0:T(8,128)S(1)}, f32[13,15,64]{2,1,0:T(8,128)S(1)}, u32[]{:S(2)}, u32[]{:S(2)}) collective-permute-start(f32[13,15,64]{2,1,0:T(8,128)S(1)} %get-tuple-element.37), channel_id=1, source_target_pairs={{0,1},{1,2},{2,3},{3,4},{4,5},{5,6},{6,7},{8,9},{9,10},{10,11},{11... | collective-permute-start | bytes 149768 | tf_op jit(solution)/shard_map/ppermute | solution.py:21
  46.7 2.3 %copy-start.37 = (f32[3,6,13,13]{3,2,1,0:T(8,128)S(1)}, f32[3,6,13,13]{3,2,1,0:T(8,128)}, u32[]{:S(2)}) copy-start(f32[3,6,13,13]{3,2,1,0:T(8,128)} %param.29) | copy-start | bytes 36508
  49.1 1.1 %copy-start.14 = (f32[6,35,128]{2,0,1:T(8,128)S(1)}, f32[6,35,128]{2,0,1:T(8,128)}, u32[]{:S(2)}) copy-start(f32[6,35,128]{2,0,1:T(8,128)} %copy-done.13) | copy-start | bytes 322564
  51.2 1.5 %copy-start.29 = (f32[3,4,128]{2,0,1:T(4,128)S(1)}, f32[3,4,128]{2,0,1:T(4,128)}, u32[]{:S(2)}) copy-start(f32[3,4,128]{2,0,1:T(4,128)} %copy-done.28) | copy-start | bytes 18436
  52.7 2.7 %copy-start.16 = (f32[4,35,15,1]{1,2,0,3:T(8,128)S(1)}, f32[4,35,15,1]{1,2,0,3:T(8,128)}, u32[]{:S(2)}) copy-start(f32[4,35,15,1]{1,2,0,3:T(8,128)} %constant.69) | copy-start | bytes 25204
  52.7 3.3 %copy-start.38 = (f32[3,6,13,13]{3,2,1,0:T(8,128)S(1)}, f32[3,6,13,13]{3,2,1,0:T(8,128)}, u32[]{:S(2)}) copy-start(f32[3,6,13,13]{3,2,1,0:T(8,128)} %param.29) | copy-start | bytes 36508
  56.0 8.3 %copy-start.18 = (f32[10,5]{1,0:T(8,128)S(1)}, f32[10,5]{1,0:T(8,128)}, u32[]{:S(2)}) copy-start(f32[10,5]{1,0:T(8,128)} %multiply_reduce_fusion.2) | copy-start | bytes 604
  59.0 4.9 %collective-permute-start.4 = (f32[6,35,64]{2,1,0:T(8,128)S(1)}, f32[6,35,64]{2,1,0:T(8,128)S(1)}, u32[]{:S(2)}, u32[]{:S(2)}) collective-permute-start(f32[6,35,64]{2,1,0:T(8,128)S(1)} %slice_select_fusion.1), channel_id=1, source_target_pairs={{0,16},{8,24},{16,0},{24,8},{1,17},{9,25},{17,1},{25,9},{2,18},{10... | collective-permute-start | bytes 161288 | tf_op jit(solution)/shard_map/ppermute | solution.py:156
  64.2 1.4 %collective-permute-start.5 = (f32[6,35,32]{2,1,0:T(8,128)S(1)}, f32[6,35,32]{2,1,0:T(8,128)S(1)}, u32[]{:S(2)}, u32[]{:S(2)}) collective-permute-start(f32[6,35,32]{2,1,0:T(8,128)S(1)} %slice_select_fusion), channel_id=1, source_target_pairs={{0,8},{8,0},{16,24},{24,16},{1,9},{9,1},{17,25},{25,17},{2,10},{10... | collective-permute-start | bytes 80648 | tf_op jit(solution)/shard_map/ppermute | solution.py:156
  66.7 12.8 %all-to-all-start = ((f32[32,1,60]{2,1,0:T(1,128)}), f32[32,1,60]{2,1,0:T(1,128)S(1)}, u32[]{:S(2)}, u32[]{:S(2)}) async-start(f32[32,1,60]{2,1,0:T(1,128)} %broadcast_in_dim.16), calls=%async_computation | async-start | bytes 32768 | tf_op jit(solution)/shard_map/all_to_all | solution.py:296

commit v19 on v16

--- a/solution.py
+++ b/solution.py
@@ -149,27 +149,19 @@
     )
 
 
-def halving_sum(values, axis, count):
+def halving_round(work, axis, count, bit):
     position = lax.axis_index(axis)
-    work = values
-    bit = count // 2
-    while bit >= 1:
-        width = work.shape[-1] // 2
-        upper = (position & bit) != 0
-        low = work[..., :width]
-        high = work[..., width:]
-        sent = lax.ppermute(
-            jnp.where(upper, low, high), axis, [(i, i ^ bit) for i in range(count)]
-        )
-        work = jnp.where(upper, high, low) + sent
-        bit //= 2
-    return work
-
-
-def search_direction(grad_share, step_share, change_share, gram, combine_sums):
+    width = work.shape[-1] // 2
+    upper = (position & bit) != 0
+    low = work[..., :width]
+    high = work[..., width:]
+    sent = lax.ppermute(jnp.where(upper, low, high), axis, [(i, i ^ bit) for i in range(count)])
+    return jnp.where(upper, high, low) + sent
+
+
+def search_direction(grad_share, with_grad, step_share, change_share, gram, combine_sums):
     pairs = step_share.shape[0]
     both_share = jnp.concatenate([step_share, change_share], axis=0)
-    with_grad = jnp.sum(both_share * grad_share[None], axis=(1, 2, 3))
     summed = combine_sums(jnp.concatenate([with_grad, gram.reshape(-1)]))
     lanes = 0.0 * step_share[0, 0, :8, :]
     summed = summed[:, None, None] + lanes[None]
@@ -268,6 +260,19 @@
     step_share = both_share[:pairs]
     change_share = both_share[pairs:]
     gram = jnp.sum(both_share[:, None] * change_share[None, :], axis=(2, 3, 4))
+    half_width = elements // 2
+    half_bit = shot_count // 2
+    half_start = ((lax.axis_index("shot") & half_bit) != 0).astype(jnp.int32) * half_width
+    half_pick = (
+        jnp.arange(elements, dtype=jnp.int32)[:, None]
+        == half_start + jnp.arange(half_width, dtype=jnp.int32)[None, :]
+    ).astype(jnp.float32)
+    both_half = jnp.einsum(
+        "ipae,ej->ipaj",
+        jnp.concatenate([history_steps, history_changes], axis=0),
+        half_pick,
+        precision=MIX,
+    )
     gradient = jnp.zeros((params, node_count, elements), jnp.float32)
     for step_index in range(forward_states.shape[1]):
         inner_trace = adjoint[:, face_nodes.T, :]
@@ -275,8 +280,8 @@
         sent_traces = jnp.einsum("fns,sj->fnj", flat_trace, send_pick, precision=MIX)
         extended = padded(sent_traces, (("mesh", 2),), border)
         if step_index == 0:
-            step_share, change_share, gram, extended = lax.optimization_barrier(
-                (step_share, change_share, gram, extended)
+            step_share, change_share, gram, both_half, extended = lax.optimization_barrier(
+                (step_share, change_share, gram, both_half, extended)
             )
         gathered = jnp.einsum("fns,sj->fnj", flat_trace, local_pick, precision=MIX)
         gathered = gathered + jnp.einsum(
@@ -300,8 +305,14 @@
         spread = jnp.broadcast_to(values[None], (device_count,) + values.shape)
         return jnp.sum(lax.all_to_all(spread, ("shot", "mesh"), 0, 0, tiled=False), axis=0)
 
-    grad_share = halving_sum(gradient, "shot", shot_count)
-    result = search_direction(grad_share, step_share, change_share, gram, combine_sums)
+    grad_half = halving_round(gradient, "shot", shot_count, half_bit)
+    with_grad = jnp.sum(both_half * grad_half[None], axis=(1, 2, 3))
+    grad_share = grad_half
+    bit = half_bit // 2
+    while bit >= 1:
+        grad_share = halving_round(grad_share, "shot", shot_count, bit)
+        bit //= 2
+    result = search_direction(grad_share, with_grad, step_share, change_share, gram, combine_sums)
     return (adjoint[None], result)
 
 

time: 76.2 us -> 95.3 us (1.25)
  local copies, waits for them, and re-layouts: 15.8 us -> 23.5 us
  matrix products: 17 us -> 22 us
  other arithmetic: 9.07 us -> 12.7 us
  waiting for transfers between devices: 11.5 us -> 13.9 us
    ppermute x2, waiting for transfers between devices: 0.99 us -> 4.99 us  [padded(): after = lax.ppermute(first, axis, down)]
    reshape x2, local copies, waits for them, and re-layouts: 0.29 us -> 3.86 us  [shards(): jump_trace = turned.reshape(fields, face_width, 4, elements) - inner_trace]
    ppermute x2, waiting for transfers between devices: 4.6 us -> 2.27 us  [halving_round(): lax.ppermute(jnp.where(upper, low, high), axis, [(i, i ^ bit) for i in ra...]
    sub x2, other arithmetic: 0.16 us -> 2.23 us  [shards(): jump_trace = turned.reshape(fields, face_width, 4, elements) - inner_trace]
    dot_general x2, matrix products: 0.92 us -> 2.86 us  [shards(): gathered = jnp.einsum('fns,sj->fnj', flat_trace, local_pick, precision=MIX)]
    gather x2, local copies, waits for them, and re-layouts: 1.64 us -> 3.24 us  [shards(): face_material = material[:, face_nodes.T, :]]
    unnamed x96 -> x111, local copies, waits for them, and re-layouts: 7.64 us -> 6.04 us
    reduce_sum x2, other arithmetic: 1.24 us -> 2.79 us  [shards(): turned = jnp.sum(gathered[:, :, None, :] * node_turn[None], axis=1)]
  transfers between devices with their start and end apart: 7 -> 7, of which waited for: 4 -> 3; matrix products, arithmetic and copies ran while one was open for 22% -> 23% of each run, Pallas kernels for 0% -> 0%
where the time goes in v19:
time: 95.3 us; the launch traced here: 94.5 us
  local copies, waits for them, and re-layouts  23.5 us (25%)
  matrix products  22 us (23%)
  starting transfers between devices  20.7 us (22%)
  waiting for transfers between devices  13.9 us (15%)
  other arithmetic  12.7 us (13%)
  between operations  1.62 us (2%)
    ppermute x2, starting transfers between devices, padded(): before = lax.ppermute(last, axis, up)  10.2 us
    all_to_all x1, waiting for transfers between devices, combine_sums(): lax.all_to_all(spread, ('shot', 'mesh'), 0, 0, tiled=False)  6.65 us
    all_to_all x1, starting transfers between devices, combine_sums(): lax.all_to_all(spread, ('shot', 'mesh'), 0, 0, tiled=False)  6.07 us
    unnamed x111, local copies, waits for them, and re-layouts  6.04 us
    ppermute x2, waiting for transfers between devices, padded(): after = lax.ppermute(first, axis, down)  4.99 us
    reshape x2, local copies, waits for them, and re-layouts, shards(): jump_trace = turned.reshape(fields, face_width, 4, elements) - inner_trace  3.86 us
    dot_general x2, matrix products, volume_term(): mixing = jnp.einsum('dpfg,dfae->pgae', coupling, spatial, precision=MIX)  3.29 us
    gather x4, local copies, waits for them, and re-layouts, shards(): inner_trace = adjoint[:, face_nodes.T, :]  3.25 us
  transfers between devices with their start and end apart: 7, of which 3 were waited for; matrix products, arithmetic and copies ran while one was open for 23% of the time, Pallas kernels for 0%

profile of v19, /device:TPU:0, one launch (start us, length us, event | category | flops | bytes accessed | tf_op | source)
XLA Modules:
  0.0 94.5 jit_solution(16594440077429283520)
XLA Ops:
  0.6 0.7 pad_clamp_fusion
  1.3 1.0 %copy.358 = f32[1,13,35,128]{3,1,2,0:T(8,128)S(1)} copy(f32[1,13,35,128]{3,0,2,1:T(1,128)} %param.26) | data formatting | bytes 465920
  2.3 0.6 gather_fusion.1
  3.3 0.3 fusion.33
  3.6 0.7 fusion.149
  4.3 5.5 %collective-permute-start = (f32[13,15,64]{2,1,0:T(8,128)}, f32[13,15,64]{2,1,0:T(8,128)}, u32[]{:S(2)}, u32[]{:S(2)}) collective-permute-start(f32[13,15,64]{2,1,0:T(8,128)} %get-tuple-element.52), channel_id=1, source_target_pairs={{0,1},{1,2},{2,3},{3,4},{4,5},{5,6},{6,7},{8,9},{9,10},{10,11},{11... | collective-permute-start | bytes 149768 | tf_op jit(solution)/shard_map/ppermute | solution.py:21
  9.8 1.3 %collective-permute-start.1 = (f32[13,15,64]{2,1,0:T(8,128)}, f32[13,15,64]{2,1,0:T(8,128)}, u32[]{:S(2)}, u32[]{:S(2)}) collective-permute-start(f32[13,15,64]{2,1,0:T(8,128)} %get-tuple-element.53), channel_id=1, source_target_pairs={{1,0},{2,1},{3,2},{4,3},{5,4},{6,5},{7,6},{9,8},{10,9},{11,10},{12... | collective-permute-start | bytes 149768 | tf_op jit(solution)/shard_map/ppermute | solution.py:22
  11.2 1.1 %constant_dynamic-update-slice_fusion = f32[10,6,35,128]{3,2,1,0:T(8,128)S(1)} fusion(f32[10,6,35,128]{3,2,1,0:T(8,128)S(1)} %constant_dynamic-update-slice_fusion.1, f32[5,6,35,128]{3,2,1,0:T(8,128)} %param.37), kind=kLoop, calls=%fused_computation.111 | loop fusion | bytes 1152000 | tf_op jit(solution)/shard_map/concatenate | solution.py:255
  12.3 1.6 %fusion.53 = f32[10,6,35,32]{2,3,1,0:T(8,128)S(1)} fusion(f32[10,6,35,128]{3,2,1,0:T(8,128)S(1)} %constant_dynamic-update-slice_fusion, s32[32]{0:T(128)S(1)} %iota_add_fusion.1), kind=kOutput, calls=%fused_computation.128 | convolution fusion | flops 51613696 | bytes 1344128 | tf_op jit(solution)/shard_map/ipae,ej->ipaj/dot_general | solution.py:253
  14.0 0.9 fusion.145
  14.9 0.6 multiply_reduce_fusion.2
  15.5 0.5 fusion.49
  16.5 1.2 %fusion.26 = f32[13,15,512]{2,1,0:T(8,128)} fusion(f32[13,15,512]{2,1,0:T(8,128)S(1)} %copy-done.2, pred[640,512]{1,0:T(32,128)(4,1)S(1)} %iota_compare_fusion), kind=kOutput, calls=%fused_computation.56 | convolution fusion | flops 306708480 | bytes 1087488 | tf_op jit(solution)/shard_map/fns,sj->fnj/dot_general | solution.py:286
  17.8 0.5 convolution_bitcast_fusion.3
  18.4 0.4 fusion.146
  18.8 0.5 convolution_bitcast_fusion
  19.5 0.5 convolution_bitcast_fusion.1
  20.3 0.7 copy-done.18
  21.0 1.6 %fusion.5 = f32[13,35,128]{2,0,1:T(8,128)} fusion(f32[3,13,35,128,1]{3,2,1,0,4:T(8,128)S(1)} %maximum_bitcast_fusion, f32[6,35,128]{2,0,1:T(8,128)S(1)} %copy.238, f32[3,6,13,13]{3,2,1,0:T(8,128)S(1)} %copy-done.18), kind=kOutput, calls=%fused_computation.17 | convolution fusion | flops 82409600 | bytes 1051528 | tf_op jit(solution)/shard_map/dpfg,dfae->pgae/dot_general | solution.py:133
  22.7 1.0 %maximum_bitcast_fusion.3 = f32[3,13,35,128,1]{3,2,1,0,4:T(8,128)} fusion(f32[1,13,35,128]{3,2,1,0:T(8,128)S(1)} %get-tuple-element.39, f32[1,13,35,128]{3,2,1,0:T(8,128)S(1)} %get-tuple-element.38, f32[1,13,35,128]{3,2,1,0:T(8,128)S(1)} %get-tuple-element.37), kind=kLoop, calls=%fused_computation.50 | loop fusion | flops 349440 | bytes 1397760 | tf_op jit(solution)/shard_map/stack | solution.py:128
  23.7 0.3 multiply_add_fusion
  23.9 1.0 %maximum_bitcast_fusion.2 = f32[3,13,35,128,1]{3,2,1,0,4:T(8,128)} fusion(f32[1,13,35,128]{3,2,1,0:T(8,128)S(1)} %get-tuple-element.36, f32[1,13,35,128]{3,2,1,0:T(8,128)S(1)} %get-tuple-element.35, f32[1,13,35,128]{3,2,1,0:T(8,128)S(1)} %get-tuple-element.34), kind=kLoop, calls=%fused_computation.49 | loop fusion | flops 349440 | bytes 1397760 | tf_op jit(solution)/shard_map/stack | solution.py:128
  24.9 1.5 %gather_fusion = f32[60,6,128]{2,0,1:T(8,128)} fusion(f32[6,35,128]{2,1,0:T(8,128)S(1)} %copy-done, s32[1024]{0:T(1024)S(1)} %pad_clamp_fusion), kind=kCustom, calls=%fused_computation | custom fusion | bytes 368880 | tf_op jit(solution)/shard_map/gather | solution.py:224
  26.4 1.7 %copy.298 = f32[60,6,128]{2,1,0:T(8,128)} copy(f32[60,6,128]{2,0,1:T(8,128)} %gather_fusion) | data formatting | bytes 368640 | tf_op jit(solution)/shard_map/gather | solution.py:224
  28.2 1.1 %pad_maximum_fusion = f32[13,15,256]{2,1,0:T(8,128)S(1)} fusion(f32[13,15,64]{2,1,0:T(8,128)} %collective-permute-done.1, f32[13,15,128]{2,1,0:T(8,128)S(1)} %copy-done.7, f32[13,15,64]{2,1,0:T(8,128)} %collective-permute-done), kind=kLoop, calls=%fused_computation.86 | loop fusion | flops 99840 | bytes 399360 | tf_op jit(solution)/shard_map/concatenate | solution.py:23
  29.3 1.3 %convolution_add_fusion.3 = f32[13,15,512]{2,1,0:T(8,128)S(1)} fusion(f32[13,15,512]{2,1,0:T(8,128)} %fusion.26, f32[13,15,256]{2,1,0:T(8,128)S(1)} %pad_maximum_fusion, pred[640,512]{1,0:T(32,128)(4,1)S(1)} %iota_compare_fusion), kind=kOutput, calls=%fused_computation.31 | convolution fusion | flops 38438400 | bytes 937984 | tf_op jit(solution)/shard_map/fns,sj->fnj/dot_general | solution.py:287
  30.6 0.3 convolution_add_fusion.2
  31.0 1.4 %multiply_reduce_fusion.1 = f32[13,15,512]{2,1,0:T(8,128)} fusion(f32[15,15,512]{2,1,0:T(8,128)S(1)} %multiply_add_fusion, f32[13,15,512]{2,1,0:T(8,128)S(1)} %convolution_add_fusion.2), kind=kLoop, calls=%fused_computation.4 | loop fusion | flops 2895360 | bytes 1259520 | tf_op jit(solution)/shard_map/reduce_sum | solution.py:293
  32.3 1.9 %reshape.373 = f32[13,15,4,128]{3,2,1,0:T(4,128)} reshape(f32[13,15,512]{2,1,0:T(8,128)} %multiply_reduce_fusion.1) | data formatting | bytes 798720 | tf_op jit(solution)/shard_map/reshape | solution.py:294
  34.3 1.1 %copy_subtract_fusion.1 = f32[13,15,4,128]{3,0,2,1:T(8,128)S(1)} fusion(f32[13,15,4,128]{3,0,2,1:T(8,128)S(1)} %bitcast.782, f32[13,15,4,128]{3,2,1,0:T(4,128)} %reshape.373), kind=kLoop, calls=%fused_computation.58 | loop fusion | flops 99840 | bytes 1198080 | tf_op jit(solution)/shard_map/sub | solution.py:294
  35.4 1.5 %fusion.1 = f32[13,15,4,128]{3,0,2,1:T(8,128)S(1)} fusion(f32[6,15,4,128]{3,0,2,1:T(8,128)S(1)} %bitcast.798, f32[13,15,4,128]{3,0,2,1:T(8,128)S(1)} %copy_subtract_fusion.1, f32[3,4,128]{2,0,1:T(4,128)S(1)} %copy.242, f32[3,6,13,13]{3,2,1,0:T(8,128)S(1)} %copy-done.19), kind=kOutput, calls=%fused_computation.9 | convolution fusion | flops 141573120 | bytes 1001352 | tf_op jit(solution)/shard_map/dpfg,dfnxe->pgnxe/dot_general | solution.py:145
  37.0 0.8 copy-done.11
  37.9 0.6 fusion.12
  38.5 1.4 %convolution_bitcast_fusion.2 = f32[3,13,35,128]{3,2,1,0:T(8,128)} fusion(f32[3,35,35,1]{2,1,3,0:T(8,128)S(1)} %copy-done.14, f32[13,35,128]{2,1,0:T(8,128)S(1)} %fusion.12), kind=kOutput, calls=%fused_computation.25 | convolution fusion | flops 36691200 | bytes 946540 | tf_op jit(solution)/shard_map/rab,fbe->rfae/dot_general | solution.py:121
  39.9 0.8 copy.252
  40.6 1.6 %gather_fusion.2 = f32[60,13,128]{2,1,0:T(8,128)S(1)} fusion(f32[13,35,128]{2,0,1:T(8,128)} %copy.252, s32[1024]{0:T(1024)S(1)} %pad_clamp_fusion), kind=kCustom, calls=%fused_computation.2 | custom fusion | bytes 798960 | tf_op jit(solution)/shard_map/gather | solution.py:278
  42.2 0.9 copy.253
  43.1 1.9 %reshape.374 = f32[13,15,512]{2,1,0:T(8,128)} reshape(f32[13,15,4,128]{3,2,1,0:T(4,128)} %copy.253) | data formatting | bytes 798720 | tf_op jit(solution)/shard_map/reshape | solution.py:279
  45.1 1.4 %fusion.31 = f32[13,15,128]{2,1,0:T(8,128)S(1)} fusion(f32[13,15,512]{2,1,0:T(8,128)} %reshape.374, s32[128]{0:T(128)S(1)} %copy-done.50), kind=kOutput, calls=%fused_computation.84 | convolution fusion | flops 76742656 | bytes 499712 | tf_op jit(solution)/shard_map/fns,sj->fnj/dot_general | solution.py:280
  46.5 1.6 %fusion.25 = f32[13,15,512]{2,1,0:T(8,128)S(1)} fusion(f32[13,15,512]{2,1,0:T(8,128)} %reshape.374, pred[640,512]{1,0:T(32,128)(4,1)S(1)} %iota_compare_fusion), kind=kOutput, calls=%fused_computation.55 | convolution fusion | flops 306708480 | bytes 1060864 | tf_op jit(solution)/shard_map/fns,sj->fnj/dot_general | solution.py:286
  48.4 4.7 %collective-permute-start.2 = (f32[13,15,64]{2,1,0:T(8,128)S(1)}, f32[13,15,64]{2,1,0:T(8,128)S(1)}, u32[]{:S(2)}, u32[]{:S(2)}) collective-permute-start(f32[13,15,64]{2,1,0:T(8,128)S(1)} %get-tuple-element.51), channel_id=1, source_target_pairs={{0,1},{1,2},{2,3},{3,4},{4,5},{5,6},{6,7},{8,9},{9,10},{10,11},{11... | collective-permute-start | bytes 149768 | tf_op jit(solution)/shard_map/ppermute | solution.py:21
  53.2 1.8 %fusion.3 = f32[6,35,128]{2,0,1:T(8,128)} fusion(f32[3,13,35,128,1]{3,2,1,0,4:T(8,128)S(1)} %copy-done.16, f32[13,35,128]{2,0,1:T(8,128)S(1)} %copy-done.8, f32[3,6,13,13]{3,2,1,0:T(8,128)S(1)} %copy-done.20), kind=kOutput, calls=%fused_computation.13 | convolution fusion | flops 82440960 | bytes 1051528 | tf_op jit(solution)/shard_map/dpfg,dgae->pfae/dot_general | solution.py:139
  55.0 0.8 copy-done.10
  55.8 1.6 %fusion.4 = f32[13,35,128]{2,0,1:T(8,128)} fusion(f32[3,13,35,128,1]{3,2,1,0,4:T(8,128)S(1)} %maximum_bitcast_fusion.1, f32[6,35,128]{2,0,1:T(8,128)S(1)} %copy-done.10, f32[3,6,13,13]{3,2,1,0:T(8,128)S(1)} %copy-done.20), kind=kOutput, calls=%fused_computation.15 | convolution fusion | flops 82409600 | bytes 1051528 | tf_op jit(solution)/shard_map/dpfg,dfae->pgae/dot_general | solution.py:133
  57.5 1.3 %collective-permute-start.3 = (f32[13,15,64]{2,1,0:T(8,128)S(1)}, f32[13,15,64]{2,1,0:T(8,128)S(1)}, u32[]{:S(2)}, u32[]{:S(2)}) collective-permute-start(f32[13,15,64]{2,1,0:T(8,128)S(1)} %get-tuple-element.50), channel_id=1, source_target_pairs={{1,0},{2,1},{3,2},{4,3},{5,4},{6,5},{7,6},{9,8},{10,9},{11,10},{12... | collective-permute-start | bytes 149768 | tf_op jit(solution)/shard_map/ppermute | solution.py:22
  58.8 0.3 convolution_add_fusion.1
  59.1 5.0 %collective-permute-done.3 = f32[13,15,64]{2,1,0:T(8,128)S(1)} collective-permute-done((f32[13,15,64]{2,1,0:T(8,128)S(1)}, f32[13,15,64]{2,1,0:T(8,128)S(1)}, u32[]{:S(2)}, u32[]{:S(2)}) %collective-permute-start.3) | collective-permute-done | bytes 49952 | tf_op jit(solution)/shard_map/ppermute | solution.py:22
  64.1 0.3 convolution_add_fusion
  64.4 1.4 %multiply_reduce_fusion = f32[13,15,512]{2,1,0:T(8,128)} fusion(f32[13,15,512]{2,1,0:T(8,128)S(1)} %convolution_add_fusion, f32[15,15,512]{2,1,0:T(8,128)S(1)} %multiply_add_fusion), kind=kLoop, calls=%fused_computation.3 | loop fusion | flops 2895360 | bytes 1259520 | tf_op jit(solution)/shard_map/reduce_sum | solution.py:293
  65.8 1.9 %reshape.375 = f32[13,15,4,128]{3,2,1,0:T(4,128)} reshape(f32[13,15,512]{2,1,0:T(8,128)} %multiply_reduce_fusion) | data formatting | bytes 798720 | tf_op jit(solution)/shard_map/reshape | solution.py:294
  67.7 1.1 %copy_subtract_fusion = f32[13,15,4,128]{3,0,2,1:T(8,128)S(1)} fusion(f32[13,15,4,128]{3,0,2,1:T(8,128)S(1)} %bitcast.784, f32[13,15,4,128]{3,2,1,0:T(4,128)} %reshape.375), kind=kLoop, calls=%fused_computation.57 | loop fusion | flops 99840 | bytes 1198080 | tf_op jit(solution)/shard_map/sub | solution.py:294
  68.8 1.5 %fusion = f32[13,15,4,128]{3,0,2,1:T(8,128)S(1)} fusion(f32[6,15,4,128]{3,0,2,1:T(8,128)S(1)} %bitcast.799, f32[13,15,4,128]{3,0,2,1:T(8,128)S(1)} %copy_subtract_fusion, f32[3,4,128]{2,0,1:T(4,128)S(1)} %copy-done.45, f32[3,6,13,13]{3,2,1,0:T(8,128)S(1)} %copy-done.21), kind=kOutput, calls=%fused_computation.7 | convolution fusion | flops 141573120 | bytes 1001352 | tf_op jit(solution)/shard_map/dpfg,dfnxe->pgnxe/dot_general | solution.py:145
  70.4 0.9 copy-done.12
  71.3 0.6 fusion.15
  72.0 0.5 copy-done.15
  72.4 1.1 %fusion.2 = f32[6,35,128]{2,0,1:T(8,128)S(1)} fusion(f32[3,13,35,128,1]{3,2,1,0,4:T(8,128)S(1)} %copy-done.15, f32[13,35,128]{2,0,1:T(8,128)S(1)} %copy.265, f32[3,6,13,13]{3,2,1,0:T(8,128)S(1)} %copy-done.21), kind=kOutput, calls=%fused_computation.11 | convolution fusion | flops 82440960 | bytes 1051528 | tf_op jit(solution)/shard_map/dpfg,dgae->pfae/dot_general | solution.py:139
  73.7 1.6 %collective-permute-start.4 = (f32[6,35,64]{2,1,0:T(8,128)S(1)}, f32[6,35,64]{2,1,0:T(8,128)S(1)}, u32[]{:S(2)}, u32[]{:S(2)}) collective-permute-start(f32[6,35,64]{2,1,0:T(8,128)S(1)} %slice_select_fusion.1), channel_id=1, source_target_pairs={{0,16},{8,24},{16,0},{24,8},{1,17},{9,25},{17,1},{25,9},{2,18},{10... | collective-permute-start | bytes 161288 | tf_op jit(solution)/shard_map/ppermute | solution.py:158
  75.5 0.9 copy.271
  76.4 2.3 %collective-permute-done.4 = f32[6,35,64]{2,1,0:T(8,128)S(1)} collective-permute-done((f32[6,35,64]{2,1,0:T(8,128)S(1)}, f32[6,35,64]{2,1,0:T(8,128)S(1)}, u32[]{:S(2)}, u32[]{:S(2)}) %collective-permute-start.4) | collective-permute-done | bytes 53792 | tf_op jit(solution)/shard_map/ppermute | solution.py:158
  79.1 0.6 broadcast_in_dim.16
  79.7 6.1 %all-to-all-start = ((f32[32,1,60]{2,1,0:T(1,128)}), f32[32,1,60]{2,1,0:T(1,128)S(1)}, u32[]{:S(2)}, u32[]{:S(2)}) async-start(f32[32,1,60]{2,1,0:T(1,128)} %broadcast_in_dim.16), calls=%async_computation | async-start | bytes 32768 | tf_op jit(solution)/shard_map/all_to_all | solution.py:306
  85.9 0.3 collective-permute-start.5
  86.2 6.6 %all-to-all-done = f32[32,1,60]{2,1,0:T(1,128)S(1)} async-done(((f32[32,1,60]{2,1,0:T(1,128)}), f32[32,1,60]{2,1,0:T(1,128)S(1)}, u32[]{:S(2)}, u32[]{:S(2)}) %all-to-all-start) | async-done | bytes 7712 | tf_op jit(solution)/shard_map/all_to_all | solution.py:306
  93.9 0.6 neg.22
  (153 shorter events, 3.8 us)
Async XLA Ops:
  2.3 1.0 %copy-start.49 = (s32[128]{0:T(128)S(1)}, s32[128]{0:T(128)}, u32[]{:S(2)}) copy-start(s32[128]{0:T(128)} %param.35) | copy-start | bytes 1540
  2.9 8.2 %copy-start.17 = (f32[5,6,35,128]{3,2,1,0:T(8,128)S(1)}, f32[5,6,35,128]{3,2,1,0:T(8,128)}, u32[]{:S(2)}) copy-start(f32[5,6,35,128]{3,2,1,0:T(8,128)} %param.36) | copy-start | bytes 1612804
  3.3 7.9 %copy-start.1 = (f32[13,15,512]{2,1,0:T(8,128)}, f32[13,15,512]{2,1,0:T(8,128)S(1)}, u32[]{:S(2)}) copy-start(f32[13,15,512]{2,1,0:T(8,128)S(1)} %reshape.372) | copy-start | bytes 1198084
  3.6 7.6 %copy-start.6 = (f32[13,15,128]{2,1,0:T(8,128)}, f32[13,15,128]{2,1,0:T(8,128)S(1)}, u32[]{:S(2)}) copy-start(f32[13,15,128]{2,1,0:T(8,128)S(1)} %fusion.33) | copy-start | bytes 299524
  4.3 23.9 %collective-permute-start = (f32[13,15,64]{2,1,0:T(8,128)}, f32[13,15,64]{2,1,0:T(8,128)}, u32[]{:S(2)}, u32[]{:S(2)}) collective-permute-start(f32[13,15,64]{2,1,0:T(8,128)} %get-tuple-element.52), channel_id=1, source_target_pairs={{0,1},{1,2},{2,3},{3,4},{4,5},{5,6},{6,7},{8,9},{9,10},{10,11},{11... | collective-permute-start | bytes 149768 | tf_op jit(solution)/shard_map/ppermute | solution.py:21
  9.8 18.4 %collective-permute-start.1 = (f32[13,15,64]{2,1,0:T(8,128)}, f32[13,15,64]{2,1,0:T(8,128)}, u32[]{:S(2)}, u32[]{:S(2)}) collective-permute-start(f32[13,15,64]{2,1,0:T(8,128)} %get-tuple-element.53), channel_id=1, source_target_pairs={{1,0},{2,1},{3,2},{4,3},{5,4},{6,5},{7,6},{9,8},{10,9},{11,10},{12... | collective-permute-start | bytes 149768 | tf_op jit(solution)/shard_map/ppermute | solution.py:22
  15.5 0.7 copy-start.48
  15.5 1.0 %copy-start.2 = (f32[13,15,512]{2,1,0:T(8,128)S(1)}, f32[13,15,512]{2,1,0:T(8,128)}, u32[]{:S(2)}) copy-start(f32[13,15,512]{2,1,0:T(8,128)} %copy-done.1) | copy-start | bytes 1198084
  16.0 1.7 %copy-start.51 = (s32[4,128]{1,0:T(4,128)S(1)}, s32[4,128]{1,0:T(4,128)}, u32[]{:S(2)}) copy-start(s32[4,128]{1,0:T(4,128)} %param.34) | copy-start | bytes 6148
  16.1 1.7 %copy-start.52 = (f32[4,128]{1,0:T(4,128)S(1)}, f32[4,128]{1,0:T(4,128)}, u32[]{:S(2)}) copy-start(f32[4,128]{1,0:T(4,128)} %param.32) | copy-start | bytes 6148
  16.1 1.7 %copy-start.47 = (f32[3,3,128]{2,1,0:T(4,128)S(1)}, f32[3,3,128]{2,1,0:T(4,128)}, u32[]{:S(2)}) copy-start(f32[3,3,128]{2,1,0:T(4,128)} %param.30) | copy-start | bytes 13828
  16.1 1.7 %copy-start.4 = (f32[1,13,35,128]{3,0,2,1:T(1,128)S(1)}, f32[1,13,35,128]{3,0,2,1:T(1,128)}, u32[]{:S(2)}) copy-start(f32[1,13,35,128]{3,0,2,1:T(1,128)} %param.26) | copy-start | bytes 698884
  16.1 1.7 %copy-start.13 = (f32[3,35,35,1]{2,1,3,0:T(8,128)S(1)}, f32[3,35,35,1]{2,1,3,0:T(8,128)}, u32[]{:S(2)}) copy-start(f32[3,35,35,1]{2,1,3,0:T(8,128)} %constant.71) | copy-start | bytes 44104
  16.2 2.2 %copy-start = (f32[6,35,128]{2,1,0:T(8,128)S(1)}, f32[6,35,128]{2,1,0:T(8,128)}, u32[]{:S(2)}) copy-start(f32[6,35,128]{2,1,0:T(8,128)} %param.28) | copy-start | bytes 322564
  16.5 1.9 %copy-start.22 = (f32[1,2,13,35,128]{4,1,3,2,0:T(2,128)S(1)}, f32[1,2,13,35,128]{4,1,3,2,0:T(2,128)}, u32[]{:S(2)}) copy-start(f32[1,2,13,35,128]{4,1,3,2,0:T(2,128)} %param.27) | copy-start | bytes 1397764
  17.8 2.2 %copy-start.28 = (f32[128]{0:T(128)}, f32[128]{0:T(128)S(1)}, u32[]{:S(2)}) copy-start(f32[128]{0:T(128)S(1)} %get-tuple-element.58) | copy-start | bytes 1540
  17.8 2.2 %copy-start.30 = (f32[128]{0:T(128)}, f32[128]{0:T(128)S(1)}, u32[]{:S(2)}) copy-start(f32[128]{0:T(128)S(1)} %get-tuple-element.59) | copy-start | bytes 1540
  17.8 2.2 %copy-start.32 = (f32[128]{0:T(128)}, f32[128]{0:T(128)S(1)}, u32[]{:S(2)}) copy-start(f32[128]{0:T(128)S(1)} %get-tuple-element.60) | copy-start | bytes 1540
  17.8 2.2 %copy-start.34 = (f32[128]{0:T(128)}, f32[128]{0:T(128)S(1)}, u32[]{:S(2)}) copy-start(f32[128]{0:T(128)S(1)} %get-tuple-element.61) | copy-start | bytes 1540
  17.8 2.2 %copy-start.36 = (f32[128]{0:T(128)}, f32[128]{0:T(128)S(1)}, u32[]{:S(2)}) copy-start(f32[128]{0:T(128)S(1)} %get-tuple-element.62) | copy-start | bytes 1540
  18.4 1.9 %copy-start.9 = (f32[6,35,128]{2,0,1:T(8,128)}, f32[6,35,128]{2,0,1:T(8,128)S(1)}, u32[]{:S(2)}) copy-start(f32[6,35,128]{2,0,1:T(8,128)S(1)} %copy.238) | copy-start | bytes 322564
  20.1 0.9 copy-start.18
  21.0 2.7 %copy-start.38 = (f32[15,15]{1,0:T(8,128)S(1)}, f32[15,15]{1,0:T(8,128)}, u32[]{:S(2)}) copy-start(f32[15,15]{1,0:T(8,128)} %constant.59.clone) | copy-start | bytes 2704
  21.0 2.7 %copy-start.39 = (f32[15,15]{1,0:T(8,128)S(1)}, f32[15,15]{1,0:T(8,128)}, u32[]{:S(2)}) copy-start(f32[15,15]{1,0:T(8,128)} %constant.60.clone) | copy-start | bytes 2704
  21.0 2.7 %copy-start.40 = (f32[15,15]{1,0:T(8,128)S(1)}, f32[15,15]{1,0:T(8,128)}, u32[]{:S(2)}) copy-start(f32[15,15]{1,0:T(8,128)} %constant.61.clone) | copy-start | bytes 2704
  21.0 2.7 %copy-start.41 = (f32[15,15]{1,0:T(8,128)S(1)}, f32[15,15]{1,0:T(8,128)}, u32[]{:S(2)}) copy-start(f32[15,15]{1,0:T(8,128)} %constant.62.clone) | copy-start | bytes 2704
  21.0 2.7 %copy-start.42 = (f32[15,15]{1,0:T(8,128)S(1)}, f32[15,15]{1,0:T(8,128)}, u32[]{:S(2)}) copy-start(f32[15,15]{1,0:T(8,128)} %constant.63.clone) | copy-start | bytes 2704
  21.0 2.7 %copy-start.43 = (f32[15,15]{1,0:T(8,128)S(1)}, f32[15,15]{1,0:T(8,128)}, u32[]{:S(2)}) copy-start(f32[15,15]{1,0:T(8,128)} %constant.64.clone) | copy-start | bytes 2704
  24.9 3.3 %copy-start.46 = (f32[3,4,128]{2,1,0:T(4,128)S(1)}, f32[3,4,128]{2,1,0:T(4,128)}, u32[]{:S(2)}) copy-start(f32[3,4,128]{2,1,0:T(4,128)} %param.31) | copy-start | bytes 18436
  24.9 3.3 %copy-start.7 = (f32[13,15,128]{2,1,0:T(8,128)S(1)}, f32[13,15,128]{2,1,0:T(8,128)}, u32[]{:S(2)}) copy-start(f32[13,15,128]{2,1,0:T(8,128)} %copy-done.6) | copy-start | bytes 299524
  28.2 7.2 %copy-start.44 = (f32[3,4,128]{2,0,1:T(4,128)}, f32[3,4,128]{2,0,1:T(4,128)S(1)}, u32[]{:S(2)}) copy-start(f32[3,4,128]{2,0,1:T(4,128)S(1)} %copy.242) | copy-start | bytes 18436
  34.3 1.1 %copy-start.19 = (f32[3,6,13,13]{3,2,1,0:T(8,128)S(1)}, f32[3,6,13,13]{3,2,1,0:T(8,128)}, u32[]{:S(2)}) copy-start(f32[3,6,13,13]{3,2,1,0:T(8,128)} %param.29) | copy-start | bytes 36508
  34.3 1.1 %copy-start.23 = (f32[60,6,128]{2,1,0:T(8,128)S(1)}, f32[60,6,128]{2,1,0:T(8,128)}, u32[]{:S(2)}) copy-start(f32[60,6,128]{2,1,0:T(8,128)} %copy.298) | copy-start | bytes 552964
  36.9 1.0 %copy-start.11 = (f32[13,35,128]{2,0,1:T(8,128)S(1)}, f32[13,35,128]{2,0,1:T(8,128)}, u32[]{:S(2)}) copy-start(f32[13,35,128]{2,0,1:T(8,128)} %fusion.5) | copy-start | bytes 698884
  36.9 1.0 %copy-start.26 = (f32[4,35,15,1]{1,2,0,3:T(8,128)S(1)}, f32[4,35,15,1]{1,2,0,3:T(8,128)}, u32[]{:S(2)}) copy-start(f32[4,35,15,1]{1,2,0,3:T(8,128)} %constant.72) | copy-start | bytes 25204
  36.9 1.6 %copy-start.14 = (f32[3,35,35,1]{2,1,3,0:T(8,128)S(1)}, f32[3,35,35,1]{2,1,3,0:T(8,128)}, u32[]{:S(2)}) copy-start(f32[3,35,35,1]{2,1,3,0:T(8,128)} %constant.71) | copy-start | bytes 44104
  40.6 4.4 %copy-start.50 = (s32[128]{0:T(128)S(1)}, s32[128]{0:T(128)}, u32[]{:S(2)}) copy-start(s32[128]{0:T(128)} %param.35) | copy-start | bytes 1540
  43.1 5.0 %copy-start.29 = (f32[128]{0:T(128)S(1)}, f32[128]{0:T(128)}, u32[]{:S(2)}) copy-start(f32[128]{0:T(128)} %copy-done.28) | copy-start | bytes 1540
  43.1 5.0 %copy-start.31 = (f32[128]{0:T(128)S(1)}, f32[128]{0:T(128)}, u32[]{:S(2)}) copy-start(f32[128]{0:T(128)} %copy-done.30) | copy-start | bytes 1540
  43.1 5.0 %copy-start.33 = (f32[128]{0:T(128)S(1)}, f32[128]{0:T(128)}, u32[]{:S(2)}) copy-start(f32[128]{0:T(128)} %copy-done.32) | copy-start | bytes 1540
  43.1 5.0 %copy-start.35 = (f32[128]{0:T(128)S(1)}, f32[128]{0:T(128)}, u32[]{:S(2)}) copy-start(f32[128]{0:T(128)} %copy-done.34) | copy-start | bytes 1540
  43.1 5.0 %copy-start.37 = (f32[128]{0:T(128)S(1)}, f32[128]{0:T(128)}, u32[]{:S(2)}) copy-start(f32[128]{0:T(128)} %copy-done.36) | copy-start | bytes 1540
  45.1 3.1 %copy-start.3 = (f32[3,13,35,128]{3,2,1,0:T(8,128)S(1)}, f32[3,13,35,128]{3,2,1,0:T(8,128)}, u32[]{:S(2)}) copy-start(f32[3,13,35,128]{3,2,1,0:T(8,128)} %convolution_bitcast_fusion.2) | copy-start | bytes 2096644
  48.2 5.0 %copy-start.8 = (f32[13,35,128]{2,0,1:T(8,128)S(1)}, f32[13,35,128]{2,0,1:T(8,128)}, u32[]{:S(2)}) copy-start(f32[13,35,128]{2,0,1:T(8,128)} %copy.252) | copy-start | bytes 698884
  48.2 5.0 %copy-start.16 = (f32[3,13,35,128,1]{3,2,1,0,4:T(8,128)S(1)}, f32[3,13,35,128,1]{3,2,1,0,4:T(8,128)}, u32[]{:S(2)}) copy-start(f32[3,13,35,128,1]{3,2,1,0,4:T(8,128)} %maximum_bitcast_fusion.2) | copy-start | bytes 2096644
  48.2 5.0 %copy-start.20 = (f32[3,6,13,13]{3,2,1,0:T(8,128)S(1)}, f32[3,6,13,13]{3,2,1,0:T(8,128)}, u32[]{:S(2)}) copy-start(f32[3,6,13,13]{3,2,1,0:T(8,128)} %param.29) | copy-start | bytes 36508
  48.4 10.3 %collective-permute-start.2 = (f32[13,15,64]{2,1,0:T(8,128)S(1)}, f32[13,15,64]{2,1,0:T(8,128)S(1)}, u32[]{:S(2)}, u32[]{:S(2)}) collective-permute-start(f32[13,15,64]{2,1,0:T(8,128)S(1)} %get-tuple-element.51), channel_id=1, source_target_pairs={{0,1},{1,2},{2,3},{3,4},{4,5},{5,6},{6,7},{8,9},{9,10},{10,11},{11... | collective-permute-start | bytes 149768 | tf_op jit(solution)/shard_map/ppermute | solution.py:21
  54.9 0.9 copy-start.10
  57.5 6.6 %collective-permute-start.3 = (f32[13,15,64]{2,1,0:T(8,128)S(1)}, f32[13,15,64]{2,1,0:T(8,128)S(1)}, u32[]{:S(2)}, u32[]{:S(2)}) collective-permute-start(f32[13,15,64]{2,1,0:T(8,128)S(1)} %get-tuple-element.50), channel_id=1, source_target_pairs={{1,0},{2,1},{3,2},{4,3},{5,4},{6,5},{7,6},{9,8},{10,9},{11,10},{12... | collective-permute-start | bytes 149768 | tf_op jit(solution)/shard_map/ppermute | solution.py:22
  65.8 3.1 %copy-start.21 = (f32[3,6,13,13]{3,2,1,0:T(8,128)S(1)}, f32[3,6,13,13]{3,2,1,0:T(8,128)}, u32[]{:S(2)}) copy-start(f32[3,6,13,13]{3,2,1,0:T(8,128)} %param.29) | copy-start | bytes 36508
  65.8 3.1 %copy-start.45 = (f32[3,4,128]{2,0,1:T(4,128)S(1)}, f32[3,4,128]{2,0,1:T(4,128)}, u32[]{:S(2)}) copy-start(f32[3,4,128]{2,0,1:T(4,128)} %copy-done.44) | copy-start | bytes 18436
  67.7 1.1 %copy-start.24 = (f32[60,6,128]{2,1,0:T(8,128)S(1)}, f32[60,6,128]{2,1,0:T(8,128)}, u32[]{:S(2)}) copy-start(f32[60,6,128]{2,1,0:T(8,128)} %copy.298) | copy-start | bytes 552964
  70.3 1.0 %copy-start.12 = (f32[13,35,128]{2,0,1:T(8,128)S(1)}, f32[13,35,128]{2,0,1:T(8,128)}, u32[]{:S(2)}) copy-start(f32[13,35,128]{2,0,1:T(8,128)} %fusion.4) | copy-start | bytes 698884
  70.3 1.0 %copy-start.27 = (f32[4,35,15,1]{1,2,0,3:T(8,128)S(1)}, f32[4,35,15,1]{1,2,0,3:T(8,128)}, u32[]{:S(2)}) copy-start(f32[4,35,15,1]{1,2,0,3:T(8,128)} %constant.72) | copy-start | bytes 25204
  71.3 1.1 %copy-start.15 = (f32[3,13,35,128,1]{3,2,1,0,4:T(8,128)S(1)}, f32[3,13,35,128,1]{3,2,1,0,4:T(8,128)}, u32[]{:S(2)}) copy-start(f32[3,13,35,128,1]{3,2,1,0,4:T(8,128)} %maximum_bitcast_fusion.3) | copy-start | bytes 2096644
  71.9 1.7 %copy-start.25 = (f32[6,35,128]{2,0,1:T(8,128)S(1)}, f32[6,35,128]{2,0,1:T(8,128)}, u32[]{:S(2)}) copy-start(f32[6,35,128]{2,0,1:T(8,128)} %fusion.3) | copy-start | bytes 322564
  72.4 2.9 %copy-start.5 = (f32[5,6,35,32]{2,3,1,0:T(8,128)S(1)}, f32[5,6,35,32]{2,3,1,0:T(8,128)}, u32[]{:S(2)}) copy-start(f32[5,6,35,32]{2,3,1,0:T(8,128)} %get-tuple-element.10) | copy-start | bytes 403204
  73.7 4.9 %collective-permute-start.4 = (f32[6,35,64]{2,1,0:T(8,128)S(1)}, f32[6,35,64]{2,1,0:T(8,128)S(1)}, u32[]{:S(2)}, u32[]{:S(2)}) collective-permute-start(f32[6,35,64]{2,1,0:T(8,128)S(1)} %slice_select_fusion.1), channel_id=1, source_target_pairs={{0,16},{8,24},{16,0},{24,8},{1,17},{9,25},{17,1},{25,9},{2,18},{10... | collective-permute-start | bytes 161288 | tf_op jit(solution)/shard_map/ppermute | solution.py:158
  79.7 13.2 %all-to-all-start = ((f32[32,1,60]{2,1,0:T(1,128)}), f32[32,1,60]{2,1,0:T(1,128)S(1)}, u32[]{:S(2)}, u32[]{:S(2)}) async-start(f32[32,1,60]{2,1,0:T(1,128)} %broadcast_in_dim.16), calls=%async_computation | async-start | bytes 32768 | tf_op jit(solution)/shard_map/all_to_all | solution.py:306
  85.9 7.6 %collective-permute-start.5 = (f32[6,35,32]{2,1,0:T(8,128)S(1)}, f32[6,35,32]{2,1,0:T(8,128)S(1)}, u32[]{:S(2)}, u32[]{:S(2)}) collective-permute-start(f32[6,35,32]{2,1,0:T(8,128)S(1)} %slice_select_fusion), channel_id=1, source_target_pairs={{0,8},{8,0},{16,24},{24,16},{1,9},{9,1},{17,25},{25,17},{2,10},{10... | collective-permute-start | bytes 80648 | tf_op jit(solution)/shard_map/ppermute | solution.py:158
